TPU v7x, 32 devices: a whole 2x2x4 slice. The times are simulated.
32 devices in a mesh: req: 8 (over y, x, core), kv: 4 (over z).
Axes of the slice: x: 2, y: 2, z: 4, core: 2. Of those that a mesh axis runs over, the one named last changes fastest.
Arguments:
- hidden: bfloat16 [128, 8192], P('req', 'kv')
- cache_len: int32 [2, 128], replicated, may hold values from 1 to 4096, as said below
- request_serving_order: int32 [128], replicated, may hold values from 0 to 127, as said below
- rotated_key_cache: bfloat16 [2, 65536, 1024], P(None, 'req', 'kv'), as said below
- stored_value_cache: bfloat16 [2, 65536, 1024], P(None, 'req', 'kv'), may hold values from -6 to 6
- attn_gain: bfloat16 [8192], P('kv'), may hold values from 0.099609375 to 1.8984375
- w_query: bfloat16 [8192, 8192], P('req', 'kv'), may hold values from -0.0625 to 0.0625
- key_projection_weight: bfloat16 [8192, 1024], P('req', 'kv'), may hold values from -0.0625 to 0.0625
- value_projection_weight: bfloat16 [8192, 1024], P('req', 'kv'), may hold values from -0.0625 to 0.0625
- b_query: bfloat16 [8192], P('kv'), may hold values from -3 to 3
- key_bias: bfloat16 [1024], P('kv'), may hold values from -4.5 to 4.5
- value_bias: bfloat16 [1024], P('kv'), may hold values from -4.5 to 4.5
- w_out: bfloat16 [8192, 8192], P('req', 'kv'), may hold values from -0.0625 to 0.0625
- mlp_gain: bfloat16 [8192], P('kv'), may hold values from 0.099609375 to 1.8984375
- w_gate: bfloat16 [8192, 29568], P('kv', 'req'), may hold values from -0.0625 to 0.0625
- w_up: bfloat16 [8192, 29568], P('kv', 'req'), may hold values from -0.0625 to 0.0625
- w_down: bfloat16 [29568, 8192], P('req', 'kv'), may hold values from -0.03125 to 0.03125
Outputs:
- residual: float32 [128, 8192], P('req', 'kv')
Inputs may be any that keep to these rules, and one draw needn't show every extreme that they name: `request_serving_order`: A permutation of the requests. `cache_len`: in each layer the caches of the requests of one serving index of req sum to at most 8192 rows, and to exactly 8192 for one index; some request of that index has exactly 4096. `rotated_key_cache`: rows of an index beyond its requests' caches hold no cached tokens.
All inputs are finite; a program needn't handle non-finite values.
Results may differ from a plain program's by a relative error of at most 0.015.
Values may be sent and summed in bfloat16 or wider, within the bound.
No kernel may reach another device: no remote copies, remote signals or barrier semaphores. Data moves between devices by JAX's collectives and lax.ppermute only.
A program may use at most 256 MiB of HBM per device.

v0:
```python
import math

import jax
import jax.numpy as jnp
from jax import lax
from jax.sharding import PartitionSpec as P

MODEL_WIDTH = 8192
HEAD_SIZE = 128
LAYER_COUNT = 2


EPS = 1e-06
LOG_BASE = math.log(1000000.0)


def broadcast(block, axis, owner):
    block = jnp.where(lax.axis_index(axis) == owner, block, jnp.zeros_like(block))
    return lax.psum(block, axis)


def apply_rotation(values, token_positions):
    half_width = values.shape[-1] // 2
    frequency = jnp.exp(
        -LOG_BASE * jnp.arange(half_width, dtype=jnp.float32) * 2.0 / values.shape[-1]
    )
    angles = token_positions[:, None] * frequency[None, :]
    reshape_to = (angles.shape[0],) + (1,) * (values.ndim - 2) + (half_width,)
    cosine = jnp.cos(angles).reshape(reshape_to)
    sine_part = jnp.sin(angles).reshape(reshape_to)
    front_half = values[..., :half_width]
    back_half = values[..., half_width:]
    return jnp.concatenate(
        [front_half * cosine - back_half * sine_part, back_half * cosine + front_half * sine_part],
        axis=-1,
    )


def normalize(residual, gains):
    square_sum = jnp.sum(residual * residual, axis=1)
    all_squares = lax.psum(square_sum, "kv")
    inv_norm = lax.rsqrt(all_squares / MODEL_WIDTH + EPS)
    return (residual * inv_norm[:, None] * gains.astype(jnp.float32)[None, :]).astype(jnp.bfloat16)


def attend(query_rows, fresh_key, fresh_value, cached_keys, cached_values, lengths):
    score_scale = 1.0 / math.sqrt(query_rows.shape[-1])
    finish = jnp.cumsum(lengths)
    starts = finish - lengths
    capacity = cached_keys.shape[0]
    block_size = min(512, capacity)
    block_count = capacity // block_size
    self_score = (
        jnp.einsum("igrd,igd->igr", query_rows, fresh_key, preferred_element_type=jnp.float32)
        * score_scale
    )
    start_out = fresh_value.astype(jnp.float32)[:, :, None, :] * jnp.ones(
        query_rows.shape, jnp.float32
    )

    def one_block(block_index, carried):
        running_max, running_sum, accumulated = carried
        first_row = block_index * block_size
        key_block = lax.dynamic_slice_in_dim(cached_keys, first_row, block_size, 0)
        value_block = lax.dynamic_slice_in_dim(cached_values, first_row, block_size, 0)
        scores = (
            jnp.einsum("igrd,tgd->igrt", query_rows, key_block, preferred_element_type=jnp.float32)
            * score_scale
        )
        key_rows = first_row + jnp.arange(block_size, dtype=jnp.int32)
        inside = (key_rows[None, :] >= starts[:, None]) & (key_rows[None, :] < finish[:, None])
        inside = inside[:, None, None, :]
        block_max = jnp.max(jnp.where(inside, scores, -jnp.inf), axis=-1)
        new_max = jnp.maximum(running_max, block_max)
        exps = jnp.where(inside, jnp.exp(scores - new_max[..., None]), 0.0)
        rescale = jnp.exp(running_max - new_max)
        new_sum = running_sum * rescale + jnp.sum(exps, axis=-1)
        contribution = jnp.einsum(
            "igrt,tgd->igrd",
            exps.astype(jnp.bfloat16),
            value_block,
            preferred_element_type=jnp.float32,
        )
        return (new_max, new_sum, accumulated * rescale[..., None] + contribution)

    running_max, running_sum, accumulated = lax.fori_loop(
        0, block_count, one_block, (self_score, jnp.ones_like(self_score), start_out)
    )
    return (accumulated / running_sum[..., None]).astype(jnp.bfloat16)


def body(
    hidden,
    cache_len,
    request_serving_order,
    rotated_key_cache,
    stored_value_cache,
    attn_gain,
    w_query,
    key_projection_weight,
    value_projection_weight,
    b_query,
    key_bias,
    value_bias,
    w_out,
    mlp_gain,
    w_gate,
    w_up,
    w_down,
):
    req_size = lax.axis_size("req")
    kv_size = lax.axis_size("kv")
    group_ratio = req_size // kv_size
    req_index = lax.axis_index("req")
    own_rows = hidden.shape[0]
    head_dim = HEAD_SIZE
    query_width = w_query.shape[1]
    key_width = key_projection_weight.shape[1]
    kv_heads = key_width // head_dim
    capacity = rotated_key_cache.shape[1]
    w_joint = jnp.concatenate([w_query, key_projection_weight, value_projection_weight], axis=1)
    b_joint = jnp.concatenate([b_query, key_bias, value_bias]).astype(jnp.float32)
    inverse = jnp.argsort(request_serving_order)
    my_slots = lax.dynamic_slice_in_dim(request_serving_order, req_index * own_rows, own_rows)
    residual = hidden.astype(jnp.float32)
    for current_layer_index in range(LAYER_COUNT):
        normed = normalize(residual, attn_gain)
        gathered = lax.all_gather(normed, "req", axis=0, tiled=True)
        slab_width = gathered.shape[1] // group_ratio
        portion = lax.dynamic_slice_in_dim(
            gathered, req_index % group_ratio * slab_width, slab_width, 1
        )
        columns = broadcast(portion, "kv", req_index // group_ratio)
        picked = jnp.take(columns, request_serving_order, axis=0)
        combined = (
            lax.psum_scatter(
                jnp.dot(picked, w_joint, preferred_element_type=jnp.float32),
                "req",
                scatter_dimension=0,
                tiled=True,
            )
            + b_joint[None, :]
        )
        lengths = jnp.take(cache_len[current_layer_index], my_slots)
        token_positions = lengths.astype(jnp.float32)
        query_rows = apply_rotation(
            combined[:, :query_width].reshape(own_rows, kv_heads, -1, head_dim), token_positions
        ).astype(jnp.bfloat16)
        fresh_key = apply_rotation(
            combined[:, query_width : query_width + key_width].reshape(
                own_rows, kv_heads, head_dim
            ),
            token_positions,
        ).astype(jnp.bfloat16)
        fresh_value = (
            combined[:, query_width + key_width :]
            .reshape(own_rows, kv_heads, head_dim)
            .astype(jnp.bfloat16)
        )
        cached_keys = rotated_key_cache[current_layer_index].reshape(capacity, kv_heads, head_dim)
        cached_values = stored_value_cache[current_layer_index].reshape(
            capacity, kv_heads, head_dim
        )
        attention_output = attend(
            query_rows, fresh_key, fresh_value, cached_keys, cached_values, lengths
        ).reshape(own_rows, query_width)
        heads_gathered = lax.all_gather(attention_output, "req", axis=0, tiled=True)
        head_width = heads_gathered.shape[1] // group_ratio
        head_portion = lax.dynamic_slice_in_dim(
            heads_gathered, req_index % group_ratio * head_width, head_width, 1
        )
        head_rows = broadcast(head_portion, "kv", req_index // group_ratio)
        project_picked = jnp.take(head_rows, inverse, axis=0)
        residual = residual + lax.psum_scatter(
            jnp.dot(project_picked, w_out, preferred_element_type=jnp.float32),
            "req",
            scatter_dimension=0,
            tiled=True,
        )
        normed_mlp = normalize(residual, mlp_gain)
        tokens = lax.all_gather(normed_mlp, "req", axis=0, tiled=True)
        hidden_cols = w_gate.shape[1]
        gate_up = lax.psum_scatter(
            jnp.concatenate(
                [
                    jnp.dot(tokens, w_gate, preferred_element_type=jnp.float32),
                    jnp.dot(tokens, w_up, preferred_element_type=jnp.float32),
                ],
                axis=1,
            ),
            "kv",
            scatter_dimension=0,
            tiled=True,
        )
        local_hidden = (jax.nn.silu(gate_up[:, :hidden_cols]) * gate_up[:, hidden_cols:]).astype(
            jnp.bfloat16
        )
        hidden_all = lax.all_gather(local_hidden, "kv", axis=0, tiled=True)
        residual = residual + lax.psum_scatter(
            jnp.dot(hidden_all, w_down, preferred_element_type=jnp.float32),
            "req",
            scatter_dimension=0,
            tiled=True,
        )
    return residual


def solution(mesh):
    return jax.shard_map(
        body,
        mesh=mesh,
        in_specs=(
            P("req", "kv"),
            P(),
            P(),
            P(None, "req", "kv"),
            P(None, "req", "kv"),
            P("kv"),
            P("req", "kv"),
            P("req", "kv"),
            P("req", "kv"),
            P("kv"),
            P("kv"),
            P("kv"),
            P("req", "kv"),
            P("kv"),
            P("kv", "req"),
            P("kv", "req"),
            P("req", "kv"),
        ),
        out_specs=P("req", "kv"),
        check_vma=False,
    )
```

profile of v0, /device:TPU:18, one launch (start us, length us, event | category | flops | bytes accessed | tf_op | source)
XLA Modules:
  0.0 850.0 jit_solution(730094470468017407)
XLA Ops:
  8.2 9.0 %psum.56 = f32[16]{0:T(128)S(1)} all-reduce(f32[16]{0:T(128)S(1)} %fusion.46), channel_id=1, replica_groups=mesh['req'=8,'kv'=4] {'kv'}, use_global_device_ids=true, to_apply=%region_1.2 | all-reduce | flops 16 | bytes 128 | tf_op jit(solution)/shard_map/psum | solution.py:41
  18.1 9.9 %all_gather.24 = bf16[128,2048]{1,0:T(8,128)(2,1)S(1)} all-gather(bf16[16,2048]{1,0:T(8,128)(2,1)S(1)} %fusion.48), channel_id=1, replica_groups=mesh['req'=8,'kv'=4] {'req'}, dimensions={0}, use_global_device_ids=true | all-gather | bytes 589824 | tf_op jit(solution)/shard_map/all_gather | solution.py:128
  29.5 4.8 constant_dynamic-update-slice_fusion.2
  35.8 5.9 fusion.72
  44.0 6.4 copy.108
  50.4 13.7 %all-reduce.5.cloned.1.call-done = bf16[128,1024]{1,0:T(8,128)(2,1)} async-done(((bf16[128,1024]{1,0:T(8,128)(2,1)}), bf16[128,1024]{1,0:T(8,128)(2,1)}) %all-reduce.5.cloned.1.call-update) | async-done | bytes 262160 | tf_op jit(solution)/shard_map/psum | solution.py:19
  66.1 4.4 fusion.40
  70.7 5.8 fusion.71
  76.5 6.5 copy.109
  83.0 2.6 sort.17
  85.9 22.2 %reduce-scatter.13.cloned.1.call-done = f32[16,2560]{1,0:T(8,128)} async-done(((f32[128,2560]{1,0:T(8,128)}), f32[16,2560]{1,0:T(8,128)}) %reduce-scatter.13.cloned.1.call-update) | async-done | bytes 163856 | tf_op jit(solution)/shard_map/reduce_scatter | solution.py:136
  109.8 46.3 %while.36 = (s32[]{:T(128)}, f32[16,2,8]{0,2,1:T(8,128)S(1)}, f32[16,2,8]{0,2,1:T(8,128)S(1)}, f32[16,2,8,128]{3,0,2,1:T(8,128)S(1)}, s32[16]{0:T(128)S(1)}, /*i...) while((s32[]{:T(128)}, f32[16,2,8]{0,2,1:T(8,128)S(1)}, ...), condition=%wide.region_8.11_spmd.clone, body=%wide.region_5.10_spmd.clone.sunk | while | flops 68379904 | bytes 2478401 | solution.py:86
  156.4 9.0 %all_gather.25 = bf16[128,2048]{1,0:T(8,128)(2,1)S(1)} all-gather(bf16[16,2048]{1,0:T(8,128)(2,1)S(1)} %bitcast.130), channel_id=1, replica_groups=mesh['req'=8,'kv'=4] {'req'}, dimensions={0}, use_global_device_ids=true | all-gather | bytes 589824 | tf_op jit(solution)/shard_map/all_gather | solution.py:167
  166.2 36.0 %all-reduce.7.cloned.1.call-done = bf16[128,1024]{1,0:T(8,128)(2,1)} async-done(((bf16[128,1024]{1,0:T(8,128)(2,1)}), bf16[128,1024]{1,0:T(8,128)(2,1)}) %all-reduce.7.cloned.1.call-update) | async-done | bytes 262160 | tf_op jit(solution)/shard_map/psum | solution.py:19
  204.2 3.9 fusion.38
  208.2 36.1 %reduce-scatter.15.cloned.1.call-done = f32[16,2048]{1,0:T(8,128)} async-done(((f32[128,2048]{1,0:T(8,128)}), f32[16,2048]{1,0:T(8,128)}) %reduce-scatter.15.cloned.1.call-update) | async-done | bytes 131088 | tf_op jit(solution)/shard_map/reduce_scatter | solution.py:174
  245.4 8.9 %psum.59 = f32[16]{0:T(128)S(1)} all-reduce(f32[16]{0:T(128)S(1)} %multiply_reduce_fusion.2), channel_id=1, replica_groups=mesh['req'=8,'kv'=4] {'kv'}, use_global_device_ids=true, to_apply=%region_13.16 | all-reduce | flops 16 | bytes 128 | tf_op jit(solution)/shard_map/psum | solution.py:41
  255.3 9.1 %all_gather.26 = bf16[128,2048]{1,0:T(8,128)(2,1)S(1)} all-gather(bf16[16,2048]{1,0:T(8,128)(2,1)S(1)} %multiply_convert_fusion.2), channel_id=1, replica_groups=mesh['req'=8,'kv'=4] {'req'}, dimensions={0}, use_global_device_ids=true | all-gather | bytes 589824 | tf_op jit(solution)/shard_map/all_gather | solution.py:181
  264.4 7.6 fusion.75
  272.1 7.6 fusion.76
  279.7 2.1 pad_maximum_fusion
  281.7 5.3 copy.98
  287.1 71.9 %reduce-scatter.25.cloned.1.call-done = f32[32,7392]{1,0:T(8,128)} async-done(((f32[128,7392]{1,0:T(8,128)}), f32[32,7392]{1,0:T(8,128)}) %reduce-scatter.25.cloned.1.call-update) | async-done | bytes 946192 | tf_op jit(solution)/shard_map/reduce_scatter | solution.py:183
  360.4 18.8 %all_gather.27 = bf16[128,3696]{1,0:T(8,128)(2,1)S(1)} all-gather(bf16[32,3696]{1,0:T(8,128)(2,1)S(1)} %fusion.33), channel_id=1, replica_groups=mesh['req'=8,'kv'=4] {'kv'}, dimensions={0}, use_global_device_ids=true | all-gather | bytes 1182720 | tf_op jit(solution)/shard_map/all_gather | solution.py:198
  379.3 8.7 %fusion.77 = f32[128,2048]{1,0:T(8,128)} fusion(bf16[128,3696]{1,0:T(8,128)(2,1)S(1)} %all_gather.27, bf16[3696,2048]{1,0:T(8,128)(2,1)} %param.41), kind=kOutput, calls=%fused_computation.167 | convolution fusion | flops 1937768448 | bytes 17133568 | tf_op jit(solution)/shard_map/dot_general | solution.py:200
  388.1 37.4 %reduce-scatter.17.cloned.1.call-done = f32[16,2048]{1,0:T(8,128)} async-done(((f32[128,2048]{1,0:T(8,128)}), f32[16,2048]{1,0:T(8,128)}) %reduce-scatter.17.cloned.1.call-update) | async-done | bytes 131088 | tf_op jit(solution)/shard_map/reduce_scatter | solution.py:199
  426.5 8.9 %psum.60 = f32[16]{0:T(128)S(1)} all-reduce(f32[16]{0:T(128)S(1)} %get-tuple-element.479), channel_id=1, replica_groups=mesh['req'=8,'kv'=4] {'kv'}, use_global_device_ids=true, to_apply=%region_17.20 | all-reduce | flops 16 | bytes 128 | tf_op jit(solution)/shard_map/psum | solution.py:41
  435.5 9.0 %all_gather.28 = bf16[128,2048]{1,0:T(8,128)(2,1)S(1)} all-gather(bf16[16,2048]{1,0:T(8,128)(2,1)S(1)} %multiply_convert_fusion.1), channel_id=1, replica_groups=mesh['req'=8,'kv'=4] {'req'}, dimensions={0}, use_global_device_ids=true | all-gather | bytes 589824 | tf_op jit(solution)/shard_map/all_gather | solution.py:128
  445.3 36.1 %all-reduce.9.cloned.1.call-done = bf16[128,1024]{1,0:T(8,128)(2,1)} async-done(((bf16[128,1024]{1,0:T(8,128)(2,1)}), bf16[128,1024]{1,0:T(8,128)(2,1)}) %all-reduce.9.cloned.1.call-update) | async-done | bytes 262160 | tf_op jit(solution)/shard_map/psum | solution.py:19
  483.4 4.5 fusion.36
  488.1 6.4 copy.112
  494.5 6.5 copy.113
  501.0 24.3 %reduce-scatter.19.cloned.1.call-done = f32[16,2560]{1,0:T(8,128)} async-done(((f32[128,2560]{1,0:T(8,128)}), f32[16,2560]{1,0:T(8,128)}) %reduce-scatter.19.cloned.1.call-update) | async-done | bytes 163856 | tf_op jit(solution)/shard_map/reduce_scatter | solution.py:136
  527.1 46.3 %while.37 = (s32[]{:T(128)}, f32[16,2,8]{0,2,1:T(8,128)S(1)}, f32[16,2,8]{0,2,1:T(8,128)S(1)}, f32[16,2,8,128]{3,0,2,1:T(8,128)S(1)}, s32[16]{0:T(128)S(1)}, /*i...) while((s32[]{:T(128)}, f32[16,2,8]{0,2,1:T(8,128)S(1)}, ...), condition=%wide.region_24.27_spmd.clone, body=%wide.region_21.26_spmd.clone.sunk | while | flops 68379904 | bytes 2478401 | solution.py:86
  573.6 8.9 %all_gather.29 = bf16[128,2048]{1,0:T(8,128)(2,1)S(1)} all-gather(bf16[16,2048]{1,0:T(8,128)(2,1)S(1)} %bitcast.131), channel_id=1, replica_groups=mesh['req'=8,'kv'=4] {'req'}, dimensions={0}, use_global_device_ids=true | all-gather | bytes 589824 | tf_op jit(solution)/shard_map/all_gather | solution.py:167
  583.3 36.1 %all-reduce.11.cloned.1.call-done = bf16[128,1024]{1,0:T(8,128)(2,1)} async-done(((bf16[128,1024]{1,0:T(8,128)(2,1)}), bf16[128,1024]{1,0:T(8,128)(2,1)}) %all-reduce.11.cloned.1.call-update) | async-done | bytes 262160 | tf_op jit(solution)/shard_map/psum | solution.py:19
  621.4 4.0 fusion.34
  625.5 36.1 %reduce-scatter.21.cloned.1.call-done = f32[16,2048]{1,0:T(8,128)} async-done(((f32[128,2048]{1,0:T(8,128)}), f32[16,2048]{1,0:T(8,128)}) %reduce-scatter.21.cloned.1.call-update) | async-done | bytes 131088 | tf_op jit(solution)/shard_map/reduce_scatter | solution.py:174
  662.6 8.9 %psum.63 = f32[16]{0:T(128)S(1)} all-reduce(f32[16]{0:T(128)S(1)} %get-tuple-element.477), channel_id=1, replica_groups=mesh['req'=8,'kv'=4] {'kv'}, use_global_device_ids=true, to_apply=%region_28.31 | all-reduce | flops 16 | bytes 128 | tf_op jit(solution)/shard_map/psum | solution.py:41
  671.7 8.9 %all_gather.30 = bf16[128,2048]{1,0:T(8,128)(2,1)S(1)} all-gather(bf16[16,2048]{1,0:T(8,128)(2,1)S(1)} %multiply_convert_fusion), channel_id=1, replica_groups=mesh['req'=8,'kv'=4] {'req'}, dimensions={0}, use_global_device_ids=true | all-gather | bytes 589824 | tf_op jit(solution)/shard_map/all_gather | solution.py:181
  680.6 7.6 fusion.78
  688.2 7.6 fusion.79
  695.8 2.1 pad_maximum_fusion.1
  698.0 5.3 copy.100
  703.4 71.9 %reduce-scatter.27.cloned.1.call-done = f32[32,7392]{1,0:T(8,128)} async-done(((f32[128,7392]{1,0:T(8,128)}), f32[32,7392]{1,0:T(8,128)}) %reduce-scatter.27.cloned.1.call-update) | async-done | bytes 946192 | tf_op jit(solution)/shard_map/reduce_scatter | solution.py:183
  776.7 18.8 %all_gather.31 = bf16[128,3696]{1,0:T(8,128)(2,1)S(1)} all-gather(bf16[32,3696]{1,0:T(8,128)(2,1)S(1)} %fusion.32), channel_id=1, replica_groups=mesh['req'=8,'kv'=4] {'kv'}, dimensions={0}, use_global_device_ids=true | all-gather | bytes 1182720 | tf_op jit(solution)/shard_map/all_gather | solution.py:198
  795.5 8.7 %fusion.80 = f32[128,2048]{1,0:T(8,128)} fusion(bf16[128,3696]{1,0:T(8,128)(2,1)S(1)} %all_gather.31, bf16[3696,2048]{1,0:T(8,128)(2,1)} %param.41), kind=kOutput, calls=%fused_computation.170 | convolution fusion | flops 1937768448 | bytes 17133568 | tf_op jit(solution)/shard_map/dot_general | solution.py:200
  804.2 37.4 %reduce-scatter.23.cloned.1.call-done = f32[16,2048]{1,0:T(8,128)} async-done(((f32[128,2048]{1,0:T(8,128)}), f32[16,2048]{1,0:T(8,128)}) %reduce-scatter.23.cloned.1.call-update) | async-done | bytes 131088 | tf_op jit(solution)/shard_map/reduce_scatter | solution.py:199
  (388 shorter events, 122.1 us)
Async XLA Ops:
  6.5 57.6 %all-reduce.5.cloned.1.call-start = ((), (), s32[]{:S(2)}) async-start(), calls=%async_computation.8 | async-start | bytes 524288 | tf_op jit(solution)/shard_map/psum | solution.py:19
  28.8 79.3 %reduce-scatter.13.cloned.1.call-start = ((), (), s32[]{:S(2)}) async-start(), calls=%async_computation.9 | async-start | bytes 1474560 | tf_op jit(solution)/shard_map/reduce_scatter | solution.py:136
  29.5 4.8 copy-start.6
  29.5 4.9 copy-start.7
  35.8 5.9 copy-start.2
  35.8 6.8 copy-start.3
  70.6 131.6 %all-reduce.7.cloned.1.call-start = ((), (), s32[]{:S(2)}) async-start(), calls=%async_computation.10 | async-start | bytes 524288 | tf_op jit(solution)/shard_map/psum | solution.py:19
  76.5 9.1 %copy-start.4 = (bf16[2048]{0:T(1024)(128)(2,1)S(1)}, bf16[2048]{0:T(1024)(128)(2,1)}, u32[]{:S(2)}) copy-start(bf16[2048]{0:T(1024)(128)(2,1)} %param.34) | copy-start | bytes 12292
  76.5 9.1 %copy-start.8 = (bf16[256]{0:T(256)(128)(2,1)S(1)}, bf16[256]{0:T(256)(128)(2,1)}, u32[]{:S(2)}) copy-start(bf16[256]{0:T(256)(128)(2,1)} %param.36) | copy-start | bytes 1540
  76.5 9.2 %copy-start.9 = (bf16[256]{0:T(256)(128)(2,1)S(1)}, bf16[256]{0:T(256)(128)(2,1)}, u32[]{:S(2)}) copy-start(bf16[256]{0:T(256)(128)(2,1)} %param.35) | copy-start | bytes 1540
  166.1 78.2 %reduce-scatter.15.cloned.1.call-start = ((), (), s32[]{:S(2)}) async-start(), calls=%async_computation.11 | async-start | bytes 1179648 | tf_op jit(solution)/shard_map/reduce_scatter | solution.py:174
  166.2 42.0 %copy-start.5 = (bf16[2048]{0:T(1024)(128)(2,1)S(1)}, bf16[2048]{0:T(1024)(128)(2,1)}, u32[]{:S(2)}) copy-start(bf16[2048]{0:T(1024)(128)(2,1)} %param.38) | copy-start | bytes 12292
  166.2 78.1 %copy-start = (bf16[16,2048]{1,0:T(8,128)(2,1)S(1)}, bf16[16,2048]{1,0:T(8,128)(2,1)}, u32[]{:S(2)}) copy-start(bf16[16,2048]{1,0:T(8,128)(2,1)} %param.25) | copy-start | bytes 196612
  208.2 150.9 %reduce-scatter.25.cloned.1.call-start = ((), (), s32[]{:S(2)}) async-start(), calls=%async_computation.18 | async-start | bytes 4751360 | tf_op jit(solution)/shard_map/reduce_scatter | solution.py:183
  287.1 138.3 %reduce-scatter.17.cloned.1.call-start = ((), (), s32[]{:S(2)}) async-start(), calls=%async_computation.12 | async-start | bytes 1179648 | tf_op jit(solution)/shard_map/reduce_scatter | solution.py:199
  379.3 46.2 %copy-start.1 = (f32[16,2048]{1,0:T(8,128)S(1)}, f32[16,2048]{1,0:T(8,128)}, u32[]{:S(2)}) copy-start(f32[16,2048]{1,0:T(8,128)} %reduce-scatter.15.cloned.1.call-done) | copy-start | bytes 393220
  388.0 93.3 %all-reduce.9.cloned.1.call-start = ((), (), s32[]{:S(2)}) async-start(), calls=%async_computation.13 | async-start | bytes 524288 | tf_op jit(solution)/shard_map/psum | solution.py:19
  445.2 80.1 %reduce-scatter.19.cloned.1.call-start = ((), (), s32[]{:S(2)}) async-start(), calls=%async_computation.14 | async-start | bytes 1474560 | tf_op jit(solution)/shard_map/reduce_scatter | solution.py:136
  487.8 131.6 %all-reduce.11.cloned.1.call-start = ((), (), s32[]{:S(2)}) async-start(), calls=%async_computation.15 | async-start | bytes 524288 | tf_op jit(solution)/shard_map/psum | solution.py:19
  583.3 78.3 %reduce-scatter.21.cloned.1.call-start = ((), (), s32[]{:S(2)}) async-start(), calls=%async_computation.16 | async-start | bytes 1179648 | tf_op jit(solution)/shard_map/reduce_scatter | solution.py:174
  625.4 149.9 %reduce-scatter.27.cloned.1.call-start = ((), (), s32[]{:S(2)}) async-start(), calls=%async_computation.19 | async-start | bytes 4751360 | tf_op jit(solution)/shard_map/reduce_scatter | solution.py:183
  703.3 138.3 %reduce-scatter.23.cloned.1.call-start = ((), (), s32[]{:S(2)}) async-start(), calls=%async_computation.17 | async-start | bytes 1179648 | tf_op jit(solution)/shard_map/reduce_scatter | solution.py:199
Sparse Core Ops, SparseCore 0:
  28.9 35.1 all-reduce.4
  70.7 37.2 reduce-scatter.12
  166.2 35.9 all-reduce.6
  208.3 35.9 reduce-scatter.14
  287.2 71.8 reduce-scatter.24
  388.1 37.2 reduce-scatter.16
  445.3 35.9 all-reduce.8
  488.0 37.2 reduce-scatter.18
  583.4 35.9 all-reduce.10
  625.5 36.0 reduce-scatter.20
  703.4 71.8 reduce-scatter.26
  804.3 37.1 reduce-scatter.22
where the time goes:
time: 855 us; the launch traced here: 850 us
  waiting for transfers between devices  459 us (54%)
  matrix products  145 us (17%)
  blocking collectives  128 us (15%)
  local copies, waits for them, and re-layouts  65 us (8%)
  other arithmetic  35.7 us (4%)
  between operations  14 us (2%)
    reduce_scatter x2, waiting for transfers between devices, body(): lax.psum_scatter(jnp.concatenate([jnp.dot(tokens, w_gate, preferred_eleme...  144 us
    psum x4, waiting for transfers between devices, broadcast(): return lax.psum(block, axis)  122 us
    reduce_scatter x2, waiting for transfers between devices, body(): lax.psum_scatter(jnp.dot(hidden_all, w_down, preferred_element_type=jnp.f...  74.7 us
    reduce_scatter x2, waiting for transfers between devices, body(): lax.psum_scatter(jnp.dot(project_picked, w_out, preferred_element_type=jn...  72.2 us
    reduce_scatter x2, waiting for transfers between devices, body(): lax.psum_scatter(jnp.dot(picked, w_joint, preferred_element_type=jnp.floa...  46.4 us
    unnamed x34, local copies, waits for them, and re-layouts  42.2 us
    dot_general x32, matrix products, one_block(): jnp.einsum('igrt,tgd->igrd', exps.astype(jnp.bfloat16), value_block, pref...  40.2 us
    dot_general x32, matrix products, one_block(): jnp.einsum('igrd,tgd->igrt', query_rows, key_block, preferred_element_typ...  39.8 us
  transfers between devices with their start and end apart: 12, of which 12 were waited for; matrix products, arithmetic and copies ran while one was open for 6% of the time, Pallas kernels for 0%

commit v1 on v0

--- a/solution.py
+++ b/solution.py
@@ -14,9 +14,22 @@
 LOG_BASE = math.log(1000000.0)
 
 
-def broadcast(block, axis, owner):
-    block = jnp.where(lax.axis_index(axis) == owner, block, jnp.zeros_like(block))
-    return lax.psum(block, axis)
+def scatter_sum(block, axis):
+    count = lax.axis_size(axis)
+    index = lax.axis_index(axis)
+    chunks = block.reshape(count, block.shape[0] // count, *block.shape[1:])
+    total = jnp.take(chunks, index, axis=0)
+    for shift in range(1, count):
+        piece = jnp.take(chunks, (index + shift) % count, axis=0)
+        total = total + lax.ppermute(
+            piece, axis, [(j, (j + shift) % count) for j in range(count)]
+        )
+    return total
+
+
+def rows_for_weights(block):
+    wide = lax.all_gather(block, "kv", axis=1, tiled=True)
+    return lax.all_to_all(wide, "req", 1, 0, tiled=True)
 
 
 def apply_rotation(values, token_positions):
@@ -125,20 +138,10 @@
     residual = hidden.astype(jnp.float32)
     for current_layer_index in range(LAYER_COUNT):
         normed = normalize(residual, attn_gain)
-        gathered = lax.all_gather(normed, "req", axis=0, tiled=True)
-        slab_width = gathered.shape[1] // group_ratio
-        portion = lax.dynamic_slice_in_dim(
-            gathered, req_index % group_ratio * slab_width, slab_width, 1
-        )
-        columns = broadcast(portion, "kv", req_index // group_ratio)
+        columns = rows_for_weights(normed)
         picked = jnp.take(columns, request_serving_order, axis=0)
         combined = (
-            lax.psum_scatter(
-                jnp.dot(picked, w_joint, preferred_element_type=jnp.float32),
-                "req",
-                scatter_dimension=0,
-                tiled=True,
-            )
+            scatter_sum(jnp.dot(picked, w_joint, preferred_element_type=jnp.float32), "req")
             + b_joint[None, :]
         )
         lengths = jnp.take(cache_len[current_layer_index], my_slots)
@@ -164,18 +167,10 @@
         attention_output = attend(
             query_rows, fresh_key, fresh_value, cached_keys, cached_values, lengths
         ).reshape(own_rows, query_width)
-        heads_gathered = lax.all_gather(attention_output, "req", axis=0, tiled=True)
-        head_width = heads_gathered.shape[1] // group_ratio
-        head_portion = lax.dynamic_slice_in_dim(
-            heads_gathered, req_index % group_ratio * head_width, head_width, 1
-        )
-        head_rows = broadcast(head_portion, "kv", req_index // group_ratio)
+        head_rows = rows_for_weights(attention_output)
         project_picked = jnp.take(head_rows, inverse, axis=0)
-        residual = residual + lax.psum_scatter(
-            jnp.dot(project_picked, w_out, preferred_element_type=jnp.float32),
-            "req",
-            scatter_dimension=0,
-            tiled=True,
+        residual = residual + scatter_sum(
+            jnp.dot(project_picked, w_out, preferred_element_type=jnp.float32), "req"
         )
         normed_mlp = normalize(residual, mlp_gain)
         tokens = lax.all_gather(normed_mlp, "req", axis=0, tiled=True)
@@ -196,11 +191,8 @@
             jnp.bfloat16
         )
         hidden_all = lax.all_gather(local_hidden, "kv", axis=0, tiled=True)
-        residual = residual + lax.psum_scatter(
-            jnp.dot(hidden_all, w_down, preferred_element_type=jnp.float32),
-            "req",
-            scatter_dimension=0,
-            tiled=True,
+        residual = residual + scatter_sum(
+            jnp.dot(hidden_all, w_down, preferred_element_type=jnp.float32), "req"
         )
     return residual
 

time: 855 us -> 660 us (0.77)
  waiting for transfers between devices: 459 us -> 183 us
  starting transfers between devices: 0.68 us -> 56.6 us
  blocking collectives: 128 us -> 169 us
    reduce_scatter x6 -> x0, waiting for transfers between devices: 193 us -> none  [the longest x2 74.7 us: body(): lax.psum_scatter(jnp.dot(hidden_all, w_down, preferred_element_type=jnp.f...]
    psum x4 -> x0, waiting for transfers between devices: 122 us -> none  [broadcast(): return lax.psum(block, axis)]
    ppermute x0 -> x42, starting transfers between devices: none -> 46.9 us  [scatter_sum(): lax.ppermute(piece, axis, [(j, (j + shift) % count) for j in range(count)])]
    ppermute x0 -> x42, waiting for transfers between devices: none -> 33 us  [scatter_sum(): lax.ppermute(piece, axis, [(j, (j + shift) % count) for j in range(count)])]
    all_gather x4, blocking collectives: 36.7 us -> 58.1 us  [rows_for_weights(): wide = lax.all_gather(block, 'kv', axis=1, tiled=True)]
    all_to_all x0 -> x2, blocking collectives: none -> 17.6 us  [rows_for_weights(): return lax.all_to_all(wide, 'req', 1, 0, tiled=True)]
    all_to_all x0 -> x2, starting transfers between devices: none -> 9.71 us  [rows_for_weights(): return lax.all_to_all(wide, 'req', 1, 0, tiled=True)]
  transfers between devices with their start and end apart: 12 -> 46, of which waited for: 12 -> 16; matrix products, arithmetic and copies ran while one was open for 6% -> 8% of each run, Pallas kernels for 0% -> 0%
where the time goes in v1:
time: 660 us; the launch traced here: 653 us
  waiting for transfers between devices  183 us (28%)
  blocking collectives  169 us (26%)
  matrix products  139 us (21%)
  local copies, waits for them, and re-layouts  61.5 us (9%)
  starting transfers between devices  56.6 us (9%)
  other arithmetic  27.8 us (4%)
  between operations  14.1 us (2%)
    reduce_scatter x2, waiting for transfers between devices, body(): lax.psum_scatter(jnp.concatenate([jnp.dot(tokens, w_gate, preferred_eleme...  144 us
    all_gather x4, blocking collectives, rows_for_weights(): wide = lax.all_gather(block, 'kv', axis=1, tiled=True)  58.1 us
    ppermute x42, starting transfers between devices, scatter_sum(): lax.ppermute(piece, axis, [(j, (j + shift) % count) for j in range(count)])  46.9 us
    unnamed x34, local copies, waits for them, and re-layouts  42.2 us
    dot_general x32, matrix products, one_block(): jnp.einsum('igrt,tgd->igrd', exps.astype(jnp.bfloat16), value_block, pref...  40.3 us
    dot_general x32, matrix products, one_block(): jnp.einsum('igrd,tgd->igrt', query_rows, key_block, preferred_element_typ...  39.8 us
    all_gather x2, blocking collectives, body(): hidden_all = lax.all_gather(local_hidden, 'kv', axis=0, tiled=True)  37.9 us
    psum x4, blocking collectives, normalize(): all_squares = lax.psum(square_sum, 'kv')  34.4 us
  transfers between devices with their start and end apart: 46, of which 16 were waited for; matrix products, arithmetic and copies ran while one was open for 8% of the time, Pallas kernels for 0%

profile of v1, /device:TPU:18, one launch (start us, length us, event | category | flops | bytes accessed | tf_op | source)
XLA Modules:
  0.0 652.7 jit_solution(5651597795348831521)
XLA Ops:
  8.2 9.0 %psum.28 = f32[16]{0:T(128)S(1)} all-reduce(f32[16]{0:T(128)S(1)} %fusion.60), channel_id=1, replica_groups=mesh['req'=8,'kv'=4] {'kv'}, use_global_device_ids=true, to_apply=%region_1.2 | all-reduce | flops 16 | bytes 128 | tf_op jit(solution)/shard_map/psum | solution.py:54
  18.1 14.9 %all_gather.24 = bf16[16,8192]{1,0:T(8,128)(2,1)S(1)} all-gather(bf16[16,2048]{1,0:T(8,128)(2,1)S(1)} %fusion.62), channel_id=1, replica_groups=mesh['req'=8,'kv'=4] {'kv'}, dimensions={1}, use_global_device_ids=true | all-gather | bytes 327680 | tf_op jit(solution)/shard_map/all_gather | solution.py:31
  33.7 4.3 all-to-all-start
  39.4 4.8 constant_dynamic-update-slice_fusion.2
  45.6 5.7 fusion.111
  51.3 5.9 fusion.110
  59.5 2.5 sort.17
  63.0 3.4 fusion.40
  76.0 6.4 copy.106
  82.4 6.5 copy.107
  89.8 46.3 %while.38 = (s32[]{:T(128)}, f32[16,2,8]{0,2,1:T(8,128)S(1)}, f32[16,2,8]{0,2,1:T(8,128)S(1)}, f32[16,2,8,128]{3,0,2,1:T(8,128)S(1)}, s32[16]{0:T(128)S(1)}, /*i...) while((s32[]{:T(128)}, f32[16,2,8]{0,2,1:T(8,128)S(1)}, ...), condition=%wide.region_6.10_spmd.clone, body=%wide.region_3.9_spmd.clone.sunk | while | flops 68379904 | bytes 2478401 | solution.py:99
  136.3 14.3 %all_gather.25 = bf16[16,8192]{1,0:T(8,128)(2,1)S(1)} all-gather(bf16[16,2048]{1,0:T(8,128)(2,1)S(1)} %bitcast.371), channel_id=1, replica_groups=mesh['req'=8,'kv'=4] {'kv'}, dimensions={1}, use_global_device_ids=true | all-gather | bytes 327680 | tf_op jit(solution)/shard_map/all_gather | solution.py:31
  151.4 5.5 all-to-all-start.1
  156.8 5.5 all-to-all-done.1
  163.2 3.0 fusion.38
  170.7 6.1 collective-permute-done.10
  177.9 3.9 collective-permute-done.8
  182.0 8.1 %psum.29 = f32[16]{0:T(128)S(1)} all-reduce(f32[16]{0:T(128)S(1)} %get-tuple-element.505), channel_id=1, replica_groups=mesh['req'=8,'kv'=4] {'kv'}, use_global_device_ids=true, to_apply=%region_9.14 | all-reduce | flops 16 | bytes 128 | tf_op jit(solution)/shard_map/psum | solution.py:54
  190.2 11.6 %all_gather.26 = bf16[128,2048]{1,0:T(8,128)(2,1)S(1)} all-gather(bf16[16,2048]{1,0:T(8,128)(2,1)S(1)} %multiply_convert_fusion.2), channel_id=1, replica_groups=mesh['req'=8,'kv'=4] {'req'}, dimensions={0}, use_global_device_ids=true | all-gather | bytes 589824 | tf_op jit(solution)/shard_map/all_gather | solution.py:176
  201.8 7.6 %fusion.112 = f32[128,3696]{0,1:T(8,128)S(1)} fusion(bf16[128,2048]{1,0:T(8,128)(2,1)S(1)} %all_gather.26, bf16[2048,3696]{0,1:T(8,128)(2,1)} %param.43), kind=kOutput, calls=%fused_computation.247 | convolution fusion | flops 1937768448 | bytes 17555456 | tf_op jit(solution)/shard_map/dot_general | solution.py:181
  209.5 7.6 %fusion.113 = f32[128,3696]{0,1:T(8,128)S(1)} fusion(bf16[128,2048]{1,0:T(8,128)(2,1)S(1)} %all_gather.26, bf16[2048,3696]{0,1:T(8,128)(2,1)} %param.44), kind=kOutput, calls=%fused_computation.248 | convolution fusion | flops 1937768448 | bytes 17555456 | tf_op jit(solution)/shard_map/dot_general | solution.py:182
  219.2 5.3 copy.98
  224.6 71.8 %reduce-scatter.7.cloned.1.call-done = f32[32,7392]{1,0:T(8,128)} async-done(((f32[128,7392]{1,0:T(8,128)}), f32[32,7392]{1,0:T(8,128)}) %reduce-scatter.7.cloned.1.call-update) | async-done | bytes 946192 | tf_op jit(solution)/shard_map/reduce_scatter | solution.py:178
  297.7 18.8 %all_gather.27 = bf16[128,3696]{1,0:T(8,128)(2,1)S(1)} all-gather(bf16[32,3696]{1,0:T(8,128)(2,1)S(1)} %fusion.33), channel_id=1, replica_groups=mesh['req'=8,'kv'=4] {'kv'}, dimensions={0}, use_global_device_ids=true | all-gather | bytes 1182720 | tf_op jit(solution)/shard_map/all_gather | solution.py:193
  316.5 7.7 %fusion.114 = f32[128,2048]{1,0:T(8,128)S(1)} fusion(bf16[128,3696]{1,0:T(8,128)(2,1)S(1)} %all_gather.27, bf16[3696,2048]{1,0:T(8,128)(2,1)} %param.45), kind=kOutput, calls=%fused_computation.249 | convolution fusion | flops 1937768448 | bytes 17133568 | tf_op jit(solution)/shard_map/dot_general | solution.py:195
  333.1 5.7 collective-permute-done.18
  339.0 9.2 %psum.30 = f32[16]{0:T(128)S(1)} all-reduce(f32[16]{0:T(128)S(1)} %get-tuple-element.503), channel_id=1, replica_groups=mesh['req'=8,'kv'=4] {'kv'}, use_global_device_ids=true, to_apply=%region_12.17 | all-reduce | flops 16 | bytes 128 | tf_op jit(solution)/shard_map/psum | solution.py:54
  348.3 15.1 %all_gather.28 = bf16[16,8192]{1,0:T(8,128)(2,1)S(1)} all-gather(bf16[16,2048]{1,0:T(8,128)(2,1)S(1)} %multiply_convert_fusion.1), channel_id=1, replica_groups=mesh['req'=8,'kv'=4] {'kv'}, dimensions={1}, use_global_device_ids=true | all-gather | bytes 327680 | tf_op jit(solution)/shard_map/all_gather | solution.py:31
  363.4 9.0 %all_to_all.76 = bf16[16,8,1024]{2,0,1:T(8,128)(2,1)S(1)} all-to-all(bf16[16,8,1024]{2,0,1:T(8,128)(2,1)S(1)} %bitcast.369), channel_id=1, replica_groups=mesh['req'=8,'kv'=4] {'req'}, dimensions={1} | all-to-all | bytes 524288 | tf_op jit(solution)/shard_map/all_to_all | solution.py:32
  373.3 3.4 fusion.36
  382.7 2.5 collective-permute-start.26
  385.2 2.9 collective-permute-start.27
  388.1 6.4 copy.108
  394.6 6.5 copy.109
  401.9 46.4 %while.39 = (s32[]{:T(128)}, f32[16,2,8]{0,2,1:T(8,128)S(1)}, f32[16,2,8]{0,2,1:T(8,128)S(1)}, f32[16,2,8,128]{3,0,2,1:T(8,128)S(1)}, s32[16]{0:T(128)S(1)}, /*i...) while((s32[]{:T(128)}, f32[16,2,8]{0,2,1:T(8,128)S(1)}, ...), condition=%wide.region_17.22_spmd.clone, body=%wide.region_14.21_spmd.clone.sunk | while | flops 68379904 | bytes 2478401 | solution.py:99
  448.5 13.9 %all_gather.29 = bf16[16,8192]{1,0:T(8,128)(2,1)S(1)} all-gather(bf16[16,2048]{1,0:T(8,128)(2,1)S(1)} %bitcast.372), channel_id=1, replica_groups=mesh['req'=8,'kv'=4] {'kv'}, dimensions={1}, use_global_device_ids=true | all-gather | bytes 327680 | tf_op jit(solution)/shard_map/all_gather | solution.py:31
  462.4 8.6 %all_to_all.77 = bf16[16,8,1024]{2,0,1:T(8,128)(2,1)S(1)} all-to-all(bf16[16,8,1024]{2,0,1:T(8,128)(2,1)S(1)} %bitcast.370), channel_id=1, replica_groups=mesh['req'=8,'kv'=4] {'req'}, dimensions={1} | all-to-all | bytes 524288 | tf_op jit(solution)/shard_map/all_to_all | solution.py:32
  471.8 2.9 fusion.34
  484.8 4.5 collective-permute-done.31
  489.9 8.0 %psum.31 = f32[16]{0:T(128)S(1)} all-reduce(f32[16]{0:T(128)S(1)} %get-tuple-element.501), channel_id=1, replica_groups=mesh['req'=8,'kv'=4] {'kv'}, use_global_device_ids=true, to_apply=%region_19.24 | all-reduce | flops 16 | bytes 128 | tf_op jit(solution)/shard_map/psum | solution.py:54
  498.0 9.4 %all_gather.30 = bf16[128,2048]{1,0:T(8,128)(2,1)S(1)} all-gather(bf16[16,2048]{1,0:T(8,128)(2,1)S(1)} %multiply_convert_fusion), channel_id=1, replica_groups=mesh['req'=8,'kv'=4] {'req'}, dimensions={0}, use_global_device_ids=true | all-gather | bytes 589824 | tf_op jit(solution)/shard_map/all_gather | solution.py:176
  507.4 7.6 %fusion.115 = f32[128,3696]{0,1:T(8,128)S(1)} fusion(bf16[128,2048]{1,0:T(8,128)(2,1)S(1)} %all_gather.30, bf16[2048,3696]{0,1:T(8,128)(2,1)} %param.43), kind=kOutput, calls=%fused_computation.250 | convolution fusion | flops 1937768448 | bytes 17555456 | tf_op jit(solution)/shard_map/dot_general | solution.py:181
  515.1 7.6 %fusion.116 = f32[128,3696]{0,1:T(8,128)S(1)} fusion(bf16[128,2048]{1,0:T(8,128)(2,1)S(1)} %all_gather.30, bf16[2048,3696]{0,1:T(8,128)(2,1)} %param.44), kind=kOutput, calls=%fused_computation.251 | convolution fusion | flops 1937768448 | bytes 17555456 | tf_op jit(solution)/shard_map/dot_general | solution.py:182
  524.7 5.3 copy.100
  530.1 72.3 %reduce-scatter.9.cloned.1.call-done = f32[32,7392]{1,0:T(8,128)} async-done(((f32[128,7392]{1,0:T(8,128)}), f32[32,7392]{1,0:T(8,128)}) %reduce-scatter.9.cloned.1.call-update) | async-done | bytes 946192 | tf_op jit(solution)/shard_map/reduce_scatter | solution.py:178
  603.7 19.1 %all_gather.31 = bf16[128,3696]{1,0:T(8,128)(2,1)S(1)} all-gather(bf16[32,3696]{1,0:T(8,128)(2,1)S(1)} %fusion.32), channel_id=1, replica_groups=mesh['req'=8,'kv'=4] {'kv'}, dimensions={0}, use_global_device_ids=true | all-gather | bytes 1182720 | tf_op jit(solution)/shard_map/all_gather | solution.py:193
  622.8 7.7 %fusion.117 = f32[128,2048]{1,0:T(8,128)S(1)} fusion(bf16[128,3696]{1,0:T(8,128)(2,1)S(1)} %all_gather.31, bf16[3696,2048]{1,0:T(8,128)(2,1)} %param.45), kind=kOutput, calls=%fused_computation.252 | convolution fusion | flops 1937768448 | bytes 17133568 | tf_op jit(solution)/shard_map/dot_general | solution.py:195
  639.4 5.7 collective-permute-done.39
  (452 shorter events, 163.1 us)
Async XLA Ops:
  33.7 28.4 %all-to-all-start = ((bf16[16,8,1024]{2,0,1:T(8,128)(2,1)}), bf16[16,8,1024]{2,0,1:T(8,128)(2,1)S(1)}, u32[]{:S(2)}, u32[]{:S(2)}) async-start(bf16[16,8,1024]{2,0,1:T(8,128)(2,1)} %bitcast.324), calls=%async_computation | async-start | bytes 524288 | tf_op jit(solution)/shard_map/all_to_all | solution.py:32
  66.5 5.9 collective-permute-start
  66.7 7.0 %collective-permute-start.1 = (f32[16,2560]{1,0:T(8,128)S(1)}, f32[16,2560]{1,0:T(8,128)S(1)}, u32[]{:S(2)}, u32[]{:S(2)}) collective-permute-start(f32[16,2560]{1,0:T(8,128)S(1)} %get-tuple-element.528), channel_id=1, source_target_pairs={{0,8},{4,12},{8,16},{12,20},{16,24},{20,28},{24,0},{28,4},{1,9},{5... | collective-permute-start | bytes 491528 | tf_op jit(solution)/shard_map/ppermute | solution.py:24
  68.3 20.6 %collective-permute-start.2 = (f32[16,2560]{1,0:T(8,128)S(1)}, f32[16,2560]{1,0:T(8,128)S(1)}, u32[]{:S(2)}, u32[]{:S(2)}) collective-permute-start(f32[16,2560]{1,0:T(8,128)S(1)} %get-tuple-element.527), channel_id=1, source_target_pairs={{0,12},{4,16},{8,20},{12,24},{16,28},{20,0},{24,4},{28,8},{1,13},{... | collective-permute-start | bytes 491528 | tf_op jit(solution)/shard_map/ppermute | solution.py:24
  69.4 19.5 %collective-permute-start.3 = (f32[16,2560]{1,0:T(8,128)S(1)}, f32[16,2560]{1,0:T(8,128)S(1)}, u32[]{:S(2)}, u32[]{:S(2)}) collective-permute-start(f32[16,2560]{1,0:T(8,128)S(1)} %get-tuple-element.526), channel_id=1, source_target_pairs={{0,16},{4,20},{8,24},{12,28},{16,0},{20,4},{24,8},{28,12},{1,17},{... | collective-permute-start | bytes 491528 | tf_op jit(solution)/shard_map/ppermute | solution.py:24
  71.1 17.7 %collective-permute-start.4 = (f32[16,2560]{1,0:T(8,128)S(1)}, f32[16,2560]{1,0:T(8,128)S(1)}, u32[]{:S(2)}, u32[]{:S(2)}) collective-permute-start(f32[16,2560]{1,0:T(8,128)S(1)} %get-tuple-element.525), channel_id=1, source_target_pairs={{0,20},{4,24},{8,28},{12,0},{16,4},{20,8},{24,12},{28,16},{1,21},{... | collective-permute-start | bytes 491528 | tf_op jit(solution)/shard_map/ppermute | solution.py:24
  72.4 16.5 %collective-permute-start.5 = (f32[16,2560]{1,0:T(8,128)S(1)}, f32[16,2560]{1,0:T(8,128)S(1)}, u32[]{:S(2)}, u32[]{:S(2)}) collective-permute-start(f32[16,2560]{1,0:T(8,128)S(1)} %get-tuple-element.524), channel_id=1, source_target_pairs={{0,24},{4,28},{8,0},{12,4},{16,8},{20,12},{24,16},{28,20},{1,25},{... | collective-permute-start | bytes 491528 | tf_op jit(solution)/shard_map/ppermute | solution.py:24
  73.7 15.2 %collective-permute-start.6 = (f32[16,2560]{1,0:T(8,128)S(1)}, f32[16,2560]{1,0:T(8,128)S(1)}, u32[]{:S(2)}, u32[]{:S(2)}) collective-permute-start(f32[16,2560]{1,0:T(8,128)S(1)} %get-tuple-element.523), channel_id=1, source_target_pairs={{0,28},{4,0},{8,4},{12,8},{16,12},{20,16},{24,20},{28,24},{1,29},{... | collective-permute-start | bytes 491528 | tf_op jit(solution)/shard_map/ppermute | solution.py:24
  151.4 10.9 %all-to-all-start.1 = ((bf16[16,8,1024]{2,0,1:T(8,128)(2,1)}), bf16[16,8,1024]{2,0,1:T(8,128)(2,1)S(1)}, u32[]{:S(2)}, u32[]{:S(2)}) async-start(bf16[16,8,1024]{2,0,1:T(8,128)(2,1)} %bitcast.323), calls=%async_computation.1 | async-start | bytes 524288 | tf_op jit(solution)/shard_map/all_to_all | solution.py:32
  156.8 139.5 %reduce-scatter.7.cloned.1.call-start = ((), (), s32[]{:S(2)}) async-start(), calls=%async_computation.6 | async-start | bytes 4751360 | tf_op jit(solution)/shard_map/reduce_scatter | solution.py:178
  163.2 13.7 %copy-start.4 = (bf16[2048]{0:T(1024)(128)(2,1)S(1)}, bf16[2048]{0:T(1024)(128)(2,1)}, u32[]{:S(2)}) copy-start(bf16[2048]{0:T(1024)(128)(2,1)} %param.42) | copy-start | bytes 12292
  163.2 18.6 %copy-start = (bf16[16,2048]{1,0:T(8,128)(2,1)S(1)}, bf16[16,2048]{1,0:T(8,128)(2,1)}, u32[]{:S(2)}) copy-start(bf16[16,2048]{1,0:T(8,128)(2,1)} %param.29) | copy-start | bytes 196612
  166.3 10.5 %collective-permute-start.10 = (f32[16,2048]{1,0:T(8,128)S(1)}, f32[16,2048]{1,0:T(8,128)S(1)}, u32[]{:S(2)}, u32[]{:S(2)}) collective-permute-start(f32[16,2048]{1,0:T(8,128)S(1)} %get-tuple-element.554), channel_id=1, source_target_pairs={{0,16},{4,20},{8,24},{12,28},{16,0},{20,4},{24,8},{28,12},{1,17},{... | collective-permute-start | bytes 393224 | tf_op jit(solution)/shard_map/ppermute | solution.py:24
  166.9 9.9 %collective-permute-start.11 = (f32[16,2048]{1,0:T(8,128)S(1)}, f32[16,2048]{1,0:T(8,128)S(1)}, u32[]{:S(2)}, u32[]{:S(2)}) collective-permute-start(f32[16,2048]{1,0:T(8,128)S(1)} %get-tuple-element.553), channel_id=1, source_target_pairs={{0,20},{4,24},{8,28},{12,0},{16,4},{20,8},{24,12},{28,16},{1,21},{... | collective-permute-start | bytes 393224 | tf_op jit(solution)/shard_map/ppermute | solution.py:24
  167.6 9.3 %collective-permute-start.12 = (f32[16,2048]{1,0:T(8,128)S(1)}, f32[16,2048]{1,0:T(8,128)S(1)}, u32[]{:S(2)}, u32[]{:S(2)}) collective-permute-start(f32[16,2048]{1,0:T(8,128)S(1)} %get-tuple-element.552), channel_id=1, source_target_pairs={{0,24},{4,28},{8,0},{12,4},{16,8},{20,12},{24,16},{28,20},{1,25},{... | collective-permute-start | bytes 393224 | tf_op jit(solution)/shard_map/ppermute | solution.py:24
  168.4 8.5 %collective-permute-start.13 = (f32[16,2048]{1,0:T(8,128)S(1)}, f32[16,2048]{1,0:T(8,128)S(1)}, u32[]{:S(2)}, u32[]{:S(2)}) collective-permute-start(f32[16,2048]{1,0:T(8,128)S(1)} %get-tuple-element.551), channel_id=1, source_target_pairs={{0,28},{4,0},{8,4},{12,8},{16,12},{20,16},{24,20},{28,24},{1,29},{... | collective-permute-start | bytes 393224 | tf_op jit(solution)/shard_map/ppermute | solution.py:24
  170.7 7.1 %collective-permute-start.7 = (f32[16,2048]{1,0:T(8,128)S(1)}, f32[16,2048]{1,0:T(8,128)S(1)}, u32[]{:S(2)}, u32[]{:S(2)}) collective-permute-start(f32[16,2048]{1,0:T(8,128)S(1)} %get-tuple-element.550), channel_id=1, source_target_pairs={{0,4},{4,8},{8,12},{12,16},{16,20},{20,24},{24,28},{28,0},{1,5},{5... | collective-permute-start | bytes 393224 | tf_op jit(solution)/shard_map/ppermute | solution.py:24
  176.8 5.0 collective-permute-start.8
  176.8 5.0 collective-permute-start.9
  224.5 377.9 %reduce-scatter.9.cloned.1.call-start = ((), (), s32[]{:S(2)}) async-start(), calls=%async_computation.7 | async-start | bytes 4751360 | tf_op jit(solution)/shard_map/reduce_scatter | solution.py:178
  324.3 5.3 collective-permute-start.14
  324.4 6.5 collective-permute-start.15
  325.9 7.2 %collective-permute-start.16 = (f32[16,2048]{1,0:T(8,128)S(1)}, f32[16,2048]{1,0:T(8,128)S(1)}, u32[]{:S(2)}, u32[]{:S(2)}) collective-permute-start(f32[16,2048]{1,0:T(8,128)S(1)} %get-tuple-element.548), channel_id=1, source_target_pairs={{0,12},{4,16},{8,20},{12,24},{16,28},{20,0},{24,4},{28,8},{1,13},{... | collective-permute-start | bytes 393224 | tf_op jit(solution)/shard_map/ppermute | solution.py:24
  327.1 6.0 collective-permute-start.17
  328.8 10.0 %collective-permute-start.18 = (f32[16,2048]{1,0:T(8,128)S(1)}, f32[16,2048]{1,0:T(8,128)S(1)}, u32[]{:S(2)}, u32[]{:S(2)}) collective-permute-start(f32[16,2048]{1,0:T(8,128)S(1)} %get-tuple-element.546), channel_id=1, source_target_pairs={{0,20},{4,24},{8,28},{12,0},{16,4},{20,8},{24,12},{28,16},{1,21},{... | collective-permute-start | bytes 393224 | tf_op jit(solution)/shard_map/ppermute | solution.py:24
  329.6 9.2 %collective-permute-start.19 = (f32[16,2048]{1,0:T(8,128)S(1)}, f32[16,2048]{1,0:T(8,128)S(1)}, u32[]{:S(2)}, u32[]{:S(2)}) collective-permute-start(f32[16,2048]{1,0:T(8,128)S(1)} %get-tuple-element.545), channel_id=1, source_target_pairs={{0,24},{4,28},{8,0},{12,4},{16,8},{20,12},{24,16},{28,20},{1,25},{... | collective-permute-start | bytes 393224 | tf_op jit(solution)/shard_map/ppermute | solution.py:24
  330.9 7.9 %collective-permute-start.20 = (f32[16,2048]{1,0:T(8,128)S(1)}, f32[16,2048]{1,0:T(8,128)S(1)}, u32[]{:S(2)}, u32[]{:S(2)}) collective-permute-start(f32[16,2048]{1,0:T(8,128)S(1)} %get-tuple-element.544), channel_id=1, source_target_pairs={{0,28},{4,0},{8,4},{12,8},{16,12},{20,16},{24,20},{28,24},{1,29},{... | collective-permute-start | bytes 393224 | tf_op jit(solution)/shard_map/ppermute | solution.py:24
  376.8 6.0 collective-permute-start.21
  376.8 8.4 %collective-permute-start.22 = (f32[16,2560]{1,0:T(8,128)S(1)}, f32[16,2560]{1,0:T(8,128)S(1)}, u32[]{:S(2)}, u32[]{:S(2)}) collective-permute-start(f32[16,2560]{1,0:T(8,128)S(1)} %get-tuple-element.521), channel_id=1, source_target_pairs={{0,8},{4,12},{8,16},{12,20},{16,24},{20,28},{24,0},{28,4},{1,9},{5... | collective-permute-start | bytes 491528 | tf_op jit(solution)/shard_map/ppermute | solution.py:24
  378.4 22.7 %collective-permute-start.23 = (f32[16,2560]{1,0:T(8,128)S(1)}, f32[16,2560]{1,0:T(8,128)S(1)}, u32[]{:S(2)}, u32[]{:S(2)}) collective-permute-start(f32[16,2560]{1,0:T(8,128)S(1)} %get-tuple-element.520), channel_id=1, source_target_pairs={{0,12},{4,16},{8,20},{12,24},{16,28},{20,0},{24,4},{28,8},{1,13},{... | collective-permute-start | bytes 491528 | tf_op jit(solution)/shard_map/ppermute | solution.py:24
  380.7 20.4 %collective-permute-start.24 = (f32[16,2560]{1,0:T(8,128)S(1)}, f32[16,2560]{1,0:T(8,128)S(1)}, u32[]{:S(2)}, u32[]{:S(2)}) collective-permute-start(f32[16,2560]{1,0:T(8,128)S(1)} %get-tuple-element.519), channel_id=1, source_target_pairs={{0,16},{4,20},{8,24},{12,28},{16,0},{20,4},{24,8},{28,12},{1,17},{... | collective-permute-start | bytes 491528 | tf_op jit(solution)/shard_map/ppermute | solution.py:24
  381.2 19.8 %collective-permute-start.25 = (f32[16,2560]{1,0:T(8,128)S(1)}, f32[16,2560]{1,0:T(8,128)S(1)}, u32[]{:S(2)}, u32[]{:S(2)}) collective-permute-start(f32[16,2560]{1,0:T(8,128)S(1)} %get-tuple-element.518), channel_id=1, source_target_pairs={{0,20},{4,24},{8,28},{12,0},{16,4},{20,8},{24,12},{28,16},{1,21},{... | collective-permute-start | bytes 491528 | tf_op jit(solution)/shard_map/ppermute | solution.py:24
  382.7 18.3 %collective-permute-start.26 = (f32[16,2560]{1,0:T(8,128)S(1)}, f32[16,2560]{1,0:T(8,128)S(1)}, u32[]{:S(2)}, u32[]{:S(2)}) collective-permute-start(f32[16,2560]{1,0:T(8,128)S(1)} %get-tuple-element.517), channel_id=1, source_target_pairs={{0,24},{4,28},{8,0},{12,4},{16,8},{20,12},{24,16},{28,20},{1,25},{... | collective-permute-start | bytes 491528 | tf_op jit(solution)/shard_map/ppermute | solution.py:24
  385.2 15.8 %collective-permute-start.27 = (f32[16,2560]{1,0:T(8,128)S(1)}, f32[16,2560]{1,0:T(8,128)S(1)}, u32[]{:S(2)}, u32[]{:S(2)}) collective-permute-start(f32[16,2560]{1,0:T(8,128)S(1)} %get-tuple-element.516), channel_id=1, source_target_pairs={{0,28},{4,0},{8,4},{12,8},{16,12},{20,16},{24,20},{28,24},{1,29},{... | collective-permute-start | bytes 491528 | tf_op jit(solution)/shard_map/ppermute | solution.py:24
  474.9 5.3 collective-permute-start.28
  474.9 7.7 %collective-permute-start.29 = (f32[16,2048]{1,0:T(8,128)S(1)}, f32[16,2048]{1,0:T(8,128)S(1)}, u32[]{:S(2)}, u32[]{:S(2)}) collective-permute-start(f32[16,2048]{1,0:T(8,128)S(1)} %get-tuple-element.542), channel_id=1, source_target_pairs={{0,8},{4,12},{8,16},{12,20},{16,24},{20,28},{24,0},{28,4},{1,9},{5... | collective-permute-start | bytes 393224 | tf_op jit(solution)/shard_map/ppermute | solution.py:24
  476.5 8.4 %collective-permute-start.30 = (f32[16,2048]{1,0:T(8,128)S(1)}, f32[16,2048]{1,0:T(8,128)S(1)}, u32[]{:S(2)}, u32[]{:S(2)}) collective-permute-start(f32[16,2048]{1,0:T(8,128)S(1)} %get-tuple-element.541), channel_id=1, source_target_pairs={{0,12},{4,16},{8,20},{12,24},{16,28},{20,0},{24,4},{28,8},{1,13},{... | collective-permute-start | bytes 393224 | tf_op jit(solution)/shard_map/ppermute | solution.py:24
  478.8 10.6 %collective-permute-start.31 = (f32[16,2048]{1,0:T(8,128)S(1)}, f32[16,2048]{1,0:T(8,128)S(1)}, u32[]{:S(2)}, u32[]{:S(2)}) collective-permute-start(f32[16,2048]{1,0:T(8,128)S(1)} %get-tuple-element.540), channel_id=1, source_target_pairs={{0,16},{4,20},{8,24},{12,28},{16,0},{20,4},{24,8},{28,12},{1,17},{... | collective-permute-start | bytes 393224 | tf_op jit(solution)/shard_map/ppermute | solution.py:24
  479.3 10.3 %collective-permute-start.32 = (f32[16,2048]{1,0:T(8,128)S(1)}, f32[16,2048]{1,0:T(8,128)S(1)}, u32[]{:S(2)}, u32[]{:S(2)}) collective-permute-start(f32[16,2048]{1,0:T(8,128)S(1)} %get-tuple-element.539), channel_id=1, source_target_pairs={{0,20},{4,24},{8,28},{12,0},{16,4},{20,8},{24,12},{28,16},{1,21},{... | collective-permute-start | bytes 393224 | tf_op jit(solution)/shard_map/ppermute | solution.py:24
  480.1 9.5 %collective-permute-start.33 = (f32[16,2048]{1,0:T(8,128)S(1)}, f32[16,2048]{1,0:T(8,128)S(1)}, u32[]{:S(2)}, u32[]{:S(2)}) collective-permute-start(f32[16,2048]{1,0:T(8,128)S(1)} %get-tuple-element.538), channel_id=1, source_target_pairs={{0,24},{4,28},{8,0},{12,4},{16,8},{20,12},{24,16},{28,20},{1,25},{... | collective-permute-start | bytes 393224 | tf_op jit(solution)/shard_map/ppermute | solution.py:24
  482.6 7.1 %collective-permute-start.34 = (f32[16,2048]{1,0:T(8,128)S(1)}, f32[16,2048]{1,0:T(8,128)S(1)}, u32[]{:S(2)}, u32[]{:S(2)}) collective-permute-start(f32[16,2048]{1,0:T(8,128)S(1)} %get-tuple-element.537), channel_id=1, source_target_pairs={{0,28},{4,0},{8,4},{12,8},{16,12},{20,16},{24,20},{28,24},{1,29},{... | collective-permute-start | bytes 393224 | tf_op jit(solution)/shard_map/ppermute | solution.py:24
  630.6 5.3 collective-permute-start.35
  630.7 6.5 collective-permute-start.36
  632.2 7.2 %collective-permute-start.37 = (f32[16,2048]{1,0:T(8,128)S(1)}, f32[16,2048]{1,0:T(8,128)S(1)}, u32[]{:S(2)}, u32[]{:S(2)}) collective-permute-start(f32[16,2048]{1,0:T(8,128)S(1)} %get-tuple-element.534), channel_id=1, source_target_pairs={{0,12},{4,16},{8,20},{12,24},{16,28},{20,0},{24,4},{28,8},{1,13},{... | collective-permute-start | bytes 393224 | tf_op jit(solution)/shard_map/ppermute | solution.py:24
  633.4 6.0 collective-permute-start.38
  635.1 10.0 %collective-permute-start.39 = (f32[16,2048]{1,0:T(8,128)S(1)}, f32[16,2048]{1,0:T(8,128)S(1)}, u32[]{:S(2)}, u32[]{:S(2)}) collective-permute-start(f32[16,2048]{1,0:T(8,128)S(1)} %get-tuple-element.532), channel_id=1, source_target_pairs={{0,20},{4,24},{8,28},{12,0},{16,4},{20,8},{24,12},{28,16},{1,21},{... | collective-permute-start | bytes 393224 | tf_op jit(solution)/shard_map/ppermute | solution.py:24
  635.9 9.2 %collective-permute-start.40 = (f32[16,2048]{1,0:T(8,128)S(1)}, f32[16,2048]{1,0:T(8,128)S(1)}, u32[]{:S(2)}, u32[]{:S(2)}) collective-permute-start(f32[16,2048]{1,0:T(8,128)S(1)} %get-tuple-element.531), channel_id=1, source_target_pairs={{0,24},{4,28},{8,0},{12,4},{16,8},{20,12},{24,16},{28,20},{1,25},{... | collective-permute-start | bytes 393224 | tf_op jit(solution)/shard_map/ppermute | solution.py:24
  637.2 7.9 %collective-permute-start.41 = (f32[16,2048]{1,0:T(8,128)S(1)}, f32[16,2048]{1,0:T(8,128)S(1)}, u32[]{:S(2)}, u32[]{:S(2)}) collective-permute-start(f32[16,2048]{1,0:T(8,128)S(1)} %get-tuple-element.530), channel_id=1, source_target_pairs={{0,28},{4,0},{8,4},{12,8},{16,12},{20,16},{24,20},{28,24},{1,29},{... | collective-permute-start | bytes 393224 | tf_op jit(solution)/shard_map/ppermute | solution.py:24
  (7 other events, 41.8 us)
Sparse Core Ops, SparseCore 0:
  224.6 71.6 reduce-scatter.6
  530.2 72.1 reduce-scatter.8

commit v2 on v1

--- a/solution.py
+++ b/solution.py
@@ -51,7 +51,12 @@
 
 def normalize(residual, gains):
     square_sum = jnp.sum(residual * residual, axis=1)
-    all_squares = lax.psum(square_sum, "kv")
+    count = lax.axis_size("kv")
+    all_squares = square_sum
+    for shift in range(1, count):
+        all_squares = all_squares + lax.ppermute(
+            square_sum, "kv", [(j, (j + shift) % count) for j in range(count)]
+        )
     inv_norm = lax.rsqrt(all_squares / MODEL_WIDTH + EPS)
     return (residual * inv_norm[:, None] * gains.astype(jnp.float32)[None, :]).astype(jnp.bfloat16)
 
@@ -61,45 +66,31 @@
     finish = jnp.cumsum(lengths)
     starts = finish - lengths
     capacity = cached_keys.shape[0]
-    block_size = min(512, capacity)
-    block_count = capacity // block_size
+    key_rows = jnp.arange(capacity, dtype=jnp.int32)
+    inside = (key_rows[None, :] >= starts[:, None]) & (key_rows[None, :] < finish[:, None])
+    inside = inside[:, None, None, :]
+    scores = (
+        jnp.einsum("igrd,tgd->igrt", query_rows, cached_keys, preferred_element_type=jnp.float32)
+        * score_scale
+    )
     self_score = (
         jnp.einsum("igrd,igd->igr", query_rows, fresh_key, preferred_element_type=jnp.float32)
         * score_scale
     )
-    start_out = fresh_value.astype(jnp.float32)[:, :, None, :] * jnp.ones(
-        query_rows.shape, jnp.float32
-    )
-
-    def one_block(block_index, carried):
-        running_max, running_sum, accumulated = carried
-        first_row = block_index * block_size
-        key_block = lax.dynamic_slice_in_dim(cached_keys, first_row, block_size, 0)
-        value_block = lax.dynamic_slice_in_dim(cached_values, first_row, block_size, 0)
-        scores = (
-            jnp.einsum("igrd,tgd->igrt", query_rows, key_block, preferred_element_type=jnp.float32)
-            * score_scale
-        )
-        key_rows = first_row + jnp.arange(block_size, dtype=jnp.int32)
-        inside = (key_rows[None, :] >= starts[:, None]) & (key_rows[None, :] < finish[:, None])
-        inside = inside[:, None, None, :]
-        block_max = jnp.max(jnp.where(inside, scores, -jnp.inf), axis=-1)
-        new_max = jnp.maximum(running_max, block_max)
-        exps = jnp.where(inside, jnp.exp(scores - new_max[..., None]), 0.0)
-        rescale = jnp.exp(running_max - new_max)
-        new_sum = running_sum * rescale + jnp.sum(exps, axis=-1)
-        contribution = jnp.einsum(
-            "igrt,tgd->igrd",
-            exps.astype(jnp.bfloat16),
-            value_block,
-            preferred_element_type=jnp.float32,
-        )
-        return (new_max, new_sum, accumulated * rescale[..., None] + contribution)
-
-    running_max, running_sum, accumulated = lax.fori_loop(
-        0, block_count, one_block, (self_score, jnp.ones_like(self_score), start_out)
-    )
-    return (accumulated / running_sum[..., None]).astype(jnp.bfloat16)
+    top = jnp.maximum(jnp.max(jnp.where(inside, scores, -jnp.inf), axis=-1), self_score)
+    exps = jnp.where(inside, jnp.exp(scores - top[..., None]), 0.0)
+    self_exp = jnp.exp(self_score - top)
+    total = jnp.sum(exps, axis=-1) + self_exp
+    combined = jnp.einsum(
+        "igrt,tgd->igrd",
+        exps.astype(jnp.bfloat16),
+        cached_values,
+        preferred_element_type=jnp.float32,
+    )
+    combined = combined + self_exp.astype(jnp.bfloat16).astype(jnp.float32)[..., None] * (
+        fresh_value.astype(jnp.float32)[:, :, None, :]
+    )
+    return (combined / total[..., None]).astype(jnp.bfloat16)
 
 
 def body(

time: 660 us -> 573 us (0.87)
  the two profiles are of different devices: /device:TPU:18 before, /device:TPU:1 now
where the time goes in v2:
time: 573 us; the launch traced here: 563 us
  waiting for transfers between devices  193 us (34%)
  blocking collectives  129 us (23%)
  starting transfers between devices  77 us (13%)
  matrix products  64.8 us (11%)
  local copies, waits for them, and re-layouts  62 us (11%)
  other arithmetic  22.7 us (4%)
  between operations  14.8 us (3%)
    reduce_scatter x2, waiting for transfers between devices, body(): lax.psum_scatter(jnp.concatenate([jnp.dot(tokens, w_gate, preferred_eleme...  138 us
    all_gather x4, blocking collectives, rows_for_weights(): wide = lax.all_gather(block, 'kv', axis=1, tiled=True)  46.8 us
    ppermute x42, starting transfers between devices, scatter_sum(): lax.ppermute(piece, axis, [(j, (j + shift) % count) for j in range(count)])  46.6 us
    unnamed x78, local copies, waits for them, and re-layouts  42.8 us
    ppermute x42, waiting for transfers between devices, scatter_sum(): lax.ppermute(piece, axis, [(j, (j + shift) % count) for j in range(count)])  40.9 us
    all_gather x2, blocking collectives, body(): hidden_all = lax.all_gather(local_hidden, 'kv', axis=0, tiled=True)  38.3 us
    all_to_all x2, blocking collectives, rows_for_weights(): return lax.all_to_all(wide, 'req', 1, 0, tiled=True)  22.8 us
    all_gather x2, blocking collectives, body(): tokens = lax.all_gather(normed_mlp, 'req', axis=0, tiled=True)  21.5 us
  transfers between devices with their start and end apart: 58, of which 31 were waited for; matrix products, arithmetic and copies ran while one was open for 9% of the time, Pallas kernels for 0%

profile of v2, /device:TPU:1, one launch (start us, length us, event | category | flops | bytes accessed | tf_op | source)
XLA Modules:
  0.0 563.2 jit_solution(9212854493439928175)
XLA Ops:
  13.8 4.8 constant_dynamic-update-slice_fusion.2
  20.5 5.8 %fusion.128 = (bf16[1,8192,256]{2,1,0:T(8,128)(2,1)}, bf16[1,8192,256]{2,1,0:T(8,128)(2,1)}) fusion(bf16[2,8192,256]{2,1,0:T(8,128)(2,1)} %param.28), kind=kLoop, calls=%fused_computation.243 | loop fusion | bytes 16777216 | tf_op jit(solution)/shard_map/slice | solution.py:154
  26.3 5.8 %fusion.129 = (bf16[1,8192,256]{2,1,0:T(8,128)(2,1)}, bf16[1,8192,256]{2,1,0:T(8,128)(2,1)}) fusion(bf16[2,8192,256]{2,1,0:T(8,128)(2,1)} %param.29), kind=kLoop, calls=%fused_computation.244 | loop fusion | bytes 16777216 | tf_op jit(solution)/shard_map/slice | solution.py:155
  35.0 11.0 %all_gather.24 = bf16[16,8192]{1,0:T(8,128)(2,1)S(1)} all-gather(bf16[16,2048]{1,0:T(8,128)(2,1)S(1)} %fusion.72), channel_id=1, replica_groups=mesh['req'=8,'kv'=4] {'kv'}, dimensions={1}, use_global_device_ids=true | all-gather | bytes 327680 | tf_op jit(solution)/shard_map/all_gather | solution.py:31
  46.7 8.4 %all-to-all-start = ((bf16[16,8,1024]{2,0,1:T(8,128)(2,1)}), bf16[16,8,1024]{2,0,1:T(8,128)(2,1)S(1)}, u32[]{:S(2)}, u32[]{:S(2)}) async-start(bf16[16,8,1024]{2,0,1:T(8,128)(2,1)} %bitcast.346), calls=%async_computation | async-start | bytes 524288 | tf_op jit(solution)/shard_map/all_to_all | solution.py:32
  57.7 3.1 all-to-all-done
  61.6 3.4 fusion.50
  69.8 2.9 collective-permute-start.7
  72.7 3.5 collective-permute-done.4
  76.7 6.4 %copy.120 = bf16[1,8192,256]{1,2,0:T(8,128)(2,1)} copy(bf16[1,8192,256]{2,1,0:T(8,128)(2,1)} %get-tuple-element.40) | data formatting | bytes 8388608
  83.2 6.5 %copy.121 = bf16[1,8192,256]{1,2,0:T(8,128)(2,1)} copy(bf16[1,8192,256]{2,1,0:T(8,128)(2,1)} %get-tuple-element.42) | data formatting | bytes 8388608
  91.4 4.0 select_reduce_fusion.1
  99.7 11.5 %all_gather.25 = bf16[16,8192]{1,0:T(8,128)(2,1)S(1)} all-gather(bf16[16,2048]{1,0:T(8,128)(2,1)S(1)} %bitcast.381), channel_id=1, replica_groups=mesh['req'=8,'kv'=4] {'kv'}, dimensions={1}, use_global_device_ids=true | all-gather | bytes 327680 | tf_op jit(solution)/shard_map/all_gather | solution.py:31
  111.9 6.5 %all-to-all-start.1 = ((bf16[16,8,1024]{2,0,1:T(8,128)(2,1)}), bf16[16,8,1024]{2,0,1:T(8,128)(2,1)S(1)}, u32[]{:S(2)}, u32[]{:S(2)}) async-start(bf16[16,8,1024]{2,0,1:T(8,128)(2,1)} %bitcast.345), calls=%async_computation.1 | async-start | bytes 524288 | tf_op jit(solution)/shard_map/all_to_all | solution.py:32
  118.5 5.6 all-to-all-done.1
  124.9 3.1 fusion.48
  132.2 2.9 collective-permute-start.14
  139.6 4.5 collective-permute-done.13
  148.9 10.5 %all_gather.26 = bf16[128,2048]{1,0:T(8,128)(2,1)S(1)} all-gather(bf16[16,2048]{1,0:T(8,128)(2,1)S(1)} %multiply_convert_fusion.2), channel_id=1, replica_groups=mesh['req'=8,'kv'=4] {'req'}, dimensions={0}, use_global_device_ids=true | all-gather | bytes 589824 | tf_op jit(solution)/shard_map/all_gather | solution.py:167
  159.4 7.8 %fusion.132 = f32[128,3696]{0,1:T(8,128)S(1)} fusion(bf16[128,2048]{1,0:T(8,128)(2,1)S(1)} %all_gather.26, bf16[2048,3696]{0,1:T(8,128)(2,1)} %param.39), kind=kOutput, calls=%fused_computation.247 | convolution fusion | flops 1937768448 | bytes 17555456 | tf_op jit(solution)/shard_map/dot_general | solution.py:172
  167.3 4.3 fusion.133
  173.7 5.3 copy.114
  179.1 69.8 %reduce-scatter.7.cloned.1.call-done = f32[32,7392]{1,0:T(8,128)} async-done(((f32[128,7392]{1,0:T(8,128)}), f32[32,7392]{1,0:T(8,128)}) %reduce-scatter.7.cloned.1.call-update) | async-done | bytes 946192 | tf_op jit(solution)/shard_map/reduce_scatter | solution.py:169
  250.3 19.2 %all_gather.27 = bf16[128,3696]{1,0:T(8,128)(2,1)S(1)} all-gather(bf16[32,3696]{1,0:T(8,128)(2,1)S(1)} %fusion.43), channel_id=1, replica_groups=mesh['req'=8,'kv'=4] {'kv'}, dimensions={0}, use_global_device_ids=true | all-gather | bytes 1182720 | tf_op jit(solution)/shard_map/all_gather | solution.py:184
  269.5 7.7 %fusion.134 = f32[128,2048]{1,0:T(8,128)S(1)} fusion(bf16[128,3696]{1,0:T(8,128)(2,1)S(1)} %all_gather.27, bf16[3696,2048]{1,0:T(8,128)(2,1)} %param.41), kind=kOutput, calls=%fused_computation.249 | convolution fusion | flops 1937768448 | bytes 17133568 | tf_op jit(solution)/shard_map/dot_general | solution.py:186
  277.3 3.6 collective-permute-start.20
  290.7 3.2 collective-permute-done.23
  299.2 12.3 %all_gather.28 = bf16[16,8192]{1,0:T(8,128)(2,1)S(1)} all-gather(bf16[16,2048]{1,0:T(8,128)(2,1)S(1)} %multiply_convert_fusion.1), channel_id=1, replica_groups=mesh['req'=8,'kv'=4] {'kv'}, dimensions={1}, use_global_device_ids=true | all-gather | bytes 327680 | tf_op jit(solution)/shard_map/all_gather | solution.py:31
  311.5 11.8 %all_to_all.76 = bf16[16,8,1024]{2,0,1:T(8,128)(2,1)S(1)} all-to-all(bf16[16,8,1024]{2,0,1:T(8,128)(2,1)S(1)} %bitcast.379), channel_id=1, replica_groups=mesh['req'=8,'kv'=4] {'req'}, dimensions={1} | all-to-all | bytes 524288 | tf_op jit(solution)/shard_map/all_to_all | solution.py:32
  324.3 3.4 fusion.46
  331.7 2.9 collective-permute-start.34
  334.9 4.0 collective-permute-done.31
  338.9 6.4 %copy.124 = bf16[1,8192,256]{1,2,0:T(8,128)(2,1)} copy(bf16[1,8192,256]{2,1,0:T(8,128)(2,1)} %get-tuple-element.39) | data formatting | bytes 8388608
  345.4 6.4 %copy.125 = bf16[1,8192,256]{1,2,0:T(8,128)(2,1)} copy(bf16[1,8192,256]{2,1,0:T(8,128)(2,1)} %get-tuple-element.41) | data formatting | bytes 8388608
  353.5 4.0 select_reduce_fusion
  361.9 12.0 %all_gather.29 = bf16[16,8192]{1,0:T(8,128)(2,1)S(1)} all-gather(bf16[16,2048]{1,0:T(8,128)(2,1)S(1)} %bitcast.382), channel_id=1, replica_groups=mesh['req'=8,'kv'=4] {'kv'}, dimensions={1}, use_global_device_ids=true | all-gather | bytes 327680 | tf_op jit(solution)/shard_map/all_gather | solution.py:31
  373.9 10.9 %all_to_all.77 = bf16[16,8,1024]{2,0,1:T(8,128)(2,1)S(1)} all-to-all(bf16[16,8,1024]{2,0,1:T(8,128)(2,1)S(1)} %bitcast.380), channel_id=1, replica_groups=mesh['req'=8,'kv'=4] {'req'}, dimensions={1} | all-to-all | bytes 524288 | tf_op jit(solution)/shard_map/all_to_all | solution.py:32
  385.7 3.1 fusion.44
  400.2 4.4 collective-permute-done.40
  410.7 11.0 %all_gather.30 = bf16[128,2048]{1,0:T(8,128)(2,1)S(1)} all-gather(bf16[16,2048]{1,0:T(8,128)(2,1)S(1)} %multiply_convert_fusion), channel_id=1, replica_groups=mesh['req'=8,'kv'=4] {'req'}, dimensions={0}, use_global_device_ids=true | all-gather | bytes 589824 | tf_op jit(solution)/shard_map/all_gather | solution.py:167
  421.7 7.8 %fusion.135 = f32[128,3696]{0,1:T(8,128)S(1)} fusion(bf16[128,2048]{1,0:T(8,128)(2,1)S(1)} %all_gather.30, bf16[2048,3696]{0,1:T(8,128)(2,1)} %param.39), kind=kOutput, calls=%fused_computation.250 | convolution fusion | flops 1937768448 | bytes 17555456 | tf_op jit(solution)/shard_map/dot_general | solution.py:172
  429.5 4.3 fusion.136
  436.0 5.3 copy.116
  441.3 68.4 %reduce-scatter.9.cloned.1.call-done = f32[32,7392]{1,0:T(8,128)} async-done(((f32[128,7392]{1,0:T(8,128)}), f32[32,7392]{1,0:T(8,128)}) %reduce-scatter.9.cloned.1.call-update) | async-done | bytes 946192 | tf_op jit(solution)/shard_map/reduce_scatter | solution.py:169
  511.1 19.1 %all_gather.31 = bf16[128,3696]{1,0:T(8,128)(2,1)S(1)} all-gather(bf16[32,3696]{1,0:T(8,128)(2,1)S(1)} %fusion.42), channel_id=1, replica_groups=mesh['req'=8,'kv'=4] {'kv'}, dimensions={0}, use_global_device_ids=true | all-gather | bytes 1182720 | tf_op jit(solution)/shard_map/all_gather | solution.py:184
  530.3 7.7 %fusion.137 = f32[128,2048]{1,0:T(8,128)S(1)} fusion(bf16[128,3696]{1,0:T(8,128)(2,1)S(1)} %all_gather.31, bf16[3696,2048]{1,0:T(8,128)(2,1)} %param.41), kind=kOutput, calls=%fused_computation.252 | convolution fusion | flops 1937768448 | bytes 17133568 | tf_op jit(solution)/shard_map/dot_general | solution.py:186
  538.1 3.7 collective-permute-start.47
  551.5 3.2 collective-permute-done.50
  (263 shorter events, 105.0 us)
Async XLA Ops:
  7.5 26.8 %collective-permute-start = (f32[16]{0:T(128)S(1)}, f32[16]{0:T(128)S(1)}, u32[]{:S(2)}, u32[]{:S(2)}) collective-permute-start(f32[16]{0:T(128)S(1)} %fusion.70), channel_id=1, source_target_pairs={{0,1},{1,2},{2,3},{3,0},{4,5},{5,6},{6,7},{7,4},{8,9},{9,10},{10,1... | collective-permute-start | bytes 200 | tf_op jit(solution)/shard_map/ppermute | solution.py:57
  9.7 24.6 %collective-permute-start.1 = (f32[16]{0:T(128)S(1)}, f32[16]{0:T(128)S(1)}, u32[]{:S(2)}, u32[]{:S(2)}) collective-permute-start(f32[16]{0:T(128)S(1)} %fusion.70), channel_id=1, source_target_pairs={{0,2},{1,3},{2,0},{3,1},{4,6},{5,7},{6,4},{7,5},{8,10},{9,11},{10,... | collective-permute-start | bytes 200 | tf_op jit(solution)/shard_map/ppermute | solution.py:57
  12.0 22.3 %collective-permute-start.2 = (f32[16]{0:T(128)S(1)}, f32[16]{0:T(128)S(1)}, u32[]{:S(2)}, u32[]{:S(2)}) collective-permute-start(f32[16]{0:T(128)S(1)} %fusion.70), channel_id=1, source_target_pairs={{0,3},{1,0},{2,1},{3,2},{4,7},{5,4},{6,5},{7,6},{8,11},{9,8},{10,9... | collective-permute-start | bytes 200 | tf_op jit(solution)/shard_map/ppermute | solution.py:57
  46.7 14.1 %all-to-all-start = ((bf16[16,8,1024]{2,0,1:T(8,128)(2,1)}), bf16[16,8,1024]{2,0,1:T(8,128)(2,1)S(1)}, u32[]{:S(2)}, u32[]{:S(2)}) async-start(bf16[16,8,1024]{2,0,1:T(8,128)(2,1)} %bitcast.346), calls=%async_computation | async-start | bytes 524288 | tf_op jit(solution)/shard_map/all_to_all | solution.py:32
  65.1 7.6 %collective-permute-start.3 = (f32[16,2560]{1,0:T(8,128)S(1)}, f32[16,2560]{1,0:T(8,128)S(1)}, u32[]{:S(2)}, u32[]{:S(2)}) collective-permute-start(f32[16,2560]{1,0:T(8,128)S(1)} %get-tuple-element.50), channel_id=1, source_target_pairs={{0,4},{4,8},{8,12},{12,16},{16,20},{20,24},{24,28},{28,0},{1,5},{5... | collective-permute-start | bytes 491528 | tf_op jit(solution)/shard_map/ppermute | solution.py:24
  66.7 9.6 %collective-permute-start.4 = (f32[16,2560]{1,0:T(8,128)S(1)}, f32[16,2560]{1,0:T(8,128)S(1)}, u32[]{:S(2)}, u32[]{:S(2)}) collective-permute-start(f32[16,2560]{1,0:T(8,128)S(1)} %get-tuple-element.56), channel_id=1, source_target_pairs={{0,8},{4,12},{8,16},{12,20},{16,24},{20,28},{24,0},{28,4},{1,9},{5... | collective-permute-start | bytes 491528 | tf_op jit(solution)/shard_map/ppermute | solution.py:24
  68.6 21.0 %collective-permute-start.5 = (f32[16,2560]{1,0:T(8,128)S(1)}, f32[16,2560]{1,0:T(8,128)S(1)}, u32[]{:S(2)}, u32[]{:S(2)}) collective-permute-start(f32[16,2560]{1,0:T(8,128)S(1)} %get-tuple-element.55), channel_id=1, source_target_pairs={{0,12},{4,16},{8,20},{12,24},{16,28},{20,0},{24,4},{28,8},{1,13},{... | collective-permute-start | bytes 491528 | tf_op jit(solution)/shard_map/ppermute | solution.py:24
  68.6 21.0 %collective-permute-start.6 = (f32[16,2560]{1,0:T(8,128)S(1)}, f32[16,2560]{1,0:T(8,128)S(1)}, u32[]{:S(2)}, u32[]{:S(2)}) collective-permute-start(f32[16,2560]{1,0:T(8,128)S(1)} %get-tuple-element.54), channel_id=1, source_target_pairs={{0,16},{4,20},{8,24},{12,28},{16,0},{20,4},{24,8},{28,12},{1,17},{... | collective-permute-start | bytes 491528 | tf_op jit(solution)/shard_map/ppermute | solution.py:24
  69.8 19.9 %collective-permute-start.7 = (f32[16,2560]{1,0:T(8,128)S(1)}, f32[16,2560]{1,0:T(8,128)}, u32[]{:S(2)}, u32[]{:S(2)}) collective-permute-start(f32[16,2560]{1,0:T(8,128)S(1)} %get-tuple-element.53), channel_id=1, source_target_pairs={{0,20},{4,24},{8,28},{12,0},{16,4},{20,8},{24,12},{28,16},{1,21},{... | collective-permute-start | bytes 491528 | tf_op jit(solution)/shard_map/ppermute | solution.py:24
  72.7 17.0 %collective-permute-start.8 = (f32[16,2560]{1,0:T(8,128)S(1)}, f32[16,2560]{1,0:T(8,128)S(1)}, u32[]{:S(2)}, u32[]{:S(2)}) collective-permute-start(f32[16,2560]{1,0:T(8,128)S(1)} %get-tuple-element.52), channel_id=1, source_target_pairs={{0,24},{4,28},{8,0},{12,4},{16,8},{20,12},{24,16},{28,20},{1,25},{... | collective-permute-start | bytes 491528 | tf_op jit(solution)/shard_map/ppermute | solution.py:24
  76.2 13.4 %collective-permute-start.9 = (f32[16,2560]{1,0:T(8,128)S(1)}, f32[16,2560]{1,0:T(8,128)S(1)}, u32[]{:S(2)}, u32[]{:S(2)}) collective-permute-start(f32[16,2560]{1,0:T(8,128)S(1)} %get-tuple-element.51), channel_id=1, source_target_pairs={{0,28},{4,0},{8,4},{12,8},{16,12},{20,16},{24,20},{28,24},{1,29},{... | collective-permute-start | bytes 491528 | tf_op jit(solution)/shard_map/ppermute | solution.py:24
  111.9 12.1 %all-to-all-start.1 = ((bf16[16,8,1024]{2,0,1:T(8,128)(2,1)}), bf16[16,8,1024]{2,0,1:T(8,128)(2,1)S(1)}, u32[]{:S(2)}, u32[]{:S(2)}) async-start(bf16[16,8,1024]{2,0,1:T(8,128)(2,1)} %bitcast.345), calls=%async_computation.1 | async-start | bytes 524288 | tf_op jit(solution)/shard_map/all_to_all | solution.py:32
  118.4 130.5 %reduce-scatter.7.cloned.1.call-start = ((), (), s32[]{:S(2)}) async-start(), calls=%async_computation.6 | async-start | bytes 4751360 | tf_op jit(solution)/shard_map/reduce_scatter | solution.py:169
  128.2 7.0 %collective-permute-start.10 = (f32[16,2048]{1,0:T(8,128)S(1)}, f32[16,2048]{1,0:T(8,128)S(1)}, u32[]{:S(2)}, u32[]{:S(2)}) collective-permute-start(f32[16,2048]{1,0:T(8,128)S(1)} %get-tuple-element.78), channel_id=1, source_target_pairs={{0,4},{4,8},{8,12},{12,16},{16,20},{20,24},{24,28},{28,0},{1,5},{5... | collective-permute-start | bytes 393224 | tf_op jit(solution)/shard_map/ppermute | solution.py:24
  129.9 8.2 %collective-permute-start.11 = (f32[16,2048]{1,0:T(8,128)S(1)}, f32[16,2048]{1,0:T(8,128)S(1)}, u32[]{:S(2)}, u32[]{:S(2)}) collective-permute-start(f32[16,2048]{1,0:T(8,128)S(1)} %get-tuple-element.84), channel_id=1, source_target_pairs={{0,8},{4,12},{8,16},{12,20},{16,24},{20,28},{24,0},{28,4},{1,9},{5... | collective-permute-start | bytes 393224 | tf_op jit(solution)/shard_map/ppermute | solution.py:24
  131.0 8.6 %collective-permute-start.12 = (f32[16,2048]{1,0:T(8,128)S(1)}, f32[16,2048]{1,0:T(8,128)S(1)}, u32[]{:S(2)}, u32[]{:S(2)}) collective-permute-start(f32[16,2048]{1,0:T(8,128)S(1)} %get-tuple-element.83), channel_id=1, source_target_pairs={{0,12},{4,16},{8,20},{12,24},{16,28},{20,0},{24,4},{28,8},{1,13},{... | collective-permute-start | bytes 393224 | tf_op jit(solution)/shard_map/ppermute | solution.py:24
  131.0 13.0 %collective-permute-start.13 = (f32[16,2048]{1,0:T(8,128)S(1)}, f32[16,2048]{1,0:T(8,128)S(1)}, u32[]{:S(2)}, u32[]{:S(2)}) collective-permute-start(f32[16,2048]{1,0:T(8,128)S(1)} %get-tuple-element.82), channel_id=1, source_target_pairs={{0,16},{4,20},{8,24},{12,28},{16,0},{20,4},{24,8},{28,12},{1,17},{... | collective-permute-start | bytes 393224 | tf_op jit(solution)/shard_map/ppermute | solution.py:24
  132.2 11.9 %collective-permute-start.14 = (f32[16,2048]{1,0:T(8,128)S(1)}, f32[16,2048]{1,0:T(8,128)S(1)}, u32[]{:S(2)}, u32[]{:S(2)}) collective-permute-start(f32[16,2048]{1,0:T(8,128)S(1)} %get-tuple-element.81), channel_id=1, source_target_pairs={{0,20},{4,24},{8,28},{12,0},{16,4},{20,8},{24,12},{28,16},{1,21},{... | collective-permute-start | bytes 393224 | tf_op jit(solution)/shard_map/ppermute | solution.py:24
  135.2 9.0 %collective-permute-start.15 = (f32[16,2048]{1,0:T(8,128)S(1)}, f32[16,2048]{1,0:T(8,128)S(1)}, u32[]{:S(2)}, u32[]{:S(2)}) collective-permute-start(f32[16,2048]{1,0:T(8,128)S(1)} %get-tuple-element.80), channel_id=1, source_target_pairs={{0,24},{4,28},{8,0},{12,4},{16,8},{20,12},{24,16},{28,20},{1,25},{... | collective-permute-start | bytes 393224 | tf_op jit(solution)/shard_map/ppermute | solution.py:24
  179.1 330.7 %reduce-scatter.9.cloned.1.call-start = ((), (), s32[]{:S(2)}) async-start(), calls=%async_computation.7 | async-start | bytes 4751360 | tf_op jit(solution)/shard_map/reduce_scatter | solution.py:169
  277.3 7.8 %collective-permute-start.20 = (f32[16,2048]{1,0:T(8,128)S(1)}, f32[16,2048]{1,0:T(8,128)S(1)}, u32[]{:S(2)}, u32[]{:S(2)}) collective-permute-start(f32[16,2048]{1,0:T(8,128)S(1)} %get-tuple-element.71), channel_id=1, source_target_pairs={{0,4},{4,8},{8,12},{12,16},{16,20},{20,24},{24,28},{28,0},{1,5},{5... | collective-permute-start | bytes 393224 | tf_op jit(solution)/shard_map/ppermute | solution.py:24
  280.9 7.0 %collective-permute-start.21 = (f32[16,2048]{1,0:T(8,128)S(1)}, f32[16,2048]{1,0:T(8,128)S(1)}, u32[]{:S(2)}, u32[]{:S(2)}) collective-permute-start(f32[16,2048]{1,0:T(8,128)S(1)} %get-tuple-element.77), channel_id=1, source_target_pairs={{0,8},{4,12},{8,16},{12,20},{16,24},{20,28},{24,0},{28,4},{1,9},{5... | collective-permute-start | bytes 393224 | tf_op jit(solution)/shard_map/ppermute | solution.py:24
  282.1 8.6 %collective-permute-start.22 = (f32[16,2048]{1,0:T(8,128)S(1)}, f32[16,2048]{1,0:T(8,128)S(1)}, u32[]{:S(2)}, u32[]{:S(2)}) collective-permute-start(f32[16,2048]{1,0:T(8,128)S(1)} %get-tuple-element.76), channel_id=1, source_target_pairs={{0,12},{4,16},{8,20},{12,24},{16,28},{20,0},{24,4},{28,8},{1,13},{... | collective-permute-start | bytes 393224 | tf_op jit(solution)/shard_map/ppermute | solution.py:24
  282.5 11.4 %collective-permute-start.23 = (f32[16,2048]{1,0:T(8,128)S(1)}, f32[16,2048]{1,0:T(8,128)S(1)}, u32[]{:S(2)}, u32[]{:S(2)}) collective-permute-start(f32[16,2048]{1,0:T(8,128)S(1)} %get-tuple-element.75), channel_id=1, source_target_pairs={{0,16},{4,20},{8,24},{12,28},{16,0},{20,4},{24,8},{28,12},{1,17},{... | collective-permute-start | bytes 393224 | tf_op jit(solution)/shard_map/ppermute | solution.py:24
  282.8 11.3 %collective-permute-start.24 = (f32[16,2048]{1,0:T(8,128)S(1)}, f32[16,2048]{1,0:T(8,128)S(1)}, u32[]{:S(2)}, u32[]{:S(2)}) collective-permute-start(f32[16,2048]{1,0:T(8,128)S(1)} %get-tuple-element.74), channel_id=1, source_target_pairs={{0,20},{4,24},{8,28},{12,0},{16,4},{20,8},{24,12},{28,16},{1,21},{... | collective-permute-start | bytes 393224 | tf_op jit(solution)/shard_map/ppermute | solution.py:24
  285.1 8.9 %collective-permute-start.25 = (f32[16,2048]{1,0:T(8,128)S(1)}, f32[16,2048]{1,0:T(8,128)S(1)}, u32[]{:S(2)}, u32[]{:S(2)}) collective-permute-start(f32[16,2048]{1,0:T(8,128)S(1)} %get-tuple-element.73), channel_id=1, source_target_pairs={{0,24},{4,28},{8,0},{12,4},{16,8},{20,12},{24,16},{28,20},{1,25},{... | collective-permute-start | bytes 393224 | tf_op jit(solution)/shard_map/ppermute | solution.py:24
  287.9 6.4 %collective-permute-start.26 = (f32[16,2048]{1,0:T(8,128)S(1)}, f32[16,2048]{1,0:T(8,128)S(1)}, u32[]{:S(2)}, u32[]{:S(2)}) collective-permute-start(f32[16,2048]{1,0:T(8,128)S(1)} %get-tuple-element.72), channel_id=1, source_target_pairs={{0,28},{4,0},{8,4},{12,8},{16,12},{20,16},{24,20},{28,24},{1,29},{... | collective-permute-start | bytes 393224 | tf_op jit(solution)/shard_map/ppermute | solution.py:24
  327.8 6.8 %collective-permute-start.30 = (f32[16,2560]{1,0:T(8,128)S(1)}, f32[16,2560]{1,0:T(8,128)S(1)}, u32[]{:S(2)}, u32[]{:S(2)}) collective-permute-start(f32[16,2560]{1,0:T(8,128)S(1)} %get-tuple-element.43), channel_id=1, source_target_pairs={{0,4},{4,8},{8,12},{12,16},{16,20},{20,24},{24,28},{28,0},{1,5},{5... | collective-permute-start | bytes 491528 | tf_op jit(solution)/shard_map/ppermute | solution.py:24
  329.4 9.6 %collective-permute-start.31 = (f32[16,2560]{1,0:T(8,128)S(1)}, f32[16,2560]{1,0:T(8,128)S(1)}, u32[]{:S(2)}, u32[]{:S(2)}) collective-permute-start(f32[16,2560]{1,0:T(8,128)S(1)} %get-tuple-element.49), channel_id=1, source_target_pairs={{0,8},{4,12},{8,16},{12,20},{16,24},{20,28},{24,0},{28,4},{1,9},{5... | collective-permute-start | bytes 491528 | tf_op jit(solution)/shard_map/ppermute | solution.py:24
  330.5 21.2 %collective-permute-start.32 = (f32[16,2560]{1,0:T(8,128)S(1)}, f32[16,2560]{1,0:T(8,128)S(1)}, u32[]{:S(2)}, u32[]{:S(2)}) collective-permute-start(f32[16,2560]{1,0:T(8,128)S(1)} %get-tuple-element.48), channel_id=1, source_target_pairs={{0,12},{4,16},{8,20},{12,24},{16,28},{20,0},{24,4},{28,8},{1,13},{... | collective-permute-start | bytes 491528 | tf_op jit(solution)/shard_map/ppermute | solution.py:24
  330.6 21.2 %collective-permute-start.33 = (f32[16,2560]{1,0:T(8,128)S(1)}, f32[16,2560]{1,0:T(8,128)S(1)}, u32[]{:S(2)}, u32[]{:S(2)}) collective-permute-start(f32[16,2560]{1,0:T(8,128)S(1)} %get-tuple-element.47), channel_id=1, source_target_pairs={{0,16},{4,20},{8,24},{12,28},{16,0},{20,4},{24,8},{28,12},{1,17},{... | collective-permute-start | bytes 491528 | tf_op jit(solution)/shard_map/ppermute | solution.py:24
  331.7 20.1 %collective-permute-start.34 = (f32[16,2560]{1,0:T(8,128)S(1)}, f32[16,2560]{1,0:T(8,128)}, u32[]{:S(2)}, u32[]{:S(2)}) collective-permute-start(f32[16,2560]{1,0:T(8,128)S(1)} %get-tuple-element.46), channel_id=1, source_target_pairs={{0,20},{4,24},{8,28},{12,0},{16,4},{20,8},{24,12},{28,16},{1,21},{... | collective-permute-start | bytes 491528 | tf_op jit(solution)/shard_map/ppermute | solution.py:24
  334.7 17.1 %collective-permute-start.35 = (f32[16,2560]{1,0:T(8,128)S(1)}, f32[16,2560]{1,0:T(8,128)S(1)}, u32[]{:S(2)}, u32[]{:S(2)}) collective-permute-start(f32[16,2560]{1,0:T(8,128)S(1)} %get-tuple-element.45), channel_id=1, source_target_pairs={{0,24},{4,28},{8,0},{12,4},{16,8},{20,12},{24,16},{28,20},{1,25},{... | collective-permute-start | bytes 491528 | tf_op jit(solution)/shard_map/ppermute | solution.py:24
  338.9 12.9 %collective-permute-start.36 = (f32[16,2560]{1,0:T(8,128)S(1)}, f32[16,2560]{1,0:T(8,128)S(1)}, u32[]{:S(2)}, u32[]{:S(2)}) collective-permute-start(f32[16,2560]{1,0:T(8,128)S(1)} %get-tuple-element.44), channel_id=1, source_target_pairs={{0,28},{4,0},{8,4},{12,8},{16,12},{20,16},{24,20},{28,24},{1,29},{... | collective-permute-start | bytes 491528 | tf_op jit(solution)/shard_map/ppermute | solution.py:24
  388.9 6.9 %collective-permute-start.37 = (f32[16,2048]{1,0:T(8,128)S(1)}, f32[16,2048]{1,0:T(8,128)S(1)}, u32[]{:S(2)}, u32[]{:S(2)}) collective-permute-start(f32[16,2048]{1,0:T(8,128)S(1)} %get-tuple-element.64), channel_id=1, source_target_pairs={{0,4},{4,8},{8,12},{12,16},{16,20},{20,24},{24,28},{28,0},{1,5},{5... | collective-permute-start | bytes 393224 | tf_op jit(solution)/shard_map/ppermute | solution.py:24
  390.5 8.2 %collective-permute-start.38 = (f32[16,2048]{1,0:T(8,128)S(1)}, f32[16,2048]{1,0:T(8,128)S(1)}, u32[]{:S(2)}, u32[]{:S(2)}) collective-permute-start(f32[16,2048]{1,0:T(8,128)S(1)} %get-tuple-element.70), channel_id=1, source_target_pairs={{0,8},{4,12},{8,16},{12,20},{16,24},{20,28},{24,0},{28,4},{1,9},{5... | collective-permute-start | bytes 393224 | tf_op jit(solution)/shard_map/ppermute | solution.py:24
  391.6 8.6 %collective-permute-start.39 = (f32[16,2048]{1,0:T(8,128)S(1)}, f32[16,2048]{1,0:T(8,128)S(1)}, u32[]{:S(2)}, u32[]{:S(2)}) collective-permute-start(f32[16,2048]{1,0:T(8,128)S(1)} %get-tuple-element.69), channel_id=1, source_target_pairs={{0,12},{4,16},{8,20},{12,24},{16,28},{20,0},{24,4},{28,8},{1,13},{... | collective-permute-start | bytes 393224 | tf_op jit(solution)/shard_map/ppermute | solution.py:24
  391.6 13.0 %collective-permute-start.40 = (f32[16,2048]{1,0:T(8,128)S(1)}, f32[16,2048]{1,0:T(8,128)S(1)}, u32[]{:S(2)}, u32[]{:S(2)}) collective-permute-start(f32[16,2048]{1,0:T(8,128)S(1)} %get-tuple-element.68), channel_id=1, source_target_pairs={{0,16},{4,20},{8,24},{12,28},{16,0},{20,4},{24,8},{28,12},{1,17},{... | collective-permute-start | bytes 393224 | tf_op jit(solution)/shard_map/ppermute | solution.py:24
  392.8 11.9 %collective-permute-start.41 = (f32[16,2048]{1,0:T(8,128)S(1)}, f32[16,2048]{1,0:T(8,128)S(1)}, u32[]{:S(2)}, u32[]{:S(2)}) collective-permute-start(f32[16,2048]{1,0:T(8,128)S(1)} %get-tuple-element.67), channel_id=1, source_target_pairs={{0,20},{4,24},{8,28},{12,0},{16,4},{20,8},{24,12},{28,16},{1,21},{... | collective-permute-start | bytes 393224 | tf_op jit(solution)/shard_map/ppermute | solution.py:24
  395.8 9.0 %collective-permute-start.42 = (f32[16,2048]{1,0:T(8,128)S(1)}, f32[16,2048]{1,0:T(8,128)S(1)}, u32[]{:S(2)}, u32[]{:S(2)}) collective-permute-start(f32[16,2048]{1,0:T(8,128)S(1)} %get-tuple-element.66), channel_id=1, source_target_pairs={{0,24},{4,28},{8,0},{12,4},{16,8},{20,12},{24,16},{28,20},{1,25},{... | collective-permute-start | bytes 393224 | tf_op jit(solution)/shard_map/ppermute | solution.py:24
  398.6 6.1 %collective-permute-start.43 = (f32[16,2048]{1,0:T(8,128)S(1)}, f32[16,2048]{1,0:T(8,128)S(1)}, u32[]{:S(2)}, u32[]{:S(2)}) collective-permute-start(f32[16,2048]{1,0:T(8,128)S(1)} %get-tuple-element.65), channel_id=1, source_target_pairs={{0,28},{4,0},{8,4},{12,8},{16,12},{20,16},{24,20},{28,24},{1,29},{... | collective-permute-start | bytes 393224 | tf_op jit(solution)/shard_map/ppermute | solution.py:24
  538.1 7.9 %collective-permute-start.47 = (f32[16,2048]{1,0:T(8,128)S(1)}, f32[16,2048]{1,0:T(8,128)S(1)}, u32[]{:S(2)}, u32[]{:S(2)}) collective-permute-start(f32[16,2048]{1,0:T(8,128)S(1)} %get-tuple-element.57), channel_id=1, source_target_pairs={{0,4},{4,8},{8,12},{12,16},{16,20},{20,24},{24,28},{28,0},{1,5},{5... | collective-permute-start | bytes 393224 | tf_op jit(solution)/shard_map/ppermute | solution.py:24
  541.8 7.0 %collective-permute-start.48 = (f32[16,2048]{1,0:T(8,128)S(1)}, f32[16,2048]{1,0:T(8,128)S(1)}, u32[]{:S(2)}, u32[]{:S(2)}) collective-permute-start(f32[16,2048]{1,0:T(8,128)S(1)} %get-tuple-element.63), channel_id=1, source_target_pairs={{0,8},{4,12},{8,16},{12,20},{16,24},{20,28},{24,0},{28,4},{1,9},{5... | collective-permute-start | bytes 393224 | tf_op jit(solution)/shard_map/ppermute | solution.py:24
  543.0 8.6 %collective-permute-start.49 = (f32[16,2048]{1,0:T(8,128)S(1)}, f32[16,2048]{1,0:T(8,128)S(1)}, u32[]{:S(2)}, u32[]{:S(2)}) collective-permute-start(f32[16,2048]{1,0:T(8,128)S(1)} %get-tuple-element.62), channel_id=1, source_target_pairs={{0,12},{4,16},{8,20},{12,24},{16,28},{20,0},{24,4},{28,8},{1,13},{... | collective-permute-start | bytes 393224 | tf_op jit(solution)/shard_map/ppermute | solution.py:24
  543.3 11.4 %collective-permute-start.50 = (f32[16,2048]{1,0:T(8,128)S(1)}, f32[16,2048]{1,0:T(8,128)S(1)}, u32[]{:S(2)}, u32[]{:S(2)}) collective-permute-start(f32[16,2048]{1,0:T(8,128)S(1)} %get-tuple-element.61), channel_id=1, source_target_pairs={{0,16},{4,20},{8,24},{12,28},{16,0},{20,4},{24,8},{28,12},{1,17},{... | collective-permute-start | bytes 393224 | tf_op jit(solution)/shard_map/ppermute | solution.py:24
  543.6 11.3 %collective-permute-start.51 = (f32[16,2048]{1,0:T(8,128)S(1)}, f32[16,2048]{1,0:T(8,128)S(1)}, u32[]{:S(2)}, u32[]{:S(2)}) collective-permute-start(f32[16,2048]{1,0:T(8,128)S(1)} %get-tuple-element.60), channel_id=1, source_target_pairs={{0,20},{4,24},{8,28},{12,0},{16,4},{20,8},{24,12},{28,16},{1,21},{... | collective-permute-start | bytes 393224 | tf_op jit(solution)/shard_map/ppermute | solution.py:24
  546.0 8.9 %collective-permute-start.52 = (f32[16,2048]{1,0:T(8,128)S(1)}, f32[16,2048]{1,0:T(8,128)S(1)}, u32[]{:S(2)}, u32[]{:S(2)}) collective-permute-start(f32[16,2048]{1,0:T(8,128)S(1)} %get-tuple-element.59), channel_id=1, source_target_pairs={{0,24},{4,28},{8,0},{12,4},{16,8},{20,12},{24,16},{28,20},{1,25},{... | collective-permute-start | bytes 393224 | tf_op jit(solution)/shard_map/ppermute | solution.py:24
  548.8 6.4 %collective-permute-start.53 = (f32[16,2048]{1,0:T(8,128)S(1)}, f32[16,2048]{1,0:T(8,128)S(1)}, u32[]{:S(2)}, u32[]{:S(2)}) collective-permute-start(f32[16,2048]{1,0:T(8,128)S(1)} %get-tuple-element.58), channel_id=1, source_target_pairs={{0,28},{4,0},{8,4},{12,8},{16,12},{20,16},{24,20},{28,24},{1,29},{... | collective-permute-start | bytes 393224 | tf_op jit(solution)/shard_map/ppermute | solution.py:24
  (42 other events, 555.2 us)
Sparse Core Ops, SparseCore 0:
  179.2 69.6 reduce-scatter.6
  441.5 68.2 reduce-scatter.8

commit v3 on v2

--- a/solution.py
+++ b/solution.py
@@ -61,36 +61,52 @@
     return (residual * inv_norm[:, None] * gains.astype(jnp.float32)[None, :]).astype(jnp.bfloat16)
 
 
-def attend(query_rows, fresh_key, fresh_value, cached_keys, cached_values, lengths):
+def attend(query_rows, fresh_key, fresh_value, key_cache, value_cache, layer, lengths):
     score_scale = 1.0 / math.sqrt(query_rows.shape[-1])
+    requests, kv_heads, group, head_dim = query_rows.shape
     finish = jnp.cumsum(lengths)
     starts = finish - lengths
-    capacity = cached_keys.shape[0]
+    capacity = key_cache.shape[1]
     key_rows = jnp.arange(capacity, dtype=jnp.int32)
     inside = (key_rows[None, :] >= starts[:, None]) & (key_rows[None, :] < finish[:, None])
-    inside = inside[:, None, None, :]
-    scores = (
-        jnp.einsum("igrd,tgd->igrt", query_rows, cached_keys, preferred_element_type=jnp.float32)
-        * score_scale
-    )
-    self_score = (
-        jnp.einsum("igrd,igd->igr", query_rows, fresh_key, preferred_element_type=jnp.float32)
-        * score_scale
-    )
-    top = jnp.maximum(jnp.max(jnp.where(inside, scores, -jnp.inf), axis=-1), self_score)
-    exps = jnp.where(inside, jnp.exp(scores - top[..., None]), 0.0)
-    self_exp = jnp.exp(self_score - top)
-    total = jnp.sum(exps, axis=-1) + self_exp
-    combined = jnp.einsum(
-        "igrt,tgd->igrd",
-        exps.astype(jnp.bfloat16),
-        cached_values,
-        preferred_element_type=jnp.float32,
-    )
-    combined = combined + self_exp.astype(jnp.bfloat16).astype(jnp.float32)[..., None] * (
-        fresh_value.astype(jnp.float32)[:, :, None, :]
-    )
-    return (combined / total[..., None]).astype(jnp.bfloat16)
+    inside = jnp.broadcast_to(inside[:, None, :], (requests, group, capacity)).reshape(
+        requests * group, capacity
+    )
+    outputs = []
+    for head in range(kv_heads):
+        columns = slice(head * head_dim, (head + 1) * head_dim)
+        head_queries = query_rows[:, head].reshape(requests * group, head_dim)
+        scores = (
+            lax.dot_general(
+                head_queries,
+                key_cache[layer, :, columns],
+                (((1,), (1,)), ((), ())),
+                preferred_element_type=jnp.float32,
+            )
+            * score_scale
+        )
+        self_score = (
+            jnp.einsum(
+                "ird,id->ir",
+                query_rows[:, head],
+                fresh_key[:, head],
+                preferred_element_type=jnp.float32,
+            ).reshape(requests * group)
+            * score_scale
+        )
+        top = jnp.maximum(jnp.max(jnp.where(inside, scores, -jnp.inf), axis=-1), self_score)
+        exps = jnp.where(inside, jnp.exp(scores - top[:, None]), 0.0)
+        self_exp = jnp.exp(self_score - top)
+        total = jnp.sum(exps, axis=-1) + self_exp
+        combined = jnp.dot(
+            exps.astype(jnp.bfloat16),
+            value_cache[layer, :, columns],
+            preferred_element_type=jnp.float32,
+        )
+        fresh = jnp.repeat(fresh_value[:, head].astype(jnp.float32), group, axis=0)
+        combined = combined + self_exp.astype(jnp.bfloat16).astype(jnp.float32)[:, None] * fresh
+        outputs.append((combined / total[:, None]).astype(jnp.bfloat16).reshape(requests, group, head_dim))
+    return jnp.stack(outputs, axis=1)
 
 
 def body(
@@ -151,12 +167,14 @@
             .reshape(own_rows, kv_heads, head_dim)
             .astype(jnp.bfloat16)
         )
-        cached_keys = rotated_key_cache[current_layer_index].reshape(capacity, kv_heads, head_dim)
-        cached_values = stored_value_cache[current_layer_index].reshape(
-            capacity, kv_heads, head_dim
-        )
         attention_output = attend(
-            query_rows, fresh_key, fresh_value, cached_keys, cached_values, lengths
+            query_rows,
+            fresh_key,
+            fresh_value,
+            rotated_key_cache,
+            stored_value_cache,
+            current_layer_index,
+            lengths,
         ).reshape(own_rows, query_width)
         head_rows = rows_for_weights(attention_output)
         project_picked = jnp.take(head_rows, inverse, axis=0)

time: 573 us -> 564 us (0.984)
  the two profiles are of different devices: /device:TPU:1 before, /device:TPU:0 now
where the time goes in v3:
time: 564 us; the launch traced here: 554 us
  waiting for transfers between devices  226 us (40%)
  blocking collectives  135 us (24%)
  matrix products  71.2 us (13%)
  starting transfers between devices  61 us (11%)
  local copies, waits for them, and re-layouts  25.2 us (4%)
  other arithmetic  21.3 us (4%)
  between operations  14.8 us (3%)
    reduce_scatter x2, waiting for transfers between devices, body(): lax.psum_scatter(jnp.concatenate([jnp.dot(tokens, w_gate, preferred_eleme...  137 us
    ppermute x42, waiting for transfers between devices, scatter_sum(): lax.ppermute(piece, axis, [(j, (j + shift) % count) for j in range(count)])  64.5 us
    all_gather x4, blocking collectives, rows_for_weights(): wide = lax.all_gather(block, 'kv', axis=1, tiled=True)  56 us
    all_gather x2, blocking collectives, body(): hidden_all = lax.all_gather(local_hidden, 'kv', axis=0, tiled=True)  40.9 us
    ppermute x42, starting transfers between devices, scatter_sum(): lax.ppermute(piece, axis, [(j, (j + shift) % count) for j in range(count)])  37.9 us
    all_to_all x2, blocking collectives, rows_for_weights(): return lax.all_to_all(wide, 'req', 1, 0, tiled=True)  19.2 us
    all_gather x2, blocking collectives, body(): tokens = lax.all_gather(normed_mlp, 'req', axis=0, tiled=True)  18.4 us
    unnamed x62, local copies, waits for them, and re-layouts  16.6 us
  transfers between devices with their start and end apart: 58, of which 43 were waited for; matrix products, arithmetic and copies ran while one was open for 3% of the time, Pallas kernels for 0%

profile of v3, /device:TPU:0, one launch (start us, length us, event | category | flops | bytes accessed | tf_op | source)
XLA Modules:
  0.0 554.2 jit_solution(6385373207251709814)
XLA Ops:
  7.5 5.1 collective-permute-start.2
  18.4 4.9 constant_dynamic-update-slice_fusion.2
  25.7 13.9 %all_gather.24 = bf16[16,8192]{1,0:T(8,128)(2,1)S(1)} all-gather(bf16[16,2048]{1,0:T(8,128)(2,1)S(1)} %fusion.160), channel_id=1, replica_groups=mesh['req'=8,'kv'=4] {'kv'}, dimensions={1}, use_global_device_ids=true | all-gather | bytes 327680 | tf_op jit(solution)/shard_map/all_gather | solution.py:31
  40.3 3.7 all-to-all-start
  46.6 4.4 all-to-all-done
  51.8 3.4 fusion.138
  55.4 2.6 collective-permute-start.9
  68.0 5.5 collective-permute-done.6
  76.7 2.8 fusion
  79.6 3.6 fusion.4
  87.0 13.9 %all_gather.25 = bf16[16,8192]{1,0:T(8,128)(2,1)S(1)} all-gather(bf16[16,2048]{1,0:T(8,128)(2,1)S(1)} %bitcast.511), channel_id=1, replica_groups=mesh['req'=8,'kv'=4] {'kv'}, dimensions={1}, use_global_device_ids=true | all-gather | bytes 327680 | tf_op jit(solution)/shard_map/all_gather | solution.py:31
  101.7 3.4 all-to-all-start.1
  105.2 6.8 %all-to-all-done.1 = bf16[16,8,1024]{2,0,1:T(8,128)(2,1)S(1)} async-done(((bf16[16,8,1024]{2,0,1:T(8,128)(2,1)}), bf16[16,8,1024]{2,0,1:T(8,128)(2,1)S(1)}, u32[]{:S(2)}, u32[]{:S(2)}) %all-to-all-start.1) | async-done | bytes 262176 | tf_op jit(solution)/shard_map/all_to_all | solution.py:32
  112.8 3.1 fusion.136
  116.3 2.6 collective-permute-start.16
  127.9 4.5 collective-permute-done.12
  132.6 3.4 collective-permute-start.19
  137.3 3.1 collective-permute-done.18
  141.5 9.1 %all_gather.26 = bf16[128,2048]{1,0:T(8,128)(2,1)S(1)} all-gather(bf16[16,2048]{1,0:T(8,128)(2,1)S(1)} %multiply_convert_fusion.2), channel_id=1, replica_groups=mesh['req'=8,'kv'=4] {'req'}, dimensions={0}, use_global_device_ids=true | all-gather | bytes 589824 | tf_op jit(solution)/shard_map/all_gather | solution.py:185
  150.5 7.8 %fusion.249 = f32[128,3696]{0,1:T(8,128)S(1)} fusion(bf16[128,2048]{1,0:T(8,128)(2,1)S(1)} %all_gather.26, bf16[2048,3696]{0,1:T(8,128)(2,1)} %param.40), kind=kOutput, calls=%fused_computation.332 | convolution fusion | flops 1937768448 | bytes 17555456 | tf_op jit(solution)/shard_map/dot_general | solution.py:191
  158.4 4.3 fusion.248
  164.9 5.3 copy.76
  170.3 68.5 %reduce-scatter.7.cloned.1.call-done = f32[32,7392]{1,0:T(8,128)} async-done(((f32[128,7392]{1,0:T(8,128)}), f32[32,7392]{1,0:T(8,128)}) %reduce-scatter.7.cloned.1.call-update) | async-done | bytes 946192 | tf_op jit(solution)/shard_map/reduce_scatter | solution.py:187
  240.1 20.5 %all_gather.27 = bf16[128,3696]{1,0:T(8,128)(2,1)S(1)} all-gather(bf16[32,3696]{1,0:T(8,128)(2,1)S(1)} %fusion.131), channel_id=1, replica_groups=mesh['req'=8,'kv'=4] {'kv'}, dimensions={0}, use_global_device_ids=true | all-gather | bytes 1182720 | tf_op jit(solution)/shard_map/all_gather | solution.py:202
  260.6 7.7 %fusion.250 = f32[128,2048]{1,0:T(8,128)S(1)} fusion(bf16[128,3696]{1,0:T(8,128)(2,1)S(1)} %all_gather.27, bf16[3696,2048]{1,0:T(8,128)(2,1)} %param.41), kind=kOutput, calls=%fused_computation.333 | convolution fusion | flops 1937768448 | bytes 17133568 | tf_op jit(solution)/shard_map/dot_general | solution.py:204
  268.5 2.6 collective-permute-start.26
  280.3 4.6 collective-permute-done.22
  288.7 3.0 collective-permute-done.28
  292.7 13.9 %all_gather.28 = bf16[16,8192]{1,0:T(8,128)(2,1)S(1)} all-gather(bf16[16,2048]{1,0:T(8,128)(2,1)S(1)} %multiply_convert_fusion.1), channel_id=1, replica_groups=mesh['req'=8,'kv'=4] {'kv'}, dimensions={1}, use_global_device_ids=true | all-gather | bytes 327680 | tf_op jit(solution)/shard_map/all_gather | solution.py:31
  306.6 9.9 %all_to_all.76 = bf16[16,8,1024]{2,0,1:T(8,128)(2,1)S(1)} all-to-all(bf16[16,8,1024]{2,0,1:T(8,128)(2,1)S(1)} %bitcast.509), channel_id=1, replica_groups=mesh['req'=8,'kv'=4] {'req'}, dimensions={1} | all-to-all | bytes 524288 | tf_op jit(solution)/shard_map/all_to_all | solution.py:32
  317.4 3.4 fusion.134
  325.4 3.0 collective-permute-done.30
  328.5 3.2 collective-permute-done.35
  333.6 5.5 collective-permute-done.33
  341.1 2.8 fusion.2
  343.9 3.6 fusion.8
  351.4 14.3 %all_gather.29 = bf16[16,8192]{1,0:T(8,128)(2,1)S(1)} all-gather(bf16[16,2048]{1,0:T(8,128)(2,1)S(1)} %bitcast.512), channel_id=1, replica_groups=mesh['req'=8,'kv'=4] {'kv'}, dimensions={1}, use_global_device_ids=true | all-gather | bytes 327680 | tf_op jit(solution)/shard_map/all_gather | solution.py:31
  365.7 9.3 %all_to_all.77 = bf16[16,8,1024]{2,0,1:T(8,128)(2,1)S(1)} all-to-all(bf16[16,8,1024]{2,0,1:T(8,128)(2,1)S(1)} %bitcast.510), channel_id=1, replica_groups=mesh['req'=8,'kv'=4] {'req'}, dimensions={1} | all-to-all | bytes 524288 | tf_op jit(solution)/shard_map/all_to_all | solution.py:32
  375.9 3.1 fusion.132
  390.8 4.6 collective-permute-done.39
  402.7 9.3 %all_gather.30 = bf16[128,2048]{1,0:T(8,128)(2,1)S(1)} all-gather(bf16[16,2048]{1,0:T(8,128)(2,1)S(1)} %multiply_convert_fusion), channel_id=1, replica_groups=mesh['req'=8,'kv'=4] {'req'}, dimensions={0}, use_global_device_ids=true | all-gather | bytes 589824 | tf_op jit(solution)/shard_map/all_gather | solution.py:185
  412.0 7.8 %fusion.252 = f32[128,3696]{0,1:T(8,128)S(1)} fusion(bf16[128,2048]{1,0:T(8,128)(2,1)S(1)} %all_gather.30, bf16[2048,3696]{0,1:T(8,128)(2,1)} %param.40), kind=kOutput, calls=%fused_computation.335 | convolution fusion | flops 1937768448 | bytes 17555456 | tf_op jit(solution)/shard_map/dot_general | solution.py:191
  419.9 4.3 fusion.251
  426.3 5.3 copy.78
  431.6 68.5 %reduce-scatter.9.cloned.1.call-done = f32[32,7392]{1,0:T(8,128)} async-done(((f32[128,7392]{1,0:T(8,128)}), f32[32,7392]{1,0:T(8,128)}) %reduce-scatter.9.cloned.1.call-update) | async-done | bytes 946192 | tf_op jit(solution)/shard_map/reduce_scatter | solution.py:187
  501.5 20.4 %all_gather.31 = bf16[128,3696]{1,0:T(8,128)(2,1)S(1)} all-gather(bf16[32,3696]{1,0:T(8,128)(2,1)S(1)} %fusion.130), channel_id=1, replica_groups=mesh['req'=8,'kv'=4] {'kv'}, dimensions={0}, use_global_device_ids=true | all-gather | bytes 1182720 | tf_op jit(solution)/shard_map/all_gather | solution.py:202
  522.0 7.7 %fusion.253 = f32[128,2048]{1,0:T(8,128)S(1)} fusion(bf16[128,3696]{1,0:T(8,128)(2,1)S(1)} %all_gather.31, bf16[3696,2048]{1,0:T(8,128)(2,1)} %param.41), kind=kOutput, calls=%fused_computation.336 | convolution fusion | flops 1937768448 | bytes 17133568 | tf_op jit(solution)/shard_map/dot_general | solution.py:204
  541.6 4.6 collective-permute-done.49
  (265 shorter events, 110.6 us)
Async XLA Ops:
  7.5 18.0 %collective-permute-start.2 = (f32[16]{0:T(128)S(1)}, f32[16]{0:T(128)S(1)}, u32[]{:S(2)}, u32[]{:S(2)}) collective-permute-start(f32[16]{0:T(128)S(1)} %fusion.158), channel_id=1, source_target_pairs={{0,3},{1,0},{2,1},{3,2},{4,7},{5,4},{6,5},{7,6},{8,11},{9,8},{10,9... | collective-permute-start | bytes 200 | tf_op jit(solution)/shard_map/ppermute | solution.py:57
  12.6 13.0 %collective-permute-start.1 = (f32[16]{0:T(128)S(1)}, f32[16]{0:T(128)S(1)}, u32[]{:S(2)}, u32[]{:S(2)}) collective-permute-start(f32[16]{0:T(128)S(1)} %fusion.158), channel_id=1, source_target_pairs={{0,2},{1,3},{2,0},{3,1},{4,6},{5,7},{6,4},{7,5},{8,10},{9,11},{10,... | collective-permute-start | bytes 200 | tf_op jit(solution)/shard_map/ppermute | solution.py:57
  12.6 13.0 %collective-permute-start = (f32[16]{0:T(128)S(1)}, f32[16]{0:T(128)S(1)}, u32[]{:S(2)}, u32[]{:S(2)}) collective-permute-start(f32[16]{0:T(128)S(1)} %fusion.158), channel_id=1, source_target_pairs={{0,1},{1,2},{2,3},{3,0},{4,5},{5,6},{6,7},{7,4},{8,9},{9,10},{10,1... | collective-permute-start | bytes 200 | tf_op jit(solution)/shard_map/ppermute | solution.py:57
  40.3 10.7 %all-to-all-start = ((bf16[16,8,1024]{2,0,1:T(8,128)(2,1)}), bf16[16,8,1024]{2,0,1:T(8,128)(2,1)S(1)}, u32[]{:S(2)}, u32[]{:S(2)}) async-start(bf16[16,8,1024]{2,0,1:T(8,128)(2,1)} %bitcast.480), calls=%async_computation | async-start | bytes 524288 | tf_op jit(solution)/shard_map/all_to_all | solution.py:32
  55.3 7.5 %collective-permute-start.3 = (f32[16,2560]{1,0:T(8,128)S(1)}, f32[16,2560]{1,0:T(8,128)S(1)}, u32[]{:S(2)}, u32[]{:S(2)}) collective-permute-start(f32[16,2560]{1,0:T(8,128)S(1)} %get-tuple-element.58), channel_id=1, source_target_pairs={{0,4},{4,8},{8,12},{12,16},{16,20},{20,24},{24,28},{28,0},{1,5},{5... | collective-permute-start | bytes 491528 | tf_op jit(solution)/shard_map/ppermute | solution.py:24
  55.4 7.4 %collective-permute-start.9 = (f32[16,2560]{1,0:T(8,128)S(1)}, f32[16,2560]{1,0:T(8,128)S(1)}, u32[]{:S(2)}, u32[]{:S(2)}) collective-permute-start(f32[16,2560]{1,0:T(8,128)S(1)} %get-tuple-element.59), channel_id=1, source_target_pairs={{0,28},{4,0},{8,4},{12,8},{16,12},{20,16},{24,20},{28,24},{1,29},{... | collective-permute-start | bytes 491528 | tf_op jit(solution)/shard_map/ppermute | solution.py:24
  58.8 7.5 %collective-permute-start.8 = (f32[16,2560]{1,0:T(8,128)S(1)}, f32[16,2560]{1,0:T(8,128)S(1)}, u32[]{:S(2)}, u32[]{:S(2)}) collective-permute-start(f32[16,2560]{1,0:T(8,128)S(1)} %get-tuple-element.60), channel_id=1, source_target_pairs={{0,24},{4,28},{8,0},{12,4},{16,8},{20,12},{24,16},{28,20},{1,25},{... | collective-permute-start | bytes 491528 | tf_op jit(solution)/shard_map/ppermute | solution.py:24
  58.8 9.3 %collective-permute-start.7 = (f32[16,2560]{1,0:T(8,128)S(1)}, f32[16,2560]{1,0:T(8,128)S(1)}, u32[]{:S(2)}, u32[]{:S(2)}) collective-permute-start(f32[16,2560]{1,0:T(8,128)S(1)} %get-tuple-element.61), channel_id=1, source_target_pairs={{0,20},{4,24},{8,28},{12,0},{16,4},{20,8},{24,12},{28,16},{1,21},{... | collective-permute-start | bytes 491528 | tf_op jit(solution)/shard_map/ppermute | solution.py:24
  59.0 14.5 %collective-permute-start.6 = (f32[16,2560]{1,0:T(8,128)S(1)}, f32[16,2560]{1,0:T(8,128)S(1)}, u32[]{:S(2)}, u32[]{:S(2)}) collective-permute-start(f32[16,2560]{1,0:T(8,128)S(1)} %get-tuple-element.62), channel_id=1, source_target_pairs={{0,16},{4,20},{8,24},{12,28},{16,0},{20,4},{24,8},{28,12},{1,17},{... | collective-permute-start | bytes 491528 | tf_op jit(solution)/shard_map/ppermute | solution.py:24
  62.8 11.9 %collective-permute-start.5 = (f32[16,2560]{1,0:T(8,128)S(1)}, f32[16,2560]{1,0:T(8,128)S(1)}, u32[]{:S(2)}, u32[]{:S(2)}) collective-permute-start(f32[16,2560]{1,0:T(8,128)S(1)} %get-tuple-element.63), channel_id=1, source_target_pairs={{0,12},{4,16},{8,20},{12,24},{16,28},{20,0},{24,4},{28,8},{1,13},{... | collective-permute-start | bytes 491528 | tf_op jit(solution)/shard_map/ppermute | solution.py:24
  62.8 11.9 %collective-permute-start.4 = (f32[16,2560]{1,0:T(8,128)S(1)}, f32[16,2560]{1,0:T(8,128)}, u32[]{:S(2)}, u32[]{:S(2)}) collective-permute-start(f32[16,2560]{1,0:T(8,128)S(1)} %get-tuple-element.64), channel_id=1, source_target_pairs={{0,8},{4,12},{8,16},{12,20},{16,24},{20,28},{24,0},{28,4},{1,9},{5... | collective-permute-start | bytes 491528 | tf_op jit(solution)/shard_map/ppermute | solution.py:24
  101.7 10.3 %all-to-all-start.1 = ((bf16[16,8,1024]{2,0,1:T(8,128)(2,1)}), bf16[16,8,1024]{2,0,1:T(8,128)(2,1)S(1)}, u32[]{:S(2)}, u32[]{:S(2)}) async-start(bf16[16,8,1024]{2,0,1:T(8,128)(2,1)} %bitcast.479), calls=%async_computation.1 | async-start | bytes 524288 | tf_op jit(solution)/shard_map/all_to_all | solution.py:32
  105.1 133.7 %reduce-scatter.7.cloned.1.call-start = ((), (), s32[]{:S(2)}) async-start(), calls=%async_computation.6 | async-start | bytes 4751360 | tf_op jit(solution)/shard_map/reduce_scatter | solution.py:187
  116.0 6.9 %collective-permute-start.10 = (f32[16,2048]{1,0:T(8,128)S(1)}, f32[16,2048]{1,0:T(8,128)S(1)}, u32[]{:S(2)}, u32[]{:S(2)}) collective-permute-start(f32[16,2048]{1,0:T(8,128)S(1)} %get-tuple-element.86), channel_id=1, source_target_pairs={{0,4},{4,8},{8,12},{12,16},{16,20},{20,24},{24,28},{28,0},{1,5},{5... | collective-permute-start | bytes 393224 | tf_op jit(solution)/shard_map/ppermute | solution.py:24
  116.3 6.7 %collective-permute-start.16 = (f32[16,2048]{1,0:T(8,128)S(1)}, f32[16,2048]{1,0:T(8,128)S(1)}, u32[]{:S(2)}, u32[]{:S(2)}) collective-permute-start(f32[16,2048]{1,0:T(8,128)S(1)} %get-tuple-element.87), channel_id=1, source_target_pairs={{0,28},{4,0},{8,4},{12,8},{16,12},{20,16},{24,20},{28,24},{1,29},{... | collective-permute-start | bytes 393224 | tf_op jit(solution)/shard_map/ppermute | solution.py:24
  118.9 6.8 %collective-permute-start.15 = (f32[16,2048]{1,0:T(8,128)S(1)}, f32[16,2048]{1,0:T(8,128)S(1)}, u32[]{:S(2)}, u32[]{:S(2)}) collective-permute-start(f32[16,2048]{1,0:T(8,128)S(1)} %get-tuple-element.88), channel_id=1, source_target_pairs={{0,24},{4,28},{8,0},{12,4},{16,8},{20,12},{24,16},{28,20},{1,25},{... | collective-permute-start | bytes 393224 | tf_op jit(solution)/shard_map/ppermute | solution.py:24
  118.9 7.9 %collective-permute-start.14 = (f32[16,2048]{1,0:T(8,128)S(1)}, f32[16,2048]{1,0:T(8,128)S(1)}, u32[]{:S(2)}, u32[]{:S(2)}) collective-permute-start(f32[16,2048]{1,0:T(8,128)S(1)} %get-tuple-element.89), channel_id=1, source_target_pairs={{0,20},{4,24},{8,28},{12,0},{16,4},{20,8},{24,12},{28,16},{1,21},{... | collective-permute-start | bytes 393224 | tf_op jit(solution)/shard_map/ppermute | solution.py:24
  119.2 8.7 %collective-permute-start.13 = (f32[16,2048]{1,0:T(8,128)S(1)}, f32[16,2048]{1,0:T(8,128)S(1)}, u32[]{:S(2)}, u32[]{:S(2)}) collective-permute-start(f32[16,2048]{1,0:T(8,128)S(1)} %get-tuple-element.90), channel_id=1, source_target_pairs={{0,16},{4,20},{8,24},{12,28},{16,0},{20,4},{24,8},{28,12},{1,17},{... | collective-permute-start | bytes 393224 | tf_op jit(solution)/shard_map/ppermute | solution.py:24
  123.0 9.5 %collective-permute-start.12 = (f32[16,2048]{1,0:T(8,128)S(1)}, f32[16,2048]{1,0:T(8,128)S(1)}, u32[]{:S(2)}, u32[]{:S(2)}) collective-permute-start(f32[16,2048]{1,0:T(8,128)S(1)} %get-tuple-element.91), channel_id=1, source_target_pairs={{0,12},{4,16},{8,20},{12,24},{16,28},{20,0},{24,4},{28,8},{1,13},{... | collective-permute-start | bytes 393224 | tf_op jit(solution)/shard_map/ppermute | solution.py:24
  123.0 9.5 %collective-permute-start.11 = (f32[16,2048]{1,0:T(8,128)S(1)}, f32[16,2048]{1,0:T(8,128)S(1)}, u32[]{:S(2)}, u32[]{:S(2)}) collective-permute-start(f32[16,2048]{1,0:T(8,128)S(1)} %get-tuple-element.92), channel_id=1, source_target_pairs={{0,8},{4,12},{8,16},{12,20},{16,24},{20,28},{24,0},{28,4},{1,9},{5... | collective-permute-start | bytes 393224 | tf_op jit(solution)/shard_map/ppermute | solution.py:24
  170.2 329.9 %reduce-scatter.9.cloned.1.call-start = ((), (), s32[]{:S(2)}) async-start(), calls=%async_computation.7 | async-start | bytes 4751360 | tf_op jit(solution)/shard_map/reduce_scatter | solution.py:187
  268.4 5.3 collective-permute-start.20
  268.5 6.5 %collective-permute-start.26 = (f32[16,2048]{1,0:T(8,128)S(1)}, f32[16,2048]{1,0:T(8,128)S(1)}, u32[]{:S(2)}, u32[]{:S(2)}) collective-permute-start(f32[16,2048]{1,0:T(8,128)S(1)} %get-tuple-element.80), channel_id=1, source_target_pairs={{0,28},{4,0},{8,4},{12,8},{16,12},{20,16},{24,20},{28,24},{1,29},{... | collective-permute-start | bytes 393224 | tf_op jit(solution)/shard_map/ppermute | solution.py:24
  271.1 7.9 %collective-permute-start.25 = (f32[16,2048]{1,0:T(8,128)S(1)}, f32[16,2048]{1,0:T(8,128)S(1)}, u32[]{:S(2)}, u32[]{:S(2)}) collective-permute-start(f32[16,2048]{1,0:T(8,128)S(1)} %get-tuple-element.81), channel_id=1, source_target_pairs={{0,24},{4,28},{8,0},{12,4},{16,8},{20,12},{24,16},{28,20},{1,25},{... | collective-permute-start | bytes 393224 | tf_op jit(solution)/shard_map/ppermute | solution.py:24
  272.9 7.4 %collective-permute-start.24 = (f32[16,2048]{1,0:T(8,128)S(1)}, f32[16,2048]{1,0:T(8,128)S(1)}, u32[]{:S(2)}, u32[]{:S(2)}) collective-permute-start(f32[16,2048]{1,0:T(8,128)S(1)} %get-tuple-element.82), channel_id=1, source_target_pairs={{0,20},{4,24},{8,28},{12,0},{16,4},{20,8},{24,12},{28,16},{1,21},{... | collective-permute-start | bytes 393224 | tf_op jit(solution)/shard_map/ppermute | solution.py:24
  272.9 7.4 %collective-permute-start.23 = (f32[16,2048]{1,0:T(8,128)S(1)}, f32[16,2048]{1,0:T(8,128)S(1)}, u32[]{:S(2)}, u32[]{:S(2)}) collective-permute-start(f32[16,2048]{1,0:T(8,128)S(1)} %get-tuple-element.83), channel_id=1, source_target_pairs={{0,16},{4,20},{8,24},{12,28},{16,0},{20,4},{24,8},{28,12},{1,17},{... | collective-permute-start | bytes 393224 | tf_op jit(solution)/shard_map/ppermute | solution.py:24
  273.8 11.1 %collective-permute-start.22 = (f32[16,2048]{1,0:T(8,128)S(1)}, f32[16,2048]{1,0:T(8,128)S(1)}, u32[]{:S(2)}, u32[]{:S(2)}) collective-permute-start(f32[16,2048]{1,0:T(8,128)S(1)} %get-tuple-element.84), channel_id=1, source_target_pairs={{0,12},{4,16},{8,20},{12,24},{16,28},{20,0},{24,4},{28,8},{1,13},{... | collective-permute-start | bytes 393224 | tf_op jit(solution)/shard_map/ppermute | solution.py:24
  275.0 9.9 %collective-permute-start.21 = (f32[16,2048]{1,0:T(8,128)S(1)}, f32[16,2048]{1,0:T(8,128)S(1)}, u32[]{:S(2)}, u32[]{:S(2)}) collective-permute-start(f32[16,2048]{1,0:T(8,128)S(1)} %get-tuple-element.85), channel_id=1, source_target_pairs={{0,8},{4,12},{8,16},{12,20},{16,24},{20,28},{24,0},{28,4},{1,9},{5... | collective-permute-start | bytes 393224 | tf_op jit(solution)/shard_map/ppermute | solution.py:24
  320.9 7.5 %collective-permute-start.30 = (f32[16,2560]{1,0:T(8,128)S(1)}, f32[16,2560]{1,0:T(8,128)S(1)}, u32[]{:S(2)}, u32[]{:S(2)}) collective-permute-start(f32[16,2560]{1,0:T(8,128)S(1)} %get-tuple-element.51), channel_id=1, source_target_pairs={{0,4},{4,8},{8,12},{12,16},{16,20},{20,24},{24,28},{28,0},{1,5},{5... | collective-permute-start | bytes 491528 | tf_op jit(solution)/shard_map/ppermute | solution.py:24
  320.9 7.4 %collective-permute-start.36 = (f32[16,2560]{1,0:T(8,128)S(1)}, f32[16,2560]{1,0:T(8,128)S(1)}, u32[]{:S(2)}, u32[]{:S(2)}) collective-permute-start(f32[16,2560]{1,0:T(8,128)S(1)} %get-tuple-element.52), channel_id=1, source_target_pairs={{0,28},{4,0},{8,4},{12,8},{16,12},{20,16},{24,20},{28,24},{1,29},{... | collective-permute-start | bytes 491528 | tf_op jit(solution)/shard_map/ppermute | solution.py:24
  323.6 8.2 %collective-permute-start.35 = (f32[16,2560]{1,0:T(8,128)S(1)}, f32[16,2560]{1,0:T(8,128)S(1)}, u32[]{:S(2)}, u32[]{:S(2)}) collective-permute-start(f32[16,2560]{1,0:T(8,128)S(1)} %get-tuple-element.53), channel_id=1, source_target_pairs={{0,24},{4,28},{8,0},{12,4},{16,8},{20,12},{24,16},{28,20},{1,25},{... | collective-permute-start | bytes 491528 | tf_op jit(solution)/shard_map/ppermute | solution.py:24
  323.6 10.0 %collective-permute-start.34 = (f32[16,2560]{1,0:T(8,128)S(1)}, f32[16,2560]{1,0:T(8,128)S(1)}, u32[]{:S(2)}, u32[]{:S(2)}) collective-permute-start(f32[16,2560]{1,0:T(8,128)S(1)} %get-tuple-element.54), channel_id=1, source_target_pairs={{0,20},{4,24},{8,28},{12,0},{16,4},{20,8},{24,12},{28,16},{1,21},{... | collective-permute-start | bytes 491528 | tf_op jit(solution)/shard_map/ppermute | solution.py:24
  323.9 15.2 %collective-permute-start.33 = (f32[16,2560]{1,0:T(8,128)S(1)}, f32[16,2560]{1,0:T(8,128)S(1)}, u32[]{:S(2)}, u32[]{:S(2)}) collective-permute-start(f32[16,2560]{1,0:T(8,128)S(1)} %get-tuple-element.55), channel_id=1, source_target_pairs={{0,16},{4,20},{8,24},{12,28},{16,0},{20,4},{24,8},{28,12},{1,17},{... | collective-permute-start | bytes 491528 | tf_op jit(solution)/shard_map/ppermute | solution.py:24
  328.3 11.6 %collective-permute-start.32 = (f32[16,2560]{1,0:T(8,128)S(1)}, f32[16,2560]{1,0:T(8,128)S(1)}, u32[]{:S(2)}, u32[]{:S(2)}) collective-permute-start(f32[16,2560]{1,0:T(8,128)S(1)} %get-tuple-element.56), channel_id=1, source_target_pairs={{0,12},{4,16},{8,20},{12,24},{16,28},{20,0},{24,4},{28,8},{1,13},{... | collective-permute-start | bytes 491528 | tf_op jit(solution)/shard_map/ppermute | solution.py:24
  328.3 11.6 %collective-permute-start.31 = (f32[16,2560]{1,0:T(8,128)S(1)}, f32[16,2560]{1,0:T(8,128)S(1)}, u32[]{:S(2)}, u32[]{:S(2)}) collective-permute-start(f32[16,2560]{1,0:T(8,128)S(1)} %get-tuple-element.57), channel_id=1, source_target_pairs={{0,8},{4,12},{8,16},{12,20},{16,24},{20,28},{24,0},{28,4},{1,9},{5... | collective-permute-start | bytes 491528 | tf_op jit(solution)/shard_map/ppermute | solution.py:24
  379.1 6.8 %collective-permute-start.37 = (f32[16,2048]{1,0:T(8,128)S(1)}, f32[16,2048]{1,0:T(8,128)S(1)}, u32[]{:S(2)}, u32[]{:S(2)}) collective-permute-start(f32[16,2048]{1,0:T(8,128)S(1)} %get-tuple-element.72), channel_id=1, source_target_pairs={{0,4},{4,8},{8,12},{12,16},{16,20},{20,24},{24,28},{28,0},{1,5},{5... | collective-permute-start | bytes 393224 | tf_op jit(solution)/shard_map/ppermute | solution.py:24
  379.2 6.7 %collective-permute-start.43 = (f32[16,2048]{1,0:T(8,128)S(1)}, f32[16,2048]{1,0:T(8,128)S(1)}, u32[]{:S(2)}, u32[]{:S(2)}) collective-permute-start(f32[16,2048]{1,0:T(8,128)S(1)} %get-tuple-element.73), channel_id=1, source_target_pairs={{0,28},{4,0},{8,4},{12,8},{16,12},{20,16},{24,20},{28,24},{1,29},{... | collective-permute-start | bytes 393224 | tf_op jit(solution)/shard_map/ppermute | solution.py:24
  381.8 6.8 %collective-permute-start.42 = (f32[16,2048]{1,0:T(8,128)S(1)}, f32[16,2048]{1,0:T(8,128)S(1)}, u32[]{:S(2)}, u32[]{:S(2)}) collective-permute-start(f32[16,2048]{1,0:T(8,128)S(1)} %get-tuple-element.74), channel_id=1, source_target_pairs={{0,24},{4,28},{8,0},{12,4},{16,8},{20,12},{24,16},{28,20},{1,25},{... | collective-permute-start | bytes 393224 | tf_op jit(solution)/shard_map/ppermute | solution.py:24
  381.8 7.9 %collective-permute-start.41 = (f32[16,2048]{1,0:T(8,128)S(1)}, f32[16,2048]{1,0:T(8,128)S(1)}, u32[]{:S(2)}, u32[]{:S(2)}) collective-permute-start(f32[16,2048]{1,0:T(8,128)S(1)} %get-tuple-element.75), channel_id=1, source_target_pairs={{0,20},{4,24},{8,28},{12,0},{16,4},{20,8},{24,12},{28,16},{1,21},{... | collective-permute-start | bytes 393224 | tf_op jit(solution)/shard_map/ppermute | solution.py:24
  382.1 8.6 %collective-permute-start.40 = (f32[16,2048]{1,0:T(8,128)S(1)}, f32[16,2048]{1,0:T(8,128)S(1)}, u32[]{:S(2)}, u32[]{:S(2)}) collective-permute-start(f32[16,2048]{1,0:T(8,128)S(1)} %get-tuple-element.76), channel_id=1, source_target_pairs={{0,16},{4,20},{8,24},{12,28},{16,0},{20,4},{24,8},{28,12},{1,17},{... | collective-permute-start | bytes 393224 | tf_op jit(solution)/shard_map/ppermute | solution.py:24
  385.9 9.5 %collective-permute-start.39 = (f32[16,2048]{1,0:T(8,128)S(1)}, f32[16,2048]{1,0:T(8,128)S(1)}, u32[]{:S(2)}, u32[]{:S(2)}) collective-permute-start(f32[16,2048]{1,0:T(8,128)S(1)} %get-tuple-element.77), channel_id=1, source_target_pairs={{0,12},{4,16},{8,20},{12,24},{16,28},{20,0},{24,4},{28,8},{1,13},{... | collective-permute-start | bytes 393224 | tf_op jit(solution)/shard_map/ppermute | solution.py:24
  385.9 9.5 %collective-permute-start.38 = (f32[16,2048]{1,0:T(8,128)S(1)}, f32[16,2048]{1,0:T(8,128)S(1)}, u32[]{:S(2)}, u32[]{:S(2)}) collective-permute-start(f32[16,2048]{1,0:T(8,128)S(1)} %get-tuple-element.78), channel_id=1, source_target_pairs={{0,8},{4,12},{8,16},{12,20},{16,24},{20,28},{24,0},{28,4},{1,9},{5... | collective-permute-start | bytes 393224 | tf_op jit(solution)/shard_map/ppermute | solution.py:24
  529.8 6.6 %collective-permute-start.53 = (f32[16,2048]{1,0:T(8,128)S(1)}, f32[16,2048]{1,0:T(8,128)S(1)}, u32[]{:S(2)}, u32[]{:S(2)}) collective-permute-start(f32[16,2048]{1,0:T(8,128)S(1)} %get-tuple-element.66), channel_id=1, source_target_pairs={{0,28},{4,0},{8,4},{12,8},{16,12},{20,16},{24,20},{28,24},{1,29},{... | collective-permute-start | bytes 393224 | tf_op jit(solution)/shard_map/ppermute | solution.py:24
  532.5 8.0 %collective-permute-start.52 = (f32[16,2048]{1,0:T(8,128)S(1)}, f32[16,2048]{1,0:T(8,128)S(1)}, u32[]{:S(2)}, u32[]{:S(2)}) collective-permute-start(f32[16,2048]{1,0:T(8,128)S(1)} %get-tuple-element.67), channel_id=1, source_target_pairs={{0,24},{4,28},{8,0},{12,4},{16,8},{20,12},{24,16},{28,20},{1,25},{... | collective-permute-start | bytes 393224 | tf_op jit(solution)/shard_map/ppermute | solution.py:24
  534.2 7.4 %collective-permute-start.51 = (f32[16,2048]{1,0:T(8,128)S(1)}, f32[16,2048]{1,0:T(8,128)S(1)}, u32[]{:S(2)}, u32[]{:S(2)}) collective-permute-start(f32[16,2048]{1,0:T(8,128)S(1)} %get-tuple-element.68), channel_id=1, source_target_pairs={{0,20},{4,24},{8,28},{12,0},{16,4},{20,8},{24,12},{28,16},{1,21},{... | collective-permute-start | bytes 393224 | tf_op jit(solution)/shard_map/ppermute | solution.py:24
  534.2 7.4 %collective-permute-start.50 = (f32[16,2048]{1,0:T(8,128)S(1)}, f32[16,2048]{1,0:T(8,128)S(1)}, u32[]{:S(2)}, u32[]{:S(2)}) collective-permute-start(f32[16,2048]{1,0:T(8,128)S(1)} %get-tuple-element.69), channel_id=1, source_target_pairs={{0,16},{4,20},{8,24},{12,28},{16,0},{20,4},{24,8},{28,12},{1,17},{... | collective-permute-start | bytes 393224 | tf_op jit(solution)/shard_map/ppermute | solution.py:24
  535.1 11.1 %collective-permute-start.49 = (f32[16,2048]{1,0:T(8,128)S(1)}, f32[16,2048]{1,0:T(8,128)S(1)}, u32[]{:S(2)}, u32[]{:S(2)}) collective-permute-start(f32[16,2048]{1,0:T(8,128)S(1)} %get-tuple-element.70), channel_id=1, source_target_pairs={{0,12},{4,16},{8,20},{12,24},{16,28},{20,0},{24,4},{28,8},{1,13},{... | collective-permute-start | bytes 393224 | tf_op jit(solution)/shard_map/ppermute | solution.py:24
  536.5 9.8 %collective-permute-start.48 = (f32[16,2048]{1,0:T(8,128)S(1)}, f32[16,2048]{1,0:T(8,128)S(1)}, u32[]{:S(2)}, u32[]{:S(2)}) collective-permute-start(f32[16,2048]{1,0:T(8,128)S(1)} %get-tuple-element.71), channel_id=1, source_target_pairs={{0,8},{4,12},{8,16},{12,20},{16,24},{20,28},{24,0},{28,4},{1,9},{5... | collective-permute-start | bytes 393224 | tf_op jit(solution)/shard_map/ppermute | solution.py:24
  (36 other events, 509.3 us)
Sparse Core Ops, SparseCore 0:
  170.3 68.3 reduce-scatter.6
  431.7 68.3 reduce-scatter.8

commit v4 on v3

--- a/solution.py
+++ b/solution.py
@@ -28,8 +28,26 @@
 
 
 def rows_for_weights(block):
-    wide = lax.all_gather(block, "kv", axis=1, tiled=True)
-    return lax.all_to_all(wide, "req", 1, 0, tiled=True)
+    req_size = lax.axis_size("req")
+    kv_size = lax.axis_size("kv")
+    ratio = req_size // kv_size
+    width = block.shape[1] // ratio
+    source_row = lax.axis_index("req")
+    source_column = lax.axis_index("kv")
+    received = []
+    for step in range(req_size):
+        part = (source_row - step) % req_size // kv_size
+        piece = lax.dynamic_slice_in_dim(block, part * width, width, 1)
+        pairs = []
+        for row in range(req_size):
+            for column in range(kv_size):
+                slot = (row - step) % req_size
+                target_row = column * ratio + slot // kv_size
+                pairs.append((row * kv_size + column, target_row * kv_size + slot % kv_size))
+        received.append(lax.ppermute(piece, ("req", "kv"), pairs))
+    base = source_row % ratio * kv_size + source_column
+    stacked = jnp.roll(jnp.stack(received), base, axis=0)
+    return stacked.reshape(req_size * block.shape[0], width)
 
 
 def apply_rotation(values, token_positions):

time: 564 us -> 631 us (1.12)
  the two profiles are of different devices: /device:TPU:0 before, /device:TPU:18 now
where the time goes in v4:
time: 631 us; the launch traced here: 619 us
  waiting for transfers between devices  246 us (39%)
  starting transfers between devices  181 us (29%)
  matrix products  71.2 us (11%)
  blocking collectives  59.7 us (9%)
  local copies, waits for them, and re-layouts  23.9 us (4%)
  other arithmetic  22.5 us (4%)
  between operations  15.5 us (2%)
    reduce_scatter x2, waiting for transfers between devices, body(): lax.psum_scatter(jnp.concatenate([jnp.dot(tokens, w_gate, preferred_eleme...  140 us
    ppermute x32, starting transfers between devices, rows_for_weights(): received.append(lax.ppermute(piece, ('req', 'kv'), pairs))  117 us
    ppermute x42, waiting for transfers between devices, scatter_sum(): lax.ppermute(piece, axis, [(j, (j + shift) % count) for j in range(count)])  58.4 us
    ppermute x42, starting transfers between devices, scatter_sum(): lax.ppermute(piece, axis, [(j, (j + shift) % count) for j in range(count)])  42.3 us
    all_gather x2, blocking collectives, body(): hidden_all = lax.all_gather(local_hidden, 'kv', axis=0, tiled=True)  37.8 us
    ppermute x32, waiting for transfers between devices, rows_for_weights(): received.append(lax.ppermute(piece, ('req', 'kv'), pairs))  36.2 us
    all_gather x2, blocking collectives, body(): tokens = lax.all_gather(normed_mlp, 'req', axis=0, tiled=True)  21.9 us
    ppermute x12, starting transfers between devices, normalize(): lax.ppermute(square_sum, 'kv', [(j, (j + shift) % count) for j in range(c...  21.4 us
  transfers between devices with their start and end apart: 88, of which 46 were waited for; matrix products, arithmetic and copies ran while one was open for 3% of the time, Pallas kernels for 0%

profile of v4, /device:TPU:18, one launch (start us, length us, event | category | flops | bytes accessed | tf_op | source)
XLA Modules:
  0.0 619.0 jit_solution(18376138791773731042)
XLA Ops:
  8.0 3.5 collective-permute-start.1
  20.8 4.9 constant_dynamic-update-slice_fusion.10
  27.7 3.4 collective-permute-start.3
  34.7 5.2 collective-permute-start.9
  43.1 3.5 collective-permute-start.4
  48.6 7.0 %collective-permute-start.5 = (bf16[16,1024]{1,0:T(8,128)(2,1)S(1)}, bf16[16,1024]{1,0:T(8,128)(2,1)S(1)}, u32[]{:S(2)}, u32[]{:S(2)}) collective-permute-start(bf16[16,1024]{1,0:T(8,128)(2,1)S(1)} %get-tuple-element.127), channel_id=1, source_target_pairs={{0,6},{1,14},{2,22},{3,30},{4,7},{5,15},{6,23},{7,31},{8,0},{9,8},... | collective-permute-start | bytes 98312 | tf_op jit(solution)/shard_map/ppermute | solution.py:47
  57.1 5.2 collective-permute-start.6
  77.4 3.5 collective-permute-done.16
  84.1 3.8 collective-permute-done.14
  92.9 3.6 fusion.4
  103.3 8.7 %collective-permute-start.25 = (bf16[16,1024]{1,0:T(8,128)(2,1)S(1)}, bf16[16,1024]{1,0:T(8,128)(2,1)S(1)}, u32[]{:S(2)}, u32[]{:S(2)}) collective-permute-start(bf16[16,1024]{1,0:T(8,128)(2,1)S(1)} %get-tuple-element.114), channel_id=1, source_target_pairs={{0,1},{1,9},{2,17},{3,25},{4,2},{5,10},{6,18},{7,26},{8,3},{9,11},... | collective-permute-start | bytes 98312 | tf_op jit(solution)/shard_map/ppermute | solution.py:47
  113.9 6.8 %collective-permute-start.23 = (bf16[16,1024]{1,0:T(8,128)(2,1)S(1)}, bf16[16,1024]{1,0:T(8,128)(2,1)S(1)}, u32[]{:S(2)}, u32[]{:S(2)}) collective-permute-start(bf16[16,1024]{1,0:T(8,128)(2,1)S(1)} %get-tuple-element.116), channel_id=1, source_target_pairs={{0,3},{1,11},{2,19},{3,27},{4,4},{5,12},{6,20},{7,28},{8,5},{9,13}... | collective-permute-start | bytes 98312 | tf_op jit(solution)/shard_map/ppermute | solution.py:47
  120.8 4.5 collective-permute-start.19
  126.9 3.5 collective-permute-start.20
  130.5 4.4 collective-permute-done.20
  137.2 4.6 collective-permute-done.21
  157.1 4.3 collective-permute-done.29
  171.6 10.8 %all_gather.12 = bf16[128,2048]{1,0:T(8,128)(2,1)S(1)} all-gather(bf16[16,2048]{1,0:T(8,128)(2,1)S(1)} %multiply_convert_fusion.2), channel_id=1, replica_groups=mesh['req'=8,'kv'=4] {'req'}, dimensions={0}, use_global_device_ids=true | all-gather | bytes 589824 | tf_op jit(solution)/shard_map/all_gather | solution.py:203
  182.4 7.8 %fusion.253 = f32[128,3696]{0,1:T(8,128)S(1)} fusion(bf16[128,2048]{1,0:T(8,128)(2,1)S(1)} %all_gather.12, bf16[2048,3696]{0,1:T(8,128)(2,1)} %param.42), kind=kOutput, calls=%fused_computation.404 | convolution fusion | flops 1937768448 | bytes 17555456 | tf_op jit(solution)/shard_map/dot_general | solution.py:209
  190.2 4.3 fusion.252
  196.7 5.3 copy.58
  202.1 70.1 %reduce-scatter.7.cloned.1.call-done = f32[32,7392]{1,0:T(8,128)} async-done(((f32[128,7392]{1,0:T(8,128)}), f32[32,7392]{1,0:T(8,128)}) %reduce-scatter.7.cloned.1.call-update) | async-done | bytes 946192 | tf_op jit(solution)/shard_map/reduce_scatter | solution.py:205
  273.6 19.0 %all_gather.13 = bf16[128,3696]{1,0:T(8,128)(2,1)S(1)} all-gather(bf16[32,3696]{1,0:T(8,128)(2,1)S(1)} %fusion.131), channel_id=1, replica_groups=mesh['req'=8,'kv'=4] {'kv'}, dimensions={0}, use_global_device_ids=true | all-gather | bytes 1182720 | tf_op jit(solution)/shard_map/all_gather | solution.py:220
  292.6 7.7 %fusion.254 = f32[128,2048]{1,0:T(8,128)S(1)} fusion(bf16[128,3696]{1,0:T(8,128)(2,1)S(1)} %all_gather.13, bf16[3696,2048]{1,0:T(8,128)(2,1)} %param.43), kind=kOutput, calls=%fused_computation.405 | convolution fusion | flops 1937768448 | bytes 17133568 | tf_op jit(solution)/shard_map/dot_general | solution.py:222
  312.2 4.8 collective-permute-done.39
  317.9 3.6 collective-permute-start.44
  330.5 3.8 collective-permute-start.52
  337.7 6.0 collective-permute-start.47
  345.5 4.9 collective-permute-start.48
  356.8 3.7 collective-permute-done.49
  375.7 4.3 collective-permute-done.58
  379.9 3.5 collective-permute-done.57
  387.5 3.6 fusion.8
  398.2 7.5 %collective-permute-start.68 = (bf16[16,1024]{1,0:T(8,128)(2,1)S(1)}, bf16[16,1024]{1,0:T(8,128)(2,1)S(1)}, u32[]{:S(2)}, u32[]{:S(2)}) collective-permute-start(bf16[16,1024]{1,0:T(8,128)(2,1)S(1)} %get-tuple-element.98), channel_id=1, source_target_pairs={{0,1},{1,9},{2,17},{3,25},{4,2},{5,10},{6,18},{7,26},{8,3},{9,11},... | collective-permute-start | bytes 98312 | tf_op jit(solution)/shard_map/ppermute | solution.py:47
  407.6 5.9 collective-permute-start.66
  413.6 4.6 collective-permute-start.62
  419.8 3.5 collective-permute-start.63
  423.3 4.8 collective-permute-done.63
  430.0 5.3 collective-permute-done.64
  457.7 4.1 collective-permute-start.77
  465.5 11.1 %all_gather.14 = bf16[128,2048]{1,0:T(8,128)(2,1)S(1)} all-gather(bf16[16,2048]{1,0:T(8,128)(2,1)S(1)} %multiply_convert_fusion), channel_id=1, replica_groups=mesh['req'=8,'kv'=4] {'req'}, dimensions={0}, use_global_device_ids=true | all-gather | bytes 589824 | tf_op jit(solution)/shard_map/all_gather | solution.py:203
  476.6 7.8 %fusion.256 = f32[128,3696]{0,1:T(8,128)S(1)} fusion(bf16[128,2048]{1,0:T(8,128)(2,1)S(1)} %all_gather.14, bf16[2048,3696]{0,1:T(8,128)(2,1)} %param.42), kind=kOutput, calls=%fused_computation.407 | convolution fusion | flops 1937768448 | bytes 17555456 | tf_op jit(solution)/shard_map/dot_general | solution.py:209
  484.4 4.3 fusion.255
  490.9 5.3 copy.60
  496.2 70.2 %reduce-scatter.9.cloned.1.call-done = f32[32,7392]{1,0:T(8,128)} async-done(((f32[128,7392]{1,0:T(8,128)}), f32[32,7392]{1,0:T(8,128)}) %reduce-scatter.9.cloned.1.call-update) | async-done | bytes 946192 | tf_op jit(solution)/shard_map/reduce_scatter | solution.py:205
  567.7 18.8 %all_gather.15 = bf16[128,3696]{1,0:T(8,128)(2,1)S(1)} all-gather(bf16[32,3696]{1,0:T(8,128)(2,1)S(1)} %fusion.130), channel_id=1, replica_groups=mesh['req'=8,'kv'=4] {'kv'}, dimensions={0}, use_global_device_ids=true | all-gather | bytes 1182720 | tf_op jit(solution)/shard_map/all_gather | solution.py:220
  586.5 7.7 %fusion.257 = f32[128,2048]{1,0:T(8,128)S(1)} fusion(bf16[128,3696]{1,0:T(8,128)(2,1)S(1)} %all_gather.15, bf16[3696,2048]{1,0:T(8,128)(2,1)} %param.43), kind=kOutput, calls=%fused_computation.408 | convolution fusion | flops 1937768448 | bytes 17133568 | tf_op jit(solution)/shard_map/dot_general | solution.py:222
  606.1 4.8 collective-permute-done.82
  (341 shorter events, 194.2 us)
Async XLA Ops:
  6.5 265.7 %reduce-scatter.7.cloned.1.call-start = ((), (), s32[]{:S(2)}) async-start(), calls=%async_computation.2 | async-start | bytes 4751360 | tf_op jit(solution)/shard_map/reduce_scatter | solution.py:205
  7.5 20.1 %collective-permute-start.2 = (f32[16]{0:T(128)S(1)}, f32[16]{0:T(128)S(1)}, u32[]{:S(2)}, u32[]{:S(2)}) collective-permute-start(f32[16]{0:T(128)S(1)} %fusion.162), channel_id=1, source_target_pairs={{0,3},{1,0},{2,1},{3,2},{4,7},{5,4},{6,5},{7,6},{8,11},{9,8},{10,9... | collective-permute-start | bytes 200 | tf_op jit(solution)/shard_map/ppermute | solution.py:75
  8.0 19.6 %collective-permute-start.1 = (f32[16]{0:T(128)S(1)}, f32[16]{0:T(128)S(1)}, u32[]{:S(2)}, u32[]{:S(2)}) collective-permute-start(f32[16]{0:T(128)S(1)} %fusion.162), channel_id=1, source_target_pairs={{0,2},{1,3},{2,0},{3,1},{4,6},{5,7},{6,4},{7,5},{8,10},{9,11},{10,... | collective-permute-start | bytes 200 | tf_op jit(solution)/shard_map/ppermute | solution.py:75
  11.5 16.1 %collective-permute-start = (f32[16]{0:T(128)S(1)}, f32[16]{0:T(128)S(1)}, u32[]{:S(2)}, u32[]{:S(2)}) collective-permute-start(f32[16]{0:T(128)S(1)} %fusion.162), channel_id=1, source_target_pairs={{0,1},{1,2},{2,3},{3,0},{4,5},{5,6},{6,7},{7,4},{8,9},{9,10},{10,1... | collective-permute-start | bytes 200 | tf_op jit(solution)/shard_map/ppermute | solution.py:75
  27.7 15.4 %collective-permute-start.3 = (bf16[16,1024]{1,0:T(8,128)(2,1)S(1)}, bf16[16,1024]{1,0:T(8,128)(2,1)S(1)}, u32[]{:S(2)}, u32[]{:S(2)}) collective-permute-start(bf16[16,1024]{1,0:T(8,128)(2,1)S(1)} %get-tuple-element.129), channel_id=1, source_target_pairs={{0,0},{1,8},{2,16},{3,24},{4,1},{5,9},{6,17},{7,25},{8,2},{9,10},{... | collective-permute-start | bytes 98312 | tf_op jit(solution)/shard_map/ppermute | solution.py:47
  31.3 33.0 %collective-permute-start.10 = (bf16[16,1024]{1,0:T(8,128)(2,1)S(1)}, bf16[16,1024]{1,0:T(8,128)(2,1)S(1)}, u32[]{:S(2)}, u32[]{:S(2)}) collective-permute-start(bf16[16,1024]{1,0:T(8,128)(2,1)S(1)} %get-tuple-element.122), channel_id=1, source_target_pairs={{0,1},{1,9},{2,17},{3,25},{4,2},{5,10},{6,18},{7,26},{8,3},{9,11},... | collective-permute-start | bytes 98312 | tf_op jit(solution)/shard_map/ppermute | solution.py:47
  34.7 29.6 %collective-permute-start.9 = (bf16[16,1024]{1,0:T(8,128)(2,1)S(1)}, bf16[16,1024]{1,0:T(8,128)(2,1)S(1)}, u32[]{:S(2)}, u32[]{:S(2)}) collective-permute-start(bf16[16,1024]{1,0:T(8,128)(2,1)S(1)} %get-tuple-element.123), channel_id=1, source_target_pairs={{0,2},{1,10},{2,18},{3,26},{4,3},{5,11},{6,19},{7,27},{8,4},{9,12}... | collective-permute-start | bytes 98312 | tf_op jit(solution)/shard_map/ppermute | solution.py:47
  39.9 24.4 %collective-permute-start.8 = (bf16[16,1024]{1,0:T(8,128)(2,1)S(1)}, bf16[16,1024]{1,0:T(8,128)(2,1)S(1)}, u32[]{:S(2)}, u32[]{:S(2)}) collective-permute-start(bf16[16,1024]{1,0:T(8,128)(2,1)S(1)} %get-tuple-element.124), channel_id=1, source_target_pairs={{0,3},{1,11},{2,19},{3,27},{4,4},{5,12},{6,20},{7,28},{8,5},{9,13}... | collective-permute-start | bytes 98312 | tf_op jit(solution)/shard_map/ppermute | solution.py:47
  43.0 21.2 %collective-permute-start.7 = (bf16[16,1024]{1,0:T(8,128)(2,1)S(1)}, bf16[16,1024]{1,0:T(8,128)(2,1)S(1)}, u32[]{:S(2)}, u32[]{:S(2)}) collective-permute-start(bf16[16,1024]{1,0:T(8,128)(2,1)S(1)} %get-tuple-element.125), channel_id=1, source_target_pairs={{0,4},{1,12},{2,20},{3,28},{4,5},{5,13},{6,21},{7,29},{8,6},{9,14}... | collective-permute-start | bytes 98312 | tf_op jit(solution)/shard_map/ppermute | solution.py:47
  70.9 9.9 %collective-permute-start.16 = (f32[16,2560]{1,0:T(8,128)S(1)}, f32[16,2560]{1,0:T(8,128)S(1)}, u32[]{:S(2)}, u32[]{:S(2)}) collective-permute-start(f32[16,2560]{1,0:T(8,128)S(1)} %get-tuple-element.61), channel_id=1, source_target_pairs={{0,24},{4,28},{8,0},{12,4},{16,8},{20,12},{24,16},{28,20},{1,25},{... | collective-permute-start | bytes 491528 | tf_op jit(solution)/shard_map/ppermute | solution.py:24
  73.6 10.5 %collective-permute-start.15 = (f32[16,2560]{1,0:T(8,128)S(1)}, f32[16,2560]{1,0:T(8,128)S(1)}, u32[]{:S(2)}, u32[]{:S(2)}) collective-permute-start(f32[16,2560]{1,0:T(8,128)S(1)} %get-tuple-element.62), channel_id=1, source_target_pairs={{0,20},{4,24},{8,28},{12,0},{16,4},{20,8},{24,12},{28,16},{1,21},{... | collective-permute-start | bytes 491528 | tf_op jit(solution)/shard_map/ppermute | solution.py:24
  73.6 14.3 %collective-permute-start.14 = (f32[16,2560]{1,0:T(8,128)S(1)}, f32[16,2560]{1,0:T(8,128)S(1)}, u32[]{:S(2)}, u32[]{:S(2)}) collective-permute-start(f32[16,2560]{1,0:T(8,128)S(1)} %get-tuple-element.63), channel_id=1, source_target_pairs={{0,16},{4,20},{8,24},{12,28},{16,0},{20,4},{24,8},{28,12},{1,17},{... | collective-permute-start | bytes 491528 | tf_op jit(solution)/shard_map/ppermute | solution.py:24
  73.7 14.4 %collective-permute-start.13 = (f32[16,2560]{1,0:T(8,128)S(1)}, f32[16,2560]{1,0:T(8,128)S(1)}, u32[]{:S(2)}, u32[]{:S(2)}) collective-permute-start(f32[16,2560]{1,0:T(8,128)S(1)} %get-tuple-element.64), channel_id=1, source_target_pairs={{0,12},{4,16},{8,20},{12,24},{16,28},{20,0},{24,4},{28,8},{1,13},{... | collective-permute-start | bytes 491528 | tf_op jit(solution)/shard_map/ppermute | solution.py:24
  76.3 11.8 %collective-permute-start.12 = (f32[16,2560]{1,0:T(8,128)S(1)}, f32[16,2560]{1,0:T(8,128)}, u32[]{:S(2)}, u32[]{:S(2)}) collective-permute-start(f32[16,2560]{1,0:T(8,128)S(1)} %get-tuple-element.65), channel_id=1, source_target_pairs={{0,8},{4,12},{8,16},{12,20},{16,24},{20,28},{24,0},{28,4},{1,9},{5... | collective-permute-start | bytes 491528 | tf_op jit(solution)/shard_map/ppermute | solution.py:24
  100.4 20.4 %collective-permute-start.18 = (bf16[16,1024]{1,0:T(8,128)(2,1)S(1)}, bf16[16,1024]{1,0:T(8,128)(2,1)S(1)}, u32[]{:S(2)}, u32[]{:S(2)}) collective-permute-start(bf16[16,1024]{1,0:T(8,128)(2,1)S(1)} %get-tuple-element.121), channel_id=1, source_target_pairs={{0,0},{1,8},{2,16},{3,24},{4,1},{5,9},{6,17},{7,25},{8,2},{9,10},{... | collective-permute-start | bytes 98312 | tf_op jit(solution)/shard_map/ppermute | solution.py:47
  103.3 38.6 %collective-permute-start.25 = (bf16[16,1024]{1,0:T(8,128)(2,1)S(1)}, bf16[16,1024]{1,0:T(8,128)(2,1)S(1)}, u32[]{:S(2)}, u32[]{:S(2)}) collective-permute-start(bf16[16,1024]{1,0:T(8,128)(2,1)S(1)} %get-tuple-element.114), channel_id=1, source_target_pairs={{0,1},{1,9},{2,17},{3,25},{4,2},{5,10},{6,18},{7,26},{8,3},{9,11},... | collective-permute-start | bytes 98312 | tf_op jit(solution)/shard_map/ppermute | solution.py:47
  112.0 29.9 %collective-permute-start.24 = (bf16[16,1024]{1,0:T(8,128)(2,1)S(1)}, bf16[16,1024]{1,0:T(8,128)(2,1)S(1)}, u32[]{:S(2)}, u32[]{:S(2)}) collective-permute-start(bf16[16,1024]{1,0:T(8,128)(2,1)S(1)} %get-tuple-element.115), channel_id=1, source_target_pairs={{0,2},{1,10},{2,18},{3,26},{4,3},{5,11},{6,19},{7,27},{8,4},{9,12}... | collective-permute-start | bytes 98312 | tf_op jit(solution)/shard_map/ppermute | solution.py:47
  113.9 28.0 %collective-permute-start.23 = (bf16[16,1024]{1,0:T(8,128)(2,1)S(1)}, bf16[16,1024]{1,0:T(8,128)(2,1)S(1)}, u32[]{:S(2)}, u32[]{:S(2)}) collective-permute-start(bf16[16,1024]{1,0:T(8,128)(2,1)S(1)} %get-tuple-element.116), channel_id=1, source_target_pairs={{0,3},{1,11},{2,19},{3,27},{4,4},{5,12},{6,20},{7,28},{8,5},{9,13}... | collective-permute-start | bytes 98312 | tf_op jit(solution)/shard_map/ppermute | solution.py:47
  120.8 21.1 %collective-permute-start.22 = (bf16[16,1024]{1,0:T(8,128)(2,1)S(1)}, bf16[16,1024]{1,0:T(8,128)(2,1)S(1)}, u32[]{:S(2)}, u32[]{:S(2)}) collective-permute-start(bf16[16,1024]{1,0:T(8,128)(2,1)S(1)} %get-tuple-element.117), channel_id=1, source_target_pairs={{0,4},{1,12},{2,20},{3,28},{4,5},{5,13},{6,21},{7,29},{8,6},{9,14}... | collective-permute-start | bytes 98312 | tf_op jit(solution)/shard_map/ppermute | solution.py:47
  148.4 13.0 %collective-permute-start.29 = (f32[16,2048]{1,0:T(8,128)S(1)}, f32[16,2048]{1,0:T(8,128)S(1)}, u32[]{:S(2)}, u32[]{:S(2)}) collective-permute-start(f32[16,2048]{1,0:T(8,128)S(1)} %get-tuple-element.91), channel_id=1, source_target_pairs={{0,16},{4,20},{8,24},{12,28},{16,0},{20,4},{24,8},{28,12},{1,17},{... | collective-permute-start | bytes 393224 | tf_op jit(solution)/shard_map/ppermute | solution.py:24
  151.3 10.2 %collective-permute-start.28 = (f32[16,2048]{1,0:T(8,128)S(1)}, f32[16,2048]{1,0:T(8,128)S(1)}, u32[]{:S(2)}, u32[]{:S(2)}) collective-permute-start(f32[16,2048]{1,0:T(8,128)S(1)} %get-tuple-element.92), channel_id=1, source_target_pairs={{0,12},{4,16},{8,20},{12,24},{16,28},{20,0},{24,4},{28,8},{1,13},{... | collective-permute-start | bytes 393224 | tf_op jit(solution)/shard_map/ppermute | solution.py:24
  152.1 9.5 %collective-permute-start.27 = (f32[16,2048]{1,0:T(8,128)S(1)}, f32[16,2048]{1,0:T(8,128)S(1)}, u32[]{:S(2)}, u32[]{:S(2)}) collective-permute-start(f32[16,2048]{1,0:T(8,128)S(1)} %get-tuple-element.93), channel_id=1, source_target_pairs={{0,8},{4,12},{8,16},{12,20},{16,24},{20,28},{24,0},{28,4},{1,9},{5... | collective-permute-start | bytes 393224 | tf_op jit(solution)/shard_map/ppermute | solution.py:24
  202.1 364.3 %reduce-scatter.9.cloned.1.call-start = ((), (), s32[]{:S(2)}) async-start(), calls=%async_computation.3 | async-start | bytes 4751360 | tf_op jit(solution)/shard_map/reduce_scatter | solution.py:205
  302.2 9.3 %collective-permute-start.41 = (f32[16,2048]{1,0:T(8,128)S(1)}, f32[16,2048]{1,0:T(8,128)S(1)}, u32[]{:S(2)}, u32[]{:S(2)}) collective-permute-start(f32[16,2048]{1,0:T(8,128)S(1)} %get-tuple-element.82), channel_id=1, source_target_pairs={{0,24},{4,28},{8,0},{12,4},{16,8},{20,12},{24,16},{28,20},{1,25},{... | collective-permute-start | bytes 393224 | tf_op jit(solution)/shard_map/ppermute | solution.py:24
  303.5 13.5 %collective-permute-start.39 = (f32[16,2048]{1,0:T(8,128)S(1)}, f32[16,2048]{1,0:T(8,128)S(1)}, u32[]{:S(2)}, u32[]{:S(2)}) collective-permute-start(f32[16,2048]{1,0:T(8,128)S(1)} %get-tuple-element.84), channel_id=1, source_target_pairs={{0,16},{4,20},{8,24},{12,28},{16,0},{20,4},{24,8},{28,12},{1,17},{... | collective-permute-start | bytes 393224 | tf_op jit(solution)/shard_map/ppermute | solution.py:24
  305.2 11.9 %collective-permute-start.38 = (f32[16,2048]{1,0:T(8,128)S(1)}, f32[16,2048]{1,0:T(8,128)S(1)}, u32[]{:S(2)}, u32[]{:S(2)}) collective-permute-start(f32[16,2048]{1,0:T(8,128)S(1)} %get-tuple-element.85), channel_id=1, source_target_pairs={{0,12},{4,16},{8,20},{12,24},{16,28},{20,0},{24,4},{28,8},{1,13},{... | collective-permute-start | bytes 393224 | tf_op jit(solution)/shard_map/ppermute | solution.py:24
  307.5 9.5 %collective-permute-start.37 = (f32[16,2048]{1,0:T(8,128)S(1)}, f32[16,2048]{1,0:T(8,128)S(1)}, u32[]{:S(2)}, u32[]{:S(2)}) collective-permute-start(f32[16,2048]{1,0:T(8,128)S(1)} %get-tuple-element.86), channel_id=1, source_target_pairs={{0,8},{4,12},{8,16},{12,20},{16,24},{20,28},{24,0},{28,4},{1,9},{5... | collective-permute-start | bytes 393224 | tf_op jit(solution)/shard_map/ppermute | solution.py:24
  325.1 12.5 %collective-permute-start.46 = (bf16[16,1024]{1,0:T(8,128)(2,1)S(1)}, bf16[16,1024]{1,0:T(8,128)(2,1)S(1)}, u32[]{:S(2)}, u32[]{:S(2)}) collective-permute-start(bf16[16,1024]{1,0:T(8,128)(2,1)S(1)} %get-tuple-element.113), channel_id=1, source_target_pairs={{0,0},{1,8},{2,16},{3,24},{4,1},{5,9},{6,17},{7,25},{8,2},{9,10},{... | collective-permute-start | bytes 98312 | tf_op jit(solution)/shard_map/ppermute | solution.py:47
  328.0 32.5 %collective-permute-start.53 = (bf16[16,1024]{1,0:T(8,128)(2,1)S(1)}, bf16[16,1024]{1,0:T(8,128)(2,1)S(1)}, u32[]{:S(2)}, u32[]{:S(2)}) collective-permute-start(bf16[16,1024]{1,0:T(8,128)(2,1)S(1)} %get-tuple-element.106), channel_id=1, source_target_pairs={{0,1},{1,9},{2,17},{3,25},{4,2},{5,10},{6,18},{7,26},{8,3},{9,11},... | collective-permute-start | bytes 98312 | tf_op jit(solution)/shard_map/ppermute | solution.py:47
  330.5 30.0 %collective-permute-start.52 = (bf16[16,1024]{1,0:T(8,128)(2,1)S(1)}, bf16[16,1024]{1,0:T(8,128)(2,1)S(1)}, u32[]{:S(2)}, u32[]{:S(2)}) collective-permute-start(bf16[16,1024]{1,0:T(8,128)(2,1)S(1)} %get-tuple-element.107), channel_id=1, source_target_pairs={{0,2},{1,10},{2,18},{3,26},{4,3},{5,11},{6,19},{7,27},{8,4},{9,12}... | collective-permute-start | bytes 98312 | tf_op jit(solution)/shard_map/ppermute | solution.py:47
  334.3 26.2 %collective-permute-start.51 = (bf16[16,1024]{1,0:T(8,128)(2,1)S(1)}, bf16[16,1024]{1,0:T(8,128)(2,1)S(1)}, u32[]{:S(2)}, u32[]{:S(2)}) collective-permute-start(bf16[16,1024]{1,0:T(8,128)(2,1)S(1)} %get-tuple-element.108), channel_id=1, source_target_pairs={{0,3},{1,11},{2,19},{3,27},{4,4},{5,12},{6,20},{7,28},{8,5},{9,13}... | collective-permute-start | bytes 98312 | tf_op jit(solution)/shard_map/ppermute | solution.py:47
  336.7 23.8 %collective-permute-start.50 = (bf16[16,1024]{1,0:T(8,128)(2,1)S(1)}, bf16[16,1024]{1,0:T(8,128)(2,1)S(1)}, u32[]{:S(2)}, u32[]{:S(2)}) collective-permute-start(bf16[16,1024]{1,0:T(8,128)(2,1)S(1)} %get-tuple-element.109), channel_id=1, source_target_pairs={{0,4},{1,12},{2,20},{3,28},{4,5},{5,13},{6,21},{7,29},{8,6},{9,14}... | collective-permute-start | bytes 98312 | tf_op jit(solution)/shard_map/ppermute | solution.py:47
  369.4 10.5 %collective-permute-start.58 = (f32[16,2560]{1,0:T(8,128)S(1)}, f32[16,2560]{1,0:T(8,128)S(1)}, u32[]{:S(2)}, u32[]{:S(2)}) collective-permute-start(f32[16,2560]{1,0:T(8,128)S(1)} %get-tuple-element.55), channel_id=1, source_target_pairs={{0,20},{4,24},{8,28},{12,0},{16,4},{20,8},{24,12},{28,16},{1,21},{... | collective-permute-start | bytes 491528 | tf_op jit(solution)/shard_map/ppermute | solution.py:24
  369.4 14.0 %collective-permute-start.57 = (f32[16,2560]{1,0:T(8,128)S(1)}, f32[16,2560]{1,0:T(8,128)S(1)}, u32[]{:S(2)}, u32[]{:S(2)}) collective-permute-start(f32[16,2560]{1,0:T(8,128)S(1)} %get-tuple-element.56), channel_id=1, source_target_pairs={{0,16},{4,20},{8,24},{12,28},{16,0},{20,4},{24,8},{28,12},{1,17},{... | collective-permute-start | bytes 491528 | tf_op jit(solution)/shard_map/ppermute | solution.py:24
  369.9 13.6 %collective-permute-start.56 = (f32[16,2560]{1,0:T(8,128)S(1)}, f32[16,2560]{1,0:T(8,128)S(1)}, u32[]{:S(2)}, u32[]{:S(2)}) collective-permute-start(f32[16,2560]{1,0:T(8,128)S(1)} %get-tuple-element.57), channel_id=1, source_target_pairs={{0,12},{4,16},{8,20},{12,24},{16,28},{20,0},{24,4},{28,8},{1,13},{... | collective-permute-start | bytes 491528 | tf_op jit(solution)/shard_map/ppermute | solution.py:24
  372.1 11.4 %collective-permute-start.55 = (f32[16,2560]{1,0:T(8,128)S(1)}, f32[16,2560]{1,0:T(8,128)S(1)}, u32[]{:S(2)}, u32[]{:S(2)}) collective-permute-start(f32[16,2560]{1,0:T(8,128)S(1)} %get-tuple-element.58), channel_id=1, source_target_pairs={{0,8},{4,12},{8,16},{12,20},{16,24},{20,28},{24,0},{28,4},{1,9},{5... | collective-permute-start | bytes 491528 | tf_op jit(solution)/shard_map/ppermute | solution.py:24
  394.9 18.6 %collective-permute-start.61 = (bf16[16,1024]{1,0:T(8,128)(2,1)S(1)}, bf16[16,1024]{1,0:T(8,128)(2,1)S(1)}, u32[]{:S(2)}, u32[]{:S(2)}) collective-permute-start(bf16[16,1024]{1,0:T(8,128)(2,1)S(1)} %get-tuple-element.105), channel_id=1, source_target_pairs={{0,0},{1,8},{2,16},{3,24},{4,1},{5,9},{6,17},{7,25},{8,2},{9,10},{... | collective-permute-start | bytes 98312 | tf_op jit(solution)/shard_map/ppermute | solution.py:47
  398.2 37.2 %collective-permute-start.68 = (bf16[16,1024]{1,0:T(8,128)(2,1)S(1)}, bf16[16,1024]{1,0:T(8,128)(2,1)S(1)}, u32[]{:S(2)}, u32[]{:S(2)}) collective-permute-start(bf16[16,1024]{1,0:T(8,128)(2,1)S(1)} %get-tuple-element.98), channel_id=1, source_target_pairs={{0,1},{1,9},{2,17},{3,25},{4,2},{5,10},{6,18},{7,26},{8,3},{9,11},... | collective-permute-start | bytes 98312 | tf_op jit(solution)/shard_map/ppermute | solution.py:47
  405.6 29.7 %collective-permute-start.67 = (bf16[16,1024]{1,0:T(8,128)(2,1)S(1)}, bf16[16,1024]{1,0:T(8,128)(2,1)S(1)}, u32[]{:S(2)}, u32[]{:S(2)}) collective-permute-start(bf16[16,1024]{1,0:T(8,128)(2,1)S(1)} %get-tuple-element.99), channel_id=1, source_target_pairs={{0,2},{1,10},{2,18},{3,26},{4,3},{5,11},{6,19},{7,27},{8,4},{9,12}... | collective-permute-start | bytes 98312 | tf_op jit(solution)/shard_map/ppermute | solution.py:47
  407.6 27.8 %collective-permute-start.66 = (bf16[16,1024]{1,0:T(8,128)(2,1)S(1)}, bf16[16,1024]{1,0:T(8,128)(2,1)S(1)}, u32[]{:S(2)}, u32[]{:S(2)}) collective-permute-start(bf16[16,1024]{1,0:T(8,128)(2,1)S(1)} %get-tuple-element.100), channel_id=1, source_target_pairs={{0,3},{1,11},{2,19},{3,27},{4,4},{5,12},{6,20},{7,28},{8,5},{9,13}... | collective-permute-start | bytes 98312 | tf_op jit(solution)/shard_map/ppermute | solution.py:47
  413.5 21.8 %collective-permute-start.65 = (bf16[16,1024]{1,0:T(8,128)(2,1)S(1)}, bf16[16,1024]{1,0:T(8,128)(2,1)S(1)}, u32[]{:S(2)}, u32[]{:S(2)}) collective-permute-start(bf16[16,1024]{1,0:T(8,128)(2,1)S(1)} %get-tuple-element.101), channel_id=1, source_target_pairs={{0,4},{1,12},{2,20},{3,28},{4,5},{5,13},{6,21},{7,29},{8,6},{9,14}... | collective-permute-start | bytes 98312 | tf_op jit(solution)/shard_map/ppermute | solution.py:47
  442.8 11.8 %collective-permute-start.72 = (f32[16,2048]{1,0:T(8,128)S(1)}, f32[16,2048]{1,0:T(8,128)S(1)}, u32[]{:S(2)}, u32[]{:S(2)}) collective-permute-start(f32[16,2048]{1,0:T(8,128)S(1)} %get-tuple-element.77), channel_id=1, source_target_pairs={{0,16},{4,20},{8,24},{12,28},{16,0},{20,4},{24,8},{28,12},{1,17},{... | collective-permute-start | bytes 393224 | tf_op jit(solution)/shard_map/ppermute | solution.py:24
  444.1 10.7 %collective-permute-start.71 = (f32[16,2048]{1,0:T(8,128)S(1)}, f32[16,2048]{1,0:T(8,128)S(1)}, u32[]{:S(2)}, u32[]{:S(2)}) collective-permute-start(f32[16,2048]{1,0:T(8,128)S(1)} %get-tuple-element.78), channel_id=1, source_target_pairs={{0,12},{4,16},{8,20},{12,24},{16,28},{20,0},{24,4},{28,8},{1,13},{... | collective-permute-start | bytes 393224 | tf_op jit(solution)/shard_map/ppermute | solution.py:24
  445.4 9.3 %collective-permute-start.70 = (f32[16,2048]{1,0:T(8,128)S(1)}, f32[16,2048]{1,0:T(8,128)S(1)}, u32[]{:S(2)}, u32[]{:S(2)}) collective-permute-start(f32[16,2048]{1,0:T(8,128)S(1)} %get-tuple-element.79), channel_id=1, source_target_pairs={{0,8},{4,12},{8,16},{12,20},{16,24},{20,28},{24,0},{28,4},{1,9},{5... | collective-permute-start | bytes 393224 | tf_op jit(solution)/shard_map/ppermute | solution.py:24
  596.2 9.3 %collective-permute-start.84 = (f32[16,2048]{1,0:T(8,128)S(1)}, f32[16,2048]{1,0:T(8,128)S(1)}, u32[]{:S(2)}, u32[]{:S(2)}) collective-permute-start(f32[16,2048]{1,0:T(8,128)S(1)} %get-tuple-element.68), channel_id=1, source_target_pairs={{0,24},{4,28},{8,0},{12,4},{16,8},{20,12},{24,16},{28,20},{1,25},{... | collective-permute-start | bytes 393224 | tf_op jit(solution)/shard_map/ppermute | solution.py:24
  597.4 13.5 %collective-permute-start.82 = (f32[16,2048]{1,0:T(8,128)S(1)}, f32[16,2048]{1,0:T(8,128)S(1)}, u32[]{:S(2)}, u32[]{:S(2)}) collective-permute-start(f32[16,2048]{1,0:T(8,128)S(1)} %get-tuple-element.70), channel_id=1, source_target_pairs={{0,16},{4,20},{8,24},{12,28},{16,0},{20,4},{24,8},{28,12},{1,17},{... | collective-permute-start | bytes 393224 | tf_op jit(solution)/shard_map/ppermute | solution.py:24
  599.1 11.9 %collective-permute-start.81 = (f32[16,2048]{1,0:T(8,128)S(1)}, f32[16,2048]{1,0:T(8,128)S(1)}, u32[]{:S(2)}, u32[]{:S(2)}) collective-permute-start(f32[16,2048]{1,0:T(8,128)S(1)} %get-tuple-element.71), channel_id=1, source_target_pairs={{0,12},{4,16},{8,20},{12,24},{16,28},{20,0},{24,4},{28,8},{1,13},{... | collective-permute-start | bytes 393224 | tf_op jit(solution)/shard_map/ppermute | solution.py:24
  601.5 9.5 %collective-permute-start.80 = (f32[16,2048]{1,0:T(8,128)S(1)}, f32[16,2048]{1,0:T(8,128)S(1)}, u32[]{:S(2)}, u32[]{:S(2)}) collective-permute-start(f32[16,2048]{1,0:T(8,128)S(1)} %get-tuple-element.72), channel_id=1, source_target_pairs={{0,8},{4,12},{8,16},{12,20},{16,24},{20,28},{24,0},{28,4},{1,9},{5... | collective-permute-start | bytes 393224 | tf_op jit(solution)/shard_map/ppermute | solution.py:24
  (60 other events, 560.7 us)
Sparse Core Ops, SparseCore 0:
  202.2 70.0 reduce-scatter.6
  496.3 70.0 reduce-scatter.8

commit v5 on v3

--- a/solution.py
+++ b/solution.py
@@ -24,6 +24,19 @@
         total = total + lax.ppermute(
             piece, axis, [(j, (j + shift) % count) for j in range(count)]
         )
+    return total
+
+
+def narrow_scatter_sum(block, axis):
+    count = lax.axis_size(axis)
+    index = lax.axis_index(axis)
+    chunks = block.reshape(count, block.shape[0] // count, *block.shape[1:])
+    total = jnp.take(chunks, index, axis=0)
+    for shift in range(1, count):
+        piece = jnp.take(chunks, (index + shift) % count, axis=0).astype(jnp.bfloat16)
+        total = total + lax.ppermute(
+            piece, axis, [(j, (j + shift) % count) for j in range(count)]
+        ).astype(jnp.float32)
     return total
 
 
@@ -184,7 +197,7 @@
         normed_mlp = normalize(residual, mlp_gain)
         tokens = lax.all_gather(normed_mlp, "req", axis=0, tiled=True)
         hidden_cols = w_gate.shape[1]
-        gate_up = lax.psum_scatter(
+        gate_up = narrow_scatter_sum(
             jnp.concatenate(
                 [
                     jnp.dot(tokens, w_gate, preferred_element_type=jnp.float32),
@@ -193,8 +206,6 @@
                 axis=1,
             ),
             "kv",
-            scatter_dimension=0,
-            tiled=True,
         )
         local_hidden = (jax.nn.silu(gate_up[:, :hidden_cols]) * gate_up[:, hidden_cols:]).astype(
             jnp.bfloat16

time: 564 us -> 507 us (0.90)
  waiting for transfers between devices: 226 us -> 172 us
  between operations: 14.8 us -> 1.36 us
    reduce_scatter x2 -> x0, waiting for transfers between devices: 137 us -> none  [body(): lax.psum_scatter(jnp.concatenate([jnp.dot(tokens, w_gate, preferred_eleme...]
    ppermute x0 -> x6, waiting for transfers between devices: none -> 81.4 us  [narrow_scatter_sum(): lax.ppermute(piece, axis, [(j, (j + shift) % count) for j in range(count)])]
    unnamed x62 -> x52, local copies, waits for them, and re-layouts: 16.6 us -> 6.08 us
    concatenate x0 -> x2, local copies, waits for them, and re-layouts: none -> 10.5 us  [body(): jnp.concatenate([jnp.dot(tokens, w_gate, preferred_element_type=jnp.float...]
    ppermute x0 -> x6, starting transfers between devices: none -> 7.74 us  [narrow_scatter_sum(): lax.ppermute(piece, axis, [(j, (j + shift) % count) for j in range(count)])]
  transfers between devices with their start and end apart: 58 -> 62, of which waited for: 43 -> 47; matrix products, arithmetic and copies ran while one was open for 3% -> 3% of each run, Pallas kernels for 0% -> 0%
where the time goes in v5:
time: 507 us; the launch traced here: 498 us
  waiting for transfers between devices  172 us (34%)
  blocking collectives  132 us (26%)
  matrix products  74.2 us (15%)
  starting transfers between devices  66.6 us (13%)
  other arithmetic  25.7 us (5%)
  local copies, waits for them, and re-layouts  25.2 us (5%)
    ppermute x6, waiting for transfers between devices, narrow_scatter_sum(): lax.ppermute(piece, axis, [(j, (j + shift) % count) for j in range(count)])  81.4 us
    ppermute x42, waiting for transfers between devices, scatter_sum(): lax.ppermute(piece, axis, [(j, (j + shift) % count) for j in range(count)])  65.8 us
    all_gather x4, blocking collectives, rows_for_weights(): wide = lax.all_gather(block, 'kv', axis=1, tiled=True)  55.9 us
    all_gather x2, blocking collectives, body(): hidden_all = lax.all_gather(local_hidden, 'kv', axis=0, tiled=True)  38.6 us
    ppermute x42, starting transfers between devices, scatter_sum(): lax.ppermute(piece, axis, [(j, (j + shift) % count) for j in range(count)])  35.8 us
    all_to_all x2, blocking collectives, rows_for_weights(): return lax.all_to_all(wide, 'req', 1, 0, tiled=True)  19.5 us
    all_gather x2, blocking collectives, body(): tokens = lax.all_gather(normed_mlp, 'req', axis=0, tiled=True)  18.5 us
    ppermute x12, starting transfers between devices, normalize(): lax.ppermute(square_sum, 'kv', [(j, (j + shift) % count) for j in range(c...  16 us
  transfers between devices with their start and end apart: 62, of which 47 were waited for; matrix products, arithmetic and copies ran while one was open for 3% of the time, Pallas kernels for 0%

profile of v5, /device:TPU:0, one launch (start us, length us, event | category | flops | bytes accessed | tf_op | source)
XLA Modules:
  0.0 497.6 jit_solution(5102372492308608574)
XLA Ops:
  1.0 5.1 %collective-permute-start.2 = (f32[16]{0:T(128)S(1)}, f32[16]{0:T(128)S(1)}, u32[]{:S(2)}, u32[]{:S(2)}) collective-permute-start(f32[16]{0:T(128)S(1)} %fusion.162), channel_id=1, source_target_pairs={{0,3},{1,0},{2,1},{3,2},{4,7},{5,4},{6,5},{7,6},{8,11},{9,8},{10,9... | collective-permute-start | bytes 200 | tf_op jit(solution)/shard_map/ppermute | solution.py:70
  11.9 4.9 constant_dynamic-update-slice_fusion.2
  19.2 13.9 %all_gather.24 = bf16[16,8192]{1,0:T(8,128)(2,1)S(1)} all-gather(bf16[16,2048]{1,0:T(8,128)(2,1)S(1)} %fusion.164), channel_id=1, replica_groups=mesh['req'=8,'kv'=4] {'kv'}, dimensions={1}, use_global_device_ids=true | all-gather | bytes 327680 | tf_op jit(solution)/shard_map/all_gather | solution.py:44
  33.7 3.7 all-to-all-start
  40.0 4.4 all-to-all-done
  45.3 3.4 fusion.142
  61.5 5.5 %collective-permute-done.6 = f32[16,2560]{1,0:T(8,128)S(1)} collective-permute-done((f32[16,2560]{1,0:T(8,128)S(1)}, f32[16,2560]{1,0:T(8,128)S(1)}, u32[]{:S(2)}, u32[]{:S(2)}) %collective-permute-start.6) | collective-permute-done | bytes 163872 | tf_op jit(solution)/shard_map/ppermute | solution.py:24
  73.1 3.6 fusion.4
  80.5 13.9 %all_gather.25 = bf16[16,8192]{1,0:T(8,128)(2,1)S(1)} all-gather(bf16[16,2048]{1,0:T(8,128)(2,1)S(1)} %bitcast.537), channel_id=1, replica_groups=mesh['req'=8,'kv'=4] {'kv'}, dimensions={1}, use_global_device_ids=true | all-gather | bytes 327680 | tf_op jit(solution)/shard_map/all_gather | solution.py:44
  95.1 3.4 all-to-all-start.1
  98.6 6.8 %all-to-all-done.1 = bf16[16,8,1024]{2,0,1:T(8,128)(2,1)S(1)} async-done(((bf16[16,8,1024]{2,0,1:T(8,128)(2,1)}), bf16[16,8,1024]{2,0,1:T(8,128)(2,1)S(1)}, u32[]{:S(2)}, u32[]{:S(2)}) %all-to-all-start.1) | async-done | bytes 262176 | tf_op jit(solution)/shard_map/all_to_all | solution.py:45
  120.8 4.9 collective-permute-done.12
  125.8 3.4 collective-permute-start.19
  130.5 3.1 collective-permute-done.18
  134.7 9.1 %all_gather.26 = bf16[128,2048]{1,0:T(8,128)(2,1)S(1)} all-gather(bf16[16,2048]{1,0:T(8,128)(2,1)S(1)} %multiply_convert_fusion.2), channel_id=1, replica_groups=mesh['req'=8,'kv'=4] {'req'}, dimensions={0}, use_global_device_ids=true | all-gather | bytes 589824 | tf_op jit(solution)/shard_map/all_gather | solution.py:198
  143.8 7.6 %fusion.253 = f32[128,3696]{0,1:T(8,128)S(1)} fusion(bf16[128,2048]{1,0:T(8,128)(2,1)S(1)} %all_gather.26, bf16[2048,3696]{0,1:T(8,128)(2,1)} %param.42), kind=kOutput, calls=%fused_computation.344 | convolution fusion | flops 1937768448 | bytes 17555456 | tf_op jit(solution)/shard_map/dot_general | solution.py:204
  151.4 7.6 %fusion.252 = f32[128,3696]{0,1:T(8,128)S(1)} fusion(bf16[128,2048]{1,0:T(8,128)(2,1)S(1)} %all_gather.26, bf16[2048,3696]{0,1:T(8,128)(2,1)} %param.41), kind=kOutput, calls=%fused_computation.343 | convolution fusion | flops 1937768448 | bytes 17555456 | tf_op jit(solution)/shard_map/dot_general | solution.py:203
  161.3 5.3 %copy.58 = f32[128,7392]{1,0:T(8,128)} copy(f32[128,7392]{0,1:T(8,128)} %pad_maximum_fusion) | data formatting | bytes 7569408 | tf_op jit(solution)/shard_map/concatenate | solution.py:201
  168.5 3.8 collective-permute-start.22
  172.3 11.7 %collective-permute-done.20 = bf16[32,7392]{1,0:T(8,128)(2,1)S(1)} collective-permute-done((bf16[32,7392]{1,0:T(8,128)(2,1)S(1)}, bf16[32,7392]{1,0:T(8,128)(2,1)S(1)}, u32[]{:S(2)}, u32[]{:S(2)}) %collective-permute-start.20) | collective-permute-done | bytes 473120 | tf_op jit(solution)/shard_map/ppermute | solution.py:37
  184.0 7.9 %collective-permute-done.22 = bf16[32,7392]{1,0:T(8,128)(2,1)S(1)} collective-permute-done((bf16[32,7392]{1,0:T(8,128)(2,1)S(1)}, bf16[32,7392]{1,0:T(8,128)(2,1)S(1)}, u32[]{:S(2)}, u32[]{:S(2)}) %collective-permute-start.22) | collective-permute-done | bytes 473120 | tf_op jit(solution)/shard_map/ppermute | solution.py:37
  192.0 21.0 %collective-permute-done.21 = bf16[32,7392]{1,0:T(8,128)(2,1)S(1)} collective-permute-done((bf16[32,7392]{1,0:T(8,128)(2,1)S(1)}, bf16[32,7392]{1,0:T(8,128)(2,1)S(1)}, u32[]{:S(2)}, u32[]{:S(2)}) %collective-permute-start.21) | collective-permute-done | bytes 473120 | tf_op jit(solution)/shard_map/ppermute | solution.py:37
  214.6 19.3 %all_gather.27 = bf16[128,3696]{1,0:T(8,128)(2,1)S(1)} all-gather(bf16[32,3696]{1,0:T(8,128)(2,1)S(1)} %fusion.135), channel_id=1, replica_groups=mesh['req'=8,'kv'=4] {'kv'}, dimensions={0}, use_global_device_ids=true | all-gather | bytes 1182720 | tf_op jit(solution)/shard_map/all_gather | solution.py:213
  233.9 7.7 %fusion.254 = f32[128,2048]{1,0:T(8,128)S(1)} fusion(bf16[128,3696]{1,0:T(8,128)(2,1)S(1)} %all_gather.27, bf16[3696,2048]{1,0:T(8,128)(2,1)} %param.43), kind=kOutput, calls=%fused_computation.345 | convolution fusion | flops 1937768448 | bytes 17133568 | tf_op jit(solution)/shard_map/dot_general | solution.py:215
  253.3 4.6 collective-permute-done.25
  261.8 3.1 collective-permute-done.31
  266.0 13.9 %all_gather.28 = bf16[16,8192]{1,0:T(8,128)(2,1)S(1)} all-gather(bf16[16,2048]{1,0:T(8,128)(2,1)S(1)} %multiply_convert_fusion.1), channel_id=1, replica_groups=mesh['req'=8,'kv'=4] {'kv'}, dimensions={1}, use_global_device_ids=true | all-gather | bytes 327680 | tf_op jit(solution)/shard_map/all_gather | solution.py:44
  279.8 10.2 %all_to_all.76 = bf16[16,8,1024]{2,0,1:T(8,128)(2,1)S(1)} all-to-all(bf16[16,8,1024]{2,0,1:T(8,128)(2,1)S(1)} %bitcast.535), channel_id=1, replica_groups=mesh['req'=8,'kv'=4] {'req'}, dimensions={1} | all-to-all | bytes 524288 | tf_op jit(solution)/shard_map/all_to_all | solution.py:45
  290.9 3.4 fusion.138
  298.9 3.0 collective-permute-done.33
  302.0 3.2 collective-permute-done.38
  307.1 5.5 %collective-permute-done.36 = f32[16,2560]{1,0:T(8,128)S(1)} collective-permute-done((f32[16,2560]{1,0:T(8,128)S(1)}, f32[16,2560]{1,0:T(8,128)S(1)}, u32[]{:S(2)}, u32[]{:S(2)}) %collective-permute-start.36) | collective-permute-done | bytes 163872 | tf_op jit(solution)/shard_map/ppermute | solution.py:24
  317.5 3.6 fusion.8
  324.9 14.3 %all_gather.29 = bf16[16,8192]{1,0:T(8,128)(2,1)S(1)} all-gather(bf16[16,2048]{1,0:T(8,128)(2,1)S(1)} %bitcast.538), channel_id=1, replica_groups=mesh['req'=8,'kv'=4] {'kv'}, dimensions={1}, use_global_device_ids=true | all-gather | bytes 327680 | tf_op jit(solution)/shard_map/all_gather | solution.py:44
  339.2 9.3 %all_to_all.77 = bf16[16,8,1024]{2,0,1:T(8,128)(2,1)S(1)} all-to-all(bf16[16,8,1024]{2,0,1:T(8,128)(2,1)S(1)} %bitcast.536), channel_id=1, replica_groups=mesh['req'=8,'kv'=4] {'req'}, dimensions={1} | all-to-all | bytes 524288 | tf_op jit(solution)/shard_map/all_to_all | solution.py:45
  349.4 3.1 fusion.136
  364.3 4.6 collective-permute-done.42
  376.2 9.3 %all_gather.30 = bf16[128,2048]{1,0:T(8,128)(2,1)S(1)} all-gather(bf16[16,2048]{1,0:T(8,128)(2,1)S(1)} %multiply_convert_fusion), channel_id=1, replica_groups=mesh['req'=8,'kv'=4] {'req'}, dimensions={0}, use_global_device_ids=true | all-gather | bytes 589824 | tf_op jit(solution)/shard_map/all_gather | solution.py:198
  385.6 7.8 %fusion.256 = f32[128,3696]{0,1:T(8,128)S(1)} fusion(bf16[128,2048]{1,0:T(8,128)(2,1)S(1)} %all_gather.30, bf16[2048,3696]{0,1:T(8,128)(2,1)} %param.42), kind=kOutput, calls=%fused_computation.347 | convolution fusion | flops 1937768448 | bytes 17555456 | tf_op jit(solution)/shard_map/dot_general | solution.py:204
  393.4 4.3 fusion.255
  399.9 5.3 %copy.64 = f32[128,7392]{1,0:T(8,128)} copy(f32[128,7392]{0,1:T(8,128)} %pad_maximum_fusion.1) | data formatting | bytes 7569408 | tf_op jit(solution)/shard_map/concatenate | solution.py:201
  407.1 3.8 collective-permute-start.52
  410.9 11.7 %collective-permute-done.50 = bf16[32,7392]{1,0:T(8,128)(2,1)S(1)} collective-permute-done((bf16[32,7392]{1,0:T(8,128)(2,1)S(1)}, bf16[32,7392]{1,0:T(8,128)(2,1)S(1)}, u32[]{:S(2)}, u32[]{:S(2)}) %collective-permute-start.50) | collective-permute-done | bytes 473120 | tf_op jit(solution)/shard_map/ppermute | solution.py:37
  422.7 7.9 %collective-permute-done.52 = bf16[32,7392]{1,0:T(8,128)(2,1)S(1)} collective-permute-done((bf16[32,7392]{1,0:T(8,128)(2,1)S(1)}, bf16[32,7392]{1,0:T(8,128)(2,1)S(1)}, u32[]{:S(2)}, u32[]{:S(2)}) %collective-permute-start.52) | collective-permute-done | bytes 473120 | tf_op jit(solution)/shard_map/ppermute | solution.py:37
  430.6 21.0 %collective-permute-done.51 = bf16[32,7392]{1,0:T(8,128)(2,1)S(1)} collective-permute-done((bf16[32,7392]{1,0:T(8,128)(2,1)S(1)}, bf16[32,7392]{1,0:T(8,128)(2,1)S(1)}, u32[]{:S(2)}, u32[]{:S(2)}) %collective-permute-start.51) | collective-permute-done | bytes 473120 | tf_op jit(solution)/shard_map/ppermute | solution.py:37
  453.3 19.3 %all_gather.31 = bf16[128,3696]{1,0:T(8,128)(2,1)S(1)} all-gather(bf16[32,3696]{1,0:T(8,128)(2,1)S(1)} %fusion.134), channel_id=1, replica_groups=mesh['req'=8,'kv'=4] {'kv'}, dimensions={0}, use_global_device_ids=true | all-gather | bytes 1182720 | tf_op jit(solution)/shard_map/all_gather | solution.py:213
  472.6 7.7 %fusion.257 = f32[128,2048]{1,0:T(8,128)S(1)} fusion(bf16[128,3696]{1,0:T(8,128)(2,1)S(1)} %all_gather.31, bf16[3696,2048]{1,0:T(8,128)(2,1)} %param.43), kind=kOutput, calls=%fused_computation.348 | convolution fusion | flops 1937768448 | bytes 17133568 | tf_op jit(solution)/shard_map/dot_general | solution.py:215
  491.9 4.5 collective-permute-done.55
  (266 shorter events, 130.6 us)
Async XLA Ops:
  1.0 18.0 %collective-permute-start.2 = (f32[16]{0:T(128)S(1)}, f32[16]{0:T(128)S(1)}, u32[]{:S(2)}, u32[]{:S(2)}) collective-permute-start(f32[16]{0:T(128)S(1)} %fusion.162), channel_id=1, source_target_pairs={{0,3},{1,0},{2,1},{3,2},{4,7},{5,4},{6,5},{7,6},{8,11},{9,8},{10,9... | collective-permute-start | bytes 200 | tf_op jit(solution)/shard_map/ppermute | solution.py:70
  6.1 13.0 %collective-permute-start.1 = (f32[16]{0:T(128)S(1)}, f32[16]{0:T(128)S(1)}, u32[]{:S(2)}, u32[]{:S(2)}) collective-permute-start(f32[16]{0:T(128)S(1)} %fusion.162), channel_id=1, source_target_pairs={{0,2},{1,3},{2,0},{3,1},{4,6},{5,7},{6,4},{7,5},{8,10},{9,11},{10,... | collective-permute-start | bytes 200 | tf_op jit(solution)/shard_map/ppermute | solution.py:70
  6.1 13.0 %collective-permute-start = (f32[16]{0:T(128)S(1)}, f32[16]{0:T(128)S(1)}, u32[]{:S(2)}, u32[]{:S(2)}) collective-permute-start(f32[16]{0:T(128)S(1)} %fusion.162), channel_id=1, source_target_pairs={{0,1},{1,2},{2,3},{3,0},{4,5},{5,6},{6,7},{7,4},{8,9},{9,10},{10,1... | collective-permute-start | bytes 200 | tf_op jit(solution)/shard_map/ppermute | solution.py:70
  33.7 10.7 %all-to-all-start = ((bf16[16,8,1024]{2,0,1:T(8,128)(2,1)}), bf16[16,8,1024]{2,0,1:T(8,128)(2,1)S(1)}, u32[]{:S(2)}, u32[]{:S(2)}) async-start(bf16[16,8,1024]{2,0,1:T(8,128)(2,1)} %bitcast.504), calls=%async_computation | async-start | bytes 524288 | tf_op jit(solution)/shard_map/all_to_all | solution.py:45
  48.8 7.4 %collective-permute-start.3 = (f32[16,2560]{1,0:T(8,128)S(1)}, f32[16,2560]{1,0:T(8,128)S(1)}, u32[]{:S(2)}, u32[]{:S(2)}) collective-permute-start(f32[16,2560]{1,0:T(8,128)S(1)} %get-tuple-element.76), channel_id=1, source_target_pairs={{0,4},{4,8},{8,12},{12,16},{16,20},{20,24},{24,28},{28,0},{1,5},{5... | collective-permute-start | bytes 491528 | tf_op jit(solution)/shard_map/ppermute | solution.py:24
  48.8 7.4 %collective-permute-start.9 = (f32[16,2560]{1,0:T(8,128)S(1)}, f32[16,2560]{1,0:T(8,128)S(1)}, u32[]{:S(2)}, u32[]{:S(2)}) collective-permute-start(f32[16,2560]{1,0:T(8,128)S(1)} %get-tuple-element.77), channel_id=1, source_target_pairs={{0,28},{4,0},{8,4},{12,8},{16,12},{20,16},{24,20},{28,24},{1,29},{... | collective-permute-start | bytes 491528 | tf_op jit(solution)/shard_map/ppermute | solution.py:24
  52.2 7.5 %collective-permute-start.8 = (f32[16,2560]{1,0:T(8,128)S(1)}, f32[16,2560]{1,0:T(8,128)S(1)}, u32[]{:S(2)}, u32[]{:S(2)}) collective-permute-start(f32[16,2560]{1,0:T(8,128)S(1)} %get-tuple-element.78), channel_id=1, source_target_pairs={{0,24},{4,28},{8,0},{12,4},{16,8},{20,12},{24,16},{28,20},{1,25},{... | collective-permute-start | bytes 491528 | tf_op jit(solution)/shard_map/ppermute | solution.py:24
  52.2 9.3 %collective-permute-start.7 = (f32[16,2560]{1,0:T(8,128)S(1)}, f32[16,2560]{1,0:T(8,128)S(1)}, u32[]{:S(2)}, u32[]{:S(2)}) collective-permute-start(f32[16,2560]{1,0:T(8,128)S(1)} %get-tuple-element.79), channel_id=1, source_target_pairs={{0,20},{4,24},{8,28},{12,0},{16,4},{20,8},{24,12},{28,16},{1,21},{... | collective-permute-start | bytes 491528 | tf_op jit(solution)/shard_map/ppermute | solution.py:24
  52.5 14.5 %collective-permute-start.6 = (f32[16,2560]{1,0:T(8,128)S(1)}, f32[16,2560]{1,0:T(8,128)S(1)}, u32[]{:S(2)}, u32[]{:S(2)}) collective-permute-start(f32[16,2560]{1,0:T(8,128)S(1)} %get-tuple-element.80), channel_id=1, source_target_pairs={{0,16},{4,20},{8,24},{12,28},{16,0},{20,4},{24,8},{28,12},{1,17},{... | collective-permute-start | bytes 491528 | tf_op jit(solution)/shard_map/ppermute | solution.py:24
  56.2 11.9 %collective-permute-start.5 = (f32[16,2560]{1,0:T(8,128)S(1)}, f32[16,2560]{1,0:T(8,128)S(1)}, u32[]{:S(2)}, u32[]{:S(2)}) collective-permute-start(f32[16,2560]{1,0:T(8,128)S(1)} %get-tuple-element.81), channel_id=1, source_target_pairs={{0,12},{4,16},{8,20},{12,24},{16,28},{20,0},{24,4},{28,8},{1,13},{... | collective-permute-start | bytes 491528 | tf_op jit(solution)/shard_map/ppermute | solution.py:24
  56.2 11.9 %collective-permute-start.4 = (f32[16,2560]{1,0:T(8,128)S(1)}, f32[16,2560]{1,0:T(8,128)}, u32[]{:S(2)}, u32[]{:S(2)}) collective-permute-start(f32[16,2560]{1,0:T(8,128)S(1)} %get-tuple-element.82), channel_id=1, source_target_pairs={{0,8},{4,12},{8,16},{12,20},{16,24},{20,28},{24,0},{28,4},{1,9},{5... | collective-permute-start | bytes 491528 | tf_op jit(solution)/shard_map/ppermute | solution.py:24
  95.1 10.3 %all-to-all-start.1 = ((bf16[16,8,1024]{2,0,1:T(8,128)(2,1)}), bf16[16,8,1024]{2,0,1:T(8,128)(2,1)S(1)}, u32[]{:S(2)}, u32[]{:S(2)}) async-start(bf16[16,8,1024]{2,0,1:T(8,128)(2,1)} %bitcast.503), calls=%async_computation.1 | async-start | bytes 524288 | tf_op jit(solution)/shard_map/all_to_all | solution.py:45
  109.3 6.7 %collective-permute-start.10 = (f32[16,2048]{1,0:T(8,128)S(1)}, f32[16,2048]{1,0:T(8,128)S(1)}, u32[]{:S(2)}, u32[]{:S(2)}) collective-permute-start(f32[16,2048]{1,0:T(8,128)S(1)} %get-tuple-element.104), channel_id=1, source_target_pairs={{0,4},{4,8},{8,12},{12,16},{16,20},{20,24},{24,28},{28,0},{1,5},{5... | collective-permute-start | bytes 393224 | tf_op jit(solution)/shard_map/ppermute | solution.py:24
  112.0 6.8 %collective-permute-start.15 = (f32[16,2048]{1,0:T(8,128)S(1)}, f32[16,2048]{1,0:T(8,128)S(1)}, u32[]{:S(2)}, u32[]{:S(2)}) collective-permute-start(f32[16,2048]{1,0:T(8,128)S(1)} %get-tuple-element.106), channel_id=1, source_target_pairs={{0,24},{4,28},{8,0},{12,4},{16,8},{20,12},{24,16},{28,20},{1,25},{... | collective-permute-start | bytes 393224 | tf_op jit(solution)/shard_map/ppermute | solution.py:24
  112.2 7.7 %collective-permute-start.14 = (f32[16,2048]{1,0:T(8,128)S(1)}, f32[16,2048]{1,0:T(8,128)S(1)}, u32[]{:S(2)}, u32[]{:S(2)}) collective-permute-start(f32[16,2048]{1,0:T(8,128)S(1)} %get-tuple-element.107), channel_id=1, source_target_pairs={{0,20},{4,24},{8,28},{12,0},{16,4},{20,8},{24,12},{28,16},{1,21},{... | collective-permute-start | bytes 393224 | tf_op jit(solution)/shard_map/ppermute | solution.py:24
  112.5 8.3 %collective-permute-start.13 = (f32[16,2048]{1,0:T(8,128)S(1)}, f32[16,2048]{1,0:T(8,128)S(1)}, u32[]{:S(2)}, u32[]{:S(2)}) collective-permute-start(f32[16,2048]{1,0:T(8,128)S(1)} %get-tuple-element.108), channel_id=1, source_target_pairs={{0,16},{4,20},{8,24},{12,28},{16,0},{20,4},{24,8},{28,12},{1,17},{... | collective-permute-start | bytes 393224 | tf_op jit(solution)/shard_map/ppermute | solution.py:24
  116.1 9.5 %collective-permute-start.12 = (f32[16,2048]{1,0:T(8,128)S(1)}, f32[16,2048]{1,0:T(8,128)S(1)}, u32[]{:S(2)}, u32[]{:S(2)}) collective-permute-start(f32[16,2048]{1,0:T(8,128)S(1)} %get-tuple-element.109), channel_id=1, source_target_pairs={{0,12},{4,16},{8,20},{12,24},{16,28},{20,0},{24,4},{28,8},{1,13},{... | collective-permute-start | bytes 393224 | tf_op jit(solution)/shard_map/ppermute | solution.py:24
  116.1 9.5 %collective-permute-start.11 = (f32[16,2048]{1,0:T(8,128)S(1)}, f32[16,2048]{1,0:T(8,128)S(1)}, u32[]{:S(2)}, u32[]{:S(2)}) collective-permute-start(f32[16,2048]{1,0:T(8,128)S(1)} %get-tuple-element.110), channel_id=1, source_target_pairs={{0,8},{4,12},{8,16},{12,20},{16,24},{20,28},{24,0},{28,4},{1,9},{5... | collective-permute-start | bytes 393224 | tf_op jit(solution)/shard_map/ppermute | solution.py:24
  168.4 15.6 %collective-permute-start.20 = (bf16[32,7392]{1,0:T(8,128)(2,1)S(1)}, bf16[32,7392]{1,0:T(8,128)(2,1)S(1)}, u32[]{:S(2)}, u32[]{:S(2)}) collective-permute-start(bf16[32,7392]{1,0:T(8,128)(2,1)S(1)} %get-tuple-element.66), channel_id=1, source_target_pairs={{0,1},{1,2},{2,3},{3,0},{4,5},{5,6},{6,7},{7,4},{8,9},{9,10},{10,1... | collective-permute-start | bytes 1419272 | tf_op jit(solution)/shard_map/ppermute | solution.py:37
  168.5 23.5 %collective-permute-start.22 = (bf16[32,7392]{1,0:T(8,128)(2,1)S(1)}, bf16[32,7392]{1,0:T(8,128)(2,1)S(1)}, u32[]{:S(2)}, u32[]{:S(2)}) collective-permute-start(bf16[32,7392]{1,0:T(8,128)(2,1)S(1)} %get-tuple-element.67), channel_id=1, source_target_pairs={{0,3},{1,0},{2,1},{3,2},{4,7},{5,4},{6,5},{7,6},{8,11},{9,8},{10,9... | collective-permute-start | bytes 1419272 | tf_op jit(solution)/shard_map/ppermute | solution.py:37
  172.3 40.7 %collective-permute-start.21 = (bf16[32,7392]{1,0:T(8,128)(2,1)S(1)}, bf16[32,7392]{1,0:T(8,128)(2,1)S(1)}, u32[]{:S(2)}, u32[]{:S(2)}) collective-permute-start(bf16[32,7392]{1,0:T(8,128)(2,1)S(1)} %get-tuple-element.68), channel_id=1, source_target_pairs={{0,2},{1,3},{2,0},{3,1},{4,6},{5,7},{6,4},{7,5},{8,10},{9,11},{10,... | collective-permute-start | bytes 1419272 | tf_op jit(solution)/shard_map/ppermute | solution.py:37
  244.4 7.7 %collective-permute-start.28 = (f32[16,2048]{1,0:T(8,128)S(1)}, f32[16,2048]{1,0:T(8,128)S(1)}, u32[]{:S(2)}, u32[]{:S(2)}) collective-permute-start(f32[16,2048]{1,0:T(8,128)S(1)} %get-tuple-element.99), channel_id=1, source_target_pairs={{0,24},{4,28},{8,0},{12,4},{16,8},{20,12},{24,16},{28,20},{1,25},{... | collective-permute-start | bytes 393224 | tf_op jit(solution)/shard_map/ppermute | solution.py:24
  245.0 8.3 %collective-permute-start.27 = (f32[16,2048]{1,0:T(8,128)S(1)}, f32[16,2048]{1,0:T(8,128)S(1)}, u32[]{:S(2)}, u32[]{:S(2)}) collective-permute-start(f32[16,2048]{1,0:T(8,128)S(1)} %get-tuple-element.100), channel_id=1, source_target_pairs={{0,20},{4,24},{8,28},{12,0},{16,4},{20,8},{24,12},{28,16},{1,21},{... | collective-permute-start | bytes 393224 | tf_op jit(solution)/shard_map/ppermute | solution.py:24
  245.7 7.6 %collective-permute-start.26 = (f32[16,2048]{1,0:T(8,128)S(1)}, f32[16,2048]{1,0:T(8,128)S(1)}, u32[]{:S(2)}, u32[]{:S(2)}) collective-permute-start(f32[16,2048]{1,0:T(8,128)S(1)} %get-tuple-element.101), channel_id=1, source_target_pairs={{0,16},{4,20},{8,24},{12,28},{16,0},{20,4},{24,8},{28,12},{1,17},{... | collective-permute-start | bytes 393224 | tf_op jit(solution)/shard_map/ppermute | solution.py:24
  247.7 10.2 %collective-permute-start.25 = (f32[16,2048]{1,0:T(8,128)S(1)}, f32[16,2048]{1,0:T(8,128)S(1)}, u32[]{:S(2)}, u32[]{:S(2)}) collective-permute-start(f32[16,2048]{1,0:T(8,128)S(1)} %get-tuple-element.102), channel_id=1, source_target_pairs={{0,12},{4,16},{8,20},{12,24},{16,28},{20,0},{24,4},{28,8},{1,13},{... | collective-permute-start | bytes 393224 | tf_op jit(solution)/shard_map/ppermute | solution.py:24
  248.1 9.8 %collective-permute-start.24 = (f32[16,2048]{1,0:T(8,128)S(1)}, f32[16,2048]{1,0:T(8,128)S(1)}, u32[]{:S(2)}, u32[]{:S(2)}) collective-permute-start(f32[16,2048]{1,0:T(8,128)S(1)} %get-tuple-element.103), channel_id=1, source_target_pairs={{0,8},{4,12},{8,16},{12,20},{16,24},{20,28},{24,0},{28,4},{1,9},{5... | collective-permute-start | bytes 393224 | tf_op jit(solution)/shard_map/ppermute | solution.py:24
  294.4 7.5 %collective-permute-start.33 = (f32[16,2560]{1,0:T(8,128)S(1)}, f32[16,2560]{1,0:T(8,128)S(1)}, u32[]{:S(2)}, u32[]{:S(2)}) collective-permute-start(f32[16,2560]{1,0:T(8,128)S(1)} %get-tuple-element.69), channel_id=1, source_target_pairs={{0,4},{4,8},{8,12},{12,16},{16,20},{20,24},{24,28},{28,0},{1,5},{5... | collective-permute-start | bytes 491528 | tf_op jit(solution)/shard_map/ppermute | solution.py:24
  294.5 7.4 %collective-permute-start.39 = (f32[16,2560]{1,0:T(8,128)S(1)}, f32[16,2560]{1,0:T(8,128)S(1)}, u32[]{:S(2)}, u32[]{:S(2)}) collective-permute-start(f32[16,2560]{1,0:T(8,128)S(1)} %get-tuple-element.70), channel_id=1, source_target_pairs={{0,28},{4,0},{8,4},{12,8},{16,12},{20,16},{24,20},{28,24},{1,29},{... | collective-permute-start | bytes 491528 | tf_op jit(solution)/shard_map/ppermute | solution.py:24
  297.1 8.2 %collective-permute-start.38 = (f32[16,2560]{1,0:T(8,128)S(1)}, f32[16,2560]{1,0:T(8,128)S(1)}, u32[]{:S(2)}, u32[]{:S(2)}) collective-permute-start(f32[16,2560]{1,0:T(8,128)S(1)} %get-tuple-element.71), channel_id=1, source_target_pairs={{0,24},{4,28},{8,0},{12,4},{16,8},{20,12},{24,16},{28,20},{1,25},{... | collective-permute-start | bytes 491528 | tf_op jit(solution)/shard_map/ppermute | solution.py:24
  297.1 10.0 %collective-permute-start.37 = (f32[16,2560]{1,0:T(8,128)S(1)}, f32[16,2560]{1,0:T(8,128)S(1)}, u32[]{:S(2)}, u32[]{:S(2)}) collective-permute-start(f32[16,2560]{1,0:T(8,128)S(1)} %get-tuple-element.72), channel_id=1, source_target_pairs={{0,20},{4,24},{8,28},{12,0},{16,4},{20,8},{24,12},{28,16},{1,21},{... | collective-permute-start | bytes 491528 | tf_op jit(solution)/shard_map/ppermute | solution.py:24
  297.4 15.2 %collective-permute-start.36 = (f32[16,2560]{1,0:T(8,128)S(1)}, f32[16,2560]{1,0:T(8,128)S(1)}, u32[]{:S(2)}, u32[]{:S(2)}) collective-permute-start(f32[16,2560]{1,0:T(8,128)S(1)} %get-tuple-element.73), channel_id=1, source_target_pairs={{0,16},{4,20},{8,24},{12,28},{16,0},{20,4},{24,8},{28,12},{1,17},{... | collective-permute-start | bytes 491528 | tf_op jit(solution)/shard_map/ppermute | solution.py:24
  301.8 11.6 %collective-permute-start.35 = (f32[16,2560]{1,0:T(8,128)S(1)}, f32[16,2560]{1,0:T(8,128)S(1)}, u32[]{:S(2)}, u32[]{:S(2)}) collective-permute-start(f32[16,2560]{1,0:T(8,128)S(1)} %get-tuple-element.74), channel_id=1, source_target_pairs={{0,12},{4,16},{8,20},{12,24},{16,28},{20,0},{24,4},{28,8},{1,13},{... | collective-permute-start | bytes 491528 | tf_op jit(solution)/shard_map/ppermute | solution.py:24
  301.8 11.6 %collective-permute-start.34 = (f32[16,2560]{1,0:T(8,128)S(1)}, f32[16,2560]{1,0:T(8,128)S(1)}, u32[]{:S(2)}, u32[]{:S(2)}) collective-permute-start(f32[16,2560]{1,0:T(8,128)S(1)} %get-tuple-element.75), channel_id=1, source_target_pairs={{0,8},{4,12},{8,16},{12,20},{16,24},{20,28},{24,0},{28,4},{1,9},{5... | collective-permute-start | bytes 491528 | tf_op jit(solution)/shard_map/ppermute | solution.py:24
  352.7 6.8 %collective-permute-start.40 = (f32[16,2048]{1,0:T(8,128)S(1)}, f32[16,2048]{1,0:T(8,128)S(1)}, u32[]{:S(2)}, u32[]{:S(2)}) collective-permute-start(f32[16,2048]{1,0:T(8,128)S(1)} %get-tuple-element.90), channel_id=1, source_target_pairs={{0,4},{4,8},{8,12},{12,16},{16,20},{20,24},{24,28},{28,0},{1,5},{5... | collective-permute-start | bytes 393224 | tf_op jit(solution)/shard_map/ppermute | solution.py:24
  352.7 6.7 %collective-permute-start.46 = (f32[16,2048]{1,0:T(8,128)S(1)}, f32[16,2048]{1,0:T(8,128)S(1)}, u32[]{:S(2)}, u32[]{:S(2)}) collective-permute-start(f32[16,2048]{1,0:T(8,128)S(1)} %get-tuple-element.91), channel_id=1, source_target_pairs={{0,28},{4,0},{8,4},{12,8},{16,12},{20,16},{24,20},{28,24},{1,29},{... | collective-permute-start | bytes 393224 | tf_op jit(solution)/shard_map/ppermute | solution.py:24
  355.4 6.8 %collective-permute-start.45 = (f32[16,2048]{1,0:T(8,128)S(1)}, f32[16,2048]{1,0:T(8,128)S(1)}, u32[]{:S(2)}, u32[]{:S(2)}) collective-permute-start(f32[16,2048]{1,0:T(8,128)S(1)} %get-tuple-element.92), channel_id=1, source_target_pairs={{0,24},{4,28},{8,0},{12,4},{16,8},{20,12},{24,16},{28,20},{1,25},{... | collective-permute-start | bytes 393224 | tf_op jit(solution)/shard_map/ppermute | solution.py:24
  355.4 7.9 %collective-permute-start.44 = (f32[16,2048]{1,0:T(8,128)S(1)}, f32[16,2048]{1,0:T(8,128)S(1)}, u32[]{:S(2)}, u32[]{:S(2)}) collective-permute-start(f32[16,2048]{1,0:T(8,128)S(1)} %get-tuple-element.93), channel_id=1, source_target_pairs={{0,20},{4,24},{8,28},{12,0},{16,4},{20,8},{24,12},{28,16},{1,21},{... | collective-permute-start | bytes 393224 | tf_op jit(solution)/shard_map/ppermute | solution.py:24
  355.7 8.6 %collective-permute-start.43 = (f32[16,2048]{1,0:T(8,128)S(1)}, f32[16,2048]{1,0:T(8,128)S(1)}, u32[]{:S(2)}, u32[]{:S(2)}) collective-permute-start(f32[16,2048]{1,0:T(8,128)S(1)} %get-tuple-element.94), channel_id=1, source_target_pairs={{0,16},{4,20},{8,24},{12,28},{16,0},{20,4},{24,8},{28,12},{1,17},{... | collective-permute-start | bytes 393224 | tf_op jit(solution)/shard_map/ppermute | solution.py:24
  359.4 9.5 %collective-permute-start.42 = (f32[16,2048]{1,0:T(8,128)S(1)}, f32[16,2048]{1,0:T(8,128)S(1)}, u32[]{:S(2)}, u32[]{:S(2)}) collective-permute-start(f32[16,2048]{1,0:T(8,128)S(1)} %get-tuple-element.95), channel_id=1, source_target_pairs={{0,12},{4,16},{8,20},{12,24},{16,28},{20,0},{24,4},{28,8},{1,13},{... | collective-permute-start | bytes 393224 | tf_op jit(solution)/shard_map/ppermute | solution.py:24
  359.4 9.5 %collective-permute-start.41 = (f32[16,2048]{1,0:T(8,128)S(1)}, f32[16,2048]{1,0:T(8,128)S(1)}, u32[]{:S(2)}, u32[]{:S(2)}) collective-permute-start(f32[16,2048]{1,0:T(8,128)S(1)} %get-tuple-element.96), channel_id=1, source_target_pairs={{0,8},{4,12},{8,16},{12,20},{16,24},{20,28},{24,0},{28,4},{1,9},{5... | collective-permute-start | bytes 393224 | tf_op jit(solution)/shard_map/ppermute | solution.py:24
  407.1 15.6 %collective-permute-start.50 = (bf16[32,7392]{1,0:T(8,128)(2,1)S(1)}, bf16[32,7392]{1,0:T(8,128)(2,1)S(1)}, u32[]{:S(2)}, u32[]{:S(2)}) collective-permute-start(bf16[32,7392]{1,0:T(8,128)(2,1)S(1)} %get-tuple-element.63), channel_id=1, source_target_pairs={{0,1},{1,2},{2,3},{3,0},{4,5},{5,6},{6,7},{7,4},{8,9},{9,10},{10,1... | collective-permute-start | bytes 1419272 | tf_op jit(solution)/shard_map/ppermute | solution.py:37
  407.1 23.5 %collective-permute-start.52 = (bf16[32,7392]{1,0:T(8,128)(2,1)S(1)}, bf16[32,7392]{1,0:T(8,128)(2,1)S(1)}, u32[]{:S(2)}, u32[]{:S(2)}) collective-permute-start(bf16[32,7392]{1,0:T(8,128)(2,1)S(1)} %get-tuple-element.64), channel_id=1, source_target_pairs={{0,3},{1,0},{2,1},{3,2},{4,7},{5,4},{6,5},{7,6},{8,11},{9,8},{10,9... | collective-permute-start | bytes 1419272 | tf_op jit(solution)/shard_map/ppermute | solution.py:37
  410.9 40.7 %collective-permute-start.51 = (bf16[32,7392]{1,0:T(8,128)(2,1)S(1)}, bf16[32,7392]{1,0:T(8,128)(2,1)S(1)}, u32[]{:S(2)}, u32[]{:S(2)}) collective-permute-start(bf16[32,7392]{1,0:T(8,128)(2,1)S(1)} %get-tuple-element.65), channel_id=1, source_target_pairs={{0,2},{1,3},{2,0},{3,1},{4,6},{5,7},{6,4},{7,5},{8,10},{9,11},{10,... | collective-permute-start | bytes 1419272 | tf_op jit(solution)/shard_map/ppermute | solution.py:37
  483.1 7.7 %collective-permute-start.58 = (f32[16,2048]{1,0:T(8,128)S(1)}, f32[16,2048]{1,0:T(8,128)S(1)}, u32[]{:S(2)}, u32[]{:S(2)}) collective-permute-start(f32[16,2048]{1,0:T(8,128)S(1)} %get-tuple-element.85), channel_id=1, source_target_pairs={{0,24},{4,28},{8,0},{12,4},{16,8},{20,12},{24,16},{28,20},{1,25},{... | collective-permute-start | bytes 393224 | tf_op jit(solution)/shard_map/ppermute | solution.py:24
  483.6 8.3 %collective-permute-start.57 = (f32[16,2048]{1,0:T(8,128)S(1)}, f32[16,2048]{1,0:T(8,128)S(1)}, u32[]{:S(2)}, u32[]{:S(2)}) collective-permute-start(f32[16,2048]{1,0:T(8,128)S(1)} %get-tuple-element.86), channel_id=1, source_target_pairs={{0,20},{4,24},{8,28},{12,0},{16,4},{20,8},{24,12},{28,16},{1,21},{... | collective-permute-start | bytes 393224 | tf_op jit(solution)/shard_map/ppermute | solution.py:24
  484.3 7.6 %collective-permute-start.56 = (f32[16,2048]{1,0:T(8,128)S(1)}, f32[16,2048]{1,0:T(8,128)S(1)}, u32[]{:S(2)}, u32[]{:S(2)}) collective-permute-start(f32[16,2048]{1,0:T(8,128)S(1)} %get-tuple-element.87), channel_id=1, source_target_pairs={{0,16},{4,20},{8,24},{12,28},{16,0},{20,4},{24,8},{28,12},{1,17},{... | collective-permute-start | bytes 393224 | tf_op jit(solution)/shard_map/ppermute | solution.py:24
  486.3 10.2 %collective-permute-start.55 = (f32[16,2048]{1,0:T(8,128)S(1)}, f32[16,2048]{1,0:T(8,128)S(1)}, u32[]{:S(2)}, u32[]{:S(2)}) collective-permute-start(f32[16,2048]{1,0:T(8,128)S(1)} %get-tuple-element.88), channel_id=1, source_target_pairs={{0,12},{4,16},{8,20},{12,24},{16,28},{20,0},{24,4},{28,8},{1,13},{... | collective-permute-start | bytes 393224 | tf_op jit(solution)/shard_map/ppermute | solution.py:24
  486.6 9.8 %collective-permute-start.54 = (f32[16,2048]{1,0:T(8,128)S(1)}, f32[16,2048]{1,0:T(8,128)S(1)}, u32[]{:S(2)}, u32[]{:S(2)}) collective-permute-start(f32[16,2048]{1,0:T(8,128)S(1)} %get-tuple-element.89), channel_id=1, source_target_pairs={{0,8},{4,12},{8,16},{12,20},{16,24},{20,28},{24,0},{28,4},{1,9},{5... | collective-permute-start | bytes 393224 | tf_op jit(solution)/shard_map/ppermute | solution.py:24
  (36 other events, 431.6 us)

commit v6 on v3

--- a/solution.py
+++ b/solution.py
@@ -18,12 +18,28 @@
     count = lax.axis_size(axis)
     index = lax.axis_index(axis)
     chunks = block.reshape(count, block.shape[0] // count, *block.shape[1:])
-    total = jnp.take(chunks, index, axis=0)
-    for shift in range(1, count):
-        piece = jnp.take(chunks, (index + shift) % count, axis=0)
-        total = total + lax.ppermute(
-            piece, axis, [(j, (j + shift) % count) for j in range(count)]
-        )
+    if count % 2 or count == 2:
+        total = jnp.take(chunks, index, axis=0)
+        for shift in range(1, count):
+            piece = jnp.take(chunks, (index + shift) % count, axis=0)
+            total = total + lax.ppermute(
+                piece, axis, [(j, (j + shift) % count) for j in range(count)]
+            )
+        return total
+    half = count // 2
+    parity = index % 2
+    grouped = chunks.reshape(half, 2, *chunks.shape[1:])
+    mine = jnp.take(grouped, parity, axis=1)
+    theirs = jnp.take(grouped, 1 - parity, axis=1)
+    partial = mine + lax.ppermute(theirs, axis, [(j, j ^ 1) for j in range(count)])
+    group_index = index // 2
+    total = jnp.take(partial, group_index, axis=0)
+    for shift in range(1, half):
+        piece = jnp.take(partial, (group_index + shift) % half, axis=0)
+        pairs = [
+            (2 * u + p, 2 * ((u + shift) % half) + p) for u in range(half) for p in range(2)
+        ]
+        total = total + lax.ppermute(piece, axis, pairs)
     return total
 
 

time: 564 us -> 533 us (0.945)
  waiting for transfers between devices: 226 us -> 209 us
  starting transfers between devices: 61 us -> 47.6 us
    ppermute x42 -> x24, waiting for transfers between devices: 64.5 us -> 45.3 us  [the longest x18 35.6 us: scatter_sum(): total = total + lax.ppermute(piece, axis, pairs)]
    ppermute x42 -> x24, starting transfers between devices: 37.9 us -> 24.2 us  [the longest x18 23.8 us: scatter_sum(): total = total + lax.ppermute(piece, axis, pairs)]
    unnamed x62 -> x52, local copies, waits for them, and re-layouts: 16.6 us -> 16.5 us
  transfers between devices with their start and end apart: 58 -> 40, of which waited for: 43 -> 34; matrix products, arithmetic and copies ran while one was open for 3% -> 3% of each run, Pallas kernels for 0% -> 0%
where the time goes in v6:
time: 533 us; the launch traced here: 524 us
  waiting for transfers between devices  209 us (39%)
  blocking collectives  137 us (26%)
  matrix products  71.2 us (13%)
  starting transfers between devices  47.6 us (9%)
  local copies, waits for them, and re-layouts  25.1 us (5%)
  other arithmetic  19.3 us (4%)
  between operations  14.9 us (3%)
    reduce_scatter x2, waiting for transfers between devices, body(): lax.psum_scatter(jnp.concatenate([jnp.dot(tokens, w_gate, preferred_eleme...  137 us
    all_gather x4, blocking collectives, rows_for_weights(): wide = lax.all_gather(block, 'kv', axis=1, tiled=True)  55.8 us
    all_gather x2, blocking collectives, body(): hidden_all = lax.all_gather(local_hidden, 'kv', axis=0, tiled=True)  40.9 us
    ppermute x18, waiting for transfers between devices, scatter_sum(): total = total + lax.ppermute(piece, axis, pairs)  35.6 us
    ppermute x18, starting transfers between devices, scatter_sum(): total = total + lax.ppermute(piece, axis, pairs)  23.8 us
    all_to_all x2, blocking collectives, rows_for_weights(): return lax.all_to_all(wide, 'req', 1, 0, tiled=True)  20.6 us
    all_gather x2, blocking collectives, body(): tokens = lax.all_gather(normed_mlp, 'req', axis=0, tiled=True)  19.4 us
    unnamed x52, local copies, waits for them, and re-layouts  16.5 us
  transfers between devices with their start and end apart: 40, of which 34 were waited for; matrix products, arithmetic and copies ran while one was open for 3% of the time, Pallas kernels for 0%

profile of v6, /device:TPU:0, one launch (start us, length us, event | category | flops | bytes accessed | tf_op | source)
XLA Modules:
  0.0 523.9 jit_solution(3162795345508459695)
XLA Ops:
  7.5 5.1 collective-permute-start.2
  17.8 4.9 constant_dynamic-update-slice_fusion.2
  24.7 13.9 %all_gather.24 = bf16[16,8192]{1,0:T(8,128)(2,1)S(1)} all-gather(bf16[16,2048]{1,0:T(8,128)(2,1)S(1)} %fusion.170), channel_id=1, replica_groups=mesh['req'=8,'kv'=4] {'kv'}, dimensions={1}, use_global_device_ids=true | all-gather | bytes 327680 | tf_op jit(solution)/shard_map/all_gather | solution.py:47
  39.3 3.7 all-to-all-start
  43.6 6.3 %all-to-all-done = bf16[16,8,1024]{2,0,1:T(8,128)(2,1)S(1)} async-done(((bf16[16,8,1024]{2,0,1:T(8,128)(2,1)}), bf16[16,8,1024]{2,0,1:T(8,128)(2,1)S(1)}, u32[]{:S(2)}, u32[]{:S(2)}) %all-to-all-start) | async-done | bytes 262176 | tf_op jit(solution)/shard_map/all_to_all | solution.py:48
  50.8 3.4 fusion.156
  54.6 2.5 sort.17
  61.1 4.4 collective-permute-done.4
  69.6 2.8 fusion
  72.5 3.6 fusion.4
  79.9 13.9 %all_gather.25 = bf16[16,8192]{1,0:T(8,128)(2,1)S(1)} all-gather(bf16[16,2048]{1,0:T(8,128)(2,1)S(1)} %bitcast.511), channel_id=1, replica_groups=mesh['req'=8,'kv'=4] {'kv'}, dimensions={1}, use_global_device_ids=true | all-gather | bytes 327680 | tf_op jit(solution)/shard_map/all_gather | solution.py:47
  94.5 3.4 all-to-all-start.1
  98.0 6.8 %all-to-all-done.1 = bf16[16,8,1024]{2,0,1:T(8,128)(2,1)S(1)} async-done(((bf16[16,8,1024]{2,0,1:T(8,128)(2,1)}), bf16[16,8,1024]{2,0,1:T(8,128)(2,1)S(1)}, u32[]{:S(2)}, u32[]{:S(2)}) %all-to-all-start.1) | async-done | bytes 262176 | tf_op jit(solution)/shard_map/all_to_all | solution.py:48
  105.7 3.1 fusion.154
  111.6 2.5 collective-permute-start.10
  114.6 3.6 collective-permute-done.8
  120.4 3.8 collective-permute-start.13
  125.6 3.1 collective-permute-done.12
  129.7 9.6 %all_gather.26 = bf16[128,2048]{1,0:T(8,128)(2,1)S(1)} all-gather(bf16[16,2048]{1,0:T(8,128)(2,1)S(1)} %multiply_convert_fusion.2), channel_id=1, replica_groups=mesh['req'=8,'kv'=4] {'req'}, dimensions={0}, use_global_device_ids=true | all-gather | bytes 589824 | tf_op jit(solution)/shard_map/all_gather | solution.py:201
  139.3 7.8 %fusion.243 = f32[128,3696]{0,1:T(8,128)S(1)} fusion(bf16[128,2048]{1,0:T(8,128)(2,1)S(1)} %all_gather.26, bf16[2048,3696]{0,1:T(8,128)(2,1)} %param.44), kind=kOutput, calls=%fused_computation.314 | convolution fusion | flops 1937768448 | bytes 17555456 | tf_op jit(solution)/shard_map/dot_general | solution.py:207
  147.2 4.3 fusion.242
  153.7 5.3 %copy.134 = f32[128,7392]{1,0:T(8,128)} copy(f32[128,7392]{0,1:T(8,128)} %pad_maximum_fusion) | data formatting | bytes 7569408
  159.1 68.5 %reduce-scatter.7.cloned.1.call-done = f32[32,7392]{1,0:T(8,128)} async-done(((f32[128,7392]{1,0:T(8,128)}), f32[32,7392]{1,0:T(8,128)}) %reduce-scatter.7.cloned.1.call-update) | async-done | bytes 946192 | tf_op jit(solution)/shard_map/reduce_scatter | solution.py:203
  228.9 20.5 %all_gather.27 = bf16[128,3696]{1,0:T(8,128)(2,1)S(1)} all-gather(bf16[32,3696]{1,0:T(8,128)(2,1)S(1)} %fusion.149), channel_id=1, replica_groups=mesh['req'=8,'kv'=4] {'kv'}, dimensions={0}, use_global_device_ids=true | all-gather | bytes 1182720 | tf_op jit(solution)/shard_map/all_gather | solution.py:218
  249.4 7.7 %fusion.244 = f32[128,2048]{1,0:T(8,128)S(1)} fusion(bf16[128,3696]{1,0:T(8,128)(2,1)S(1)} %all_gather.27, bf16[3696,2048]{1,0:T(8,128)(2,1)} %param.45), kind=kOutput, calls=%fused_computation.315 | convolution fusion | flops 1937768448 | bytes 17133568 | tf_op jit(solution)/shard_map/dot_general | solution.py:220
  264.0 2.6 collective-permute-done.15
  272.6 3.0 collective-permute-done.19
  276.6 13.8 %all_gather.28 = bf16[16,8192]{1,0:T(8,128)(2,1)S(1)} all-gather(bf16[16,2048]{1,0:T(8,128)(2,1)S(1)} %multiply_convert_fusion.1), channel_id=1, replica_groups=mesh['req'=8,'kv'=4] {'kv'}, dimensions={1}, use_global_device_ids=true | all-gather | bytes 327680 | tf_op jit(solution)/shard_map/all_gather | solution.py:47
  290.4 11.2 %all_to_all.76 = bf16[16,8,1024]{2,0,1:T(8,128)(2,1)S(1)} all-to-all(bf16[16,8,1024]{2,0,1:T(8,128)(2,1)S(1)} %bitcast.509), channel_id=1, replica_groups=mesh['req'=8,'kv'=4] {'req'}, dimensions={1} | all-to-all | bytes 524288 | tf_op jit(solution)/shard_map/all_to_all | solution.py:48
  302.5 3.4 fusion.152
  308.9 2.4 collective-permute-start.24
  312.0 4.3 collective-permute-done.22
  320.1 2.8 fusion.2
  323.0 3.6 fusion.8
  330.4 14.2 %all_gather.29 = bf16[16,8192]{1,0:T(8,128)(2,1)S(1)} all-gather(bf16[16,2048]{1,0:T(8,128)(2,1)S(1)} %bitcast.512), channel_id=1, replica_groups=mesh['req'=8,'kv'=4] {'kv'}, dimensions={1}, use_global_device_ids=true | all-gather | bytes 327680 | tf_op jit(solution)/shard_map/all_gather | solution.py:47
  344.7 9.3 %all_to_all.77 = bf16[16,8,1024]{2,0,1:T(8,128)(2,1)S(1)} all-to-all(bf16[16,8,1024]{2,0,1:T(8,128)(2,1)S(1)} %bitcast.510), channel_id=1, replica_groups=mesh['req'=8,'kv'=4] {'req'}, dimensions={1} | all-to-all | bytes 524288 | tf_op jit(solution)/shard_map/all_to_all | solution.py:48
  354.9 3.1 fusion.150
  360.7 2.4 collective-permute-start.28
  363.7 3.8 collective-permute-done.26
  373.2 2.6 collective-permute-done.30
  376.8 9.7 %all_gather.30 = bf16[128,2048]{1,0:T(8,128)(2,1)S(1)} all-gather(bf16[16,2048]{1,0:T(8,128)(2,1)S(1)} %multiply_convert_fusion), channel_id=1, replica_groups=mesh['req'=8,'kv'=4] {'req'}, dimensions={0}, use_global_device_ids=true | all-gather | bytes 589824 | tf_op jit(solution)/shard_map/all_gather | solution.py:201
  386.6 7.8 %fusion.246 = f32[128,3696]{0,1:T(8,128)S(1)} fusion(bf16[128,2048]{1,0:T(8,128)(2,1)S(1)} %all_gather.30, bf16[2048,3696]{0,1:T(8,128)(2,1)} %param.44), kind=kOutput, calls=%fused_computation.317 | convolution fusion | flops 1937768448 | bytes 17555456 | tf_op jit(solution)/shard_map/dot_general | solution.py:207
  394.4 4.3 fusion.245
  400.8 5.3 %copy.136 = f32[128,7392]{1,0:T(8,128)} copy(f32[128,7392]{0,1:T(8,128)} %pad_maximum_fusion.1) | data formatting | bytes 7569408
  406.1 68.5 %reduce-scatter.9.cloned.1.call-done = f32[32,7392]{1,0:T(8,128)} async-done(((f32[128,7392]{1,0:T(8,128)}), f32[32,7392]{1,0:T(8,128)}) %reduce-scatter.9.cloned.1.call-update) | async-done | bytes 946192 | tf_op jit(solution)/shard_map/reduce_scatter | solution.py:203
  476.0 20.5 %all_gather.31 = bf16[128,3696]{1,0:T(8,128)(2,1)S(1)} all-gather(bf16[32,3696]{1,0:T(8,128)(2,1)S(1)} %fusion.148), channel_id=1, replica_groups=mesh['req'=8,'kv'=4] {'kv'}, dimensions={0}, use_global_device_ids=true | all-gather | bytes 1182720 | tf_op jit(solution)/shard_map/all_gather | solution.py:218
  496.5 7.7 %fusion.247 = f32[128,2048]{1,0:T(8,128)S(1)} fusion(bf16[128,3696]{1,0:T(8,128)(2,1)S(1)} %all_gather.31, bf16[3696,2048]{1,0:T(8,128)(2,1)} %param.45), kind=kOutput, calls=%fused_computation.318 | convolution fusion | flops 1937768448 | bytes 17133568 | tf_op jit(solution)/shard_map/dot_general | solution.py:220
  511.1 2.5 collective-permute-done.33
  (231 shorter events, 85.5 us)
Async XLA Ops:
  7.5 17.0 %collective-permute-start.2 = (f32[16]{0:T(128)S(1)}, f32[16]{0:T(128)S(1)}, u32[]{:S(2)}, u32[]{:S(2)}) collective-permute-start(f32[16]{0:T(128)S(1)} %fusion.168), channel_id=1, source_target_pairs={{0,3},{1,0},{2,1},{3,2},{4,7},{5,4},{6,5},{7,6},{8,11},{9,8},{10,9... | collective-permute-start | bytes 200 | tf_op jit(solution)/shard_map/ppermute | solution.py:73
  12.6 11.9 %collective-permute-start.1 = (f32[16]{0:T(128)S(1)}, f32[16]{0:T(128)S(1)}, u32[]{:S(2)}, u32[]{:S(2)}) collective-permute-start(f32[16]{0:T(128)S(1)} %fusion.168), channel_id=1, source_target_pairs={{0,2},{1,3},{2,0},{3,1},{4,6},{5,7},{6,4},{7,5},{8,10},{9,11},{10,... | collective-permute-start | bytes 200 | tf_op jit(solution)/shard_map/ppermute | solution.py:73
  12.6 11.9 %collective-permute-start = (f32[16]{0:T(128)S(1)}, f32[16]{0:T(128)S(1)}, u32[]{:S(2)}, u32[]{:S(2)}) collective-permute-start(f32[16]{0:T(128)S(1)} %fusion.168), channel_id=1, source_target_pairs={{0,1},{1,2},{2,3},{3,0},{4,5},{5,6},{6,7},{7,4},{8,9},{9,10},{10,1... | collective-permute-start | bytes 200 | tf_op jit(solution)/shard_map/ppermute | solution.py:73
  39.3 10.7 %all-to-all-start = ((bf16[16,8,1024]{2,0,1:T(8,128)(2,1)}), bf16[16,8,1024]{2,0,1:T(8,128)(2,1)S(1)}, u32[]{:S(2)}, u32[]{:S(2)}) async-start(bf16[16,8,1024]{2,0,1:T(8,128)(2,1)} %bitcast.480), calls=%async_computation | async-start | bytes 524288 | tf_op jit(solution)/shard_map/all_to_all | solution.py:48
  50.8 10.3 %copy-start.4 = (bf16[2048]{0:T(1024)(128)(2,1)S(1)}, bf16[2048]{0:T(1024)(128)(2,1)}, u32[]{:S(2)}) copy-start(bf16[2048]{0:T(1024)(128)(2,1)} %param.38) | copy-start | bytes 12292
  50.8 10.2 %copy-start.7 = (bf16[256]{0:T(256)(128)(2,1)S(1)}, bf16[256]{0:T(256)(128)(2,1)}, u32[]{:S(2)}) copy-start(bf16[256]{0:T(256)(128)(2,1)} %param.40) | copy-start | bytes 1540
  50.8 10.2 %copy-start.8 = (bf16[256]{0:T(256)(128)(2,1)S(1)}, bf16[256]{0:T(256)(128)(2,1)}, u32[]{:S(2)}) copy-start(bf16[256]{0:T(256)(128)(2,1)} %param.39) | copy-start | bytes 1540
  54.3 3.1 collective-permute-start.3
  57.5 8.0 %collective-permute-start.4 = (f32[16,2560]{1,0:T(8,128)S(1)}, f32[16,2560]{1,0:T(8,128)S(1)}, u32[]{:S(2)}, u32[]{:S(2)}) collective-permute-start(f32[16,2560]{1,0:T(8,128)S(1)} %get-tuple-element.78), channel_id=1, source_target_pairs={{0,8},{4,12},{8,16},{12,20},{16,24},{20,28},{24,0},{28,4},{1,9},{5... | collective-permute-start | bytes 491528 | tf_op jit(solution)/shard_map/ppermute | solution.py:42
  58.1 9.6 %collective-permute-start.6 = (f32[16,2560]{1,0:T(8,128)S(1)}, f32[16,2560]{1,0:T(8,128)S(1)}, u32[]{:S(2)}, u32[]{:S(2)}) collective-permute-start(f32[16,2560]{1,0:T(8,128)S(1)} %get-tuple-element.79), channel_id=1, source_target_pairs={{0,24},{4,28},{8,0},{12,4},{16,8},{20,12},{24,16},{28,20},{1,25},{... | collective-permute-start | bytes 491528 | tf_op jit(solution)/shard_map/ppermute | solution.py:42
  60.5 8.1 %collective-permute-start.5 = (f32[16,2560]{1,0:T(8,128)S(1)}, f32[16,2560]{1,0:T(8,128)S(1)}, u32[]{:S(2)}, u32[]{:S(2)}) collective-permute-start(f32[16,2560]{1,0:T(8,128)S(1)} %get-tuple-element.80), channel_id=1, source_target_pairs={{0,16},{4,20},{8,24},{12,28},{16,0},{20,4},{24,8},{28,12},{1,17},{... | collective-permute-start | bytes 491528 | tf_op jit(solution)/shard_map/ppermute | solution.py:42
  94.5 10.3 %all-to-all-start.1 = ((bf16[16,8,1024]{2,0,1:T(8,128)(2,1)}), bf16[16,8,1024]{2,0,1:T(8,128)(2,1)S(1)}, u32[]{:S(2)}, u32[]{:S(2)}) async-start(bf16[16,8,1024]{2,0,1:T(8,128)(2,1)} %bitcast.479), calls=%async_computation.1 | async-start | bytes 524288 | tf_op jit(solution)/shard_map/all_to_all | solution.py:48
  97.9 129.6 %reduce-scatter.7.cloned.1.call-start = ((), (), s32[]{:S(2)}) async-start(), calls=%async_computation.6 | async-start | bytes 4751360 | tf_op jit(solution)/shard_map/reduce_scatter | solution.py:203
  105.7 9.0 %copy-start.5 = (bf16[2048]{0:T(1024)(128)(2,1)S(1)}, bf16[2048]{0:T(1024)(128)(2,1)}, u32[]{:S(2)}) copy-start(bf16[2048]{0:T(1024)(128)(2,1)} %param.42) | copy-start | bytes 12292
  105.7 41.5 %slice-start = ((s8[15138816]{0:T(1024)(128)(4,1)}), s8[4194304]{0:T(1024)(128)(4,1)S(1)}, s32[]{:S(2)}) async-start(s8[15138816]{0:T(1024)(128)(4,1)} %bitcast.483), calls=%async_computation.8 | async-start | bytes 8388608
  108.9 38.3 %slice-start.1 = ((s8[15138816]{0:T(1024)(128)(4,1)}), s8[4194304]{0:T(1024)(128)(4,1)S(1)}, s32[]{:S(2)}) async-start(s8[15138816]{0:T(1024)(128)(4,1)} %bitcast.483), calls=%async_computation.9 | async-start | bytes 8388608
  108.9 2.0 collective-permute-start.7
  111.0 7.3 %collective-permute-start.8 = (f32[16,2048]{1,0:T(8,128)S(1)}, f32[16,2048]{1,0:T(8,128)S(1)}, u32[]{:S(2)}, u32[]{:S(2)}) collective-permute-start(f32[16,2048]{1,0:T(8,128)S(1)} %get-tuple-element.90), channel_id=1, source_target_pairs={{0,8},{4,12},{8,16},{12,20},{16,24},{20,28},{24,0},{28,4},{1,9},{5... | collective-permute-start | bytes 393224 | tf_op jit(solution)/shard_map/ppermute | solution.py:42
  111.6 7.8 %collective-permute-start.10 = (f32[16,2048]{1,0:T(8,128)S(1)}, f32[16,2048]{1,0:T(8,128)S(1)}, u32[]{:S(2)}, u32[]{:S(2)}) collective-permute-start(f32[16,2048]{1,0:T(8,128)S(1)} %get-tuple-element.91), channel_id=1, source_target_pairs={{0,24},{4,28},{8,0},{12,4},{16,8},{20,12},{24,16},{28,20},{1,25},{... | collective-permute-start | bytes 393224 | tf_op jit(solution)/shard_map/ppermute | solution.py:42
  114.1 6.2 %collective-permute-start.9 = (f32[16,2048]{1,0:T(8,128)S(1)}, f32[16,2048]{1,0:T(8,128)S(1)}, u32[]{:S(2)}, u32[]{:S(2)}) collective-permute-start(f32[16,2048]{1,0:T(8,128)S(1)} %get-tuple-element.92), channel_id=1, source_target_pairs={{0,16},{4,20},{8,24},{12,28},{16,0},{20,4},{24,8},{28,12},{1,17},{... | collective-permute-start | bytes 393224 | tf_op jit(solution)/shard_map/ppermute | solution.py:42
  120.4 5.1 collective-permute-start.13
  124.3 4.4 collective-permute-start.12
  124.3 5.3 %collective-permute-start.11 = (f32[16]{0:T(128)S(1)}, f32[16]{0:T(128)S(1)}, u32[]{:S(2)}, u32[]{:S(2)}) collective-permute-start(f32[16]{0:T(128)S(1)} %get-tuple-element.69), channel_id=1, source_target_pairs={{0,1},{1,2},{2,3},{3,0},{4,5},{5,6},{6,7},{7,4},{8,9},{9,10},{10,1... | collective-permute-start | bytes 200 | tf_op jit(solution)/shard_map/ppermute | solution.py:73
  159.0 315.6 %reduce-scatter.9.cloned.1.call-start = ((), (), s32[]{:S(2)}) async-start(), calls=%async_computation.7 | async-start | bytes 4751360 | tf_op jit(solution)/shard_map/reduce_scatter | solution.py:203
  257.1 2.0 collective-permute-start.14
  259.2 7.3 %collective-permute-start.15 = (f32[16,2048]{1,0:T(8,128)S(1)}, f32[16,2048]{1,0:T(8,128)S(1)}, u32[]{:S(2)}, u32[]{:S(2)}) collective-permute-start(f32[16,2048]{1,0:T(8,128)S(1)} %get-tuple-element.87), channel_id=1, source_target_pairs={{0,8},{4,12},{8,16},{12,20},{16,24},{20,28},{24,0},{28,4},{1,9},{5... | collective-permute-start | bytes 393224 | tf_op jit(solution)/shard_map/ppermute | solution.py:42
  261.0 7.8 %collective-permute-start.17 = (f32[16,2048]{1,0:T(8,128)S(1)}, f32[16,2048]{1,0:T(8,128)S(1)}, u32[]{:S(2)}, u32[]{:S(2)}) collective-permute-start(f32[16,2048]{1,0:T(8,128)S(1)} %get-tuple-element.88), channel_id=1, source_target_pairs={{0,24},{4,28},{8,0},{12,4},{16,8},{20,12},{24,16},{28,20},{1,25},{... | collective-permute-start | bytes 393224 | tf_op jit(solution)/shard_map/ppermute | solution.py:42
  262.2 6.6 %collective-permute-start.16 = (f32[16,2048]{1,0:T(8,128)S(1)}, f32[16,2048]{1,0:T(8,128)S(1)}, u32[]{:S(2)}, u32[]{:S(2)}) collective-permute-start(f32[16,2048]{1,0:T(8,128)S(1)} %get-tuple-element.89), channel_id=1, source_target_pairs={{0,16},{4,20},{8,24},{12,28},{16,0},{20,4},{24,8},{28,12},{1,17},{... | collective-permute-start | bytes 393224 | tf_op jit(solution)/shard_map/ppermute | solution.py:42
  269.0 3.6 collective-permute-start.20
  271.1 4.4 collective-permute-start.19
  271.1 5.3 %collective-permute-start.18 = (f32[16]{0:T(128)S(1)}, f32[16]{0:T(128)S(1)}, u32[]{:S(2)}, u32[]{:S(2)}) collective-permute-start(f32[16]{0:T(128)S(1)} %get-tuple-element.67), channel_id=1, source_target_pairs={{0,1},{1,2},{2,3},{3,0},{4,5},{5,6},{6,7},{7,4},{8,9},{9,10},{10,1... | collective-permute-start | bytes 200 | tf_op jit(solution)/shard_map/ppermute | solution.py:73
  306.0 2.2 collective-permute-start.21
  308.3 8.0 %collective-permute-start.22 = (f32[16,2560]{1,0:T(8,128)S(1)}, f32[16,2560]{1,0:T(8,128)S(1)}, u32[]{:S(2)}, u32[]{:S(2)}) collective-permute-start(f32[16,2560]{1,0:T(8,128)S(1)} %get-tuple-element.75), channel_id=1, source_target_pairs={{0,8},{4,12},{8,16},{12,20},{16,24},{20,28},{24,0},{28,4},{1,9},{5... | collective-permute-start | bytes 491528 | tf_op jit(solution)/shard_map/ppermute | solution.py:42
  308.9 9.2 %collective-permute-start.24 = (f32[16,2560]{1,0:T(8,128)S(1)}, f32[16,2560]{1,0:T(8,128)S(1)}, u32[]{:S(2)}, u32[]{:S(2)}) collective-permute-start(f32[16,2560]{1,0:T(8,128)S(1)} %get-tuple-element.76), channel_id=1, source_target_pairs={{0,24},{4,28},{8,0},{12,4},{16,8},{20,12},{24,16},{28,20},{1,25},{... | collective-permute-start | bytes 491528 | tf_op jit(solution)/shard_map/ppermute | solution.py:42
  311.2 7.7 %collective-permute-start.23 = (f32[16,2560]{1,0:T(8,128)S(1)}, f32[16,2560]{1,0:T(8,128)S(1)}, u32[]{:S(2)}, u32[]{:S(2)}) collective-permute-start(f32[16,2560]{1,0:T(8,128)S(1)} %get-tuple-element.77), channel_id=1, source_target_pairs={{0,16},{4,20},{8,24},{12,28},{16,0},{20,4},{24,8},{28,12},{1,17},{... | collective-permute-start | bytes 491528 | tf_op jit(solution)/shard_map/ppermute | solution.py:42
  354.9 39.5 %slice-start.4 = ((s8[15138816]{0:T(1024)(128)(4,1)}), s8[4194304]{0:T(1024)(128)(4,1)S(1)}, s32[]{:S(2)}) async-start(s8[15138816]{0:T(1024)(128)(4,1)} %bitcast.485), calls=%async_computation.12 | async-start | bytes 8388608
  358.0 36.3 %slice-start.5 = ((s8[15138816]{0:T(1024)(128)(4,1)}), s8[4194304]{0:T(1024)(128)(4,1)S(1)}, s32[]{:S(2)}) async-start(s8[15138816]{0:T(1024)(128)(4,1)} %bitcast.485), calls=%async_computation.13 | async-start | bytes 8388608
  358.0 2.0 collective-permute-start.25
  360.1 7.3 %collective-permute-start.26 = (f32[16,2048]{1,0:T(8,128)S(1)}, f32[16,2048]{1,0:T(8,128)S(1)}, u32[]{:S(2)}, u32[]{:S(2)}) collective-permute-start(f32[16,2048]{1,0:T(8,128)S(1)} %get-tuple-element.84), channel_id=1, source_target_pairs={{0,8},{4,12},{8,16},{12,20},{16,24},{20,28},{24,0},{28,4},{1,9},{5... | collective-permute-start | bytes 393224 | tf_op jit(solution)/shard_map/ppermute | solution.py:42
  360.7 7.8 %collective-permute-start.28 = (f32[16,2048]{1,0:T(8,128)S(1)}, f32[16,2048]{1,0:T(8,128)S(1)}, u32[]{:S(2)}, u32[]{:S(2)}) collective-permute-start(f32[16,2048]{1,0:T(8,128)S(1)} %get-tuple-element.85), channel_id=1, source_target_pairs={{0,24},{4,28},{8,0},{12,4},{16,8},{20,12},{24,16},{28,20},{1,25},{... | collective-permute-start | bytes 393224 | tf_op jit(solution)/shard_map/ppermute | solution.py:42
  363.1 6.3 %collective-permute-start.27 = (f32[16,2048]{1,0:T(8,128)S(1)}, f32[16,2048]{1,0:T(8,128)S(1)}, u32[]{:S(2)}, u32[]{:S(2)}) collective-permute-start(f32[16,2048]{1,0:T(8,128)S(1)} %get-tuple-element.86), channel_id=1, source_target_pairs={{0,16},{4,20},{8,24},{12,28},{16,0},{20,4},{24,8},{28,12},{1,17},{... | collective-permute-start | bytes 393224 | tf_op jit(solution)/shard_map/ppermute | solution.py:42
  369.6 3.6 collective-permute-start.31
  371.4 4.4 collective-permute-start.30
  371.4 5.3 %collective-permute-start.29 = (f32[16]{0:T(128)S(1)}, f32[16]{0:T(128)S(1)}, u32[]{:S(2)}, u32[]{:S(2)}) collective-permute-start(f32[16]{0:T(128)S(1)} %get-tuple-element.61), channel_id=1, source_target_pairs={{0,1},{1,2},{2,3},{3,0},{4,5},{5,6},{6,7},{7,4},{8,9},{9,10},{10,1... | collective-permute-start | bytes 200 | tf_op jit(solution)/shard_map/ppermute | solution.py:73
  504.2 2.0 collective-permute-start.32
  506.3 7.3 %collective-permute-start.33 = (f32[16,2048]{1,0:T(8,128)S(1)}, f32[16,2048]{1,0:T(8,128)S(1)}, u32[]{:S(2)}, u32[]{:S(2)}) collective-permute-start(f32[16,2048]{1,0:T(8,128)S(1)} %get-tuple-element.81), channel_id=1, source_target_pairs={{0,8},{4,12},{8,16},{12,20},{16,24},{20,28},{24,0},{28,4},{1,9},{5... | collective-permute-start | bytes 393224 | tf_op jit(solution)/shard_map/ppermute | solution.py:42
  508.1 7.8 %collective-permute-start.35 = (f32[16,2048]{1,0:T(8,128)S(1)}, f32[16,2048]{1,0:T(8,128)S(1)}, u32[]{:S(2)}, u32[]{:S(2)}) collective-permute-start(f32[16,2048]{1,0:T(8,128)S(1)} %get-tuple-element.82), channel_id=1, source_target_pairs={{0,24},{4,28},{8,0},{12,4},{16,8},{20,12},{24,16},{28,20},{1,25},{... | collective-permute-start | bytes 393224 | tf_op jit(solution)/shard_map/ppermute | solution.py:42
  509.3 6.6 %collective-permute-start.34 = (f32[16,2048]{1,0:T(8,128)S(1)}, f32[16,2048]{1,0:T(8,128)S(1)}, u32[]{:S(2)}, u32[]{:S(2)}) collective-permute-start(f32[16,2048]{1,0:T(8,128)S(1)} %get-tuple-element.83), channel_id=1, source_target_pairs={{0,16},{4,20},{8,24},{12,28},{16,0},{20,4},{24,8},{28,12},{1,17},{... | collective-permute-start | bytes 393224 | tf_op jit(solution)/shard_map/ppermute | solution.py:42
  (13 other events, 80.2 us)
Sparse Core Ops, SparseCore 0:
  159.1 68.3 reduce-scatter.6
  406.2 68.3 reduce-scatter.8

commit v7 on v6

--- a/solution.py
+++ b/solution.py
@@ -43,9 +43,26 @@
     return total
 
 
+def gather_by_permute(block, axis):
+    count = lax.axis_size(axis)
+    index = lax.axis_index(axis)
+    pieces = [block]
+    for shift in range(1, count):
+        pieces.append(
+            lax.ppermute(block, axis, [(j, (j + shift) % count) for j in range(count)])
+        )
+    stacked = jnp.stack(pieces[:1] + pieces[1:][::-1])
+    return jnp.roll(stacked, index, axis=0)
+
+
 def rows_for_weights(block):
-    wide = lax.all_gather(block, "kv", axis=1, tiled=True)
-    return lax.all_to_all(wide, "req", 1, 0, tiled=True)
+    req_size = lax.axis_size("req")
+    kv_size = lax.axis_size("kv")
+    ratio = req_size // kv_size
+    rows, width = block.shape[0], block.shape[1] // ratio
+    wide = gather_by_permute(block, "kv").reshape(kv_size, rows, ratio, width)
+    wide = wide.transpose(0, 2, 1, 3).reshape(req_size * rows, width)
+    return lax.all_to_all(wide, "req", 0, 0, tiled=True)
 
 
 def apply_rotation(values, token_positions):
@@ -215,7 +232,7 @@
         local_hidden = (jax.nn.silu(gate_up[:, :hidden_cols]) * gate_up[:, hidden_cols:]).astype(
             jnp.bfloat16
         )
-        hidden_all = lax.all_gather(local_hidden, "kv", axis=0, tiled=True)
+        hidden_all = gather_by_permute(local_hidden, "kv").reshape(-1, local_hidden.shape[1])
         residual = residual + scatter_sum(
             jnp.dot(hidden_all, w_down, preferred_element_type=jnp.float32), "req"
         )

time: 533 us -> 520 us (0.976)
  the two profiles are of different devices: /device:TPU:0 before, /device:TPU:18 now
where the time goes in v7:
time: 520 us; the launch traced here: 511 us
  waiting for transfers between devices  263 us (51%)
  starting transfers between devices  71.4 us (14%)
  matrix products  71.2 us (14%)
  blocking collectives  38.4 us (7%)
  other arithmetic  28.1 us (5%)
  local copies, waits for them, and re-layouts  23.8 us (5%)
  between operations  15 us (3%)
    reduce_scatter x2, waiting for transfers between devices, body(): lax.psum_scatter(jnp.concatenate([jnp.dot(tokens, w_gate, preferred_eleme...  141 us
    ppermute x18, waiting for transfers between devices, gather_by_permute(): lax.ppermute(block, axis, [(j, (j + shift) % count) for j in range(count)])  50.2 us
    ppermute x18, waiting for transfers between devices, scatter_sum(): total = total + lax.ppermute(piece, axis, pairs)  39.9 us
    ppermute x18, starting transfers between devices, gather_by_permute(): lax.ppermute(block, axis, [(j, (j + shift) % count) for j in range(count)])  26.7 us
    ppermute x18, starting transfers between devices, scatter_sum(): total = total + lax.ppermute(piece, axis, pairs)  19.4 us
    all_gather x2, blocking collectives, body(): tokens = lax.all_gather(normed_mlp, 'req', axis=0, tiled=True)  19.3 us
    all_to_all x2, blocking collectives, rows_for_weights(): return lax.all_to_all(wide, 'req', 0, 0, tiled=True)  19.1 us
    unnamed x50, local copies, waits for them, and re-layouts  16.6 us
  transfers between devices with their start and end apart: 58, of which 51 were waited for; matrix products, arithmetic and copies ran while one was open for 4% of the time, Pallas kernels for 0%

profile of v7, /device:TPU:18, one launch (start us, length us, event | category | flops | bytes accessed | tf_op | source)
XLA Modules:
  0.0 510.7 jit_solution(11680561310641259456)
XLA Ops:
  8.0 3.5 collective-permute-start.1
  16.3 4.9 constant_dynamic-update-slice_fusion.2
  32.8 4.3 all-to-all-start
  37.7 4.9 all-to-all-done
  43.4 3.4 fusion.199
  52.3 2.5 sort.17
  56.3 2.8 collective-permute-done.9
  61.6 2.8 fusion.4
  64.4 3.6 fusion.8
  73.1 2.3 collective-permute-start.11
  75.4 2.8 collective-permute-start.10
  81.6 5.4 %all-to-all-start.1 = ((bf16[8,16,1024]{2,1,0:T(8,128)(2,1)}), bf16[8,16,1024]{2,1,0:T(8,128)(2,1)S(1)}, u32[]{:S(2)}, u32[]{:S(2)}) async-start(bf16[8,16,1024]{2,1,0:T(8,128)(2,1)} %bitcast.41), calls=%async_computation.1 | async-start | bytes 524288 | tf_op jit(solution)/shard_map/all_to_all | solution.py:65
  87.4 5.0 all-to-all-done.1
  93.3 3.1 fusion.197
  101.6 3.2 collective-permute-done.14
  104.8 2.3 collective-permute-done.16
  112.9 2.3 collective-permute-done.18
  116.3 9.5 %all_gather.6 = bf16[128,2048]{1,0:T(8,128)(2,1)S(1)} all-gather(bf16[16,2048]{1,0:T(8,128)(2,1)S(1)} %multiply_convert_fusion.2), channel_id=1, replica_groups=mesh['req'=8,'kv'=4] {'req'}, dimensions={0}, use_global_device_ids=true | all-gather | bytes 589824 | tf_op jit(solution)/shard_map/all_gather | solution.py:218
  125.9 7.8 %fusion.290 = f32[128,3696]{0,1:T(8,128)S(1)} fusion(bf16[128,2048]{1,0:T(8,128)(2,1)S(1)} %all_gather.6, bf16[2048,3696]{0,1:T(8,128)(2,1)} %param.48), kind=kOutput, calls=%fused_computation.409 | convolution fusion | flops 1937768448 | bytes 17555456 | tf_op jit(solution)/shard_map/dot_general | solution.py:224
  133.7 4.3 fusion.289
  140.2 5.3 %copy.122 = f32[128,7392]{1,0:T(8,128)} copy(f32[128,7392]{0,1:T(8,128)} %pad_maximum_fusion) | data formatting | bytes 7569408
  145.6 70.9 %reduce-scatter.7.cloned.1.call-done = f32[32,7392]{1,0:T(8,128)} async-done(((f32[128,7392]{1,0:T(8,128)}), f32[32,7392]{1,0:T(8,128)}) %reduce-scatter.7.cloned.1.call-update) | async-done | bytes 946192 | tf_op jit(solution)/shard_map/reduce_scatter | solution.py:220
  221.6 8.2 %collective-permute-done.21 = bf16[32,3696]{1,0:T(8,128)(2,1)S(1)} collective-permute-done((bf16[32,3696]{1,0:T(8,128)(2,1)S(1)}, bf16[32,3696]{1,0:T(8,128)(2,1)S(1)}, u32[]{:S(2)}, u32[]{:S(2)}) %collective-permute-start.21) | collective-permute-done | bytes 236576 | tf_op jit(solution)/shard_map/ppermute | solution.py:52
  229.8 8.8 %collective-permute-done.20 = bf16[32,3696]{1,0:T(8,128)(2,1)S(1)} collective-permute-done((bf16[32,3696]{1,0:T(8,128)(2,1)S(1)}, bf16[32,3696]{1,0:T(8,128)(2,1)S(1)}, u32[]{:S(2)}, u32[]{:S(2)}) %collective-permute-start.20) | collective-permute-done | bytes 236576 | tf_op jit(solution)/shard_map/ppermute | solution.py:52
  241.8 7.7 %fusion = f32[4,2,16,2048]{3,2,1,0:T(8,128)S(1)} fusion(bf16[4,2,16,3696]{3,2,1,0:T(8,128)(2,1)S(1)} %bitcast.498, bf16[3696,2048]{1,0:T(8,128)(2,1)} %param.49), kind=kOutput, calls=%fused_computation.6 | convolution fusion | flops 1937768448 | bytes 17133568 | tf_op jit(solution)/shard_map/dot_general | solution.py:237
  255.2 2.8 collective-permute-done.24
  258.1 3.0 collective-permute-done.26
  266.9 3.8 collective-permute-start.31
  276.0 9.5 %all_to_all.48 = bf16[8,16,1024]{2,1,0:T(8,128)(2,1)S(1)} all-to-all(bf16[8,16,1024]{2,1,0:T(8,128)(2,1)S(1)} %bitcast.501), channel_id=1, replica_groups=mesh['req'=8,'kv'=4] {'req'}, dimensions={0} | all-to-all | bytes 524288 | tf_op jit(solution)/shard_map/all_to_all | solution.py:65
  286.3 3.4 fusion.195
  295.5 3.7 collective-permute-done.34
  299.2 2.8 collective-permute-done.36
  304.7 2.8 fusion.6
  307.5 3.6 fusion.12
  318.3 2.8 collective-permute-start.37
  323.8 9.6 %all_to_all.49 = bf16[8,16,1024]{2,1,0:T(8,128)(2,1)S(1)} all-to-all(bf16[8,16,1024]{2,1,0:T(8,128)(2,1)S(1)} %bitcast.502), channel_id=1, replica_groups=mesh['req'=8,'kv'=4] {'req'}, dimensions={0} | all-to-all | bytes 524288 | tf_op jit(solution)/shard_map/all_to_all | solution.py:65
  334.3 3.1 fusion.193
  342.5 3.3 collective-permute-done.41
  357.7 9.8 %all_gather.7 = bf16[128,2048]{1,0:T(8,128)(2,1)S(1)} all-gather(bf16[16,2048]{1,0:T(8,128)(2,1)S(1)} %multiply_convert_fusion), channel_id=1, replica_groups=mesh['req'=8,'kv'=4] {'req'}, dimensions={0}, use_global_device_ids=true | all-gather | bytes 589824 | tf_op jit(solution)/shard_map/all_gather | solution.py:218
  367.4 7.8 %fusion.292 = f32[128,3696]{0,1:T(8,128)S(1)} fusion(bf16[128,2048]{1,0:T(8,128)(2,1)S(1)} %all_gather.7, bf16[2048,3696]{0,1:T(8,128)(2,1)} %param.48), kind=kOutput, calls=%fused_computation.411 | convolution fusion | flops 1937768448 | bytes 17555456 | tf_op jit(solution)/shard_map/dot_general | solution.py:224
  375.3 4.3 fusion.291
  381.7 5.3 %copy.124 = f32[128,7392]{1,0:T(8,128)} copy(f32[128,7392]{0,1:T(8,128)} %pad_maximum_fusion.1) | data formatting | bytes 7569408
  387.0 70.6 %reduce-scatter.9.cloned.1.call-done = f32[32,7392]{1,0:T(8,128)} async-done(((f32[128,7392]{1,0:T(8,128)}), f32[32,7392]{1,0:T(8,128)}) %reduce-scatter.9.cloned.1.call-update) | async-done | bytes 946192 | tf_op jit(solution)/shard_map/reduce_scatter | solution.py:220
  462.6 8.3 %collective-permute-done.48 = bf16[32,3696]{1,0:T(8,128)(2,1)S(1)} collective-permute-done((bf16[32,3696]{1,0:T(8,128)(2,1)S(1)}, bf16[32,3696]{1,0:T(8,128)(2,1)S(1)}, u32[]{:S(2)}, u32[]{:S(2)}) %collective-permute-start.48) | collective-permute-done | bytes 236576 | tf_op jit(solution)/shard_map/ppermute | solution.py:52
  470.9 8.8 %collective-permute-done.47 = bf16[32,3696]{1,0:T(8,128)(2,1)S(1)} collective-permute-done((bf16[32,3696]{1,0:T(8,128)(2,1)S(1)}, bf16[32,3696]{1,0:T(8,128)(2,1)S(1)}, u32[]{:S(2)}, u32[]{:S(2)}) %collective-permute-start.47) | collective-permute-done | bytes 236576 | tf_op jit(solution)/shard_map/ppermute | solution.py:52
  483.0 7.7 %fusion.2 = f32[4,2,16,2048]{3,2,0,1:T(8,128)S(1)} fusion(bf16[3696,2048]{1,0:T(8,128)(2,1)} %param.49, bf16[4,2,16,3696]{3,2,1,0:T(8,128)(2,1)S(1)} %bitcast.497), kind=kOutput, calls=%fused_computation.8 | convolution fusion | flops 1937768448 | bytes 17133568 | tf_op jit(solution)/shard_map/dot_general | solution.py:237
  496.4 2.8 collective-permute-done.51
  499.2 3.0 collective-permute-done.53
  (275 shorter events, 131.3 us)
Async XLA Ops:
  7.5 15.6 %collective-permute-start.2 = (f32[16]{0:T(128)S(1)}, f32[16]{0:T(128)S(1)}, u32[]{:S(2)}, u32[]{:S(2)}) collective-permute-start(f32[16]{0:T(128)S(1)} %fusion.211), channel_id=1, source_target_pairs={{0,3},{1,0},{2,1},{3,2},{4,7},{5,4},{6,5},{7,6},{8,11},{9,8},{10,9... | collective-permute-start | bytes 200 | tf_op jit(solution)/shard_map/ppermute | solution.py:90
  8.0 15.1 %collective-permute-start.1 = (f32[16]{0:T(128)S(1)}, f32[16]{0:T(128)S(1)}, u32[]{:S(2)}, u32[]{:S(2)}) collective-permute-start(f32[16]{0:T(128)S(1)} %fusion.211), channel_id=1, source_target_pairs={{0,2},{1,3},{2,0},{3,1},{4,6},{5,7},{6,4},{7,5},{8,10},{9,11},{10,... | collective-permute-start | bytes 200 | tf_op jit(solution)/shard_map/ppermute | solution.py:90
  11.5 11.6 %collective-permute-start = (f32[16]{0:T(128)S(1)}, f32[16]{0:T(128)S(1)}, u32[]{:S(2)}, u32[]{:S(2)}) collective-permute-start(f32[16]{0:T(128)S(1)} %fusion.211), channel_id=1, source_target_pairs={{0,1},{1,2},{2,3},{3,0},{4,5},{5,6},{6,7},{7,4},{8,9},{9,10},{10,1... | collective-permute-start | bytes 200 | tf_op jit(solution)/shard_map/ppermute | solution.py:90
  23.2 5.4 %collective-permute-start.4 = (bf16[16,2048]{1,0:T(8,128)(2,1)S(1)}, bf16[16,2048]{1,0:T(8,128)(2,1)S(1)}, u32[]{:S(2)}, u32[]{:S(2)}) collective-permute-start(bf16[16,2048]{1,0:T(8,128)(2,1)S(1)} %fusion.213), channel_id=1, source_target_pairs={{0,2},{1,3},{2,0},{3,1},{4,6},{5,7},{6,4},{7,5},{8,10},{9,11},{10,... | collective-permute-start | bytes 196616 | tf_op jit(solution)/shard_map/ppermute | solution.py:52
  24.3 5.5 %collective-permute-start.3 = (bf16[16,2048]{1,0:T(8,128)(2,1)S(1)}, bf16[16,2048]{1,0:T(8,128)(2,1)S(1)}, u32[]{:S(2)}, u32[]{:S(2)}) collective-permute-start(bf16[16,2048]{1,0:T(8,128)(2,1)S(1)} %fusion.213), channel_id=1, source_target_pairs={{0,3},{1,0},{2,1},{3,2},{4,7},{5,4},{6,5},{7,6},{8,11},{9,8},{10,9... | collective-permute-start | bytes 196616 | tf_op jit(solution)/shard_map/ppermute | solution.py:52
  26.2 5.5 %collective-permute-start.5 = (bf16[16,2048]{1,0:T(8,128)(2,1)S(1)}, bf16[16,2048]{1,0:T(8,128)(2,1)S(1)}, u32[]{:S(2)}, u32[]{:S(2)}) collective-permute-start(bf16[16,2048]{1,0:T(8,128)(2,1)S(1)} %fusion.213), channel_id=1, source_target_pairs={{0,1},{1,2},{2,3},{3,0},{4,5},{5,6},{6,7},{7,4},{8,9},{9,10},{10,1... | collective-permute-start | bytes 196616 | tf_op jit(solution)/shard_map/ppermute | solution.py:52
  32.8 9.7 %all-to-all-start = ((bf16[8,16,1024]{2,1,0:T(8,128)(2,1)}), bf16[8,16,1024]{2,1,0:T(8,128)(2,1)S(1)}, u32[]{:S(2)}, u32[]{:S(2)}) async-start(bf16[8,16,1024]{2,1,0:T(8,128)(2,1)} %bitcast.7), calls=%async_computation | async-start | bytes 524288 | tf_op jit(solution)/shard_map/all_to_all | solution.py:65
  49.2 7.1 %collective-permute-start.7 = (f32[16,2560]{1,0:T(8,128)S(1)}, f32[16,2560]{1,0:T(8,128)S(1)}, u32[]{:S(2)}, u32[]{:S(2)}) collective-permute-start(f32[16,2560]{1,0:T(8,128)S(1)} %get-tuple-element.80), channel_id=1, source_target_pairs={{0,8},{4,12},{8,16},{12,20},{16,24},{20,28},{24,0},{28,4},{1,9},{5... | collective-permute-start | bytes 491528 | tf_op jit(solution)/shard_map/ppermute | solution.py:42
  50.7 8.4 %collective-permute-start.9 = (f32[16,2560]{1,0:T(8,128)S(1)}, f32[16,2560]{1,0:T(8,128)S(1)}, u32[]{:S(2)}, u32[]{:S(2)}) collective-permute-start(f32[16,2560]{1,0:T(8,128)S(1)} %get-tuple-element.81), channel_id=1, source_target_pairs={{0,24},{4,28},{8,0},{12,4},{16,8},{20,12},{24,16},{28,20},{1,25},{... | collective-permute-start | bytes 491528 | tf_op jit(solution)/shard_map/ppermute | solution.py:42
  51.3 9.2 %collective-permute-start.8 = (f32[16,2560]{1,0:T(8,128)S(1)}, f32[16,2560]{1,0:T(8,128)S(1)}, u32[]{:S(2)}, u32[]{:S(2)}) collective-permute-start(f32[16,2560]{1,0:T(8,128)S(1)} %get-tuple-element.82), channel_id=1, source_target_pairs={{0,16},{4,20},{8,24},{12,28},{16,0},{20,4},{24,8},{28,12},{1,17},{... | collective-permute-start | bytes 491528 | tf_op jit(solution)/shard_map/ppermute | solution.py:42
  71.9 6.5 %collective-permute-start.12 = (bf16[16,2048]{1,0:T(8,128)(2,1)S(1)}, bf16[16,2048]{1,0:T(8,128)(2,1)S(1)}, u32[]{:S(2)}, u32[]{:S(2)}) collective-permute-start(bf16[16,2048]{1,0:T(8,128)(2,1)S(1)} %bitcast.523), channel_id=1, source_target_pairs={{0,1},{1,2},{2,3},{3,0},{4,5},{5,6},{6,7},{7,4},{8,9},{9,10},{10,1... | collective-permute-start | bytes 196616 | tf_op jit(solution)/shard_map/ppermute | solution.py:52
  73.1 5.9 %collective-permute-start.11 = (bf16[16,2048]{1,0:T(8,128)(2,1)S(1)}, bf16[16,2048]{1,0:T(8,128)(2,1)S(1)}, u32[]{:S(2)}, u32[]{:S(2)}) collective-permute-start(bf16[16,2048]{1,0:T(8,128)(2,1)S(1)} %bitcast.524), channel_id=1, source_target_pairs={{0,2},{1,3},{2,0},{3,1},{4,6},{5,7},{6,4},{7,5},{8,10},{9,11},{10,... | collective-permute-start | bytes 196616 | tf_op jit(solution)/shard_map/ppermute | solution.py:52
  75.4 5.0 collective-permute-start.10
  81.6 10.9 %all-to-all-start.1 = ((bf16[8,16,1024]{2,1,0:T(8,128)(2,1)}), bf16[8,16,1024]{2,1,0:T(8,128)(2,1)S(1)}, u32[]{:S(2)}, u32[]{:S(2)}) async-start(bf16[8,16,1024]{2,1,0:T(8,128)(2,1)} %bitcast.41), calls=%async_computation.1 | async-start | bytes 524288 | tf_op jit(solution)/shard_map/all_to_all | solution.py:65
  86.9 129.5 %reduce-scatter.7.cloned.1.call-start = ((), (), s32[]{:S(2)}) async-start(), calls=%async_computation.6 | async-start | bytes 4751360 | tf_op jit(solution)/shard_map/reduce_scatter | solution.py:220
  98.6 6.3 %collective-permute-start.14 = (f32[16,2048]{1,0:T(8,128)S(1)}, f32[16,2048]{1,0:T(8,128)S(1)}, u32[]{:S(2)}, u32[]{:S(2)}) collective-permute-start(f32[16,2048]{1,0:T(8,128)S(1)} %get-tuple-element.92), channel_id=1, source_target_pairs={{0,8},{4,12},{8,16},{12,20},{16,24},{20,28},{24,0},{28,4},{1,9},{5... | collective-permute-start | bytes 393224 | tf_op jit(solution)/shard_map/ppermute | solution.py:42
  100.1 7.0 %collective-permute-start.16 = (f32[16,2048]{1,0:T(8,128)S(1)}, f32[16,2048]{1,0:T(8,128)S(1)}, u32[]{:S(2)}, u32[]{:S(2)}) collective-permute-start(f32[16,2048]{1,0:T(8,128)S(1)} %get-tuple-element.93), channel_id=1, source_target_pairs={{0,24},{4,28},{8,0},{12,4},{16,8},{20,12},{24,16},{28,20},{1,25},{... | collective-permute-start | bytes 393224 | tf_op jit(solution)/shard_map/ppermute | solution.py:42
  100.7 7.8 %collective-permute-start.15 = (f32[16,2048]{1,0:T(8,128)S(1)}, f32[16,2048]{1,0:T(8,128)S(1)}, u32[]{:S(2)}, u32[]{:S(2)}) collective-permute-start(f32[16,2048]{1,0:T(8,128)S(1)} %get-tuple-element.94), channel_id=1, source_target_pairs={{0,16},{4,20},{8,24},{12,28},{16,0},{20,4},{24,8},{28,12},{1,17},{... | collective-permute-start | bytes 393224 | tf_op jit(solution)/shard_map/ppermute | solution.py:42
  108.6 4.3 collective-permute-start.19
  110.8 4.4 collective-permute-start.18
  145.6 312.1 %reduce-scatter.9.cloned.1.call-start = ((), (), s32[]{:S(2)}) async-start(), calls=%async_computation.7 | async-start | bytes 4751360 | tf_op jit(solution)/shard_map/reduce_scatter | solution.py:220
  217.9 11.9 %collective-permute-start.21 = (bf16[32,3696]{1,0:T(8,128)(2,1)S(1)}, bf16[32,3696]{1,0:T(8,128)(2,1)S(1)}, u32[]{:S(2)}, u32[]{:S(2)}) collective-permute-start(bf16[32,3696]{1,0:T(8,128)(2,1)S(1)} %fusion.164), channel_id=1, source_target_pairs={{0,2},{1,3},{2,0},{3,1},{4,6},{5,7},{6,4},{7,5},{8,10},{9,11},{10,... | collective-permute-start | bytes 709640 | tf_op jit(solution)/shard_map/ppermute | solution.py:52
  218.1 20.5 %collective-permute-start.20 = (bf16[32,3696]{1,0:T(8,128)(2,1)S(1)}, bf16[32,3696]{1,0:T(8,128)(2,1)S(1)}, u32[]{:S(2)}, u32[]{:S(2)}) collective-permute-start(bf16[32,3696]{1,0:T(8,128)(2,1)S(1)} %fusion.164), channel_id=1, source_target_pairs={{0,3},{1,0},{2,1},{3,2},{4,7},{5,4},{6,5},{7,6},{8,11},{9,8},{10,9... | collective-permute-start | bytes 709640 | tf_op jit(solution)/shard_map/ppermute | solution.py:52
  219.8 20.8 %collective-permute-start.22 = (bf16[32,3696]{1,0:T(8,128)(2,1)S(1)}, bf16[32,3696]{1,0:T(8,128)(2,1)S(1)}, u32[]{:S(2)}, u32[]{:S(2)}) collective-permute-start(bf16[32,3696]{1,0:T(8,128)(2,1)S(1)} %fusion.164), channel_id=1, source_target_pairs={{0,1},{1,2},{2,3},{3,0},{4,5},{5,6},{6,7},{7,4},{8,9},{9,10},{10,1... | collective-permute-start | bytes 709640 | tf_op jit(solution)/shard_map/ppermute | solution.py:52
  251.7 6.4 %collective-permute-start.24 = (f32[16,2048]{1,0:T(8,128)S(1)}, f32[16,2048]{1,0:T(8,128)S(1)}, u32[]{:S(2)}, u32[]{:S(2)}) collective-permute-start(f32[16,2048]{1,0:T(8,128)S(1)} %get-tuple-element.89), channel_id=1, source_target_pairs={{0,8},{4,12},{8,16},{12,20},{16,24},{20,28},{24,0},{28,4},{1,9},{5... | collective-permute-start | bytes 393224 | tf_op jit(solution)/shard_map/ppermute | solution.py:42
  253.2 7.9 %collective-permute-start.26 = (f32[16,2048]{1,0:T(8,128)S(1)}, f32[16,2048]{1,0:T(8,128)S(1)}, u32[]{:S(2)}, u32[]{:S(2)}) collective-permute-start(f32[16,2048]{1,0:T(8,128)S(1)} %get-tuple-element.90), channel_id=1, source_target_pairs={{0,24},{4,28},{8,0},{12,4},{16,8},{20,12},{24,16},{28,20},{1,25},{... | collective-permute-start | bytes 393224 | tf_op jit(solution)/shard_map/ppermute | solution.py:42
  253.8 7.8 %collective-permute-start.25 = (f32[16,2048]{1,0:T(8,128)S(1)}, f32[16,2048]{1,0:T(8,128)S(1)}, u32[]{:S(2)}, u32[]{:S(2)}) collective-permute-start(f32[16,2048]{1,0:T(8,128)S(1)} %get-tuple-element.91), channel_id=1, source_target_pairs={{0,16},{4,20},{8,24},{12,28},{16,0},{20,4},{24,8},{28,12},{1,17},{... | collective-permute-start | bytes 393224 | tf_op jit(solution)/shard_map/ppermute | solution.py:42
  262.2 4.4 collective-permute-start.28
  262.2 4.6 collective-permute-start.27
  266.9 6.0 %collective-permute-start.31 = (bf16[16,2048]{1,0:T(8,128)(2,1)S(1)}, bf16[16,2048]{1,0:T(8,128)(2,1)S(1)}, u32[]{:S(2)}, u32[]{:S(2)}) collective-permute-start(bf16[16,2048]{1,0:T(8,128)(2,1)S(1)} %multiply_convert_fusion.1), channel_id=1, source_target_pairs={{0,2},{1,3},{2,0},{3,1},{4,6},{5,7},{6,4},{7,5},{8,10},{9,11},{10,... | collective-permute-start | bytes 196616 | tf_op jit(solution)/shard_map/ppermute | solution.py:52
  270.6 5.0 collective-permute-start.32
  292.1 7.1 %collective-permute-start.34 = (f32[16,2560]{1,0:T(8,128)S(1)}, f32[16,2560]{1,0:T(8,128)S(1)}, u32[]{:S(2)}, u32[]{:S(2)}) collective-permute-start(f32[16,2560]{1,0:T(8,128)S(1)} %get-tuple-element.77), channel_id=1, source_target_pairs={{0,8},{4,12},{8,16},{12,20},{16,24},{20,28},{24,0},{28,4},{1,9},{5... | collective-permute-start | bytes 491528 | tf_op jit(solution)/shard_map/ppermute | solution.py:42
  293.6 8.4 %collective-permute-start.36 = (f32[16,2560]{1,0:T(8,128)S(1)}, f32[16,2560]{1,0:T(8,128)S(1)}, u32[]{:S(2)}, u32[]{:S(2)}) collective-permute-start(f32[16,2560]{1,0:T(8,128)S(1)} %get-tuple-element.78), channel_id=1, source_target_pairs={{0,24},{4,28},{8,0},{12,4},{16,8},{20,12},{24,16},{28,20},{1,25},{... | collective-permute-start | bytes 491528 | tf_op jit(solution)/shard_map/ppermute | solution.py:42
  294.4 9.2 %collective-permute-start.35 = (f32[16,2560]{1,0:T(8,128)S(1)}, f32[16,2560]{1,0:T(8,128)S(1)}, u32[]{:S(2)}, u32[]{:S(2)}) collective-permute-start(f32[16,2560]{1,0:T(8,128)S(1)} %get-tuple-element.79), channel_id=1, source_target_pairs={{0,16},{4,20},{8,24},{12,28},{16,0},{20,4},{24,8},{28,12},{1,17},{... | collective-permute-start | bytes 491528 | tf_op jit(solution)/shard_map/ppermute | solution.py:42
  315.0 6.3 %collective-permute-start.39 = (bf16[16,2048]{1,0:T(8,128)(2,1)S(1)}, bf16[16,2048]{1,0:T(8,128)(2,1)S(1)}, u32[]{:S(2)}, u32[]{:S(2)}) collective-permute-start(bf16[16,2048]{1,0:T(8,128)(2,1)S(1)} %bitcast.526), channel_id=1, source_target_pairs={{0,1},{1,2},{2,3},{3,0},{4,5},{5,6},{6,7},{7,4},{8,9},{9,10},{10,1... | collective-permute-start | bytes 196616 | tf_op jit(solution)/shard_map/ppermute | solution.py:52
  316.7 5.8 %collective-permute-start.38 = (bf16[16,2048]{1,0:T(8,128)(2,1)S(1)}, bf16[16,2048]{1,0:T(8,128)(2,1)S(1)}, u32[]{:S(2)}, u32[]{:S(2)}) collective-permute-start(bf16[16,2048]{1,0:T(8,128)(2,1)S(1)} %bitcast.527), channel_id=1, source_target_pairs={{0,2},{1,3},{2,0},{3,1},{4,6},{5,7},{6,4},{7,5},{8,10},{9,11},{10,... | collective-permute-start | bytes 196616 | tf_op jit(solution)/shard_map/ppermute | solution.py:52
  318.3 5.1 collective-permute-start.37
  339.5 6.3 %collective-permute-start.41 = (f32[16,2048]{1,0:T(8,128)S(1)}, f32[16,2048]{1,0:T(8,128)S(1)}, u32[]{:S(2)}, u32[]{:S(2)}) collective-permute-start(f32[16,2048]{1,0:T(8,128)S(1)} %get-tuple-element.86), channel_id=1, source_target_pairs={{0,8},{4,12},{8,16},{12,20},{16,24},{20,28},{24,0},{28,4},{1,9},{5... | collective-permute-start | bytes 393224 | tf_op jit(solution)/shard_map/ppermute | solution.py:42
  341.1 7.0 %collective-permute-start.43 = (f32[16,2048]{1,0:T(8,128)S(1)}, f32[16,2048]{1,0:T(8,128)S(1)}, u32[]{:S(2)}, u32[]{:S(2)}) collective-permute-start(f32[16,2048]{1,0:T(8,128)S(1)} %get-tuple-element.87), channel_id=1, source_target_pairs={{0,24},{4,28},{8,0},{12,4},{16,8},{20,12},{24,16},{28,20},{1,25},{... | collective-permute-start | bytes 393224 | tf_op jit(solution)/shard_map/ppermute | solution.py:42
  341.6 7.8 %collective-permute-start.42 = (f32[16,2048]{1,0:T(8,128)S(1)}, f32[16,2048]{1,0:T(8,128)S(1)}, u32[]{:S(2)}, u32[]{:S(2)}) collective-permute-start(f32[16,2048]{1,0:T(8,128)S(1)} %get-tuple-element.88), channel_id=1, source_target_pairs={{0,16},{4,20},{8,24},{12,28},{16,0},{20,4},{24,8},{28,12},{1,17},{... | collective-permute-start | bytes 393224 | tf_op jit(solution)/shard_map/ppermute | solution.py:42
  349.6 4.4 collective-permute-start.46
  351.8 4.4 collective-permute-start.45
  459.0 11.9 %collective-permute-start.48 = (bf16[32,3696]{1,0:T(8,128)(2,1)S(1)}, bf16[32,3696]{1,0:T(8,128)(2,1)S(1)}, u32[]{:S(2)}, u32[]{:S(2)}) collective-permute-start(bf16[32,3696]{1,0:T(8,128)(2,1)S(1)} %fusion.163), channel_id=1, source_target_pairs={{0,2},{1,3},{2,0},{3,1},{4,6},{5,7},{6,4},{7,5},{8,10},{9,11},{10,... | collective-permute-start | bytes 709640 | tf_op jit(solution)/shard_map/ppermute | solution.py:52
  459.2 20.5 %collective-permute-start.47 = (bf16[32,3696]{1,0:T(8,128)(2,1)S(1)}, bf16[32,3696]{1,0:T(8,128)(2,1)S(1)}, u32[]{:S(2)}, u32[]{:S(2)}) collective-permute-start(bf16[32,3696]{1,0:T(8,128)(2,1)S(1)} %fusion.163), channel_id=1, source_target_pairs={{0,3},{1,0},{2,1},{3,2},{4,7},{5,4},{6,5},{7,6},{8,11},{9,8},{10,9... | collective-permute-start | bytes 709640 | tf_op jit(solution)/shard_map/ppermute | solution.py:52
  461.0 20.8 %collective-permute-start.49 = (bf16[32,3696]{1,0:T(8,128)(2,1)S(1)}, bf16[32,3696]{1,0:T(8,128)(2,1)S(1)}, u32[]{:S(2)}, u32[]{:S(2)}) collective-permute-start(bf16[32,3696]{1,0:T(8,128)(2,1)S(1)} %fusion.163), channel_id=1, source_target_pairs={{0,1},{1,2},{2,3},{3,0},{4,5},{5,6},{6,7},{7,4},{8,9},{9,10},{10,1... | collective-permute-start | bytes 709640 | tf_op jit(solution)/shard_map/ppermute | solution.py:52
  492.8 6.4 %collective-permute-start.51 = (f32[16,2048]{1,0:T(8,128)S(1)}, f32[16,2048]{1,0:T(8,128)S(1)}, u32[]{:S(2)}, u32[]{:S(2)}) collective-permute-start(f32[16,2048]{1,0:T(8,128)S(1)} %get-tuple-element.83), channel_id=1, source_target_pairs={{0,8},{4,12},{8,16},{12,20},{16,24},{20,28},{24,0},{28,4},{1,9},{5... | collective-permute-start | bytes 393224 | tf_op jit(solution)/shard_map/ppermute | solution.py:42
  494.4 7.9 %collective-permute-start.53 = (f32[16,2048]{1,0:T(8,128)S(1)}, f32[16,2048]{1,0:T(8,128)S(1)}, u32[]{:S(2)}, u32[]{:S(2)}) collective-permute-start(f32[16,2048]{1,0:T(8,128)S(1)} %get-tuple-element.84), channel_id=1, source_target_pairs={{0,24},{4,28},{8,0},{12,4},{16,8},{20,12},{24,16},{28,20},{1,25},{... | collective-permute-start | bytes 393224 | tf_op jit(solution)/shard_map/ppermute | solution.py:42
  494.9 7.8 %collective-permute-start.52 = (f32[16,2048]{1,0:T(8,128)S(1)}, f32[16,2048]{1,0:T(8,128)S(1)}, u32[]{:S(2)}, u32[]{:S(2)}) collective-permute-start(f32[16,2048]{1,0:T(8,128)S(1)} %get-tuple-element.85), channel_id=1, source_target_pairs={{0,16},{4,20},{8,24},{12,28},{16,0},{20,4},{24,8},{28,12},{1,17},{... | collective-permute-start | bytes 393224 | tf_op jit(solution)/shard_map/ppermute | solution.py:42
  (30 other events, 299.6 us)
Sparse Core Ops, SparseCore 0:
  145.7 70.7 reduce-scatter.6
  387.2 70.4 reduce-scatter.8

commit v8 on v7

--- a/solution.py
+++ b/solution.py
@@ -171,9 +171,16 @@
     key_width = key_projection_weight.shape[1]
     kv_heads = key_width // head_dim
     capacity = rotated_key_cache.shape[1]
-    w_joint = jnp.concatenate([w_query, key_projection_weight, value_projection_weight], axis=1)
     b_joint = jnp.concatenate([b_query, key_bias, value_bias]).astype(jnp.float32)
-    inverse = jnp.argsort(request_serving_order)
+    request_count = request_serving_order.shape[0]
+    inverse = jnp.sum(
+        jnp.where(
+            request_serving_order[:, None] == jnp.arange(request_count, dtype=jnp.int32)[None, :],
+            jnp.arange(request_count, dtype=jnp.int32)[:, None],
+            0,
+        ),
+        axis=0,
+    )
     my_slots = lax.dynamic_slice_in_dim(request_serving_order, req_index * own_rows, own_rows)
     residual = hidden.astype(jnp.float32)
     for current_layer_index in range(LAYER_COUNT):
@@ -181,7 +188,16 @@
         columns = rows_for_weights(normed)
         picked = jnp.take(columns, request_serving_order, axis=0)
         combined = (
-            scatter_sum(jnp.dot(picked, w_joint, preferred_element_type=jnp.float32), "req")
+            scatter_sum(
+                jnp.concatenate(
+                    [
+                        jnp.dot(picked, weight, preferred_element_type=jnp.float32)
+                        for weight in (w_query, key_projection_weight, value_projection_weight)
+                    ],
+                    axis=1,
+                ),
+                "req",
+            )
             + b_joint[None, :]
         )
         lengths = jnp.take(cache_len[current_layer_index], my_slots)

time: 520 us -> 516 us (level)
  local copies, waits for them, and re-layouts: 23.8 us -> 17.1 us
    unnamed x50, local copies, waits for them, and re-layouts: 16.6 us -> 10.8 us
  transfers between devices with their start and end apart: 58 -> 58, of which waited for: 51 -> 51; matrix products, arithmetic and copies ran while one was open for 4% -> 2% of each run, Pallas kernels for 0% -> 0%
where the time goes in v8:
time: 516 us; the launch traced here: 507 us
  waiting for transfers between devices  264 us (51%)
  starting transfers between devices  71.4 us (14%)
  matrix products  71.4 us (14%)
  blocking collectives  38.4 us (7%)
  other arithmetic  29.9 us (6%)
  local copies, waits for them, and re-layouts  17.1 us (3%)
  between operations  15.1 us (3%)
    reduce_scatter x2, waiting for transfers between devices, body(): lax.psum_scatter(jnp.concatenate([jnp.dot(tokens, w_gate, preferred_eleme...  141 us
    ppermute x18, waiting for transfers between devices, gather_by_permute(): lax.ppermute(block, axis, [(j, (j + shift) % count) for j in range(count)])  49.4 us
    ppermute x18, waiting for transfers between devices, scatter_sum(): total = total + lax.ppermute(piece, axis, pairs)  42.5 us
    ppermute x18, starting transfers between devices, gather_by_permute(): lax.ppermute(block, axis, [(j, (j + shift) % count) for j in range(count)])  26.6 us
    ppermute x18, starting transfers between devices, scatter_sum(): total = total + lax.ppermute(piece, axis, pairs)  19.4 us
    all_gather x2, blocking collectives, body(): tokens = lax.all_gather(normed_mlp, 'req', axis=0, tiled=True)  19.3 us
    all_to_all x2, blocking collectives, rows_for_weights(): return lax.all_to_all(wide, 'req', 0, 0, tiled=True)  19.1 us
    dot_general x2, matrix products, body(): jnp.dot(tokens, w_up, preferred_element_type=jnp.float32)  15.5 us
  transfers between devices with their start and end apart: 58, of which 51 were waited for; matrix products, arithmetic and copies ran while one was open for 2% of the time, Pallas kernels for 0%

profile of v8, /device:TPU:18, one launch (start us, length us, event | category | flops | bytes accessed | tf_op | source)
XLA Modules:
  0.0 507.2 jit_solution(1102691370678904800)
XLA Ops:
  8.1 3.5 collective-permute-start.1
  27.7 4.3 all-to-all-start
  33.2 4.2 all-to-all-done
  38.9 3.0 fusion.275
  48.7 4.0 collective-permute-done.7
  52.6 2.8 collective-permute-done.9
  57.9 2.8 fusion.4
  60.8 3.6 fusion.8
  69.5 2.3 collective-permute-start.11
  71.8 2.8 collective-permute-start.10
  77.9 5.4 %all-to-all-start.1 = ((bf16[8,16,1024]{2,1,0:T(8,128)(2,1)}), bf16[8,16,1024]{2,1,0:T(8,128)(2,1)S(1)}, u32[]{:S(2)}, u32[]{:S(2)}) async-start(bf16[8,16,1024]{2,1,0:T(8,128)(2,1)} %bitcast.41), calls=%async_computation.1 | async-start | bytes 524288 | tf_op jit(solution)/shard_map/all_to_all | solution.py:65
  83.8 5.0 all-to-all-done.1
  89.7 3.1 fusion.195
  97.9 3.2 collective-permute-done.14
  101.2 2.3 collective-permute-done.16
  109.3 2.3 collective-permute-done.18
  112.7 9.5 %all_gather.6 = bf16[128,2048]{1,0:T(8,128)(2,1)S(1)} all-gather(bf16[16,2048]{1,0:T(8,128)(2,1)S(1)} %multiply_convert_fusion.2), channel_id=1, replica_groups=mesh['req'=8,'kv'=4] {'req'}, dimensions={0}, use_global_device_ids=true | all-gather | bytes 589824 | tf_op jit(solution)/shard_map/all_gather | solution.py:234
  122.2 7.8 %fusion.286 = f32[128,3696]{0,1:T(8,128)S(1)} fusion(bf16[128,2048]{1,0:T(8,128)(2,1)S(1)} %all_gather.6, bf16[2048,3696]{0,1:T(8,128)(2,1)} %param.48), kind=kOutput, calls=%fused_computation.408 | convolution fusion | flops 1937768448 | bytes 17555456 | tf_op jit(solution)/shard_map/dot_general | solution.py:240
  130.1 4.3 fusion.285
  136.5 5.3 %copy.147 = f32[128,7392]{1,0:T(8,128)} copy(f32[128,7392]{0,1:T(8,128)} %pad_maximum_fusion) | data formatting | bytes 7569408
  141.8 70.9 %reduce-scatter.7.cloned.1.call-done = f32[32,7392]{1,0:T(8,128)} async-done(((f32[128,7392]{1,0:T(8,128)}), f32[32,7392]{1,0:T(8,128)}) %reduce-scatter.7.cloned.1.call-update) | async-done | bytes 946192 | tf_op jit(solution)/shard_map/reduce_scatter | solution.py:236
  217.8 8.2 %collective-permute-done.21 = bf16[32,3696]{1,0:T(8,128)(2,1)S(1)} collective-permute-done((bf16[32,3696]{1,0:T(8,128)(2,1)S(1)}, bf16[32,3696]{1,0:T(8,128)(2,1)S(1)}, u32[]{:S(2)}, u32[]{:S(2)}) %collective-permute-start.21) | collective-permute-done | bytes 236576 | tf_op jit(solution)/shard_map/ppermute | solution.py:52
  226.0 8.8 %collective-permute-done.20 = bf16[32,3696]{1,0:T(8,128)(2,1)S(1)} collective-permute-done((bf16[32,3696]{1,0:T(8,128)(2,1)S(1)}, bf16[32,3696]{1,0:T(8,128)(2,1)S(1)}, u32[]{:S(2)}, u32[]{:S(2)}) %collective-permute-start.20) | collective-permute-done | bytes 236576 | tf_op jit(solution)/shard_map/ppermute | solution.py:52
  238.1 7.7 %fusion = f32[4,2,16,2048]{3,2,1,0:T(8,128)S(1)} fusion(bf16[4,2,16,3696]{3,2,1,0:T(8,128)(2,1)S(1)} %bitcast.502, bf16[3696,2048]{1,0:T(8,128)(2,1)} %param.49), kind=kOutput, calls=%fused_computation.6 | convolution fusion | flops 1937768448 | bytes 17133568 | tf_op jit(solution)/shard_map/dot_general | solution.py:253
  251.5 2.8 collective-permute-done.24
  254.3 3.0 collective-permute-done.26
  263.1 3.8 collective-permute-start.31
  272.2 9.5 %all_to_all.48 = bf16[8,16,1024]{2,1,0:T(8,128)(2,1)S(1)} all-to-all(bf16[8,16,1024]{2,1,0:T(8,128)(2,1)S(1)} %bitcast.505), channel_id=1, replica_groups=mesh['req'=8,'kv'=4] {'req'}, dimensions={0} | all-to-all | bytes 524288 | tf_op jit(solution)/shard_map/all_to_all | solution.py:65
  283.2 2.9 fusion.278
  292.0 3.7 collective-permute-done.34
  295.7 2.8 collective-permute-done.36
  301.2 2.8 fusion.6
  304.0 3.6 fusion.12
  314.8 2.8 collective-permute-start.37
  320.3 9.6 %all_to_all.49 = bf16[8,16,1024]{2,1,0:T(8,128)(2,1)S(1)} all-to-all(bf16[8,16,1024]{2,1,0:T(8,128)(2,1)S(1)} %bitcast.506), channel_id=1, replica_groups=mesh['req'=8,'kv'=4] {'req'}, dimensions={0} | all-to-all | bytes 524288 | tf_op jit(solution)/shard_map/all_to_all | solution.py:65
  330.8 3.1 fusion.193
  339.0 3.3 collective-permute-done.41
  342.3 2.3 collective-permute-done.43
  354.1 9.8 %all_gather.7 = bf16[128,2048]{1,0:T(8,128)(2,1)S(1)} all-gather(bf16[16,2048]{1,0:T(8,128)(2,1)S(1)} %multiply_convert_fusion), channel_id=1, replica_groups=mesh['req'=8,'kv'=4] {'req'}, dimensions={0}, use_global_device_ids=true | all-gather | bytes 589824 | tf_op jit(solution)/shard_map/all_gather | solution.py:234
  363.9 7.8 %fusion.288 = f32[128,3696]{0,1:T(8,128)S(1)} fusion(bf16[128,2048]{1,0:T(8,128)(2,1)S(1)} %all_gather.7, bf16[2048,3696]{0,1:T(8,128)(2,1)} %param.48), kind=kOutput, calls=%fused_computation.410 | convolution fusion | flops 1937768448 | bytes 17555456 | tf_op jit(solution)/shard_map/dot_general | solution.py:240
  371.7 4.3 fusion.287
  378.2 5.3 %copy.149 = f32[128,7392]{1,0:T(8,128)} copy(f32[128,7392]{0,1:T(8,128)} %pad_maximum_fusion.1) | data formatting | bytes 7569408
  383.5 70.6 %reduce-scatter.9.cloned.1.call-done = f32[32,7392]{1,0:T(8,128)} async-done(((f32[128,7392]{1,0:T(8,128)}), f32[32,7392]{1,0:T(8,128)}) %reduce-scatter.9.cloned.1.call-update) | async-done | bytes 946192 | tf_op jit(solution)/shard_map/reduce_scatter | solution.py:236
  459.1 8.3 %collective-permute-done.48 = bf16[32,3696]{1,0:T(8,128)(2,1)S(1)} collective-permute-done((bf16[32,3696]{1,0:T(8,128)(2,1)S(1)}, bf16[32,3696]{1,0:T(8,128)(2,1)S(1)}, u32[]{:S(2)}, u32[]{:S(2)}) %collective-permute-start.48) | collective-permute-done | bytes 236576 | tf_op jit(solution)/shard_map/ppermute | solution.py:52
  467.4 8.8 %collective-permute-done.47 = bf16[32,3696]{1,0:T(8,128)(2,1)S(1)} collective-permute-done((bf16[32,3696]{1,0:T(8,128)(2,1)S(1)}, bf16[32,3696]{1,0:T(8,128)(2,1)S(1)}, u32[]{:S(2)}, u32[]{:S(2)}) %collective-permute-start.47) | collective-permute-done | bytes 236576 | tf_op jit(solution)/shard_map/ppermute | solution.py:52
  479.4 7.8 %fusion.2 = f32[4,2,16,2048]{3,2,0,1:T(8,128)S(1)} fusion(bf16[3696,2048]{1,0:T(8,128)(2,1)} %param.49, bf16[4,2,16,3696]{3,2,1,0:T(8,128)(2,1)S(1)} %bitcast.501), kind=kOutput, calls=%fused_computation.8 | convolution fusion | flops 1937768448 | bytes 17133568 | tf_op jit(solution)/shard_map/dot_general | solution.py:253
  492.9 2.8 collective-permute-done.51
  495.7 3.0 collective-permute-done.53
  (279 shorter events, 130.5 us)
Async XLA Ops:
  7.6 9.6 %collective-permute-start.2 = (f32[16]{0:T(128)S(1)}, f32[16]{0:T(128)S(1)}, u32[]{:S(2)}, u32[]{:S(2)}) collective-permute-start(f32[16]{0:T(128)S(1)} %fusion.205), channel_id=1, source_target_pairs={{0,3},{1,0},{2,1},{3,2},{4,7},{5,4},{6,5},{7,6},{8,11},{9,8},{10,9... | collective-permute-start | bytes 200 | tf_op jit(solution)/shard_map/ppermute | solution.py:90
  8.1 9.1 %collective-permute-start.1 = (f32[16]{0:T(128)S(1)}, f32[16]{0:T(128)S(1)}, u32[]{:S(2)}, u32[]{:S(2)}) collective-permute-start(f32[16]{0:T(128)S(1)} %fusion.205), channel_id=1, source_target_pairs={{0,2},{1,3},{2,0},{3,1},{4,6},{5,7},{6,4},{7,5},{8,10},{9,11},{10,... | collective-permute-start | bytes 200 | tf_op jit(solution)/shard_map/ppermute | solution.py:90
  11.6 5.6 %collective-permute-start = (f32[16]{0:T(128)S(1)}, f32[16]{0:T(128)S(1)}, u32[]{:S(2)}, u32[]{:S(2)}) collective-permute-start(f32[16]{0:T(128)S(1)} %fusion.205), channel_id=1, source_target_pairs={{0,1},{1,2},{2,3},{3,0},{4,5},{5,6},{6,7},{7,4},{8,9},{9,10},{10,1... | collective-permute-start | bytes 200 | tf_op jit(solution)/shard_map/ppermute | solution.py:90
  18.1 5.4 %collective-permute-start.4 = (bf16[16,2048]{1,0:T(8,128)(2,1)S(1)}, bf16[16,2048]{1,0:T(8,128)(2,1)S(1)}, u32[]{:S(2)}, u32[]{:S(2)}) collective-permute-start(bf16[16,2048]{1,0:T(8,128)(2,1)S(1)} %fusion.207), channel_id=1, source_target_pairs={{0,2},{1,3},{2,0},{3,1},{4,6},{5,7},{6,4},{7,5},{8,10},{9,11},{10,... | collective-permute-start | bytes 196616 | tf_op jit(solution)/shard_map/ppermute | solution.py:52
  19.2 5.5 %collective-permute-start.3 = (bf16[16,2048]{1,0:T(8,128)(2,1)S(1)}, bf16[16,2048]{1,0:T(8,128)(2,1)S(1)}, u32[]{:S(2)}, u32[]{:S(2)}) collective-permute-start(bf16[16,2048]{1,0:T(8,128)(2,1)S(1)} %fusion.207), channel_id=1, source_target_pairs={{0,3},{1,0},{2,1},{3,2},{4,7},{5,4},{6,5},{7,6},{8,11},{9,8},{10,9... | collective-permute-start | bytes 196616 | tf_op jit(solution)/shard_map/ppermute | solution.py:52
  21.1 5.5 %collective-permute-start.5 = (bf16[16,2048]{1,0:T(8,128)(2,1)S(1)}, bf16[16,2048]{1,0:T(8,128)(2,1)S(1)}, u32[]{:S(2)}, u32[]{:S(2)}) collective-permute-start(bf16[16,2048]{1,0:T(8,128)(2,1)S(1)} %fusion.207), channel_id=1, source_target_pairs={{0,1},{1,2},{2,3},{3,0},{4,5},{5,6},{6,7},{7,4},{8,9},{9,10},{10,1... | collective-permute-start | bytes 196616 | tf_op jit(solution)/shard_map/ppermute | solution.py:52
  27.7 9.7 %all-to-all-start = ((bf16[8,16,1024]{2,1,0:T(8,128)(2,1)}), bf16[8,16,1024]{2,1,0:T(8,128)(2,1)S(1)}, u32[]{:S(2)}, u32[]{:S(2)}) async-start(bf16[8,16,1024]{2,1,0:T(8,128)(2,1)} %bitcast.7), calls=%async_computation | async-start | bytes 524288 | tf_op jit(solution)/shard_map/all_to_all | solution.py:65
  45.6 7.1 %collective-permute-start.7 = (f32[16,2560]{1,0:T(8,128)S(1)}, f32[16,2560]{1,0:T(8,128)S(1)}, u32[]{:S(2)}, u32[]{:S(2)}) collective-permute-start(f32[16,2560]{1,0:T(8,128)S(1)} %get-tuple-element.78), channel_id=1, source_target_pairs={{0,8},{4,12},{8,16},{12,20},{16,24},{20,28},{24,0},{28,4},{1,9},{5... | collective-permute-start | bytes 491528 | tf_op jit(solution)/shard_map/ppermute | solution.py:42
  47.0 8.4 %collective-permute-start.9 = (f32[16,2560]{1,0:T(8,128)S(1)}, f32[16,2560]{1,0:T(8,128)S(1)}, u32[]{:S(2)}, u32[]{:S(2)}) collective-permute-start(f32[16,2560]{1,0:T(8,128)S(1)} %get-tuple-element.79), channel_id=1, source_target_pairs={{0,24},{4,28},{8,0},{12,4},{16,8},{20,12},{24,16},{28,20},{1,25},{... | collective-permute-start | bytes 491528 | tf_op jit(solution)/shard_map/ppermute | solution.py:42
  47.6 9.2 %collective-permute-start.8 = (f32[16,2560]{1,0:T(8,128)S(1)}, f32[16,2560]{1,0:T(8,128)S(1)}, u32[]{:S(2)}, u32[]{:S(2)}) collective-permute-start(f32[16,2560]{1,0:T(8,128)S(1)} %get-tuple-element.80), channel_id=1, source_target_pairs={{0,16},{4,20},{8,24},{12,28},{16,0},{20,4},{24,8},{28,12},{1,17},{... | collective-permute-start | bytes 491528 | tf_op jit(solution)/shard_map/ppermute | solution.py:42
  68.2 6.5 %collective-permute-start.12 = (bf16[16,2048]{1,0:T(8,128)(2,1)S(1)}, bf16[16,2048]{1,0:T(8,128)(2,1)S(1)}, u32[]{:S(2)}, u32[]{:S(2)}) collective-permute-start(bf16[16,2048]{1,0:T(8,128)(2,1)S(1)} %bitcast.527), channel_id=1, source_target_pairs={{0,1},{1,2},{2,3},{3,0},{4,5},{5,6},{6,7},{7,4},{8,9},{9,10},{10,1... | collective-permute-start | bytes 196616 | tf_op jit(solution)/shard_map/ppermute | solution.py:52
  69.5 5.9 %collective-permute-start.11 = (bf16[16,2048]{1,0:T(8,128)(2,1)S(1)}, bf16[16,2048]{1,0:T(8,128)(2,1)S(1)}, u32[]{:S(2)}, u32[]{:S(2)}) collective-permute-start(bf16[16,2048]{1,0:T(8,128)(2,1)S(1)} %bitcast.528), channel_id=1, source_target_pairs={{0,2},{1,3},{2,0},{3,1},{4,6},{5,7},{6,4},{7,5},{8,10},{9,11},{10,... | collective-permute-start | bytes 196616 | tf_op jit(solution)/shard_map/ppermute | solution.py:52
  71.8 5.0 collective-permute-start.10
  77.9 10.9 %all-to-all-start.1 = ((bf16[8,16,1024]{2,1,0:T(8,128)(2,1)}), bf16[8,16,1024]{2,1,0:T(8,128)(2,1)S(1)}, u32[]{:S(2)}, u32[]{:S(2)}) async-start(bf16[8,16,1024]{2,1,0:T(8,128)(2,1)} %bitcast.41), calls=%async_computation.1 | async-start | bytes 524288 | tf_op jit(solution)/shard_map/all_to_all | solution.py:65
  83.3 129.5 %reduce-scatter.7.cloned.1.call-start = ((), (), s32[]{:S(2)}) async-start(), calls=%async_computation.6 | async-start | bytes 4751360 | tf_op jit(solution)/shard_map/reduce_scatter | solution.py:236
  94.9 6.3 %collective-permute-start.14 = (f32[16,2048]{1,0:T(8,128)S(1)}, f32[16,2048]{1,0:T(8,128)S(1)}, u32[]{:S(2)}, u32[]{:S(2)}) collective-permute-start(f32[16,2048]{1,0:T(8,128)S(1)} %get-tuple-element.90), channel_id=1, source_target_pairs={{0,8},{4,12},{8,16},{12,20},{16,24},{20,28},{24,0},{28,4},{1,9},{5... | collective-permute-start | bytes 393224 | tf_op jit(solution)/shard_map/ppermute | solution.py:42
  96.4 7.0 %collective-permute-start.16 = (f32[16,2048]{1,0:T(8,128)S(1)}, f32[16,2048]{1,0:T(8,128)S(1)}, u32[]{:S(2)}, u32[]{:S(2)}) collective-permute-start(f32[16,2048]{1,0:T(8,128)S(1)} %get-tuple-element.91), channel_id=1, source_target_pairs={{0,24},{4,28},{8,0},{12,4},{16,8},{20,12},{24,16},{28,20},{1,25},{... | collective-permute-start | bytes 393224 | tf_op jit(solution)/shard_map/ppermute | solution.py:42
  97.0 7.8 %collective-permute-start.15 = (f32[16,2048]{1,0:T(8,128)S(1)}, f32[16,2048]{1,0:T(8,128)S(1)}, u32[]{:S(2)}, u32[]{:S(2)}) collective-permute-start(f32[16,2048]{1,0:T(8,128)S(1)} %get-tuple-element.92), channel_id=1, source_target_pairs={{0,16},{4,20},{8,24},{12,28},{16,0},{20,4},{24,8},{28,12},{1,17},{... | collective-permute-start | bytes 393224 | tf_op jit(solution)/shard_map/ppermute | solution.py:42
  104.9 4.3 collective-permute-start.19
  107.1 4.4 collective-permute-start.18
  141.8 312.3 %reduce-scatter.9.cloned.1.call-start = ((), (), s32[]{:S(2)}) async-start(), calls=%async_computation.7 | async-start | bytes 4751360 | tf_op jit(solution)/shard_map/reduce_scatter | solution.py:236
  214.1 11.9 %collective-permute-start.21 = (bf16[32,3696]{1,0:T(8,128)(2,1)S(1)}, bf16[32,3696]{1,0:T(8,128)(2,1)S(1)}, u32[]{:S(2)}, u32[]{:S(2)}) collective-permute-start(bf16[32,3696]{1,0:T(8,128)(2,1)S(1)} %fusion.164), channel_id=1, source_target_pairs={{0,2},{1,3},{2,0},{3,1},{4,6},{5,7},{6,4},{7,5},{8,10},{9,11},{10,... | collective-permute-start | bytes 709640 | tf_op jit(solution)/shard_map/ppermute | solution.py:52
  214.3 20.5 %collective-permute-start.20 = (bf16[32,3696]{1,0:T(8,128)(2,1)S(1)}, bf16[32,3696]{1,0:T(8,128)(2,1)S(1)}, u32[]{:S(2)}, u32[]{:S(2)}) collective-permute-start(bf16[32,3696]{1,0:T(8,128)(2,1)S(1)} %fusion.164), channel_id=1, source_target_pairs={{0,3},{1,0},{2,1},{3,2},{4,7},{5,4},{6,5},{7,6},{8,11},{9,8},{10,9... | collective-permute-start | bytes 709640 | tf_op jit(solution)/shard_map/ppermute | solution.py:52
  216.1 20.8 %collective-permute-start.22 = (bf16[32,3696]{1,0:T(8,128)(2,1)S(1)}, bf16[32,3696]{1,0:T(8,128)(2,1)S(1)}, u32[]{:S(2)}, u32[]{:S(2)}) collective-permute-start(bf16[32,3696]{1,0:T(8,128)(2,1)S(1)} %fusion.164), channel_id=1, source_target_pairs={{0,1},{1,2},{2,3},{3,0},{4,5},{5,6},{6,7},{7,4},{8,9},{9,10},{10,1... | collective-permute-start | bytes 709640 | tf_op jit(solution)/shard_map/ppermute | solution.py:52
  247.9 6.4 %collective-permute-start.24 = (f32[16,2048]{1,0:T(8,128)S(1)}, f32[16,2048]{1,0:T(8,128)S(1)}, u32[]{:S(2)}, u32[]{:S(2)}) collective-permute-start(f32[16,2048]{1,0:T(8,128)S(1)} %get-tuple-element.87), channel_id=1, source_target_pairs={{0,8},{4,12},{8,16},{12,20},{16,24},{20,28},{24,0},{28,4},{1,9},{5... | collective-permute-start | bytes 393224 | tf_op jit(solution)/shard_map/ppermute | solution.py:42
  249.5 7.9 %collective-permute-start.26 = (f32[16,2048]{1,0:T(8,128)S(1)}, f32[16,2048]{1,0:T(8,128)S(1)}, u32[]{:S(2)}, u32[]{:S(2)}) collective-permute-start(f32[16,2048]{1,0:T(8,128)S(1)} %get-tuple-element.88), channel_id=1, source_target_pairs={{0,24},{4,28},{8,0},{12,4},{16,8},{20,12},{24,16},{28,20},{1,25},{... | collective-permute-start | bytes 393224 | tf_op jit(solution)/shard_map/ppermute | solution.py:42
  250.0 7.8 %collective-permute-start.25 = (f32[16,2048]{1,0:T(8,128)S(1)}, f32[16,2048]{1,0:T(8,128)S(1)}, u32[]{:S(2)}, u32[]{:S(2)}) collective-permute-start(f32[16,2048]{1,0:T(8,128)S(1)} %get-tuple-element.89), channel_id=1, source_target_pairs={{0,16},{4,20},{8,24},{12,28},{16,0},{20,4},{24,8},{28,12},{1,17},{... | collective-permute-start | bytes 393224 | tf_op jit(solution)/shard_map/ppermute | solution.py:42
  258.4 4.4 collective-permute-start.28
  258.5 4.6 collective-permute-start.27
  263.1 6.0 %collective-permute-start.31 = (bf16[16,2048]{1,0:T(8,128)(2,1)S(1)}, bf16[16,2048]{1,0:T(8,128)(2,1)S(1)}, u32[]{:S(2)}, u32[]{:S(2)}) collective-permute-start(bf16[16,2048]{1,0:T(8,128)(2,1)S(1)} %multiply_convert_fusion.1), channel_id=1, source_target_pairs={{0,2},{1,3},{2,0},{3,1},{4,6},{5,7},{6,4},{7,5},{8,10},{9,11},{10,... | collective-permute-start | bytes 196616 | tf_op jit(solution)/shard_map/ppermute | solution.py:52
  266.9 5.0 collective-permute-start.32
  288.6 7.1 %collective-permute-start.34 = (f32[16,2560]{1,0:T(8,128)S(1)}, f32[16,2560]{1,0:T(8,128)S(1)}, u32[]{:S(2)}, u32[]{:S(2)}) collective-permute-start(f32[16,2560]{1,0:T(8,128)S(1)} %get-tuple-element.75), channel_id=1, source_target_pairs={{0,8},{4,12},{8,16},{12,20},{16,24},{20,28},{24,0},{28,4},{1,9},{5... | collective-permute-start | bytes 491528 | tf_op jit(solution)/shard_map/ppermute | solution.py:42
  290.1 8.4 %collective-permute-start.36 = (f32[16,2560]{1,0:T(8,128)S(1)}, f32[16,2560]{1,0:T(8,128)S(1)}, u32[]{:S(2)}, u32[]{:S(2)}) collective-permute-start(f32[16,2560]{1,0:T(8,128)S(1)} %get-tuple-element.76), channel_id=1, source_target_pairs={{0,24},{4,28},{8,0},{12,4},{16,8},{20,12},{24,16},{28,20},{1,25},{... | collective-permute-start | bytes 491528 | tf_op jit(solution)/shard_map/ppermute | solution.py:42
  290.9 9.2 %collective-permute-start.35 = (f32[16,2560]{1,0:T(8,128)S(1)}, f32[16,2560]{1,0:T(8,128)S(1)}, u32[]{:S(2)}, u32[]{:S(2)}) collective-permute-start(f32[16,2560]{1,0:T(8,128)S(1)} %get-tuple-element.77), channel_id=1, source_target_pairs={{0,16},{4,20},{8,24},{12,28},{16,0},{20,4},{24,8},{28,12},{1,17},{... | collective-permute-start | bytes 491528 | tf_op jit(solution)/shard_map/ppermute | solution.py:42
  311.5 6.2 %collective-permute-start.39 = (bf16[16,2048]{1,0:T(8,128)(2,1)S(1)}, bf16[16,2048]{1,0:T(8,128)(2,1)S(1)}, u32[]{:S(2)}, u32[]{:S(2)}) collective-permute-start(bf16[16,2048]{1,0:T(8,128)(2,1)S(1)} %bitcast.530), channel_id=1, source_target_pairs={{0,1},{1,2},{2,3},{3,0},{4,5},{5,6},{6,7},{7,4},{8,9},{9,10},{10,1... | collective-permute-start | bytes 196616 | tf_op jit(solution)/shard_map/ppermute | solution.py:52
  313.2 5.8 %collective-permute-start.38 = (bf16[16,2048]{1,0:T(8,128)(2,1)S(1)}, bf16[16,2048]{1,0:T(8,128)(2,1)S(1)}, u32[]{:S(2)}, u32[]{:S(2)}) collective-permute-start(bf16[16,2048]{1,0:T(8,128)(2,1)S(1)} %bitcast.531), channel_id=1, source_target_pairs={{0,2},{1,3},{2,0},{3,1},{4,6},{5,7},{6,4},{7,5},{8,10},{9,11},{10,... | collective-permute-start | bytes 196616 | tf_op jit(solution)/shard_map/ppermute | solution.py:52
  314.8 5.1 collective-permute-start.37
  336.0 6.3 %collective-permute-start.41 = (f32[16,2048]{1,0:T(8,128)S(1)}, f32[16,2048]{1,0:T(8,128)S(1)}, u32[]{:S(2)}, u32[]{:S(2)}) collective-permute-start(f32[16,2048]{1,0:T(8,128)S(1)} %get-tuple-element.84), channel_id=1, source_target_pairs={{0,8},{4,12},{8,16},{12,20},{16,24},{20,28},{24,0},{28,4},{1,9},{5... | collective-permute-start | bytes 393224 | tf_op jit(solution)/shard_map/ppermute | solution.py:42
  337.5 7.0 %collective-permute-start.43 = (f32[16,2048]{1,0:T(8,128)S(1)}, f32[16,2048]{1,0:T(8,128)S(1)}, u32[]{:S(2)}, u32[]{:S(2)}) collective-permute-start(f32[16,2048]{1,0:T(8,128)S(1)} %get-tuple-element.85), channel_id=1, source_target_pairs={{0,24},{4,28},{8,0},{12,4},{16,8},{20,12},{24,16},{28,20},{1,25},{... | collective-permute-start | bytes 393224 | tf_op jit(solution)/shard_map/ppermute | solution.py:42
  338.1 7.8 %collective-permute-start.42 = (f32[16,2048]{1,0:T(8,128)S(1)}, f32[16,2048]{1,0:T(8,128)S(1)}, u32[]{:S(2)}, u32[]{:S(2)}) collective-permute-start(f32[16,2048]{1,0:T(8,128)S(1)} %get-tuple-element.86), channel_id=1, source_target_pairs={{0,16},{4,20},{8,24},{12,28},{16,0},{20,4},{24,8},{28,12},{1,17},{... | collective-permute-start | bytes 393224 | tf_op jit(solution)/shard_map/ppermute | solution.py:42
  346.1 4.4 collective-permute-start.46
  348.3 4.4 collective-permute-start.45
  455.4 11.9 %collective-permute-start.48 = (bf16[32,3696]{1,0:T(8,128)(2,1)S(1)}, bf16[32,3696]{1,0:T(8,128)(2,1)S(1)}, u32[]{:S(2)}, u32[]{:S(2)}) collective-permute-start(bf16[32,3696]{1,0:T(8,128)(2,1)S(1)} %fusion.163), channel_id=1, source_target_pairs={{0,2},{1,3},{2,0},{3,1},{4,6},{5,7},{6,4},{7,5},{8,10},{9,11},{10,... | collective-permute-start | bytes 709640 | tf_op jit(solution)/shard_map/ppermute | solution.py:52
  455.7 20.5 %collective-permute-start.47 = (bf16[32,3696]{1,0:T(8,128)(2,1)S(1)}, bf16[32,3696]{1,0:T(8,128)(2,1)S(1)}, u32[]{:S(2)}, u32[]{:S(2)}) collective-permute-start(bf16[32,3696]{1,0:T(8,128)(2,1)S(1)} %fusion.163), channel_id=1, source_target_pairs={{0,3},{1,0},{2,1},{3,2},{4,7},{5,4},{6,5},{7,6},{8,11},{9,8},{10,9... | collective-permute-start | bytes 709640 | tf_op jit(solution)/shard_map/ppermute | solution.py:52
  457.4 20.8 %collective-permute-start.49 = (bf16[32,3696]{1,0:T(8,128)(2,1)S(1)}, bf16[32,3696]{1,0:T(8,128)(2,1)S(1)}, u32[]{:S(2)}, u32[]{:S(2)}) collective-permute-start(bf16[32,3696]{1,0:T(8,128)(2,1)S(1)} %fusion.163), channel_id=1, source_target_pairs={{0,1},{1,2},{2,3},{3,0},{4,5},{5,6},{6,7},{7,4},{8,9},{9,10},{10,1... | collective-permute-start | bytes 709640 | tf_op jit(solution)/shard_map/ppermute | solution.py:52
  489.3 6.4 %collective-permute-start.51 = (f32[16,2048]{1,0:T(8,128)S(1)}, f32[16,2048]{1,0:T(8,128)S(1)}, u32[]{:S(2)}, u32[]{:S(2)}) collective-permute-start(f32[16,2048]{1,0:T(8,128)S(1)} %get-tuple-element.81), channel_id=1, source_target_pairs={{0,8},{4,12},{8,16},{12,20},{16,24},{20,28},{24,0},{28,4},{1,9},{5... | collective-permute-start | bytes 393224 | tf_op jit(solution)/shard_map/ppermute | solution.py:42
  490.9 7.9 %collective-permute-start.53 = (f32[16,2048]{1,0:T(8,128)S(1)}, f32[16,2048]{1,0:T(8,128)S(1)}, u32[]{:S(2)}, u32[]{:S(2)}) collective-permute-start(f32[16,2048]{1,0:T(8,128)S(1)} %get-tuple-element.82), channel_id=1, source_target_pairs={{0,24},{4,28},{8,0},{12,4},{16,8},{20,12},{24,16},{28,20},{1,25},{... | collective-permute-start | bytes 393224 | tf_op jit(solution)/shard_map/ppermute | solution.py:42
  491.4 7.8 %collective-permute-start.52 = (f32[16,2048]{1,0:T(8,128)S(1)}, f32[16,2048]{1,0:T(8,128)S(1)}, u32[]{:S(2)}, u32[]{:S(2)}) collective-permute-start(f32[16,2048]{1,0:T(8,128)S(1)} %get-tuple-element.83), channel_id=1, source_target_pairs={{0,16},{4,20},{8,24},{12,28},{16,0},{20,4},{24,8},{28,12},{1,17},{... | collective-permute-start | bytes 393224 | tf_op jit(solution)/shard_map/ppermute | solution.py:42
  (31 other events, 369.0 us)
Sparse Core Ops, SparseCore 0:
  141.9 70.7 reduce-scatter.6
  383.6 70.4 reduce-scatter.8

commit v9 on v8

--- a/solution.py
+++ b/solution.py
@@ -233,25 +233,29 @@
         normed_mlp = normalize(residual, mlp_gain)
         tokens = lax.all_gather(normed_mlp, "req", axis=0, tiled=True)
         hidden_cols = w_gate.shape[1]
-        gate_up = lax.psum_scatter(
-            jnp.concatenate(
-                [
-                    jnp.dot(tokens, w_gate, preferred_element_type=jnp.float32),
-                    jnp.dot(tokens, w_up, preferred_element_type=jnp.float32),
-                ],
-                axis=1,
-            ),
-            "kv",
-            scatter_dimension=0,
-            tiled=True,
-        )
-        local_hidden = (jax.nn.silu(gate_up[:, :hidden_cols]) * gate_up[:, hidden_cols:]).astype(
-            jnp.bfloat16
-        )
-        hidden_all = gather_by_permute(local_hidden, "kv").reshape(-1, local_hidden.shape[1])
-        residual = residual + scatter_sum(
-            jnp.dot(hidden_all, w_down, preferred_element_type=jnp.float32), "req"
-        )
+        split = hidden_cols // 2 // 128 * 128
+        down_sum = None
+        for first, last in ((0, split), (split, hidden_cols)):
+            width = last - first
+            gate_up = lax.psum_scatter(
+                jnp.concatenate(
+                    [
+                        jnp.dot(tokens, w_gate[:, first:last], preferred_element_type=jnp.float32),
+                        jnp.dot(tokens, w_up[:, first:last], preferred_element_type=jnp.float32),
+                    ],
+                    axis=1,
+                ),
+                "kv",
+                scatter_dimension=0,
+                tiled=True,
+            )
+            local_hidden = (jax.nn.silu(gate_up[:, :width]) * gate_up[:, width:]).astype(
+                jnp.bfloat16
+            )
+            hidden_all = gather_by_permute(local_hidden, "kv").reshape(-1, width)
+            part = jnp.dot(hidden_all, w_down[first:last], preferred_element_type=jnp.float32)
+            down_sum = part if down_sum is None else down_sum + part
+        residual = residual + scatter_sum(down_sum, "req")
     return residual
 
 

time: 516 us -> 578 us (1.12)
  waiting for transfers between devices: 264 us -> 289 us
  matrix products: 71.4 us -> 93.8 us
  starting transfers between devices: 71.4 us -> 81.8 us
    reduce_scatter x2, waiting for transfers between devices: 141 us -> 49.4 us  [body(): lax.psum_scatter(jnp.concatenate([jnp.dot(tokens, w_gate[:, first:last],...]
    unnamed x2 -> x6, waiting for transfers between devices: 0.03 us -> 80.4 us
    ppermute x18 -> x24, waiting for transfers between devices: 49.4 us -> 86.6 us  [gather_by_permute(): lax.ppermute(block, axis, [(j, (j + shift) % count) for j in range(count)])]
    dot_general x6 -> x12, matrix products: 39.6 us -> 62.3 us  [the longest x4 22.5 us: body(): jnp.dot(tokens, w_gate[:, first:last], preferred_element_type=jnp.float32)]
    ppermute x18 -> x24, starting transfers between devices: 26.6 us -> 33.5 us  [gather_by_permute(): lax.ppermute(block, axis, [(j, (j + shift) % count) for j in range(count)])]
  transfers between devices with their start and end apart: 58 -> 66, of which waited for: 51 -> 50; matrix products, arithmetic and copies ran while one was open for 2% -> 9% of each run, Pallas kernels for 0% -> 0%
where the time goes in v9:
time: 578 us; the launch traced here: 567 us
  waiting for transfers between devices  289 us (50%)
  matrix products  93.8 us (16%)
  starting transfers between devices  81.8 us (14%)
  blocking collectives  38.1 us (7%)
  other arithmetic  33 us (6%)
  local copies, waits for them, and re-layouts  16.4 us (3%)
  between operations  14.6 us (3%)
    ppermute x24, waiting for transfers between devices, gather_by_permute(): lax.ppermute(block, axis, [(j, (j + shift) % count) for j in range(count)])  86.6 us
    unnamed x6, waiting for transfers between devices  80.4 us
    reduce_scatter x2, waiting for transfers between devices, body(): lax.psum_scatter(jnp.concatenate([jnp.dot(tokens, w_gate[:, first:last],...  49.4 us
    ppermute x18, waiting for transfers between devices, scatter_sum(): total = total + lax.ppermute(piece, axis, pairs)  41.2 us
    ppermute x24, starting transfers between devices, gather_by_permute(): lax.ppermute(block, axis, [(j, (j + shift) % count) for j in range(count)])  33.5 us
    dot_general x4, matrix products, body(): jnp.dot(tokens, w_gate[:, first:last], preferred_element_type=jnp.float32)  22.5 us
    dot_general x4, matrix products, body(): jnp.dot(tokens, w_up[:, first:last], preferred_element_type=jnp.float32)  22.1 us
    ppermute x18, starting transfers between devices, scatter_sum(): total = total + lax.ppermute(piece, axis, pairs)  19.5 us
  transfers between devices with their start and end apart: 66, of which 50 were waited for; matrix products, arithmetic and copies ran while one was open for 9% of the time, Pallas kernels for 0%

profile of v9, /device:TPU:18, one launch (start us, length us, event | category | flops | bytes accessed | tf_op | source)
XLA Modules:
  0.0 566.7 jit_solution(4934046730959471802)
XLA Ops:
  8.1 3.5 collective-permute-start.1
  27.7 4.3 all-to-all-start
  33.2 4.2 all-to-all-done
  38.9 2.9 fusion.318
  52.6 2.8 collective-permute-done.9
  57.9 2.8 fusion.24
  60.8 3.6 fusion.28
  71.8 2.8 collective-permute-start.10
  77.9 5.4 all-to-all-start.1
  83.5 5.3 all-to-all-done.1
  89.6 3.0 fusion.236
  97.8 3.3 collective-permute-done.14
  112.5 9.6 %all_gather.6 = bf16[128,2048]{1,0:T(8,128)(2,1)S(1)} all-gather(bf16[16,2048]{1,0:T(8,128)(2,1)S(1)} %multiply_convert_fusion.4), channel_id=1, replica_groups=mesh['req'=8,'kv'=4] {'req'}, dimensions={0}, use_global_device_ids=true | all-gather | bytes 589824 | tf_op jit(solution)/shard_map/all_gather | solution.py:234
  122.1 5.6 fusion.18
  127.7 5.6 fusion.22
  134.9 5.4 fusion.6
  140.3 5.7 %fusion.10 = f32[128,1904]{0,1:T(8,128)S(1)} fusion(bf16[128,2048]{1,0:T(8,128)(2,1)S(1)} %all_gather.6, bf16[2048,3696]{0,1:T(8,128)(2,1)} %param.49), kind=kOutput, calls=%fused_computation.28 | convolution fusion | flops 998244352 | bytes 9297920 | tf_op jit(solution)/shard_map/dot_general | solution.py:243
  148.6 24.8 %reduce-scatter.9.cloned.1.call-done = f32[32,3584]{1,0:T(8,128)} async-done(((f32[128,3584]{1,0:T(8,128)}), f32[32,3584]{1,0:T(8,128)}) %reduce-scatter.9.cloned.1.call-update) | async-done | bytes 458768 | tf_op jit(solution)/shard_map/reduce_scatter | solution.py:240
  180.3 39.9 %reduce-scatter.13.cloned.1.call-done = f32[32,3808]{1,0:T(8,128)} async-done(((f32[128,3808]{1,0:T(8,128)}), f32[32,3808]{1,0:T(8,128)}) %reduce-scatter.13.cloned.1.call-update) | async-done | bytes 487440
  228.4 29.1 %collective-permute-done.25 = bf16[32,1904]{0,1:T(8,128)(2,1)S(1)} collective-permute-done((bf16[32,1904]{0,1:T(8,128)(2,1)S(1)}, bf16[32,1904]{0,1:T(8,128)(2,1)S(1)}, u32[]{:S(2)}, u32[]{:S(2)}) %collective-permute-start.25) | collective-permute-done | bytes 121888 | tf_op jit(solution)/shard_map/ppermute | solution.py:52
  257.9 7.8 %collective-permute-done.23 = bf16[32,1904]{0,1:T(8,128)(2,1)S(1)} collective-permute-done((bf16[32,1904]{0,1:T(8,128)(2,1)S(1)}, bf16[32,1904]{0,1:T(8,128)(2,1)S(1)}, u32[]{:S(2)}, u32[]{:S(2)}) %collective-permute-start.23) | collective-permute-done | bytes 121888 | tf_op jit(solution)/shard_map/ppermute | solution.py:52
  266.6 4.5 fusion.2
  271.2 4.2 fusion.36
  281.2 2.8 collective-permute-done.27
  284.0 3.0 collective-permute-done.29
  290.1 2.9 collective-permute-start.31
  303.7 9.5 %all_to_all.48 = bf16[8,16,1024]{2,1,0:T(8,128)(2,1)S(1)} all-to-all(bf16[8,16,1024]{2,1,0:T(8,128)(2,1)S(1)} %bitcast.525), channel_id=1, replica_groups=mesh['req'=8,'kv'=4] {'req'}, dimensions={0} | all-to-all | bytes 524288 | tf_op jit(solution)/shard_map/all_to_all | solution.py:65
  314.7 2.9 fusion.321
  323.7 3.5 collective-permute-done.37
  327.2 2.8 collective-permute-done.39
  332.9 2.8 fusion.26
  335.7 3.6 fusion.32
  346.4 2.8 collective-permute-start.40
  351.9 9.4 %all_to_all.49 = bf16[8,16,1024]{2,1,0:T(8,128)(2,1)S(1)} all-to-all(bf16[8,16,1024]{2,1,0:T(8,128)(2,1)S(1)} %bitcast.526), channel_id=1, replica_groups=mesh['req'=8,'kv'=4] {'req'}, dimensions={0} | all-to-all | bytes 524288 | tf_op jit(solution)/shard_map/all_to_all | solution.py:65
  362.1 2.9 fusion.234
  370.2 3.3 collective-permute-done.44
  385.5 9.7 %all_gather.7 = bf16[128,2048]{1,0:T(8,128)(2,1)S(1)} all-gather(bf16[16,2048]{1,0:T(8,128)(2,1)S(1)} %multiply_convert_fusion.2), channel_id=1, replica_groups=mesh['req'=8,'kv'=4] {'req'}, dimensions={0}, use_global_device_ids=true | all-gather | bytes 589824 | tf_op jit(solution)/shard_map/all_gather | solution.py:234
  395.2 5.6 fusion.16
  400.9 5.6 fusion.20
  408.0 5.4 fusion.4
  413.5 5.5 fusion.8
  421.5 24.6 %reduce-scatter.11.cloned.1.call-done = f32[32,3584]{1,0:T(8,128)} async-done(((f32[128,3584]{1,0:T(8,128)}), f32[32,3584]{1,0:T(8,128)}) %reduce-scatter.11.cloned.1.call-update) | async-done | bytes 458768 | tf_op jit(solution)/shard_map/reduce_scatter | solution.py:240
  451.8 40.4 %reduce-scatter.15.cloned.1.call-done = f32[32,3808]{1,0:T(8,128)} async-done(((f32[128,3808]{1,0:T(8,128)}), f32[32,3808]{1,0:T(8,128)}) %reduce-scatter.15.cloned.1.call-update) | async-done | bytes 487440
  498.4 30.8 %collective-permute-done.55 = bf16[32,1904]{0,1:T(8,128)(2,1)S(1)} collective-permute-done((bf16[32,1904]{0,1:T(8,128)(2,1)S(1)}, bf16[32,1904]{0,1:T(8,128)(2,1)S(1)}, u32[]{:S(2)}, u32[]{:S(2)}) %collective-permute-start.55) | collective-permute-done | bytes 121888 | tf_op jit(solution)/shard_map/ppermute | solution.py:52
  529.7 7.8 %collective-permute-done.53 = bf16[32,1904]{0,1:T(8,128)(2,1)S(1)} collective-permute-done((bf16[32,1904]{0,1:T(8,128)(2,1)S(1)}, bf16[32,1904]{0,1:T(8,128)(2,1)S(1)}, u32[]{:S(2)}, u32[]{:S(2)}) %collective-permute-start.53) | collective-permute-done | bytes 121888 | tf_op jit(solution)/shard_map/ppermute | solution.py:52
  538.3 4.5 fusion
  542.9 4.3 fusion.39
  555.8 3.0 collective-permute-done.59
  (305 shorter events, 165.8 us)
Async XLA Ops:
  7.6 9.6 %collective-permute-start.2 = (f32[16]{0:T(128)S(1)}, f32[16]{0:T(128)S(1)}, u32[]{:S(2)}, u32[]{:S(2)}) collective-permute-start(f32[16]{0:T(128)S(1)} %fusion.248), channel_id=1, source_target_pairs={{0,3},{1,0},{2,1},{3,2},{4,7},{5,4},{6,5},{7,6},{8,11},{9,8},{10,9... | collective-permute-start | bytes 200 | tf_op jit(solution)/shard_map/ppermute | solution.py:90
  8.1 9.1 %collective-permute-start.1 = (f32[16]{0:T(128)S(1)}, f32[16]{0:T(128)S(1)}, u32[]{:S(2)}, u32[]{:S(2)}) collective-permute-start(f32[16]{0:T(128)S(1)} %fusion.248), channel_id=1, source_target_pairs={{0,2},{1,3},{2,0},{3,1},{4,6},{5,7},{6,4},{7,5},{8,10},{9,11},{10,... | collective-permute-start | bytes 200 | tf_op jit(solution)/shard_map/ppermute | solution.py:90
  11.6 5.6 collective-permute-start
  18.1 5.4 collective-permute-start.4
  19.2 5.5 collective-permute-start.3
  21.1 5.5 collective-permute-start.5
  27.7 9.7 %all-to-all-start = ((bf16[8,16,1024]{2,1,0:T(8,128)(2,1)}), bf16[8,16,1024]{2,1,0:T(8,128)(2,1)S(1)}, u32[]{:S(2)}, u32[]{:S(2)}) async-start(bf16[8,16,1024]{2,1,0:T(8,128)(2,1)} %bitcast.7), calls=%async_computation | async-start | bytes 524288 | tf_op jit(solution)/shard_map/all_to_all | solution.py:65
  45.5 7.1 %collective-permute-start.7 = (f32[16,2560]{1,0:T(8,128)S(1)}, f32[16,2560]{1,0:T(8,128)S(1)}, u32[]{:S(2)}, u32[]{:S(2)}) collective-permute-start(f32[16,2560]{1,0:T(8,128)S(1)} %get-tuple-element.79), channel_id=1, source_target_pairs={{0,8},{4,12},{8,16},{12,20},{16,24},{20,28},{24,0},{28,4},{1,9},{5... | collective-permute-start | bytes 491528 | tf_op jit(solution)/shard_map/ppermute | solution.py:42
  47.0 8.4 %collective-permute-start.9 = (f32[16,2560]{1,0:T(8,128)S(1)}, f32[16,2560]{1,0:T(8,128)S(1)}, u32[]{:S(2)}, u32[]{:S(2)}) collective-permute-start(f32[16,2560]{1,0:T(8,128)S(1)} %get-tuple-element.80), channel_id=1, source_target_pairs={{0,24},{4,28},{8,0},{12,4},{16,8},{20,12},{24,16},{28,20},{1,25},{... | collective-permute-start | bytes 491528 | tf_op jit(solution)/shard_map/ppermute | solution.py:42
  47.6 9.2 %collective-permute-start.8 = (f32[16,2560]{1,0:T(8,128)S(1)}, f32[16,2560]{1,0:T(8,128)S(1)}, u32[]{:S(2)}, u32[]{:S(2)}) collective-permute-start(f32[16,2560]{1,0:T(8,128)S(1)} %get-tuple-element.81), channel_id=1, source_target_pairs={{0,16},{4,20},{8,24},{12,28},{16,0},{20,4},{24,8},{28,12},{1,17},{... | collective-permute-start | bytes 491528 | tf_op jit(solution)/shard_map/ppermute | solution.py:42
  68.2 6.5 %collective-permute-start.12 = (bf16[16,2048]{1,0:T(8,128)(2,1)S(1)}, bf16[16,2048]{1,0:T(8,128)(2,1)S(1)}, u32[]{:S(2)}, u32[]{:S(2)}) collective-permute-start(bf16[16,2048]{1,0:T(8,128)(2,1)S(1)} %bitcast.558), channel_id=1, source_target_pairs={{0,1},{1,2},{2,3},{3,0},{4,5},{5,6},{6,7},{7,4},{8,9},{9,10},{10,1... | collective-permute-start | bytes 196616 | tf_op jit(solution)/shard_map/ppermute | solution.py:52
  69.4 5.9 %collective-permute-start.11 = (bf16[16,2048]{1,0:T(8,128)(2,1)S(1)}, bf16[16,2048]{1,0:T(8,128)(2,1)S(1)}, u32[]{:S(2)}, u32[]{:S(2)}) collective-permute-start(bf16[16,2048]{1,0:T(8,128)(2,1)S(1)} %bitcast.559), channel_id=1, source_target_pairs={{0,2},{1,3},{2,0},{3,1},{4,6},{5,7},{6,4},{7,5},{8,10},{9,11},{10,... | collective-permute-start | bytes 196616 | tf_op jit(solution)/shard_map/ppermute | solution.py:52
  77.9 10.9 %all-to-all-start.1 = ((bf16[8,16,1024]{2,1,0:T(8,128)(2,1)}), bf16[8,16,1024]{2,1,0:T(8,128)(2,1)S(1)}, u32[]{:S(2)}, u32[]{:S(2)}) async-start(bf16[8,16,1024]{2,1,0:T(8,128)(2,1)} %bitcast.41), calls=%async_computation.1 | async-start | bytes 524288 | tf_op jit(solution)/shard_map/all_to_all | solution.py:65
  83.3 90.1 %reduce-scatter.9.cloned.1.call-start = ((), (), s32[]{:S(2)}) async-start(), calls=%async_computation.8 | async-start | bytes 2293760 | tf_op jit(solution)/shard_map/reduce_scatter | solution.py:240
  94.8 6.3 %collective-permute-start.14 = (f32[16,2048]{1,0:T(8,128)S(1)}, f32[16,2048]{1,0:T(8,128)S(1)}, u32[]{:S(2)}, u32[]{:S(2)}) collective-permute-start(f32[16,2048]{1,0:T(8,128)S(1)} %get-tuple-element.91), channel_id=1, source_target_pairs={{0,8},{4,12},{8,16},{12,20},{16,24},{20,28},{24,0},{28,4},{1,9},{5... | collective-permute-start | bytes 393224 | tf_op jit(solution)/shard_map/ppermute | solution.py:42
  96.3 7.0 %collective-permute-start.16 = (f32[16,2048]{1,0:T(8,128)S(1)}, f32[16,2048]{1,0:T(8,128)S(1)}, u32[]{:S(2)}, u32[]{:S(2)}) collective-permute-start(f32[16,2048]{1,0:T(8,128)S(1)} %get-tuple-element.92), channel_id=1, source_target_pairs={{0,24},{4,28},{8,0},{12,4},{16,8},{20,12},{24,16},{28,20},{1,25},{... | collective-permute-start | bytes 393224 | tf_op jit(solution)/shard_map/ppermute | solution.py:42
  96.8 7.8 %collective-permute-start.15 = (f32[16,2048]{1,0:T(8,128)S(1)}, f32[16,2048]{1,0:T(8,128)S(1)}, u32[]{:S(2)}, u32[]{:S(2)}) collective-permute-start(f32[16,2048]{1,0:T(8,128)S(1)} %get-tuple-element.93), channel_id=1, source_target_pairs={{0,16},{4,20},{8,24},{12,28},{16,0},{20,4},{24,8},{28,12},{1,17},{... | collective-permute-start | bytes 393224 | tf_op jit(solution)/shard_map/ppermute | solution.py:42
  134.8 85.4 %reduce-scatter.13.cloned.1.call-start = ((), (), s32[]{:S(2)}) async-start(), calls=%async_computation.10 | async-start | bytes 2457600
  148.5 297.6 %reduce-scatter.11.cloned.1.call-start = ((), (), s32[]{:S(2)}) async-start(), calls=%async_computation.9 | async-start | bytes 2293760 | tf_op jit(solution)/shard_map/reduce_scatter | solution.py:240
  175.1 49.5 %collective-permute-start.21 = (bf16[32,1792]{1,0:T(8,128)(2,1)}, bf16[32,1792]{1,0:T(8,128)(2,1)}, u32[]{:S(2)}, u32[]{:S(2)}) collective-permute-start(bf16[32,1792]{1,0:T(8,128)(2,1)} %fusion.241), channel_id=1, source_target_pairs={{0,2},{1,3},{2,0},{3,1},{4,6},{5,7},{6,4},{7,5},{8,10},{9,11},{10,... | collective-permute-start | bytes 344072 | tf_op jit(solution)/shard_map/ppermute | solution.py:52
  176.5 49.2 %collective-permute-start.20 = (bf16[32,1792]{1,0:T(8,128)(2,1)}, bf16[32,1792]{1,0:T(8,128)(2,1)}, u32[]{:S(2)}, u32[]{:S(2)}) collective-permute-start(bf16[32,1792]{1,0:T(8,128)(2,1)} %fusion.241), channel_id=1, source_target_pairs={{0,3},{1,0},{2,1},{3,2},{4,7},{5,4},{6,5},{7,6},{8,11},{9,8},{10,9... | collective-permute-start | bytes 344072 | tf_op jit(solution)/shard_map/ppermute | solution.py:52
  177.1 48.6 %collective-permute-start.22 = (bf16[32,1792]{1,0:T(8,128)(2,1)}, bf16[32,1792]{1,0:T(8,128)(2,1)}, u32[]{:S(2)}, u32[]{:S(2)}) collective-permute-start(bf16[32,1792]{1,0:T(8,128)(2,1)} %fusion.241), channel_id=1, source_target_pairs={{0,1},{1,2},{2,3},{3,0},{4,5},{5,6},{6,7},{7,4},{8,9},{9,10},{10,1... | collective-permute-start | bytes 344072 | tf_op jit(solution)/shard_map/ppermute | solution.py:52
  222.4 35.1 %collective-permute-start.25 = (bf16[32,1904]{0,1:T(8,128)(2,1)S(1)}, bf16[32,1904]{0,1:T(8,128)(2,1)S(1)}, u32[]{:S(2)}, u32[]{:S(2)}) collective-permute-start(bf16[32,1904]{0,1:T(8,128)(2,1)S(1)} %multiply_convert_fusion.1), channel_id=1, source_target_pairs={{0,1},{1,2},{2,3},{3,0},{4,5},{5,6},{6,7},{7,4},{8,9},{9,10},{10,1... | collective-permute-start | bytes 365576 | tf_op jit(solution)/shard_map/ppermute | solution.py:52
  223.2 34.5 %collective-permute-start.24 = (bf16[32,1904]{0,1:T(8,128)(2,1)S(1)}, bf16[32,1904]{0,1:T(8,128)(2,1)S(1)}, u32[]{:S(2)}, u32[]{:S(2)}) collective-permute-start(bf16[32,1904]{0,1:T(8,128)(2,1)S(1)} %multiply_convert_fusion.1), channel_id=1, source_target_pairs={{0,2},{1,3},{2,0},{3,1},{4,6},{5,7},{6,4},{7,5},{8,10},{9,11},{10,... | collective-permute-start | bytes 365576 | tf_op jit(solution)/shard_map/ppermute | solution.py:52
  224.6 41.2 %collective-permute-start.23 = (bf16[32,1904]{0,1:T(8,128)(2,1)S(1)}, bf16[32,1904]{0,1:T(8,128)(2,1)S(1)}, u32[]{:S(2)}, u32[]{:S(2)}) collective-permute-start(bf16[32,1904]{0,1:T(8,128)(2,1)S(1)} %multiply_convert_fusion.1), channel_id=1, source_target_pairs={{0,3},{1,0},{2,1},{3,2},{4,7},{5,4},{6,5},{7,6},{8,11},{9,8},{10,9... | collective-permute-start | bytes 365576 | tf_op jit(solution)/shard_map/ppermute | solution.py:52
  277.6 6.4 %collective-permute-start.27 = (f32[16,2048]{1,0:T(8,128)S(1)}, f32[16,2048]{1,0:T(8,128)S(1)}, u32[]{:S(2)}, u32[]{:S(2)}) collective-permute-start(f32[16,2048]{1,0:T(8,128)S(1)} %get-tuple-element.88), channel_id=1, source_target_pairs={{0,8},{4,12},{8,16},{12,20},{16,24},{20,28},{24,0},{28,4},{1,9},{5... | collective-permute-start | bytes 393224 | tf_op jit(solution)/shard_map/ppermute | solution.py:42
  279.1 7.9 %collective-permute-start.29 = (f32[16,2048]{1,0:T(8,128)S(1)}, f32[16,2048]{1,0:T(8,128)S(1)}, u32[]{:S(2)}, u32[]{:S(2)}) collective-permute-start(f32[16,2048]{1,0:T(8,128)S(1)} %get-tuple-element.89), channel_id=1, source_target_pairs={{0,24},{4,28},{8,0},{12,4},{16,8},{20,12},{24,16},{28,20},{1,25},{... | collective-permute-start | bytes 393224 | tf_op jit(solution)/shard_map/ppermute | solution.py:42
  279.7 7.8 %collective-permute-start.28 = (f32[16,2048]{1,0:T(8,128)S(1)}, f32[16,2048]{1,0:T(8,128)S(1)}, u32[]{:S(2)}, u32[]{:S(2)}) collective-permute-start(f32[16,2048]{1,0:T(8,128)S(1)} %get-tuple-element.90), channel_id=1, source_target_pairs={{0,16},{4,20},{8,24},{12,28},{16,0},{20,4},{24,8},{28,12},{1,17},{... | collective-permute-start | bytes 393224 | tf_op jit(solution)/shard_map/ppermute | solution.py:42
  287.6 5.5 collective-permute-start.32
  296.7 5.2 collective-permute-start.34
  320.1 7.1 %collective-permute-start.37 = (f32[16,2560]{1,0:T(8,128)S(1)}, f32[16,2560]{1,0:T(8,128)S(1)}, u32[]{:S(2)}, u32[]{:S(2)}) collective-permute-start(f32[16,2560]{1,0:T(8,128)S(1)} %get-tuple-element.76), channel_id=1, source_target_pairs={{0,8},{4,12},{8,16},{12,20},{16,24},{20,28},{24,0},{28,4},{1,9},{5... | collective-permute-start | bytes 491528 | tf_op jit(solution)/shard_map/ppermute | solution.py:42
  321.6 8.4 %collective-permute-start.39 = (f32[16,2560]{1,0:T(8,128)S(1)}, f32[16,2560]{1,0:T(8,128)S(1)}, u32[]{:S(2)}, u32[]{:S(2)}) collective-permute-start(f32[16,2560]{1,0:T(8,128)S(1)} %get-tuple-element.77), channel_id=1, source_target_pairs={{0,24},{4,28},{8,0},{12,4},{16,8},{20,12},{24,16},{28,20},{1,25},{... | collective-permute-start | bytes 491528 | tf_op jit(solution)/shard_map/ppermute | solution.py:42
  322.6 9.2 %collective-permute-start.38 = (f32[16,2560]{1,0:T(8,128)S(1)}, f32[16,2560]{1,0:T(8,128)S(1)}, u32[]{:S(2)}, u32[]{:S(2)}) collective-permute-start(f32[16,2560]{1,0:T(8,128)S(1)} %get-tuple-element.78), channel_id=1, source_target_pairs={{0,16},{4,20},{8,24},{12,28},{16,0},{20,4},{24,8},{28,12},{1,17},{... | collective-permute-start | bytes 491528 | tf_op jit(solution)/shard_map/ppermute | solution.py:42
  343.2 6.1 %collective-permute-start.42 = (bf16[16,2048]{1,0:T(8,128)(2,1)S(1)}, bf16[16,2048]{1,0:T(8,128)(2,1)S(1)}, u32[]{:S(2)}, u32[]{:S(2)}) collective-permute-start(bf16[16,2048]{1,0:T(8,128)(2,1)S(1)} %bitcast.561), channel_id=1, source_target_pairs={{0,1},{1,2},{2,3},{3,0},{4,5},{5,6},{6,7},{7,4},{8,9},{9,10},{10,1... | collective-permute-start | bytes 196616 | tf_op jit(solution)/shard_map/ppermute | solution.py:52
  344.7 5.7 %collective-permute-start.41 = (bf16[16,2048]{1,0:T(8,128)(2,1)S(1)}, bf16[16,2048]{1,0:T(8,128)(2,1)S(1)}, u32[]{:S(2)}, u32[]{:S(2)}) collective-permute-start(bf16[16,2048]{1,0:T(8,128)(2,1)S(1)} %bitcast.562), channel_id=1, source_target_pairs={{0,2},{1,3},{2,0},{3,1},{4,6},{5,7},{6,4},{7,5},{8,10},{9,11},{10,... | collective-permute-start | bytes 196616 | tf_op jit(solution)/shard_map/ppermute | solution.py:52
  367.2 6.3 %collective-permute-start.44 = (f32[16,2048]{1,0:T(8,128)S(1)}, f32[16,2048]{1,0:T(8,128)S(1)}, u32[]{:S(2)}, u32[]{:S(2)}) collective-permute-start(f32[16,2048]{1,0:T(8,128)S(1)} %get-tuple-element.85), channel_id=1, source_target_pairs={{0,8},{4,12},{8,16},{12,20},{16,24},{20,28},{24,0},{28,4},{1,9},{5... | collective-permute-start | bytes 393224 | tf_op jit(solution)/shard_map/ppermute | solution.py:42
  368.7 7.0 %collective-permute-start.46 = (f32[16,2048]{1,0:T(8,128)S(1)}, f32[16,2048]{1,0:T(8,128)S(1)}, u32[]{:S(2)}, u32[]{:S(2)}) collective-permute-start(f32[16,2048]{1,0:T(8,128)S(1)} %get-tuple-element.86), channel_id=1, source_target_pairs={{0,24},{4,28},{8,0},{12,4},{16,8},{20,12},{24,16},{28,20},{1,25},{... | collective-permute-start | bytes 393224 | tf_op jit(solution)/shard_map/ppermute | solution.py:42
  369.3 7.8 %collective-permute-start.45 = (f32[16,2048]{1,0:T(8,128)S(1)}, f32[16,2048]{1,0:T(8,128)S(1)}, u32[]{:S(2)}, u32[]{:S(2)}) collective-permute-start(f32[16,2048]{1,0:T(8,128)S(1)} %get-tuple-element.87), channel_id=1, source_target_pairs={{0,16},{4,20},{8,24},{12,28},{16,0},{20,4},{24,8},{28,12},{1,17},{... | collective-permute-start | bytes 393224 | tf_op jit(solution)/shard_map/ppermute | solution.py:42
  408.0 84.2 %reduce-scatter.15.cloned.1.call-start = ((), (), s32[]{:S(2)}) async-start(), calls=%async_computation.11 | async-start | bytes 2457600
  447.2 49.1 %collective-permute-start.51 = (bf16[32,1792]{1,0:T(8,128)(2,1)S(1)}, bf16[32,1792]{1,0:T(8,128)(2,1)S(1)}, u32[]{:S(2)}, u32[]{:S(2)}) collective-permute-start(bf16[32,1792]{1,0:T(8,128)(2,1)S(1)} %fusion.240), channel_id=1, source_target_pairs={{0,2},{1,3},{2,0},{3,1},{4,6},{5,7},{6,4},{7,5},{8,10},{9,11},{10,... | collective-permute-start | bytes 344072 | tf_op jit(solution)/shard_map/ppermute | solution.py:52
  448.6 49.0 %collective-permute-start.50 = (bf16[32,1792]{1,0:T(8,128)(2,1)S(1)}, bf16[32,1792]{1,0:T(8,128)(2,1)S(1)}, u32[]{:S(2)}, u32[]{:S(2)}) collective-permute-start(bf16[32,1792]{1,0:T(8,128)(2,1)S(1)} %fusion.240), channel_id=1, source_target_pairs={{0,3},{1,0},{2,1},{3,2},{4,7},{5,4},{6,5},{7,6},{8,11},{9,8},{10,9... | collective-permute-start | bytes 344072 | tf_op jit(solution)/shard_map/ppermute | solution.py:52
  449.2 48.4 %collective-permute-start.52 = (bf16[32,1792]{1,0:T(8,128)(2,1)S(1)}, bf16[32,1792]{1,0:T(8,128)(2,1)S(1)}, u32[]{:S(2)}, u32[]{:S(2)}) collective-permute-start(bf16[32,1792]{1,0:T(8,128)(2,1)S(1)} %fusion.240), channel_id=1, source_target_pairs={{0,1},{1,2},{2,3},{3,0},{4,5},{5,6},{6,7},{7,4},{8,9},{9,10},{10,1... | collective-permute-start | bytes 344072 | tf_op jit(solution)/shard_map/ppermute | solution.py:52
  494.3 34.9 %collective-permute-start.55 = (bf16[32,1904]{0,1:T(8,128)(2,1)S(1)}, bf16[32,1904]{0,1:T(8,128)(2,1)S(1)}, u32[]{:S(2)}, u32[]{:S(2)}) collective-permute-start(bf16[32,1904]{0,1:T(8,128)(2,1)S(1)} %multiply_convert_fusion), channel_id=1, source_target_pairs={{0,1},{1,2},{2,3},{3,0},{4,5},{5,6},{6,7},{7,4},{8,9},{9,10},{10,1... | collective-permute-start | bytes 365576 | tf_op jit(solution)/shard_map/ppermute | solution.py:52
  494.9 34.5 %collective-permute-start.54 = (bf16[32,1904]{0,1:T(8,128)(2,1)S(1)}, bf16[32,1904]{0,1:T(8,128)(2,1)S(1)}, u32[]{:S(2)}, u32[]{:S(2)}) collective-permute-start(bf16[32,1904]{0,1:T(8,128)(2,1)S(1)} %multiply_convert_fusion), channel_id=1, source_target_pairs={{0,2},{1,3},{2,0},{3,1},{4,6},{5,7},{6,4},{7,5},{8,10},{9,11},{10,... | collective-permute-start | bytes 365576 | tf_op jit(solution)/shard_map/ppermute | solution.py:52
  496.3 41.2 %collective-permute-start.53 = (bf16[32,1904]{0,1:T(8,128)(2,1)S(1)}, bf16[32,1904]{0,1:T(8,128)(2,1)S(1)}, u32[]{:S(2)}, u32[]{:S(2)}) collective-permute-start(bf16[32,1904]{0,1:T(8,128)(2,1)S(1)} %multiply_convert_fusion), channel_id=1, source_target_pairs={{0,3},{1,0},{2,1},{3,2},{4,7},{5,4},{6,5},{7,6},{8,11},{9,8},{10,9... | collective-permute-start | bytes 365576 | tf_op jit(solution)/shard_map/ppermute | solution.py:52
  549.4 6.4 %collective-permute-start.57 = (f32[16,2048]{1,0:T(8,128)S(1)}, f32[16,2048]{1,0:T(8,128)S(1)}, u32[]{:S(2)}, u32[]{:S(2)}) collective-permute-start(f32[16,2048]{1,0:T(8,128)S(1)} %get-tuple-element.82), channel_id=1, source_target_pairs={{0,8},{4,12},{8,16},{12,20},{16,24},{20,28},{24,0},{28,4},{1,9},{5... | collective-permute-start | bytes 393224 | tf_op jit(solution)/shard_map/ppermute | solution.py:42
  550.9 7.9 %collective-permute-start.59 = (f32[16,2048]{1,0:T(8,128)S(1)}, f32[16,2048]{1,0:T(8,128)S(1)}, u32[]{:S(2)}, u32[]{:S(2)}) collective-permute-start(f32[16,2048]{1,0:T(8,128)S(1)} %get-tuple-element.83), channel_id=1, source_target_pairs={{0,24},{4,28},{8,0},{12,4},{16,8},{20,12},{24,16},{28,20},{1,25},{... | collective-permute-start | bytes 393224 | tf_op jit(solution)/shard_map/ppermute | solution.py:42
  551.4 7.8 %collective-permute-start.58 = (f32[16,2048]{1,0:T(8,128)S(1)}, f32[16,2048]{1,0:T(8,128)S(1)}, u32[]{:S(2)}, u32[]{:S(2)}) collective-permute-start(f32[16,2048]{1,0:T(8,128)S(1)} %get-tuple-element.84), channel_id=1, source_target_pairs={{0,16},{4,20},{8,24},{12,28},{16,0},{20,4},{24,8},{28,12},{1,17},{... | collective-permute-start | bytes 393224 | tf_op jit(solution)/shard_map/ppermute | solution.py:42
  (31 other events, 223.3 us)
Sparse Core Ops, SparseCore 0:
  134.9 38.3 reduce-scatter.8
  175.7 44.4 reduce-scatter.12
  408.1 37.9 reduce-scatter.10
  448.2 43.8 reduce-scatter.14

commit v10 on v8

--- a/solution.py
+++ b/solution.py
@@ -53,6 +53,19 @@
         )
     stacked = jnp.stack(pieces[:1] + pieces[1:][::-1])
     return jnp.roll(stacked, index, axis=0)
+
+
+def normed_rows_for_weights(residual, full_gain):
+    req_size = lax.axis_size("req")
+    kv_size = lax.axis_size("kv")
+    rows = residual.shape[0]
+    wide = gather_by_permute(residual, "kv").transpose(1, 0, 2).reshape(rows, -1)
+    square_sum = jnp.sum(wide * wide, axis=1)
+    inv_norm = lax.rsqrt(square_sum / MODEL_WIDTH + EPS)
+    normed = (wide * inv_norm[:, None] * full_gain.astype(jnp.float32)[None, :]).astype(
+        jnp.bfloat16
+    )
+    return lax.all_to_all(normed, "req", 1, 0, tiled=True)
 
 
 def rows_for_weights(block):
@@ -183,9 +196,9 @@
     )
     my_slots = lax.dynamic_slice_in_dim(request_serving_order, req_index * own_rows, own_rows)
     residual = hidden.astype(jnp.float32)
+    full_attn_gain = lax.all_gather(attn_gain, "kv", axis=0, tiled=True)
     for current_layer_index in range(LAYER_COUNT):
-        normed = normalize(residual, attn_gain)
-        columns = rows_for_weights(normed)
+        columns = normed_rows_for_weights(residual, full_attn_gain)
         picked = jnp.take(columns, request_serving_order, axis=0)
         combined = (
             scatter_sum(

time: 516 us -> 517 us (level)
  blocking collectives: 38.4 us -> 51.9 us
  starting transfers between devices: 71.4 us -> 58.8 us
    all_gather x0 -> x1, blocking collectives: none -> 13.5 us  [body(): full_attn_gain = lax.all_gather(attn_gain, 'kv', axis=0, tiled=True)]
    all_to_all x2 -> x1, blocking collectives: 19.1 us -> 9.27 us  [rows_for_weights(): return lax.all_to_all(wide, 'req', 0, 0, tiled=True)]
    all_to_all x0 -> x1, blocking collectives: none -> 9.77 us  [normed_rows_for_weights(): return lax.all_to_all(normed, 'req', 1, 0, tiled=True)]
    ppermute x18, starting transfers between devices: 26.6 us -> 19.6 us  [gather_by_permute(): lax.ppermute(block, axis, [(j, (j + shift) % count) for j in range(count)])]
    ppermute x12 -> x6, starting transfers between devices: 14.8 us -> 9.62 us  [normalize(): lax.ppermute(square_sum, 'kv', [(j, (j + shift) % count) for j in range(c...]
  transfers between devices with their start and end apart: 58 -> 52, of which waited for: 51 -> 43; matrix products, arithmetic and copies ran while one was open for 2% -> 2% of each run, Pallas kernels for 0% -> 0%
where the time goes in v10:
time: 517 us; the launch traced here: 508 us
  waiting for transfers between devices  265 us (51%)
  matrix products  71.5 us (14%)
  starting transfers between devices  58.8 us (11%)
  blocking collectives  51.9 us (10%)
  other arithmetic  26 us (5%)
  local copies, waits for them, and re-layouts  19.3 us (4%)
  between operations  15.1 us (3%)
    reduce_scatter x2, waiting for transfers between devices, body(): lax.psum_scatter(jnp.concatenate([jnp.dot(tokens, w_gate, preferred_eleme...  141 us
    ppermute x18, waiting for transfers between devices, gather_by_permute(): lax.ppermute(block, axis, [(j, (j + shift) % count) for j in range(count)])  53.4 us
    ppermute x18, waiting for transfers between devices, scatter_sum(): total = total + lax.ppermute(piece, axis, pairs)  42.6 us
    ppermute x18, starting transfers between devices, gather_by_permute(): lax.ppermute(block, axis, [(j, (j + shift) % count) for j in range(count)])  19.6 us
    all_gather x2, blocking collectives, body(): tokens = lax.all_gather(normed_mlp, 'req', axis=0, tiled=True)  19.3 us
    ppermute x18, starting transfers between devices, scatter_sum(): total = total + lax.ppermute(piece, axis, pairs)  19.3 us
    dot_general x2, matrix products, body(): jnp.dot(tokens, w_up, preferred_element_type=jnp.float32)  15.5 us
    dot_general x2, matrix products, body(): jnp.dot(hidden_all, w_down, preferred_element_type=jnp.float32)  15.5 us
  transfers between devices with their start and end apart: 52, of which 43 were waited for; matrix products, arithmetic and copies ran while one was open for 2% of the time, Pallas kernels for 0%

profile of v10, /device:TPU:18, one launch (start us, length us, event | category | flops | bytes accessed | tf_op | source)
XLA Modules:
  0.0 507.8 jit_solution(5081601457860830878)
XLA Ops:
  7.9 2.7 collective-permute-start
  14.1 13.5 %all_gather.9 = bf16[8192]{0:T(1024)(128)(2,1)S(1)} all-gather(bf16[2048]{0:T(1024)(128)(2,1)} %param.40), channel_id=1, replica_groups=mesh['req'=8,'kv'=4] {'kv'}, dimensions={0}, use_global_device_ids=true | all-gather | bytes 20480 | tf_op jit(solution)/shard_map/all_gather | solution.py:199
  31.0 4.3 all-to-all-start
  35.9 4.9 all-to-all-done
  42.2 2.9 fusion.275
  52.0 4.0 collective-permute-done.4
  56.0 2.8 collective-permute-done.6
  61.2 2.8 fusion.4
  64.1 3.6 fusion.8
  71.5 2.5 collective-permute-start.9
  80.4 5.1 %all-to-all-start.1 = ((bf16[8,16,1024]{2,1,0:T(8,128)(2,1)}), bf16[8,16,1024]{2,1,0:T(8,128)(2,1)S(1)}, u32[]{:S(2)}, u32[]{:S(2)}) async-start(bf16[8,16,1024]{2,1,0:T(8,128)(2,1)} %bitcast.42), calls=%async_computation.1 | async-start | bytes 524288 | tf_op jit(solution)/shard_map/all_to_all | solution.py:78
  86.0 5.0 all-to-all-done.1
  91.9 3.1 fusion.197
  100.2 3.3 collective-permute-done.11
  109.6 2.7 collective-permute-start.15
  115.9 9.5 %all_gather.10 = bf16[128,2048]{1,0:T(8,128)(2,1)S(1)} all-gather(bf16[16,2048]{1,0:T(8,128)(2,1)S(1)} %multiply_convert_fusion.3), channel_id=1, replica_groups=mesh['req'=8,'kv'=4] {'req'}, dimensions={0}, use_global_device_ids=true | all-gather | bytes 589824 | tf_op jit(solution)/shard_map/all_gather | solution.py:247
  125.4 7.8 %fusion.286 = f32[128,3696]{0,1:T(8,128)S(1)} fusion(bf16[128,2048]{1,0:T(8,128)(2,1)S(1)} %all_gather.10, bf16[2048,3696]{0,1:T(8,128)(2,1)} %param.50), kind=kOutput, calls=%fused_computation.404 | convolution fusion | flops 1937768448 | bytes 17555456 | tf_op jit(solution)/shard_map/dot_general | solution.py:253
  133.3 4.3 fusion.285
  139.7 5.3 %copy.167 = f32[128,7392]{1,0:T(8,128)} copy(f32[128,7392]{0,1:T(8,128)} %pad_maximum_fusion) | data formatting | bytes 7569408
  145.1 70.4 %reduce-scatter.7.cloned.1.call-done = f32[32,7392]{1,0:T(8,128)} async-done(((f32[128,7392]{1,0:T(8,128)}), f32[32,7392]{1,0:T(8,128)}) %reduce-scatter.7.cloned.1.call-update) | async-done | bytes 946192 | tf_op jit(solution)/shard_map/reduce_scatter | solution.py:249
  220.6 8.2 %collective-permute-done.18 = bf16[32,3696]{1,0:T(8,128)(2,1)S(1)} collective-permute-done((bf16[32,3696]{1,0:T(8,128)(2,1)S(1)}, bf16[32,3696]{1,0:T(8,128)(2,1)S(1)}, u32[]{:S(2)}, u32[]{:S(2)}) %collective-permute-start.18) | collective-permute-done | bytes 236576 | tf_op jit(solution)/shard_map/ppermute | solution.py:52
  228.8 8.8 %collective-permute-done.17 = bf16[32,3696]{1,0:T(8,128)(2,1)S(1)} collective-permute-done((bf16[32,3696]{1,0:T(8,128)(2,1)S(1)}, bf16[32,3696]{1,0:T(8,128)(2,1)S(1)}, u32[]{:S(2)}, u32[]{:S(2)}) %collective-permute-start.17) | collective-permute-done | bytes 236576 | tf_op jit(solution)/shard_map/ppermute | solution.py:52
  240.8 7.7 %fusion = f32[4,2,16,2048]{3,2,1,0:T(8,128)S(1)} fusion(bf16[4,2,16,3696]{3,2,1,0:T(8,128)(2,1)S(1)} %bitcast.508, bf16[3696,2048]{1,0:T(8,128)(2,1)} %param.51), kind=kOutput, calls=%fused_computation.6 | convolution fusion | flops 1937768448 | bytes 17133568 | tf_op jit(solution)/shard_map/dot_general | solution.py:266
  254.2 2.9 collective-permute-done.21
  257.1 3.0 collective-permute-done.23
  262.7 9.2 %collective-permute-done.26 = f32[16,2048]{1,0:T(8,128)S(1)} collective-permute-done((f32[16,2048]{1,0:T(8,128)S(1)}, f32[16,2048]{1,0:T(8,128)S(1)}, u32[]{:S(2)}, u32[]{:S(2)}) %collective-permute-start.26) | collective-permute-done | bytes 131104 | tf_op jit(solution)/shard_map/ppermute | solution.py:52
  273.2 9.8 %all_to_all.56 = bf16[16,8,1024]{2,0,1:T(8,128)(2,1)S(1)} all-to-all(bf16[16,8,1024]{2,0,1:T(8,128)(2,1)S(1)} %copy.145), channel_id=1, replica_groups=mesh['req'=8,'kv'=4] {'req'}, dimensions={1} | all-to-all | bytes 524288 | tf_op jit(solution)/shard_map/all_to_all | solution.py:68
  284.4 2.9 fusion.278
  293.2 3.7 collective-permute-done.28
  296.9 2.8 collective-permute-done.30
  302.4 2.8 fusion.6
  305.3 3.6 fusion.12
  312.7 2.9 collective-permute-start.33
  317.5 3.3 collective-permute-done.32
  321.1 9.3 %all_to_all.57 = bf16[8,16,1024]{2,1,0:T(8,128)(2,1)S(1)} all-to-all(bf16[8,16,1024]{2,1,0:T(8,128)(2,1)S(1)} %bitcast.512), channel_id=1, replica_groups=mesh['req'=8,'kv'=4] {'req'}, dimensions={0} | all-to-all | bytes 524288 | tf_op jit(solution)/shard_map/all_to_all | solution.py:78
  331.3 3.1 fusion.195
  339.5 3.3 collective-permute-done.35
  348.6 2.5 collective-permute-start.39
  354.8 9.8 %all_gather.11 = bf16[128,2048]{1,0:T(8,128)(2,1)S(1)} all-gather(bf16[16,2048]{1,0:T(8,128)(2,1)S(1)} %multiply_convert_fusion.2), channel_id=1, replica_groups=mesh['req'=8,'kv'=4] {'req'}, dimensions={0}, use_global_device_ids=true | all-gather | bytes 589824 | tf_op jit(solution)/shard_map/all_gather | solution.py:247
  364.6 7.8 %fusion.288 = f32[128,3696]{0,1:T(8,128)S(1)} fusion(bf16[128,2048]{1,0:T(8,128)(2,1)S(1)} %all_gather.11, bf16[2048,3696]{0,1:T(8,128)(2,1)} %param.50), kind=kOutput, calls=%fused_computation.406 | convolution fusion | flops 1937768448 | bytes 17555456 | tf_op jit(solution)/shard_map/dot_general | solution.py:253
  372.4 4.3 fusion.287
  378.9 5.3 %copy.169 = f32[128,7392]{1,0:T(8,128)} copy(f32[128,7392]{0,1:T(8,128)} %pad_maximum_fusion.1) | data formatting | bytes 7569408
  384.2 70.5 %reduce-scatter.9.cloned.1.call-done = f32[32,7392]{1,0:T(8,128)} async-done(((f32[128,7392]{1,0:T(8,128)}), f32[32,7392]{1,0:T(8,128)}) %reduce-scatter.9.cloned.1.call-update) | async-done | bytes 946192 | tf_op jit(solution)/shard_map/reduce_scatter | solution.py:249
  459.6 8.3 %collective-permute-done.42 = bf16[32,3696]{1,0:T(8,128)(2,1)S(1)} collective-permute-done((bf16[32,3696]{1,0:T(8,128)(2,1)S(1)}, bf16[32,3696]{1,0:T(8,128)(2,1)S(1)}, u32[]{:S(2)}, u32[]{:S(2)}) %collective-permute-start.42) | collective-permute-done | bytes 236576 | tf_op jit(solution)/shard_map/ppermute | solution.py:52
  467.9 8.8 %collective-permute-done.41 = bf16[32,3696]{1,0:T(8,128)(2,1)S(1)} collective-permute-done((bf16[32,3696]{1,0:T(8,128)(2,1)S(1)}, bf16[32,3696]{1,0:T(8,128)(2,1)S(1)}, u32[]{:S(2)}, u32[]{:S(2)}) %collective-permute-start.41) | collective-permute-done | bytes 236576 | tf_op jit(solution)/shard_map/ppermute | solution.py:52
  480.0 7.8 %fusion.2 = f32[4,2,16,2048]{3,2,0,1:T(8,128)S(1)} fusion(bf16[3696,2048]{1,0:T(8,128)(2,1)} %param.51, bf16[4,2,16,3696]{3,2,1,0:T(8,128)(2,1)S(1)} %bitcast.507), kind=kOutput, calls=%fused_computation.8 | convolution fusion | flops 1937768448 | bytes 17133568 | tf_op jit(solution)/shard_map/dot_general | solution.py:266
  493.5 2.8 collective-permute-done.45
  496.3 3.0 collective-permute-done.47
  (268 shorter events, 113.9 us)
Async XLA Ops:
  7.5 21.5 %collective-permute-start.1 = (f32[16,2048]{1,0:T(8,128)S(1)}, f32[16,2048]{1,0:T(8,128)S(1)}, u32[]{:S(2)}, u32[]{:S(2)}) collective-permute-start(f32[16,2048]{1,0:T(8,128)S(1)} %get-tuple-element.105), channel_id=1, source_target_pairs={{0,2},{1,3},{2,0},{3,1},{4,6},{5,7},{6,4},{7,5},{8,10},{9,11},{10,... | collective-permute-start | bytes 393224 | tf_op jit(solution)/shard_map/ppermute | solution.py:52
  7.9 21.1 %collective-permute-start = (f32[16,2048]{1,0:T(8,128)S(1)}, f32[16,2048]{1,0:T(8,128)S(1)}, u32[]{:S(2)}, u32[]{:S(2)}) collective-permute-start(f32[16,2048]{1,0:T(8,128)S(1)} %get-tuple-element.105), channel_id=1, source_target_pairs={{0,3},{1,0},{2,1},{3,2},{4,7},{5,4},{6,5},{7,6},{8,11},{9,8},{10,9... | collective-permute-start | bytes 393224 | tf_op jit(solution)/shard_map/ppermute | solution.py:52
  10.6 18.4 %collective-permute-start.2 = (f32[16,2048]{1,0:T(8,128)S(1)}, f32[16,2048]{1,0:T(8,128)S(1)}, u32[]{:S(2)}, u32[]{:S(2)}) collective-permute-start(f32[16,2048]{1,0:T(8,128)S(1)} %get-tuple-element.105), channel_id=1, source_target_pairs={{0,1},{1,2},{2,3},{3,0},{4,5},{5,6},{6,7},{7,4},{8,9},{9,10},{10,1... | collective-permute-start | bytes 393224 | tf_op jit(solution)/shard_map/ppermute | solution.py:52
  31.0 9.7 %all-to-all-start = ((bf16[16,8,1024]{2,0,1:T(8,128)(2,1)}), bf16[16,8,1024]{2,0,1:T(8,128)(2,1)S(1)}, u32[]{:S(2)}, u32[]{:S(2)}) async-start(bf16[16,8,1024]{2,0,1:T(8,128)(2,1)} %copy.133), calls=%async_computation | async-start | bytes 524288 | tf_op jit(solution)/shard_map/all_to_all | solution.py:68
  45.4 2.3 collective-permute-start.3
  48.9 7.1 %collective-permute-start.4 = (f32[16,2560]{1,0:T(8,128)S(1)}, f32[16,2560]{1,0:T(8,128)S(1)}, u32[]{:S(2)}, u32[]{:S(2)}) collective-permute-start(f32[16,2560]{1,0:T(8,128)S(1)} %get-tuple-element.81), channel_id=1, source_target_pairs={{0,8},{4,12},{8,16},{12,20},{16,24},{20,28},{24,0},{28,4},{1,9},{5... | collective-permute-start | bytes 491528 | tf_op jit(solution)/shard_map/ppermute | solution.py:42
  50.4 8.4 %collective-permute-start.6 = (f32[16,2560]{1,0:T(8,128)S(1)}, f32[16,2560]{1,0:T(8,128)S(1)}, u32[]{:S(2)}, u32[]{:S(2)}) collective-permute-start(f32[16,2560]{1,0:T(8,128)S(1)} %get-tuple-element.82), channel_id=1, source_target_pairs={{0,24},{4,28},{8,0},{12,4},{16,8},{20,12},{24,16},{28,20},{1,25},{... | collective-permute-start | bytes 491528 | tf_op jit(solution)/shard_map/ppermute | solution.py:42
  51.0 9.2 %collective-permute-start.5 = (f32[16,2560]{1,0:T(8,128)S(1)}, f32[16,2560]{1,0:T(8,128)S(1)}, u32[]{:S(2)}, u32[]{:S(2)}) collective-permute-start(f32[16,2560]{1,0:T(8,128)S(1)} %get-tuple-element.83), channel_id=1, source_target_pairs={{0,16},{4,20},{8,24},{12,28},{16,0},{20,4},{24,8},{28,12},{1,17},{... | collective-permute-start | bytes 491528 | tf_op jit(solution)/shard_map/ppermute | solution.py:42
  71.5 6.3 %collective-permute-start.9 = (bf16[16,2048]{1,0:T(8,128)(2,1)S(1)}, bf16[16,2048]{1,0:T(8,128)(2,1)S(1)}, u32[]{:S(2)}, u32[]{:S(2)}) collective-permute-start(bf16[16,2048]{1,0:T(8,128)(2,1)S(1)} %bitcast.533), channel_id=1, source_target_pairs={{0,1},{1,2},{2,3},{3,0},{4,5},{5,6},{6,7},{7,4},{8,9},{9,10},{10,1... | collective-permute-start | bytes 196616 | tf_op jit(solution)/shard_map/ppermute | solution.py:52
  74.0 5.3 %collective-permute-start.8 = (bf16[16,2048]{1,0:T(8,128)(2,1)S(1)}, bf16[16,2048]{1,0:T(8,128)(2,1)S(1)}, u32[]{:S(2)}, u32[]{:S(2)}) collective-permute-start(bf16[16,2048]{1,0:T(8,128)(2,1)S(1)} %bitcast.534), channel_id=1, source_target_pairs={{0,2},{1,3},{2,0},{3,1},{4,6},{5,7},{6,4},{7,5},{8,10},{9,11},{10,... | collective-permute-start | bytes 196616 | tf_op jit(solution)/shard_map/ppermute | solution.py:52
  74.6 4.7 collective-permute-start.7
  80.4 10.6 %all-to-all-start.1 = ((bf16[8,16,1024]{2,1,0:T(8,128)(2,1)}), bf16[8,16,1024]{2,1,0:T(8,128)(2,1)S(1)}, u32[]{:S(2)}, u32[]{:S(2)}) async-start(bf16[8,16,1024]{2,1,0:T(8,128)(2,1)} %bitcast.42), calls=%async_computation.1 | async-start | bytes 524288 | tf_op jit(solution)/shard_map/all_to_all | solution.py:78
  85.5 129.9 %reduce-scatter.7.cloned.1.call-start = ((), (), s32[]{:S(2)}) async-start(), calls=%async_computation.6 | async-start | bytes 4751360 | tf_op jit(solution)/shard_map/reduce_scatter | solution.py:249
  97.2 6.3 %collective-permute-start.11 = (f32[16,2048]{1,0:T(8,128)S(1)}, f32[16,2048]{1,0:T(8,128)S(1)}, u32[]{:S(2)}, u32[]{:S(2)}) collective-permute-start(f32[16,2048]{1,0:T(8,128)S(1)} %get-tuple-element.93), channel_id=1, source_target_pairs={{0,8},{4,12},{8,16},{12,20},{16,24},{20,28},{24,0},{28,4},{1,9},{5... | collective-permute-start | bytes 393224 | tf_op jit(solution)/shard_map/ppermute | solution.py:42
  98.7 7.0 %collective-permute-start.13 = (f32[16,2048]{1,0:T(8,128)S(1)}, f32[16,2048]{1,0:T(8,128)S(1)}, u32[]{:S(2)}, u32[]{:S(2)}) collective-permute-start(f32[16,2048]{1,0:T(8,128)S(1)} %get-tuple-element.94), channel_id=1, source_target_pairs={{0,24},{4,28},{8,0},{12,4},{16,8},{20,12},{24,16},{28,20},{1,25},{... | collective-permute-start | bytes 393224 | tf_op jit(solution)/shard_map/ppermute | solution.py:42
  99.3 7.8 %collective-permute-start.12 = (f32[16,2048]{1,0:T(8,128)S(1)}, f32[16,2048]{1,0:T(8,128)S(1)}, u32[]{:S(2)}, u32[]{:S(2)}) collective-permute-start(f32[16,2048]{1,0:T(8,128)S(1)} %get-tuple-element.95), channel_id=1, source_target_pairs={{0,16},{4,20},{8,24},{12,28},{16,0},{20,4},{24,8},{28,12},{1,17},{... | collective-permute-start | bytes 393224 | tf_op jit(solution)/shard_map/ppermute | solution.py:42
  107.2 5.0 collective-permute-start.16
  109.6 4.4 collective-permute-start.15
  112.2 3.5 collective-permute-start.14
  145.0 309.6 %reduce-scatter.9.cloned.1.call-start = ((), (), s32[]{:S(2)}) async-start(), calls=%async_computation.7 | async-start | bytes 4751360 | tf_op jit(solution)/shard_map/reduce_scatter | solution.py:249
  216.8 11.9 %collective-permute-start.18 = (bf16[32,3696]{1,0:T(8,128)(2,1)S(1)}, bf16[32,3696]{1,0:T(8,128)(2,1)S(1)}, u32[]{:S(2)}, u32[]{:S(2)}) collective-permute-start(bf16[32,3696]{1,0:T(8,128)(2,1)S(1)} %fusion.180), channel_id=1, source_target_pairs={{0,2},{1,3},{2,0},{3,1},{4,6},{5,7},{6,4},{7,5},{8,10},{9,11},{10,... | collective-permute-start | bytes 709640 | tf_op jit(solution)/shard_map/ppermute | solution.py:52
  217.0 20.6 %collective-permute-start.17 = (bf16[32,3696]{1,0:T(8,128)(2,1)S(1)}, bf16[32,3696]{1,0:T(8,128)(2,1)S(1)}, u32[]{:S(2)}, u32[]{:S(2)}) collective-permute-start(bf16[32,3696]{1,0:T(8,128)(2,1)S(1)} %fusion.180), channel_id=1, source_target_pairs={{0,3},{1,0},{2,1},{3,2},{4,7},{5,4},{6,5},{7,6},{8,11},{9,8},{10,9... | collective-permute-start | bytes 709640 | tf_op jit(solution)/shard_map/ppermute | solution.py:52
  218.8 20.8 %collective-permute-start.19 = (bf16[32,3696]{1,0:T(8,128)(2,1)S(1)}, bf16[32,3696]{1,0:T(8,128)(2,1)S(1)}, u32[]{:S(2)}, u32[]{:S(2)}) collective-permute-start(bf16[32,3696]{1,0:T(8,128)(2,1)S(1)} %fusion.180), channel_id=1, source_target_pairs={{0,1},{1,2},{2,3},{3,0},{4,5},{5,6},{6,7},{7,4},{8,9},{9,10},{10,1... | collective-permute-start | bytes 709640 | tf_op jit(solution)/shard_map/ppermute | solution.py:52
  250.7 6.4 %collective-permute-start.21 = (f32[16,2048]{1,0:T(8,128)S(1)}, f32[16,2048]{1,0:T(8,128)S(1)}, u32[]{:S(2)}, u32[]{:S(2)}) collective-permute-start(f32[16,2048]{1,0:T(8,128)S(1)} %get-tuple-element.90), channel_id=1, source_target_pairs={{0,8},{4,12},{8,16},{12,20},{16,24},{20,28},{24,0},{28,4},{1,9},{5... | collective-permute-start | bytes 393224 | tf_op jit(solution)/shard_map/ppermute | solution.py:42
  252.2 7.9 %collective-permute-start.23 = (f32[16,2048]{1,0:T(8,128)S(1)}, f32[16,2048]{1,0:T(8,128)S(1)}, u32[]{:S(2)}, u32[]{:S(2)}) collective-permute-start(f32[16,2048]{1,0:T(8,128)S(1)} %get-tuple-element.91), channel_id=1, source_target_pairs={{0,24},{4,28},{8,0},{12,4},{16,8},{20,12},{24,16},{28,20},{1,25},{... | collective-permute-start | bytes 393224 | tf_op jit(solution)/shard_map/ppermute | solution.py:42
  252.8 7.8 %collective-permute-start.22 = (f32[16,2048]{1,0:T(8,128)S(1)}, f32[16,2048]{1,0:T(8,128)S(1)}, u32[]{:S(2)}, u32[]{:S(2)}) collective-permute-start(f32[16,2048]{1,0:T(8,128)S(1)} %get-tuple-element.92), channel_id=1, source_target_pairs={{0,16},{4,20},{8,24},{12,28},{16,0},{20,4},{24,8},{28,12},{1,17},{... | collective-permute-start | bytes 393224 | tf_op jit(solution)/shard_map/ppermute | solution.py:42
  260.6 11.3 %collective-permute-start.26 = (f32[16,2048]{1,0:T(8,128)S(1)}, f32[16,2048]{1,0:T(8,128)S(1)}, u32[]{:S(2)}, u32[]{:S(2)}) collective-permute-start(f32[16,2048]{1,0:T(8,128)S(1)} %fusion.215), channel_id=1, source_target_pairs={{0,1},{1,2},{2,3},{3,0},{4,5},{5,6},{6,7},{7,4},{8,9},{9,10},{10,1... | collective-permute-start | bytes 393224 | tf_op jit(solution)/shard_map/ppermute | solution.py:52
  260.7 11.2 %collective-permute-start.25 = (f32[16,2048]{1,0:T(8,128)S(1)}, f32[16,2048]{1,0:T(8,128)S(1)}, u32[]{:S(2)}, u32[]{:S(2)}) collective-permute-start(f32[16,2048]{1,0:T(8,128)S(1)} %fusion.215), channel_id=1, source_target_pairs={{0,2},{1,3},{2,0},{3,1},{4,6},{5,7},{6,4},{7,5},{8,10},{9,11},{10,... | collective-permute-start | bytes 393224 | tf_op jit(solution)/shard_map/ppermute | solution.py:52
  262.6 9.3 %collective-permute-start.24 = (f32[16,2048]{1,0:T(8,128)S(1)}, f32[16,2048]{1,0:T(8,128)S(1)}, u32[]{:S(2)}, u32[]{:S(2)}) collective-permute-start(f32[16,2048]{1,0:T(8,128)S(1)} %fusion.215), channel_id=1, source_target_pairs={{0,3},{1,0},{2,1},{3,2},{4,7},{5,4},{6,5},{7,6},{8,11},{9,8},{10,9... | collective-permute-start | bytes 393224 | tf_op jit(solution)/shard_map/ppermute | solution.py:52
  287.5 2.2 collective-permute-start.27
  289.8 7.1 %collective-permute-start.28 = (f32[16,2560]{1,0:T(8,128)S(1)}, f32[16,2560]{1,0:T(8,128)S(1)}, u32[]{:S(2)}, u32[]{:S(2)}) collective-permute-start(f32[16,2560]{1,0:T(8,128)S(1)} %get-tuple-element.78), channel_id=1, source_target_pairs={{0,8},{4,12},{8,16},{12,20},{16,24},{20,28},{24,0},{28,4},{1,9},{5... | collective-permute-start | bytes 491528 | tf_op jit(solution)/shard_map/ppermute | solution.py:42
  291.3 8.4 %collective-permute-start.30 = (f32[16,2560]{1,0:T(8,128)S(1)}, f32[16,2560]{1,0:T(8,128)S(1)}, u32[]{:S(2)}, u32[]{:S(2)}) collective-permute-start(f32[16,2560]{1,0:T(8,128)S(1)} %get-tuple-element.79), channel_id=1, source_target_pairs={{0,24},{4,28},{8,0},{12,4},{16,8},{20,12},{24,16},{28,20},{1,25},{... | collective-permute-start | bytes 491528 | tf_op jit(solution)/shard_map/ppermute | solution.py:42
  292.1 9.2 %collective-permute-start.29 = (f32[16,2560]{1,0:T(8,128)S(1)}, f32[16,2560]{1,0:T(8,128)S(1)}, u32[]{:S(2)}, u32[]{:S(2)}) collective-permute-start(f32[16,2560]{1,0:T(8,128)S(1)} %get-tuple-element.80), channel_id=1, source_target_pairs={{0,16},{4,20},{8,24},{12,28},{16,0},{20,4},{24,8},{28,12},{1,17},{... | collective-permute-start | bytes 491528 | tf_op jit(solution)/shard_map/ppermute | solution.py:42
  312.7 4.8 collective-permute-start.33
  315.6 5.2 %collective-permute-start.32 = (bf16[16,2048]{1,0:T(8,128)(2,1)S(1)}, bf16[16,2048]{1,0:T(8,128)(2,1)S(1)}, u32[]{:S(2)}, u32[]{:S(2)}) collective-permute-start(bf16[16,2048]{1,0:T(8,128)(2,1)S(1)} %bitcast.537), channel_id=1, source_target_pairs={{0,2},{1,3},{2,0},{3,1},{4,6},{5,7},{6,4},{7,5},{8,10},{9,11},{10,... | collective-permute-start | bytes 196616 | tf_op jit(solution)/shard_map/ppermute | solution.py:52
  315.6 5.2 %collective-permute-start.31 = (bf16[16,2048]{1,0:T(8,128)(2,1)S(1)}, bf16[16,2048]{1,0:T(8,128)(2,1)S(1)}, u32[]{:S(2)}, u32[]{:S(2)}) collective-permute-start(bf16[16,2048]{1,0:T(8,128)(2,1)S(1)} %bitcast.538), channel_id=1, source_target_pairs={{0,3},{1,0},{2,1},{3,2},{4,7},{5,4},{6,5},{7,6},{8,11},{9,8},{10,9... | collective-permute-start | bytes 196616 | tf_op jit(solution)/shard_map/ppermute | solution.py:52
  336.6 6.3 %collective-permute-start.35 = (f32[16,2048]{1,0:T(8,128)S(1)}, f32[16,2048]{1,0:T(8,128)S(1)}, u32[]{:S(2)}, u32[]{:S(2)}) collective-permute-start(f32[16,2048]{1,0:T(8,128)S(1)} %get-tuple-element.87), channel_id=1, source_target_pairs={{0,8},{4,12},{8,16},{12,20},{16,24},{20,28},{24,0},{28,4},{1,9},{5... | collective-permute-start | bytes 393224 | tf_op jit(solution)/shard_map/ppermute | solution.py:42
  338.1 7.0 %collective-permute-start.37 = (f32[16,2048]{1,0:T(8,128)S(1)}, f32[16,2048]{1,0:T(8,128)S(1)}, u32[]{:S(2)}, u32[]{:S(2)}) collective-permute-start(f32[16,2048]{1,0:T(8,128)S(1)} %get-tuple-element.88), channel_id=1, source_target_pairs={{0,24},{4,28},{8,0},{12,4},{16,8},{20,12},{24,16},{28,20},{1,25},{... | collective-permute-start | bytes 393224 | tf_op jit(solution)/shard_map/ppermute | solution.py:42
  338.6 7.8 %collective-permute-start.36 = (f32[16,2048]{1,0:T(8,128)S(1)}, f32[16,2048]{1,0:T(8,128)S(1)}, u32[]{:S(2)}, u32[]{:S(2)}) collective-permute-start(f32[16,2048]{1,0:T(8,128)S(1)} %get-tuple-element.89), channel_id=1, source_target_pairs={{0,16},{4,20},{8,24},{12,28},{16,0},{20,4},{24,8},{28,12},{1,17},{... | collective-permute-start | bytes 393224 | tf_op jit(solution)/shard_map/ppermute | solution.py:42
  346.6 4.6 collective-permute-start.40
  348.6 4.4 collective-permute-start.39
  351.2 3.5 collective-permute-start.38
  456.0 11.9 %collective-permute-start.42 = (bf16[32,3696]{1,0:T(8,128)(2,1)S(1)}, bf16[32,3696]{1,0:T(8,128)(2,1)S(1)}, u32[]{:S(2)}, u32[]{:S(2)}) collective-permute-start(bf16[32,3696]{1,0:T(8,128)(2,1)S(1)} %fusion.179), channel_id=1, source_target_pairs={{0,2},{1,3},{2,0},{3,1},{4,6},{5,7},{6,4},{7,5},{8,10},{9,11},{10,... | collective-permute-start | bytes 709640 | tf_op jit(solution)/shard_map/ppermute | solution.py:52
  456.2 20.5 %collective-permute-start.41 = (bf16[32,3696]{1,0:T(8,128)(2,1)S(1)}, bf16[32,3696]{1,0:T(8,128)(2,1)S(1)}, u32[]{:S(2)}, u32[]{:S(2)}) collective-permute-start(bf16[32,3696]{1,0:T(8,128)(2,1)S(1)} %fusion.179), channel_id=1, source_target_pairs={{0,3},{1,0},{2,1},{3,2},{4,7},{5,4},{6,5},{7,6},{8,11},{9,8},{10,9... | collective-permute-start | bytes 709640 | tf_op jit(solution)/shard_map/ppermute | solution.py:52
  458.0 20.8 %collective-permute-start.43 = (bf16[32,3696]{1,0:T(8,128)(2,1)S(1)}, bf16[32,3696]{1,0:T(8,128)(2,1)S(1)}, u32[]{:S(2)}, u32[]{:S(2)}) collective-permute-start(bf16[32,3696]{1,0:T(8,128)(2,1)S(1)} %fusion.179), channel_id=1, source_target_pairs={{0,1},{1,2},{2,3},{3,0},{4,5},{5,6},{6,7},{7,4},{8,9},{9,10},{10,1... | collective-permute-start | bytes 709640 | tf_op jit(solution)/shard_map/ppermute | solution.py:52
  489.9 6.4 %collective-permute-start.45 = (f32[16,2048]{1,0:T(8,128)S(1)}, f32[16,2048]{1,0:T(8,128)S(1)}, u32[]{:S(2)}, u32[]{:S(2)}) collective-permute-start(f32[16,2048]{1,0:T(8,128)S(1)} %get-tuple-element.84), channel_id=1, source_target_pairs={{0,8},{4,12},{8,16},{12,20},{16,24},{20,28},{24,0},{28,4},{1,9},{5... | collective-permute-start | bytes 393224 | tf_op jit(solution)/shard_map/ppermute | solution.py:42
  491.5 7.9 %collective-permute-start.47 = (f32[16,2048]{1,0:T(8,128)S(1)}, f32[16,2048]{1,0:T(8,128)S(1)}, u32[]{:S(2)}, u32[]{:S(2)}) collective-permute-start(f32[16,2048]{1,0:T(8,128)S(1)} %get-tuple-element.85), channel_id=1, source_target_pairs={{0,24},{4,28},{8,0},{12,4},{16,8},{20,12},{24,16},{28,20},{1,25},{... | collective-permute-start | bytes 393224 | tf_op jit(solution)/shard_map/ppermute | solution.py:42
  492.0 7.8 %collective-permute-start.46 = (f32[16,2048]{1,0:T(8,128)S(1)}, f32[16,2048]{1,0:T(8,128)S(1)}, u32[]{:S(2)}, u32[]{:S(2)}) collective-permute-start(f32[16,2048]{1,0:T(8,128)S(1)} %get-tuple-element.86), channel_id=1, source_target_pairs={{0,16},{4,20},{8,24},{12,28},{16,0},{20,4},{24,8},{28,12},{1,17},{... | collective-permute-start | bytes 393224 | tf_op jit(solution)/shard_map/ppermute | solution.py:42
  (25 other events, 358.5 us)
Sparse Core Ops, SparseCore 0:
  145.1 70.2 reduce-scatter.6
  384.3 70.2 reduce-scatter.8

commit v11 on v8

--- a/solution.py
+++ b/solution.py
@@ -3,6 +3,7 @@
 import jax
 import jax.numpy as jnp
 from jax import lax
+from jax.experimental.layout import Layout, with_layout_constraint
 from jax.sharding import PartitionSpec as P
 
 MODEL_WIDTH = 8192
@@ -236,8 +237,11 @@
         gate_up = lax.psum_scatter(
             jnp.concatenate(
                 [
-                    jnp.dot(tokens, w_gate, preferred_element_type=jnp.float32),
-                    jnp.dot(tokens, w_up, preferred_element_type=jnp.float32),
+                    with_layout_constraint(
+                        jnp.dot(tokens, weight, preferred_element_type=jnp.float32),
+                        Layout(major_to_minor=(0, 1)),
+                    )
+                    for weight in (w_gate, w_up)
                 ],
                 axis=1,
             ),

time: 516 us -> 523 us (1.014)
  matrix products: 71.4 us -> 88.3 us
  local copies, waits for them, and re-layouts: 17.1 us -> 6.5 us
    dot_general x4, matrix products: 24.2 us -> 41.3 us  [body(): jnp.dot(tokens, weight, preferred_element_type=jnp.float32)]
    unnamed x50 -> x32, local copies, waits for them, and re-layouts: 10.8 us -> 0.19 us
where the time goes in v11:
time: 523 us; the launch traced here: 514 us
  waiting for transfers between devices  264 us (50%)
  matrix products  88.3 us (17%)
  starting transfers between devices  71.6 us (14%)
  blocking collectives  38.4 us (7%)
  other arithmetic  30.6 us (6%)
  between operations  14.8 us (3%)
  local copies, waits for them, and re-layouts  6.5 us (1%)
    reduce_scatter x2, waiting for transfers between devices, body(): lax.psum_scatter(jnp.concatenate([with_layout_constraint(jnp.dot(tokens,...  141 us
    ppermute x18, waiting for transfers between devices, gather_by_permute(): lax.ppermute(block, axis, [(j, (j + shift) % count) for j in range(count)])  48.9 us
    ppermute x18, waiting for transfers between devices, scatter_sum(): total = total + lax.ppermute(piece, axis, pairs)  42.6 us
    dot_general x4, matrix products, body(): jnp.dot(tokens, weight, preferred_element_type=jnp.float32)  41.3 us
    ppermute x18, starting transfers between devices, gather_by_permute(): lax.ppermute(block, axis, [(j, (j + shift) % count) for j in range(count)])  27.2 us
    all_gather x2, blocking collectives, body(): tokens = lax.all_gather(normed_mlp, 'req', axis=0, tiled=True)  19.3 us
    ppermute x18, starting transfers between devices, scatter_sum(): total = total + lax.ppermute(piece, axis, pairs)  19.3 us
    all_to_all x2, blocking collectives, rows_for_weights(): return lax.all_to_all(wide, 'req', 0, 0, tiled=True)  19.2 us
  transfers between devices with their start and end apart: 58, of which 51 were waited for; matrix products, arithmetic and copies ran while one was open for 2% of the time, Pallas kernels for 0%

profile of v11, /device:TPU:18, one launch (start us, length us, event | category | flops | bytes accessed | tf_op | source)
XLA Modules:
  0.0 513.8 jit_solution(1827046287191675287)
XLA Ops:
  8.1 3.5 collective-permute-start.1
  27.7 4.3 all-to-all-start
  33.2 4.2 all-to-all-done
  38.9 3.0 fusion.275
  48.7 4.0 collective-permute-done.7
  52.6 2.8 collective-permute-done.9
  57.9 2.8 fusion.4
  60.8 3.6 fusion.8
  69.5 2.3 collective-permute-start.11
  71.8 2.8 collective-permute-start.10
  77.9 5.4 %all-to-all-start.1 = ((bf16[8,16,1024]{2,1,0:T(8,128)(2,1)}), bf16[8,16,1024]{2,1,0:T(8,128)(2,1)S(1)}, u32[]{:S(2)}, u32[]{:S(2)}) async-start(bf16[8,16,1024]{2,1,0:T(8,128)(2,1)} %bitcast.41), calls=%async_computation.1 | async-start | bytes 524288 | tf_op jit(solution)/shard_map/all_to_all | solution.py:66
  83.6 5.2 %all-to-all-done.1 = bf16[8,16,1024]{2,1,0:T(8,128)(2,1)S(1)} async-done(((bf16[8,16,1024]{2,1,0:T(8,128)(2,1)}), bf16[8,16,1024]{2,1,0:T(8,128)(2,1)S(1)}, u32[]{:S(2)}, u32[]{:S(2)}) %all-to-all-start.1) | async-done | bytes 262176 | tf_op jit(solution)/shard_map/all_to_all | solution.py:66
  89.6 3.0 fusion.195
  97.8 3.3 collective-permute-done.14
  101.0 2.2 collective-permute-done.16
  109.1 2.3 collective-permute-done.18
  112.5 9.6 %all_gather.6 = bf16[128,2048]{1,0:T(8,128)(2,1)S(1)} all-gather(bf16[16,2048]{1,0:T(8,128)(2,1)S(1)} %multiply_convert_fusion.2), channel_id=1, replica_groups=mesh['req'=8,'kv'=4] {'req'}, dimensions={0}, use_global_device_ids=true | all-gather | bytes 589824 | tf_op jit(solution)/shard_map/all_gather | solution.py:235
  122.1 10.3 %fusion.286 = f32[128,3696]{1,0:T(8,128)S(1)} fusion(bf16[128,2048]{1,0:T(8,128)(2,1)S(1)} %all_gather.6, bf16[2048,3696]{0,1:T(8,128)(2,1)} %param.48), kind=kOutput, calls=%fused_computation.408 | convolution fusion | flops 1937768448 | bytes 17555456 | tf_op jit(solution)/shard_map/dot_general | solution.py:241
  132.4 10.3 %fusion.285 = f32[128,3696]{1,0:T(8,128)S(1)} fusion(bf16[128,2048]{1,0:T(8,128)(2,1)S(1)} %all_gather.6, bf16[2048,3696]{0,1:T(8,128)(2,1)} %param.47), kind=kOutput, calls=%fused_computation.407 | convolution fusion | flops 1937768448 | bytes 17555456 | tf_op jit(solution)/shard_map/dot_general | solution.py:241
  142.7 2.5 pad_maximum_fusion
  145.3 70.8 %reduce-scatter.3.cloned.1.call-done = f32[32,7392]{1,0:T(8,128)} async-done(((f32[128,7392]{1,0:T(8,128)}), f32[32,7392]{1,0:T(8,128)}) %reduce-scatter.3.cloned.1.call-update) | async-done | bytes 946192 | tf_op jit(solution)/shard_map/reduce_scatter | solution.py:237
  221.6 7.8 %collective-permute-done.21 = bf16[32,3696]{1,0:T(8,128)(2,1)S(1)} collective-permute-done((bf16[32,3696]{1,0:T(8,128)(2,1)S(1)}, bf16[32,3696]{1,0:T(8,128)(2,1)S(1)}, u32[]{:S(2)}, u32[]{:S(2)}) %collective-permute-start.21) | collective-permute-done | bytes 236576 | tf_op jit(solution)/shard_map/ppermute | solution.py:53
  229.4 8.8 %collective-permute-done.20 = bf16[32,3696]{1,0:T(8,128)(2,1)S(1)} collective-permute-done((bf16[32,3696]{1,0:T(8,128)(2,1)S(1)}, bf16[32,3696]{1,0:T(8,128)(2,1)S(1)}, u32[]{:S(2)}, u32[]{:S(2)}) %collective-permute-start.20) | collective-permute-done | bytes 236576 | tf_op jit(solution)/shard_map/ppermute | solution.py:53
  241.5 7.7 %fusion = f32[4,2,16,2048]{3,2,1,0:T(8,128)S(1)} fusion(bf16[4,2,16,3696]{3,2,1,0:T(8,128)(2,1)S(1)} %bitcast.496, bf16[3696,2048]{1,0:T(8,128)(2,1)} %param.49), kind=kOutput, calls=%fused_computation.6 | convolution fusion | flops 1937768448 | bytes 17133568 | tf_op jit(solution)/shard_map/dot_general | solution.py:257
  254.9 2.8 collective-permute-done.24
  257.7 3.0 collective-permute-done.26
  266.5 3.8 collective-permute-start.31
  275.6 9.5 %all_to_all.48 = bf16[8,16,1024]{2,1,0:T(8,128)(2,1)S(1)} all-to-all(bf16[8,16,1024]{2,1,0:T(8,128)(2,1)S(1)} %bitcast.499), channel_id=1, replica_groups=mesh['req'=8,'kv'=4] {'req'}, dimensions={0} | all-to-all | bytes 524288 | tf_op jit(solution)/shard_map/all_to_all | solution.py:66
  286.5 2.9 fusion.278
  295.4 3.7 collective-permute-done.34
  299.1 2.8 collective-permute-done.36
  304.5 2.8 fusion.6
  307.4 3.6 fusion.12
  318.2 2.8 collective-permute-start.37
  323.6 9.7 %all_to_all.49 = bf16[8,16,1024]{2,1,0:T(8,128)(2,1)S(1)} all-to-all(bf16[8,16,1024]{2,1,0:T(8,128)(2,1)S(1)} %bitcast.500), channel_id=1, replica_groups=mesh['req'=8,'kv'=4] {'req'}, dimensions={0} | all-to-all | bytes 524288 | tf_op jit(solution)/shard_map/all_to_all | solution.py:66
  334.2 2.9 fusion.193
  342.2 3.3 collective-permute-done.41
  353.7 2.3 collective-permute-done.45
  357.3 9.7 %all_gather.7 = bf16[128,2048]{1,0:T(8,128)(2,1)S(1)} all-gather(bf16[16,2048]{1,0:T(8,128)(2,1)S(1)} %multiply_convert_fusion), channel_id=1, replica_groups=mesh['req'=8,'kv'=4] {'req'}, dimensions={0}, use_global_device_ids=true | all-gather | bytes 589824 | tf_op jit(solution)/shard_map/all_gather | solution.py:235
  367.0 10.3 %fusion.288 = f32[128,3696]{1,0:T(8,128)S(1)} fusion(bf16[128,2048]{1,0:T(8,128)(2,1)S(1)} %all_gather.7, bf16[2048,3696]{0,1:T(8,128)(2,1)} %param.48), kind=kOutput, calls=%fused_computation.410 | convolution fusion | flops 1937768448 | bytes 17555456 | tf_op jit(solution)/shard_map/dot_general | solution.py:241
  377.4 10.3 %fusion.287 = f32[128,3696]{1,0:T(8,128)S(1)} fusion(bf16[128,2048]{1,0:T(8,128)(2,1)S(1)} %all_gather.7, bf16[2048,3696]{0,1:T(8,128)(2,1)} %param.47), kind=kOutput, calls=%fused_computation.409 | convolution fusion | flops 1937768448 | bytes 17555456 | tf_op jit(solution)/shard_map/dot_general | solution.py:241
  387.7 2.5 pad_maximum_fusion.1
  390.2 70.6 %reduce-scatter.5.cloned.1.call-done = f32[32,7392]{1,0:T(8,128)} async-done(((f32[128,7392]{1,0:T(8,128)}), f32[32,7392]{1,0:T(8,128)}) %reduce-scatter.5.cloned.1.call-update) | async-done | bytes 946192 | tf_op jit(solution)/shard_map/reduce_scatter | solution.py:237
  466.0 8.1 %collective-permute-done.48 = bf16[32,3696]{1,0:T(8,128)(2,1)S(1)} collective-permute-done((bf16[32,3696]{1,0:T(8,128)(2,1)S(1)}, bf16[32,3696]{1,0:T(8,128)(2,1)S(1)}, u32[]{:S(2)}, u32[]{:S(2)}) %collective-permute-start.48) | collective-permute-done | bytes 236576 | tf_op jit(solution)/shard_map/ppermute | solution.py:53
  474.1 8.8 %collective-permute-done.47 = bf16[32,3696]{1,0:T(8,128)(2,1)S(1)} collective-permute-done((bf16[32,3696]{1,0:T(8,128)(2,1)S(1)}, bf16[32,3696]{1,0:T(8,128)(2,1)S(1)}, u32[]{:S(2)}, u32[]{:S(2)}) %collective-permute-start.47) | collective-permute-done | bytes 236576 | tf_op jit(solution)/shard_map/ppermute | solution.py:53
  486.2 7.8 %fusion.2 = f32[4,2,16,2048]{3,2,0,1:T(8,128)S(1)} fusion(bf16[3696,2048]{1,0:T(8,128)(2,1)} %param.49, bf16[4,2,16,3696]{3,2,1,0:T(8,128)(2,1)S(1)} %bitcast.495), kind=kOutput, calls=%fused_computation.8 | convolution fusion | flops 1937768448 | bytes 17133568 | tf_op jit(solution)/shard_map/dot_general | solution.py:257
  499.7 2.8 collective-permute-done.51
  502.5 3.0 collective-permute-done.53
  (259 shorter events, 126.4 us)
Async XLA Ops:
  7.6 9.6 %collective-permute-start.2 = (f32[16]{0:T(128)S(1)}, f32[16]{0:T(128)S(1)}, u32[]{:S(2)}, u32[]{:S(2)}) collective-permute-start(f32[16]{0:T(128)S(1)} %fusion.205), channel_id=1, source_target_pairs={{0,3},{1,0},{2,1},{3,2},{4,7},{5,4},{6,5},{7,6},{8,11},{9,8},{10,9... | collective-permute-start | bytes 200 | tf_op jit(solution)/shard_map/ppermute | solution.py:91
  8.1 9.1 %collective-permute-start.1 = (f32[16]{0:T(128)S(1)}, f32[16]{0:T(128)S(1)}, u32[]{:S(2)}, u32[]{:S(2)}) collective-permute-start(f32[16]{0:T(128)S(1)} %fusion.205), channel_id=1, source_target_pairs={{0,2},{1,3},{2,0},{3,1},{4,6},{5,7},{6,4},{7,5},{8,10},{9,11},{10,... | collective-permute-start | bytes 200 | tf_op jit(solution)/shard_map/ppermute | solution.py:91
  11.6 5.6 %collective-permute-start = (f32[16]{0:T(128)S(1)}, f32[16]{0:T(128)S(1)}, u32[]{:S(2)}, u32[]{:S(2)}) collective-permute-start(f32[16]{0:T(128)S(1)} %fusion.205), channel_id=1, source_target_pairs={{0,1},{1,2},{2,3},{3,0},{4,5},{5,6},{6,7},{7,4},{8,9},{9,10},{10,1... | collective-permute-start | bytes 200 | tf_op jit(solution)/shard_map/ppermute | solution.py:91
  18.1 5.4 %collective-permute-start.4 = (bf16[16,2048]{1,0:T(8,128)(2,1)S(1)}, bf16[16,2048]{1,0:T(8,128)(2,1)S(1)}, u32[]{:S(2)}, u32[]{:S(2)}) collective-permute-start(bf16[16,2048]{1,0:T(8,128)(2,1)S(1)} %fusion.207), channel_id=1, source_target_pairs={{0,2},{1,3},{2,0},{3,1},{4,6},{5,7},{6,4},{7,5},{8,10},{9,11},{10,... | collective-permute-start | bytes 196616 | tf_op jit(solution)/shard_map/ppermute | solution.py:53
  19.2 5.5 %collective-permute-start.3 = (bf16[16,2048]{1,0:T(8,128)(2,1)S(1)}, bf16[16,2048]{1,0:T(8,128)(2,1)S(1)}, u32[]{:S(2)}, u32[]{:S(2)}) collective-permute-start(bf16[16,2048]{1,0:T(8,128)(2,1)S(1)} %fusion.207), channel_id=1, source_target_pairs={{0,3},{1,0},{2,1},{3,2},{4,7},{5,4},{6,5},{7,6},{8,11},{9,8},{10,9... | collective-permute-start | bytes 196616 | tf_op jit(solution)/shard_map/ppermute | solution.py:53
  21.1 5.5 %collective-permute-start.5 = (bf16[16,2048]{1,0:T(8,128)(2,1)S(1)}, bf16[16,2048]{1,0:T(8,128)(2,1)S(1)}, u32[]{:S(2)}, u32[]{:S(2)}) collective-permute-start(bf16[16,2048]{1,0:T(8,128)(2,1)S(1)} %fusion.207), channel_id=1, source_target_pairs={{0,1},{1,2},{2,3},{3,0},{4,5},{5,6},{6,7},{7,4},{8,9},{9,10},{10,1... | collective-permute-start | bytes 196616 | tf_op jit(solution)/shard_map/ppermute | solution.py:53
  27.7 9.7 %all-to-all-start = ((bf16[8,16,1024]{2,1,0:T(8,128)(2,1)}), bf16[8,16,1024]{2,1,0:T(8,128)(2,1)S(1)}, u32[]{:S(2)}, u32[]{:S(2)}) async-start(bf16[8,16,1024]{2,1,0:T(8,128)(2,1)} %bitcast.7), calls=%async_computation | async-start | bytes 524288 | tf_op jit(solution)/shard_map/all_to_all | solution.py:66
  45.5 7.1 %collective-permute-start.7 = (f32[16,2560]{1,0:T(8,128)S(1)}, f32[16,2560]{1,0:T(8,128)S(1)}, u32[]{:S(2)}, u32[]{:S(2)}) collective-permute-start(f32[16,2560]{1,0:T(8,128)S(1)} %get-tuple-element.78), channel_id=1, source_target_pairs={{0,8},{4,12},{8,16},{12,20},{16,24},{20,28},{24,0},{28,4},{1,9},{5... | collective-permute-start | bytes 491528 | tf_op jit(solution)/shard_map/ppermute | solution.py:43
  47.0 8.4 %collective-permute-start.9 = (f32[16,2560]{1,0:T(8,128)S(1)}, f32[16,2560]{1,0:T(8,128)S(1)}, u32[]{:S(2)}, u32[]{:S(2)}) collective-permute-start(f32[16,2560]{1,0:T(8,128)S(1)} %get-tuple-element.79), channel_id=1, source_target_pairs={{0,24},{4,28},{8,0},{12,4},{16,8},{20,12},{24,16},{28,20},{1,25},{... | collective-permute-start | bytes 491528 | tf_op jit(solution)/shard_map/ppermute | solution.py:43
  47.6 9.2 %collective-permute-start.8 = (f32[16,2560]{1,0:T(8,128)S(1)}, f32[16,2560]{1,0:T(8,128)S(1)}, u32[]{:S(2)}, u32[]{:S(2)}) collective-permute-start(f32[16,2560]{1,0:T(8,128)S(1)} %get-tuple-element.80), channel_id=1, source_target_pairs={{0,16},{4,20},{8,24},{12,28},{16,0},{20,4},{24,8},{28,12},{1,17},{... | collective-permute-start | bytes 491528 | tf_op jit(solution)/shard_map/ppermute | solution.py:43
  68.2 6.5 %collective-permute-start.12 = (bf16[16,2048]{1,0:T(8,128)(2,1)S(1)}, bf16[16,2048]{1,0:T(8,128)(2,1)S(1)}, u32[]{:S(2)}, u32[]{:S(2)}) collective-permute-start(bf16[16,2048]{1,0:T(8,128)(2,1)S(1)} %bitcast.521), channel_id=1, source_target_pairs={{0,1},{1,2},{2,3},{3,0},{4,5},{5,6},{6,7},{7,4},{8,9},{9,10},{10,1... | collective-permute-start | bytes 196616 | tf_op jit(solution)/shard_map/ppermute | solution.py:53
  69.5 5.9 %collective-permute-start.11 = (bf16[16,2048]{1,0:T(8,128)(2,1)S(1)}, bf16[16,2048]{1,0:T(8,128)(2,1)S(1)}, u32[]{:S(2)}, u32[]{:S(2)}) collective-permute-start(bf16[16,2048]{1,0:T(8,128)(2,1)S(1)} %bitcast.522), channel_id=1, source_target_pairs={{0,2},{1,3},{2,0},{3,1},{4,6},{5,7},{6,4},{7,5},{8,10},{9,11},{10,... | collective-permute-start | bytes 196616 | tf_op jit(solution)/shard_map/ppermute | solution.py:53
  71.8 5.0 collective-permute-start.10
  77.9 10.9 %all-to-all-start.1 = ((bf16[8,16,1024]{2,1,0:T(8,128)(2,1)}), bf16[8,16,1024]{2,1,0:T(8,128)(2,1)S(1)}, u32[]{:S(2)}, u32[]{:S(2)}) async-start(bf16[8,16,1024]{2,1,0:T(8,128)(2,1)} %bitcast.41), calls=%async_computation.1 | async-start | bytes 524288 | tf_op jit(solution)/shard_map/all_to_all | solution.py:66
  83.3 132.9 %reduce-scatter.3.cloned.1.call-start = ((), (), s32[]{:S(2)}) async-start(), calls=%async_computation.6 | async-start | bytes 4751360 | tf_op jit(solution)/shard_map/reduce_scatter | solution.py:237
  94.8 6.3 %collective-permute-start.14 = (f32[16,2048]{1,0:T(8,128)S(1)}, f32[16,2048]{1,0:T(8,128)S(1)}, u32[]{:S(2)}, u32[]{:S(2)}) collective-permute-start(f32[16,2048]{1,0:T(8,128)S(1)} %get-tuple-element.90), channel_id=1, source_target_pairs={{0,8},{4,12},{8,16},{12,20},{16,24},{20,28},{24,0},{28,4},{1,9},{5... | collective-permute-start | bytes 393224 | tf_op jit(solution)/shard_map/ppermute | solution.py:43
  96.3 7.0 %collective-permute-start.16 = (f32[16,2048]{1,0:T(8,128)S(1)}, f32[16,2048]{1,0:T(8,128)S(1)}, u32[]{:S(2)}, u32[]{:S(2)}) collective-permute-start(f32[16,2048]{1,0:T(8,128)S(1)} %get-tuple-element.91), channel_id=1, source_target_pairs={{0,24},{4,28},{8,0},{12,4},{16,8},{20,12},{24,16},{28,20},{1,25},{... | collective-permute-start | bytes 393224 | tf_op jit(solution)/shard_map/ppermute | solution.py:43
  96.8 7.8 %collective-permute-start.15 = (f32[16,2048]{1,0:T(8,128)S(1)}, f32[16,2048]{1,0:T(8,128)S(1)}, u32[]{:S(2)}, u32[]{:S(2)}) collective-permute-start(f32[16,2048]{1,0:T(8,128)S(1)} %get-tuple-element.92), channel_id=1, source_target_pairs={{0,16},{4,20},{8,24},{12,28},{16,0},{20,4},{24,8},{28,12},{1,17},{... | collective-permute-start | bytes 393224 | tf_op jit(solution)/shard_map/ppermute | solution.py:43
  104.8 4.3 collective-permute-start.19
  107.0 4.4 collective-permute-start.18
  145.2 315.6 %reduce-scatter.5.cloned.1.call-start = ((), (), s32[]{:S(2)}) async-start(), calls=%async_computation.7 | async-start | bytes 4751360 | tf_op jit(solution)/shard_map/reduce_scatter | solution.py:237
  217.5 11.9 %collective-permute-start.21 = (bf16[32,3696]{1,0:T(8,128)(2,1)S(1)}, bf16[32,3696]{1,0:T(8,128)(2,1)S(1)}, u32[]{:S(2)}, u32[]{:S(2)}) collective-permute-start(bf16[32,3696]{1,0:T(8,128)(2,1)S(1)} %fusion.164), channel_id=1, source_target_pairs={{0,2},{1,3},{2,0},{3,1},{4,6},{5,7},{6,4},{7,5},{8,10},{9,11},{10,... | collective-permute-start | bytes 709640 | tf_op jit(solution)/shard_map/ppermute | solution.py:53
  217.7 20.6 %collective-permute-start.20 = (bf16[32,3696]{1,0:T(8,128)(2,1)S(1)}, bf16[32,3696]{1,0:T(8,128)(2,1)S(1)}, u32[]{:S(2)}, u32[]{:S(2)}) collective-permute-start(bf16[32,3696]{1,0:T(8,128)(2,1)S(1)} %fusion.164), channel_id=1, source_target_pairs={{0,3},{1,0},{2,1},{3,2},{4,7},{5,4},{6,5},{7,6},{8,11},{9,8},{10,9... | collective-permute-start | bytes 709640 | tf_op jit(solution)/shard_map/ppermute | solution.py:53
  219.4 20.8 %collective-permute-start.22 = (bf16[32,3696]{1,0:T(8,128)(2,1)S(1)}, bf16[32,3696]{1,0:T(8,128)(2,1)S(1)}, u32[]{:S(2)}, u32[]{:S(2)}) collective-permute-start(bf16[32,3696]{1,0:T(8,128)(2,1)S(1)} %fusion.164), channel_id=1, source_target_pairs={{0,1},{1,2},{2,3},{3,0},{4,5},{5,6},{6,7},{7,4},{8,9},{9,10},{10,1... | collective-permute-start | bytes 709640 | tf_op jit(solution)/shard_map/ppermute | solution.py:53
  251.3 6.4 %collective-permute-start.24 = (f32[16,2048]{1,0:T(8,128)S(1)}, f32[16,2048]{1,0:T(8,128)S(1)}, u32[]{:S(2)}, u32[]{:S(2)}) collective-permute-start(f32[16,2048]{1,0:T(8,128)S(1)} %get-tuple-element.87), channel_id=1, source_target_pairs={{0,8},{4,12},{8,16},{12,20},{16,24},{20,28},{24,0},{28,4},{1,9},{5... | collective-permute-start | bytes 393224 | tf_op jit(solution)/shard_map/ppermute | solution.py:43
  252.8 7.9 %collective-permute-start.26 = (f32[16,2048]{1,0:T(8,128)S(1)}, f32[16,2048]{1,0:T(8,128)S(1)}, u32[]{:S(2)}, u32[]{:S(2)}) collective-permute-start(f32[16,2048]{1,0:T(8,128)S(1)} %get-tuple-element.88), channel_id=1, source_target_pairs={{0,24},{4,28},{8,0},{12,4},{16,8},{20,12},{24,16},{28,20},{1,25},{... | collective-permute-start | bytes 393224 | tf_op jit(solution)/shard_map/ppermute | solution.py:43
  253.4 7.8 %collective-permute-start.25 = (f32[16,2048]{1,0:T(8,128)S(1)}, f32[16,2048]{1,0:T(8,128)S(1)}, u32[]{:S(2)}, u32[]{:S(2)}) collective-permute-start(f32[16,2048]{1,0:T(8,128)S(1)} %get-tuple-element.89), channel_id=1, source_target_pairs={{0,16},{4,20},{8,24},{12,28},{16,0},{20,4},{24,8},{28,12},{1,17},{... | collective-permute-start | bytes 393224 | tf_op jit(solution)/shard_map/ppermute | solution.py:43
  261.8 4.4 collective-permute-start.28
  261.9 4.6 collective-permute-start.27
  266.5 6.0 %collective-permute-start.31 = (bf16[16,2048]{1,0:T(8,128)(2,1)S(1)}, bf16[16,2048]{1,0:T(8,128)(2,1)S(1)}, u32[]{:S(2)}, u32[]{:S(2)}) collective-permute-start(bf16[16,2048]{1,0:T(8,128)(2,1)S(1)} %multiply_convert_fusion.1), channel_id=1, source_target_pairs={{0,2},{1,3},{2,0},{3,1},{4,6},{5,7},{6,4},{7,5},{8,10},{9,11},{10,... | collective-permute-start | bytes 196616 | tf_op jit(solution)/shard_map/ppermute | solution.py:53
  270.3 5.0 collective-permute-start.32
  292.0 7.1 %collective-permute-start.34 = (f32[16,2560]{1,0:T(8,128)S(1)}, f32[16,2560]{1,0:T(8,128)S(1)}, u32[]{:S(2)}, u32[]{:S(2)}) collective-permute-start(f32[16,2560]{1,0:T(8,128)S(1)} %get-tuple-element.75), channel_id=1, source_target_pairs={{0,8},{4,12},{8,16},{12,20},{16,24},{20,28},{24,0},{28,4},{1,9},{5... | collective-permute-start | bytes 491528 | tf_op jit(solution)/shard_map/ppermute | solution.py:43
  293.5 8.4 %collective-permute-start.36 = (f32[16,2560]{1,0:T(8,128)S(1)}, f32[16,2560]{1,0:T(8,128)S(1)}, u32[]{:S(2)}, u32[]{:S(2)}) collective-permute-start(f32[16,2560]{1,0:T(8,128)S(1)} %get-tuple-element.76), channel_id=1, source_target_pairs={{0,24},{4,28},{8,0},{12,4},{16,8},{20,12},{24,16},{28,20},{1,25},{... | collective-permute-start | bytes 491528 | tf_op jit(solution)/shard_map/ppermute | solution.py:43
  294.2 9.2 %collective-permute-start.35 = (f32[16,2560]{1,0:T(8,128)S(1)}, f32[16,2560]{1,0:T(8,128)S(1)}, u32[]{:S(2)}, u32[]{:S(2)}) collective-permute-start(f32[16,2560]{1,0:T(8,128)S(1)} %get-tuple-element.77), channel_id=1, source_target_pairs={{0,16},{4,20},{8,24},{12,28},{16,0},{20,4},{24,8},{28,12},{1,17},{... | collective-permute-start | bytes 491528 | tf_op jit(solution)/shard_map/ppermute | solution.py:43
  314.8 6.2 %collective-permute-start.39 = (bf16[16,2048]{1,0:T(8,128)(2,1)S(1)}, bf16[16,2048]{1,0:T(8,128)(2,1)S(1)}, u32[]{:S(2)}, u32[]{:S(2)}) collective-permute-start(bf16[16,2048]{1,0:T(8,128)(2,1)S(1)} %bitcast.524), channel_id=1, source_target_pairs={{0,1},{1,2},{2,3},{3,0},{4,5},{5,6},{6,7},{7,4},{8,9},{9,10},{10,1... | collective-permute-start | bytes 196616 | tf_op jit(solution)/shard_map/ppermute | solution.py:53
  316.5 5.8 %collective-permute-start.38 = (bf16[16,2048]{1,0:T(8,128)(2,1)S(1)}, bf16[16,2048]{1,0:T(8,128)(2,1)S(1)}, u32[]{:S(2)}, u32[]{:S(2)}) collective-permute-start(bf16[16,2048]{1,0:T(8,128)(2,1)S(1)} %bitcast.525), channel_id=1, source_target_pairs={{0,2},{1,3},{2,0},{3,1},{4,6},{5,7},{6,4},{7,5},{8,10},{9,11},{10,... | collective-permute-start | bytes 196616 | tf_op jit(solution)/shard_map/ppermute | solution.py:53
  318.2 5.1 collective-permute-start.37
  339.3 6.3 %collective-permute-start.41 = (f32[16,2048]{1,0:T(8,128)S(1)}, f32[16,2048]{1,0:T(8,128)S(1)}, u32[]{:S(2)}, u32[]{:S(2)}) collective-permute-start(f32[16,2048]{1,0:T(8,128)S(1)} %get-tuple-element.84), channel_id=1, source_target_pairs={{0,8},{4,12},{8,16},{12,20},{16,24},{20,28},{24,0},{28,4},{1,9},{5... | collective-permute-start | bytes 393224 | tf_op jit(solution)/shard_map/ppermute | solution.py:43
  340.8 7.0 %collective-permute-start.43 = (f32[16,2048]{1,0:T(8,128)S(1)}, f32[16,2048]{1,0:T(8,128)S(1)}, u32[]{:S(2)}, u32[]{:S(2)}) collective-permute-start(f32[16,2048]{1,0:T(8,128)S(1)} %get-tuple-element.85), channel_id=1, source_target_pairs={{0,24},{4,28},{8,0},{12,4},{16,8},{20,12},{24,16},{28,20},{1,25},{... | collective-permute-start | bytes 393224 | tf_op jit(solution)/shard_map/ppermute | solution.py:43
  341.3 7.8 %collective-permute-start.42 = (f32[16,2048]{1,0:T(8,128)S(1)}, f32[16,2048]{1,0:T(8,128)S(1)}, u32[]{:S(2)}, u32[]{:S(2)}) collective-permute-start(f32[16,2048]{1,0:T(8,128)S(1)} %get-tuple-element.86), channel_id=1, source_target_pairs={{0,16},{4,20},{8,24},{12,28},{16,0},{20,4},{24,8},{28,12},{1,17},{... | collective-permute-start | bytes 393224 | tf_op jit(solution)/shard_map/ppermute | solution.py:43
  349.3 4.4 collective-permute-start.46
  351.5 4.4 collective-permute-start.45
  462.2 11.9 %collective-permute-start.48 = (bf16[32,3696]{1,0:T(8,128)(2,1)S(1)}, bf16[32,3696]{1,0:T(8,128)(2,1)S(1)}, u32[]{:S(2)}, u32[]{:S(2)}) collective-permute-start(bf16[32,3696]{1,0:T(8,128)(2,1)S(1)} %fusion.163), channel_id=1, source_target_pairs={{0,2},{1,3},{2,0},{3,1},{4,6},{5,7},{6,4},{7,5},{8,10},{9,11},{10,... | collective-permute-start | bytes 709640 | tf_op jit(solution)/shard_map/ppermute | solution.py:53
  462.4 20.5 %collective-permute-start.47 = (bf16[32,3696]{1,0:T(8,128)(2,1)S(1)}, bf16[32,3696]{1,0:T(8,128)(2,1)S(1)}, u32[]{:S(2)}, u32[]{:S(2)}) collective-permute-start(bf16[32,3696]{1,0:T(8,128)(2,1)S(1)} %fusion.163), channel_id=1, source_target_pairs={{0,3},{1,0},{2,1},{3,2},{4,7},{5,4},{6,5},{7,6},{8,11},{9,8},{10,9... | collective-permute-start | bytes 709640 | tf_op jit(solution)/shard_map/ppermute | solution.py:53
  464.2 20.8 %collective-permute-start.49 = (bf16[32,3696]{1,0:T(8,128)(2,1)S(1)}, bf16[32,3696]{1,0:T(8,128)(2,1)S(1)}, u32[]{:S(2)}, u32[]{:S(2)}) collective-permute-start(bf16[32,3696]{1,0:T(8,128)(2,1)S(1)} %fusion.163), channel_id=1, source_target_pairs={{0,1},{1,2},{2,3},{3,0},{4,5},{5,6},{6,7},{7,4},{8,9},{9,10},{10,1... | collective-permute-start | bytes 709640 | tf_op jit(solution)/shard_map/ppermute | solution.py:53
  496.1 6.4 %collective-permute-start.51 = (f32[16,2048]{1,0:T(8,128)S(1)}, f32[16,2048]{1,0:T(8,128)S(1)}, u32[]{:S(2)}, u32[]{:S(2)}) collective-permute-start(f32[16,2048]{1,0:T(8,128)S(1)} %get-tuple-element.81), channel_id=1, source_target_pairs={{0,8},{4,12},{8,16},{12,20},{16,24},{20,28},{24,0},{28,4},{1,9},{5... | collective-permute-start | bytes 393224 | tf_op jit(solution)/shard_map/ppermute | solution.py:43
  497.6 7.9 %collective-permute-start.53 = (f32[16,2048]{1,0:T(8,128)S(1)}, f32[16,2048]{1,0:T(8,128)S(1)}, u32[]{:S(2)}, u32[]{:S(2)}) collective-permute-start(f32[16,2048]{1,0:T(8,128)S(1)} %get-tuple-element.82), channel_id=1, source_target_pairs={{0,24},{4,28},{8,0},{12,4},{16,8},{20,12},{24,16},{28,20},{1,25},{... | collective-permute-start | bytes 393224 | tf_op jit(solution)/shard_map/ppermute | solution.py:43
  498.2 7.8 %collective-permute-start.52 = (f32[16,2048]{1,0:T(8,128)S(1)}, f32[16,2048]{1,0:T(8,128)S(1)}, u32[]{:S(2)}, u32[]{:S(2)}) collective-permute-start(f32[16,2048]{1,0:T(8,128)S(1)} %get-tuple-element.83), channel_id=1, source_target_pairs={{0,16},{4,20},{8,24},{12,28},{16,0},{20,4},{24,8},{28,12},{1,17},{... | collective-permute-start | bytes 393224 | tf_op jit(solution)/shard_map/ppermute | solution.py:43
  (23 other events, 181.1 us)
Sparse Core Ops, SparseCore 0:
  145.3 70.7 reduce-scatter.2
  390.3 70.4 reduce-scatter.4

commit v12 on v8

--- a/solution.py
+++ b/solution.py
@@ -84,12 +84,7 @@
 
 def normalize(residual, gains):
     square_sum = jnp.sum(residual * residual, axis=1)
-    count = lax.axis_size("kv")
-    all_squares = square_sum
-    for shift in range(1, count):
-        all_squares = all_squares + lax.ppermute(
-            square_sum, "kv", [(j, (j + shift) % count) for j in range(count)]
-        )
+    all_squares = lax.psum(square_sum, "kv")
     inv_norm = lax.rsqrt(all_squares / MODEL_WIDTH + EPS)
     return (residual * inv_norm[:, None] * gains.astype(jnp.float32)[None, :]).astype(jnp.bfloat16)
 

time: 516 us -> 529 us (1.025)
  blocking collectives: 38.4 us -> 73.7 us
  starting transfers between devices: 71.4 us -> 54.9 us
  waiting for transfers between devices: 264 us -> 253 us
  matrix products: 71.4 us -> 77.4 us
    psum x0 -> x4, blocking collectives: none -> 35.3 us  [normalize(): all_squares = lax.psum(square_sum, 'kv')]
    ppermute x12 -> x0, starting transfers between devices: 14.8 us -> none  [normalize(): lax.ppermute(square_sum, 'kv', [(j, (j + shift) % count) for j in range(c...]
    ppermute x12 -> x0, waiting for transfers between devices: 9.84 us -> none  [normalize(): lax.ppermute(square_sum, 'kv', [(j, (j + shift) % count) for j in range(c...]
    dot_general x2, matrix products: 8.64 us -> 15.2 us  [body(): jnp.dot(tokens, w_gate, preferred_element_type=jnp.float32)]
    unnamed x50 -> x34, local copies, waits for them, and re-layouts: 10.8 us -> 10.8 us
  transfers between devices with their start and end apart: 58 -> 46, of which waited for: 51 -> 41; matrix products, arithmetic and copies ran while one was open for 2% -> 2% of each run, Pallas kernels for 0% -> 0%
where the time goes in v12:
time: 529 us; the launch traced here: 521 us
  waiting for transfers between devices  253 us (48%)
  matrix products  77.4 us (15%)
  blocking collectives  73.7 us (14%)
  starting transfers between devices  54.9 us (10%)
  other arithmetic  29.8 us (6%)
  local copies, waits for them, and re-layouts  17.1 us (3%)
  between operations  14.9 us (3%)
    reduce_scatter x2, waiting for transfers between devices, body(): lax.psum_scatter(jnp.concatenate([jnp.dot(tokens, w_gate, preferred_eleme...  143 us
    ppermute x18, waiting for transfers between devices, gather_by_permute(): lax.ppermute(block, axis, [(j, (j + shift) % count) for j in range(count)])  46.4 us
    ppermute x18, waiting for transfers between devices, scatter_sum(): total = total + lax.ppermute(piece, axis, pairs)  42.6 us
    psum x4, blocking collectives, normalize(): all_squares = lax.psum(square_sum, 'kv')  35.3 us
    ppermute x18, starting transfers between devices, gather_by_permute(): lax.ppermute(block, axis, [(j, (j + shift) % count) for j in range(count)])  26.2 us
    all_gather x2, blocking collectives, body(): tokens = lax.all_gather(normed_mlp, 'req', axis=0, tiled=True)  19.3 us
    ppermute x18, starting transfers between devices, scatter_sum(): total = total + lax.ppermute(piece, axis, pairs)  19.2 us
    all_to_all x2, blocking collectives, rows_for_weights(): return lax.all_to_all(wide, 'req', 0, 0, tiled=True)  19 us
  transfers between devices with their start and end apart: 46, of which 41 were waited for; matrix products, arithmetic and copies ran while one was open for 2% of the time, Pallas kernels for 0%

profile of v12, /device:TPU:18, one launch (start us, length us, event | category | flops | bytes accessed | tf_op | source)
XLA Modules:
  0.0 520.6 jit_solution(4221519226833482260)
XLA Ops:
  7.6 9.0 %psum.28 = f32[16]{0:T(128)S(1)} all-reduce(f32[16]{0:T(128)S(1)} %fusion.205), channel_id=1, replica_groups=mesh['req'=8,'kv'=4] {'kv'}, use_global_device_ids=true, to_apply=%region_2.0 | all-reduce | flops 16 | bytes 128 | tf_op jit(solution)/shard_map/psum | solution.py:87
  18.2 3.4 collective-permute-start.1
  30.6 4.3 all-to-all-start
  36.1 4.2 all-to-all-done
  41.7 2.9 fusion.275
  51.5 4.0 collective-permute-done.4
  55.5 2.8 collective-permute-done.6
  60.8 2.8 fusion.4
  63.7 3.6 fusion.8
  78.6 4.6 all-to-all-start.1
  83.4 5.3 %all-to-all-done.1 = bf16[8,16,1024]{2,1,0:T(8,128)(2,1)S(1)} async-done(((bf16[8,16,1024]{2,1,0:T(8,128)(2,1)}), bf16[8,16,1024]{2,1,0:T(8,128)(2,1)S(1)}, u32[]{:S(2)}, u32[]{:S(2)}) %all-to-all-start.1) | async-done | bytes 262176 | tf_op jit(solution)/shard_map/all_to_all | solution.py:65
  89.6 3.0 fusion.195
  97.7 3.3 collective-permute-done.11
  104.8 10.3 %psum.29 = f32[16]{0:T(128)S(1)} all-reduce(f32[16]{0:T(128)S(1)} %get-tuple-element.69), channel_id=1, replica_groups=mesh['req'=8,'kv'=4] {'kv'}, use_global_device_ids=true, to_apply=%region_9.17 | all-reduce | flops 16 | bytes 128 | tf_op jit(solution)/shard_map/psum | solution.py:87
  115.1 9.6 %all_gather.6 = bf16[128,2048]{1,0:T(8,128)(2,1)S(1)} all-gather(bf16[16,2048]{1,0:T(8,128)(2,1)S(1)} %multiply_convert_fusion.2), channel_id=1, replica_groups=mesh['req'=8,'kv'=4] {'req'}, dimensions={0}, use_global_device_ids=true | all-gather | bytes 589824 | tf_op jit(solution)/shard_map/all_gather | solution.py:229
  124.7 7.6 %fusion.286 = f32[128,3696]{0,1:T(8,128)S(1)} fusion(bf16[128,2048]{1,0:T(8,128)(2,1)S(1)} %all_gather.6, bf16[2048,3696]{0,1:T(8,128)(2,1)} %param.48), kind=kOutput, calls=%fused_computation.408 | convolution fusion | flops 1937768448 | bytes 17555456 | tf_op jit(solution)/shard_map/dot_general | solution.py:235
  132.3 7.6 %fusion.285 = f32[128,3696]{0,1:T(8,128)S(1)} fusion(bf16[128,2048]{1,0:T(8,128)(2,1)S(1)} %all_gather.6, bf16[2048,3696]{0,1:T(8,128)(2,1)} %param.47), kind=kOutput, calls=%fused_computation.407 | convolution fusion | flops 1937768448 | bytes 17555456 | tf_op jit(solution)/shard_map/dot_general | solution.py:234
  142.0 5.3 %copy.147 = f32[128,7392]{1,0:T(8,128)} copy(f32[128,7392]{0,1:T(8,128)} %pad_maximum_fusion) | data formatting | bytes 7569408
  147.4 71.3 %reduce-scatter.7.cloned.1.call-done = f32[32,7392]{1,0:T(8,128)} async-done(((f32[128,7392]{1,0:T(8,128)}), f32[32,7392]{1,0:T(8,128)}) %reduce-scatter.7.cloned.1.call-update) | async-done | bytes 946192 | tf_op jit(solution)/shard_map/reduce_scatter | solution.py:231
  223.7 8.3 %collective-permute-done.15 = bf16[32,3696]{1,0:T(8,128)(2,1)S(1)} collective-permute-done((bf16[32,3696]{1,0:T(8,128)(2,1)S(1)}, bf16[32,3696]{1,0:T(8,128)(2,1)S(1)}, u32[]{:S(2)}, u32[]{:S(2)}) %collective-permute-start.15) | collective-permute-done | bytes 236576 | tf_op jit(solution)/shard_map/ppermute | solution.py:52
  232.0 8.9 %collective-permute-done.14 = bf16[32,3696]{1,0:T(8,128)(2,1)S(1)} collective-permute-done((bf16[32,3696]{1,0:T(8,128)(2,1)S(1)}, bf16[32,3696]{1,0:T(8,128)(2,1)S(1)}, u32[]{:S(2)}, u32[]{:S(2)}) %collective-permute-start.14) | collective-permute-done | bytes 236576 | tf_op jit(solution)/shard_map/ppermute | solution.py:52
  244.0 7.7 %fusion = f32[4,2,16,2048]{3,2,1,0:T(8,128)S(1)} fusion(bf16[4,2,16,3696]{3,2,1,0:T(8,128)(2,1)S(1)} %bitcast.498, bf16[3696,2048]{1,0:T(8,128)(2,1)} %param.49), kind=kOutput, calls=%fused_computation.6 | convolution fusion | flops 1937768448 | bytes 17133568 | tf_op jit(solution)/shard_map/dot_general | solution.py:248
  257.6 2.7 collective-permute-done.18
  260.3 3.0 collective-permute-done.20
  264.1 7.0 %psum.30 = f32[16]{0:T(128)S(1)} all-reduce(f32[16]{0:T(128)S(1)} %get-tuple-element.67), channel_id=1, replica_groups=mesh['req'=8,'kv'=4] {'kv'}, use_global_device_ids=true, to_apply=%region_13.22 | all-reduce | flops 16 | bytes 128 | tf_op jit(solution)/shard_map/psum | solution.py:87
  271.2 3.5 collective-permute-start.22
  279.6 9.1 %all_to_all.48 = bf16[8,16,1024]{2,1,0:T(8,128)(2,1)S(1)} all-to-all(bf16[8,16,1024]{2,1,0:T(8,128)(2,1)S(1)} %bitcast.501), channel_id=1, replica_groups=mesh['req'=8,'kv'=4] {'req'}, dimensions={0} | all-to-all | bytes 524288 | tf_op jit(solution)/shard_map/all_to_all | solution.py:65
  290.1 2.9 fusion.278
  298.7 3.9 collective-permute-done.25
  302.7 2.8 collective-permute-done.27
  308.0 2.8 fusion.6
  310.8 3.6 fusion.12
  318.2 2.8 collective-permute-start.30
  323.2 2.8 collective-permute-start.28
  328.6 9.9 %all_to_all.49 = bf16[8,16,1024]{2,1,0:T(8,128)(2,1)S(1)} all-to-all(bf16[8,16,1024]{2,1,0:T(8,128)(2,1)S(1)} %bitcast.502), channel_id=1, replica_groups=mesh['req'=8,'kv'=4] {'req'}, dimensions={0} | all-to-all | bytes 524288 | tf_op jit(solution)/shard_map/all_to_all | solution.py:65
  339.4 2.9 fusion.193
  347.5 3.3 collective-permute-done.32
  354.5 9.1 %psum.31 = f32[16]{0:T(128)S(1)} all-reduce(f32[16]{0:T(128)S(1)} %get-tuple-element.61), channel_id=1, replica_groups=mesh['req'=8,'kv'=4] {'kv'}, use_global_device_ids=true, to_apply=%region_19.28 | all-reduce | flops 16 | bytes 128 | tf_op jit(solution)/shard_map/psum | solution.py:87
  363.7 9.8 %all_gather.7 = bf16[128,2048]{1,0:T(8,128)(2,1)S(1)} all-gather(bf16[16,2048]{1,0:T(8,128)(2,1)S(1)} %multiply_convert_fusion), channel_id=1, replica_groups=mesh['req'=8,'kv'=4] {'req'}, dimensions={0}, use_global_device_ids=true | all-gather | bytes 589824 | tf_op jit(solution)/shard_map/all_gather | solution.py:229
  373.5 7.6 %fusion.288 = f32[128,3696]{0,1:T(8,128)S(1)} fusion(bf16[128,2048]{1,0:T(8,128)(2,1)S(1)} %all_gather.7, bf16[2048,3696]{0,1:T(8,128)(2,1)} %param.48), kind=kOutput, calls=%fused_computation.410 | convolution fusion | flops 1937768448 | bytes 17555456 | tf_op jit(solution)/shard_map/dot_general | solution.py:235
  381.1 7.6 %fusion.287 = f32[128,3696]{0,1:T(8,128)S(1)} fusion(bf16[128,2048]{1,0:T(8,128)(2,1)S(1)} %all_gather.7, bf16[2048,3696]{0,1:T(8,128)(2,1)} %param.47), kind=kOutput, calls=%fused_computation.409 | convolution fusion | flops 1937768448 | bytes 17555456 | tf_op jit(solution)/shard_map/dot_general | solution.py:234
  390.8 5.3 %copy.149 = f32[128,7392]{1,0:T(8,128)} copy(f32[128,7392]{0,1:T(8,128)} %pad_maximum_fusion.1) | data formatting | bytes 7569408
  396.1 71.4 %reduce-scatter.9.cloned.1.call-done = f32[32,7392]{1,0:T(8,128)} async-done(((f32[128,7392]{1,0:T(8,128)}), f32[32,7392]{1,0:T(8,128)}) %reduce-scatter.9.cloned.1.call-update) | async-done | bytes 946192 | tf_op jit(solution)/shard_map/reduce_scatter | solution.py:231
  472.5 8.3 %collective-permute-done.36 = bf16[32,3696]{1,0:T(8,128)(2,1)S(1)} collective-permute-done((bf16[32,3696]{1,0:T(8,128)(2,1)S(1)}, bf16[32,3696]{1,0:T(8,128)(2,1)S(1)}, u32[]{:S(2)}, u32[]{:S(2)}) %collective-permute-start.36) | collective-permute-done | bytes 236576 | tf_op jit(solution)/shard_map/ppermute | solution.py:52
  480.8 8.8 %collective-permute-done.35 = bf16[32,3696]{1,0:T(8,128)(2,1)S(1)} collective-permute-done((bf16[32,3696]{1,0:T(8,128)(2,1)S(1)}, bf16[32,3696]{1,0:T(8,128)(2,1)S(1)}, u32[]{:S(2)}, u32[]{:S(2)}) %collective-permute-start.35) | collective-permute-done | bytes 236576 | tf_op jit(solution)/shard_map/ppermute | solution.py:52
  492.8 7.8 %fusion.2 = f32[4,2,16,2048]{3,2,0,1:T(8,128)S(1)} fusion(bf16[3696,2048]{1,0:T(8,128)(2,1)} %param.49, bf16[4,2,16,3696]{3,2,1,0:T(8,128)(2,1)S(1)} %bitcast.497), kind=kOutput, calls=%fused_computation.8 | convolution fusion | flops 1937768448 | bytes 17133568 | tf_op jit(solution)/shard_map/dot_general | solution.py:248
  506.3 2.8 collective-permute-done.39
  509.1 3.0 collective-permute-done.41
  (241 shorter events, 111.3 us)
Async XLA Ops:
  6.5 34.6 %copy-start = (bf16[1024,256]{1,0:T(8,128)(2,1)S(1)}, bf16[1024,256]{1,0:T(8,128)(2,1)}, u32[]{:S(2)}) copy-start(bf16[1024,256]{1,0:T(8,128)(2,1)} %param.40) | copy-start | bytes 1572868
  6.5 34.9 %copy-start.2 = (bf16[1024,256]{1,0:T(8,128)(2,1)S(1)}, bf16[1024,256]{1,0:T(8,128)(2,1)}, u32[]{:S(2)}) copy-start(bf16[1024,256]{1,0:T(8,128)(2,1)} %param.41) | copy-start | bytes 1572868
  18.2 11.2 %collective-permute-start.1 = (bf16[16,2048]{1,0:T(8,128)(2,1)S(1)}, bf16[16,2048]{1,0:T(8,128)(2,1)S(1)}, u32[]{:S(2)}, u32[]{:S(2)}) collective-permute-start(bf16[16,2048]{1,0:T(8,128)(2,1)S(1)} %fusion.207), channel_id=1, source_target_pairs={{0,2},{1,3},{2,0},{3,1},{4,6},{5,7},{6,4},{7,5},{8,10},{9,11},{10,... | collective-permute-start | bytes 196616 | tf_op jit(solution)/shard_map/ppermute | solution.py:52
  21.6 7.8 %collective-permute-start = (bf16[16,2048]{1,0:T(8,128)(2,1)S(1)}, bf16[16,2048]{1,0:T(8,128)(2,1)S(1)}, u32[]{:S(2)}, u32[]{:S(2)}) collective-permute-start(bf16[16,2048]{1,0:T(8,128)(2,1)S(1)} %fusion.207), channel_id=1, source_target_pairs={{0,3},{1,0},{2,1},{3,2},{4,7},{5,4},{6,5},{7,6},{8,11},{9,8},{10,9... | collective-permute-start | bytes 196616 | tf_op jit(solution)/shard_map/ppermute | solution.py:52
  21.6 7.8 %collective-permute-start.2 = (bf16[16,2048]{1,0:T(8,128)(2,1)S(1)}, bf16[16,2048]{1,0:T(8,128)(2,1)S(1)}, u32[]{:S(2)}, u32[]{:S(2)}) collective-permute-start(bf16[16,2048]{1,0:T(8,128)(2,1)S(1)} %fusion.207), channel_id=1, source_target_pairs={{0,1},{1,2},{2,3},{3,0},{4,5},{5,6},{6,7},{7,4},{8,9},{9,10},{10,1... | collective-permute-start | bytes 196616 | tf_op jit(solution)/shard_map/ppermute | solution.py:52
  30.6 9.7 %all-to-all-start = ((bf16[8,16,1024]{2,1,0:T(8,128)(2,1)}), bf16[8,16,1024]{2,1,0:T(8,128)(2,1)S(1)}, u32[]{:S(2)}, u32[]{:S(2)}) async-start(bf16[8,16,1024]{2,1,0:T(8,128)(2,1)} %bitcast.7), calls=%async_computation | async-start | bytes 524288 | tf_op jit(solution)/shard_map/all_to_all | solution.py:65
  44.9 2.3 collective-permute-start.3
  48.4 7.1 %collective-permute-start.4 = (f32[16,2560]{1,0:T(8,128)S(1)}, f32[16,2560]{1,0:T(8,128)S(1)}, u32[]{:S(2)}, u32[]{:S(2)}) collective-permute-start(f32[16,2560]{1,0:T(8,128)S(1)} %get-tuple-element.78), channel_id=1, source_target_pairs={{0,8},{4,12},{8,16},{12,20},{16,24},{20,28},{24,0},{28,4},{1,9},{5... | collective-permute-start | bytes 491528 | tf_op jit(solution)/shard_map/ppermute | solution.py:42
  49.9 8.4 %collective-permute-start.6 = (f32[16,2560]{1,0:T(8,128)S(1)}, f32[16,2560]{1,0:T(8,128)S(1)}, u32[]{:S(2)}, u32[]{:S(2)}) collective-permute-start(f32[16,2560]{1,0:T(8,128)S(1)} %get-tuple-element.79), channel_id=1, source_target_pairs={{0,24},{4,28},{8,0},{12,4},{16,8},{20,12},{24,16},{28,20},{1,25},{... | collective-permute-start | bytes 491528 | tf_op jit(solution)/shard_map/ppermute | solution.py:42
  50.5 9.2 %collective-permute-start.5 = (f32[16,2560]{1,0:T(8,128)S(1)}, f32[16,2560]{1,0:T(8,128)S(1)}, u32[]{:S(2)}, u32[]{:S(2)}) collective-permute-start(f32[16,2560]{1,0:T(8,128)S(1)} %get-tuple-element.80), channel_id=1, source_target_pairs={{0,16},{4,20},{8,24},{12,28},{16,0},{20,4},{24,8},{28,12},{1,17},{... | collective-permute-start | bytes 491528 | tf_op jit(solution)/shard_map/ppermute | solution.py:42
  71.1 5.7 %collective-permute-start.9 = (bf16[16,2048]{1,0:T(8,128)(2,1)S(1)}, bf16[16,2048]{1,0:T(8,128)(2,1)S(1)}, u32[]{:S(2)}, u32[]{:S(2)}) collective-permute-start(bf16[16,2048]{1,0:T(8,128)(2,1)S(1)} %bitcast.523), channel_id=1, source_target_pairs={{0,1},{1,2},{2,3},{3,0},{4,5},{5,6},{6,7},{7,4},{8,9},{9,10},{10,1... | collective-permute-start | bytes 196616 | tf_op jit(solution)/shard_map/ppermute | solution.py:52
  71.5 5.3 %collective-permute-start.8 = (bf16[16,2048]{1,0:T(8,128)(2,1)S(1)}, bf16[16,2048]{1,0:T(8,128)(2,1)S(1)}, u32[]{:S(2)}, u32[]{:S(2)}) collective-permute-start(bf16[16,2048]{1,0:T(8,128)(2,1)S(1)} %bitcast.524), channel_id=1, source_target_pairs={{0,2},{1,3},{2,0},{3,1},{4,6},{5,7},{6,4},{7,5},{8,10},{9,11},{10,... | collective-permute-start | bytes 196616 | tf_op jit(solution)/shard_map/ppermute | solution.py:52
  72.6 5.0 collective-permute-start.7
  78.6 10.1 %all-to-all-start.1 = ((bf16[8,16,1024]{2,1,0:T(8,128)(2,1)}), bf16[8,16,1024]{2,1,0:T(8,128)(2,1)S(1)}, u32[]{:S(2)}, u32[]{:S(2)}) async-start(bf16[8,16,1024]{2,1,0:T(8,128)(2,1)} %bitcast.41), calls=%async_computation.1 | async-start | bytes 524288 | tf_op jit(solution)/shard_map/all_to_all | solution.py:65
  83.2 135.5 %reduce-scatter.7.cloned.1.call-start = ((), (), s32[]{:S(2)}) async-start(), calls=%async_computation.6 | async-start | bytes 4751360 | tf_op jit(solution)/shard_map/reduce_scatter | solution.py:231
  92.6 2.0 collective-permute-start.10
  94.7 6.3 %collective-permute-start.11 = (f32[16,2048]{1,0:T(8,128)S(1)}, f32[16,2048]{1,0:T(8,128)S(1)}, u32[]{:S(2)}, u32[]{:S(2)}) collective-permute-start(f32[16,2048]{1,0:T(8,128)S(1)} %get-tuple-element.90), channel_id=1, source_target_pairs={{0,8},{4,12},{8,16},{12,20},{16,24},{20,28},{24,0},{28,4},{1,9},{5... | collective-permute-start | bytes 393224 | tf_op jit(solution)/shard_map/ppermute | solution.py:42
  96.2 7.0 %collective-permute-start.13 = (f32[16,2048]{1,0:T(8,128)S(1)}, f32[16,2048]{1,0:T(8,128)S(1)}, u32[]{:S(2)}, u32[]{:S(2)}) collective-permute-start(f32[16,2048]{1,0:T(8,128)S(1)} %get-tuple-element.91), channel_id=1, source_target_pairs={{0,24},{4,28},{8,0},{12,4},{16,8},{20,12},{24,16},{28,20},{1,25},{... | collective-permute-start | bytes 393224 | tf_op jit(solution)/shard_map/ppermute | solution.py:42
  96.8 7.8 %collective-permute-start.12 = (f32[16,2048]{1,0:T(8,128)S(1)}, f32[16,2048]{1,0:T(8,128)S(1)}, u32[]{:S(2)}, u32[]{:S(2)}) collective-permute-start(f32[16,2048]{1,0:T(8,128)S(1)} %get-tuple-element.92), channel_id=1, source_target_pairs={{0,16},{4,20},{8,24},{12,28},{16,0},{20,4},{24,8},{28,12},{1,17},{... | collective-permute-start | bytes 393224 | tf_op jit(solution)/shard_map/ppermute | solution.py:42
  147.3 320.2 %reduce-scatter.9.cloned.1.call-start = ((), (), s32[]{:S(2)}) async-start(), calls=%async_computation.7 | async-start | bytes 4751360 | tf_op jit(solution)/shard_map/reduce_scatter | solution.py:231
  220.1 11.9 %collective-permute-start.15 = (bf16[32,3696]{1,0:T(8,128)(2,1)S(1)}, bf16[32,3696]{1,0:T(8,128)(2,1)S(1)}, u32[]{:S(2)}, u32[]{:S(2)}) collective-permute-start(bf16[32,3696]{1,0:T(8,128)(2,1)S(1)} %fusion.164), channel_id=1, source_target_pairs={{0,2},{1,3},{2,0},{3,1},{4,6},{5,7},{6,4},{7,5},{8,10},{9,11},{10,... | collective-permute-start | bytes 709640 | tf_op jit(solution)/shard_map/ppermute | solution.py:52
  220.3 20.6 %collective-permute-start.14 = (bf16[32,3696]{1,0:T(8,128)(2,1)S(1)}, bf16[32,3696]{1,0:T(8,128)(2,1)S(1)}, u32[]{:S(2)}, u32[]{:S(2)}) collective-permute-start(bf16[32,3696]{1,0:T(8,128)(2,1)S(1)} %fusion.164), channel_id=1, source_target_pairs={{0,3},{1,0},{2,1},{3,2},{4,7},{5,4},{6,5},{7,6},{8,11},{9,8},{10,9... | collective-permute-start | bytes 709640 | tf_op jit(solution)/shard_map/ppermute | solution.py:52
  222.1 20.8 %collective-permute-start.16 = (bf16[32,3696]{1,0:T(8,128)(2,1)S(1)}, bf16[32,3696]{1,0:T(8,128)(2,1)S(1)}, u32[]{:S(2)}, u32[]{:S(2)}) collective-permute-start(bf16[32,3696]{1,0:T(8,128)(2,1)S(1)} %fusion.164), channel_id=1, source_target_pairs={{0,1},{1,2},{2,3},{3,0},{4,5},{5,6},{6,7},{7,4},{8,9},{9,10},{10,1... | collective-permute-start | bytes 709640 | tf_op jit(solution)/shard_map/ppermute | solution.py:52
  251.8 2.0 collective-permute-start.17
  253.9 6.4 %collective-permute-start.18 = (f32[16,2048]{1,0:T(8,128)S(1)}, f32[16,2048]{1,0:T(8,128)S(1)}, u32[]{:S(2)}, u32[]{:S(2)}) collective-permute-start(f32[16,2048]{1,0:T(8,128)S(1)} %get-tuple-element.87), channel_id=1, source_target_pairs={{0,8},{4,12},{8,16},{12,20},{16,24},{20,28},{24,0},{28,4},{1,9},{5... | collective-permute-start | bytes 393224 | tf_op jit(solution)/shard_map/ppermute | solution.py:42
  255.4 7.9 %collective-permute-start.20 = (f32[16,2048]{1,0:T(8,128)S(1)}, f32[16,2048]{1,0:T(8,128)S(1)}, u32[]{:S(2)}, u32[]{:S(2)}) collective-permute-start(f32[16,2048]{1,0:T(8,128)S(1)} %get-tuple-element.88), channel_id=1, source_target_pairs={{0,24},{4,28},{8,0},{12,4},{16,8},{20,12},{24,16},{28,20},{1,25},{... | collective-permute-start | bytes 393224 | tf_op jit(solution)/shard_map/ppermute | solution.py:42
  256.2 7.8 %collective-permute-start.19 = (f32[16,2048]{1,0:T(8,128)S(1)}, f32[16,2048]{1,0:T(8,128)S(1)}, u32[]{:S(2)}, u32[]{:S(2)}) collective-permute-start(f32[16,2048]{1,0:T(8,128)S(1)} %get-tuple-element.89), channel_id=1, source_target_pairs={{0,16},{4,20},{8,24},{12,28},{16,0},{20,4},{24,8},{28,12},{1,17},{... | collective-permute-start | bytes 393224 | tf_op jit(solution)/shard_map/ppermute | solution.py:42
  271.2 5.9 %collective-permute-start.22 = (bf16[16,2048]{1,0:T(8,128)(2,1)S(1)}, bf16[16,2048]{1,0:T(8,128)(2,1)S(1)}, u32[]{:S(2)}, u32[]{:S(2)}) collective-permute-start(bf16[16,2048]{1,0:T(8,128)(2,1)S(1)} %multiply_convert_fusion.1), channel_id=1, source_target_pairs={{0,2},{1,3},{2,0},{3,1},{4,6},{5,7},{6,4},{7,5},{8,10},{9,11},{10,... | collective-permute-start | bytes 196616 | tf_op jit(solution)/shard_map/ppermute | solution.py:52
  274.7 4.3 collective-permute-start.21
  274.7 4.5 collective-permute-start.23
  293.3 2.2 collective-permute-start.24
  295.6 7.1 %collective-permute-start.25 = (f32[16,2560]{1,0:T(8,128)S(1)}, f32[16,2560]{1,0:T(8,128)S(1)}, u32[]{:S(2)}, u32[]{:S(2)}) collective-permute-start(f32[16,2560]{1,0:T(8,128)S(1)} %get-tuple-element.75), channel_id=1, source_target_pairs={{0,8},{4,12},{8,16},{12,20},{16,24},{20,28},{24,0},{28,4},{1,9},{5... | collective-permute-start | bytes 491528 | tf_op jit(solution)/shard_map/ppermute | solution.py:42
  297.1 8.4 %collective-permute-start.27 = (f32[16,2560]{1,0:T(8,128)S(1)}, f32[16,2560]{1,0:T(8,128)S(1)}, u32[]{:S(2)}, u32[]{:S(2)}) collective-permute-start(f32[16,2560]{1,0:T(8,128)S(1)} %get-tuple-element.76), channel_id=1, source_target_pairs={{0,24},{4,28},{8,0},{12,4},{16,8},{20,12},{24,16},{28,20},{1,25},{... | collective-permute-start | bytes 491528 | tf_op jit(solution)/shard_map/ppermute | solution.py:42
  297.6 9.2 %collective-permute-start.26 = (f32[16,2560]{1,0:T(8,128)S(1)}, f32[16,2560]{1,0:T(8,128)S(1)}, u32[]{:S(2)}, u32[]{:S(2)}) collective-permute-start(f32[16,2560]{1,0:T(8,128)S(1)} %get-tuple-element.77), channel_id=1, source_target_pairs={{0,16},{4,20},{8,24},{12,28},{16,0},{20,4},{24,8},{28,12},{1,17},{... | collective-permute-start | bytes 491528 | tf_op jit(solution)/shard_map/ppermute | solution.py:42
  318.2 7.8 %collective-permute-start.30 = (bf16[16,2048]{1,0:T(8,128)(2,1)S(1)}, bf16[16,2048]{1,0:T(8,128)(2,1)S(1)}, u32[]{:S(2)}, u32[]{:S(2)}) collective-permute-start(bf16[16,2048]{1,0:T(8,128)(2,1)S(1)} %bitcast.526), channel_id=1, source_target_pairs={{0,1},{1,2},{2,3},{3,0},{4,5},{5,6},{6,7},{7,4},{8,9},{9,10},{10,1... | collective-permute-start | bytes 196616 | tf_op jit(solution)/shard_map/ppermute | solution.py:52
  321.0 5.7 %collective-permute-start.29 = (bf16[16,2048]{1,0:T(8,128)(2,1)S(1)}, bf16[16,2048]{1,0:T(8,128)(2,1)S(1)}, u32[]{:S(2)}, u32[]{:S(2)}) collective-permute-start(bf16[16,2048]{1,0:T(8,128)(2,1)S(1)} %bitcast.527), channel_id=1, source_target_pairs={{0,2},{1,3},{2,0},{3,1},{4,6},{5,7},{6,4},{7,5},{8,10},{9,11},{10,... | collective-permute-start | bytes 196616 | tf_op jit(solution)/shard_map/ppermute | solution.py:52
  323.2 5.0 collective-permute-start.28
  342.4 2.0 collective-permute-start.31
  344.5 6.3 %collective-permute-start.32 = (f32[16,2048]{1,0:T(8,128)S(1)}, f32[16,2048]{1,0:T(8,128)S(1)}, u32[]{:S(2)}, u32[]{:S(2)}) collective-permute-start(f32[16,2048]{1,0:T(8,128)S(1)} %get-tuple-element.84), channel_id=1, source_target_pairs={{0,8},{4,12},{8,16},{12,20},{16,24},{20,28},{24,0},{28,4},{1,9},{5... | collective-permute-start | bytes 393224 | tf_op jit(solution)/shard_map/ppermute | solution.py:42
  346.0 7.0 %collective-permute-start.34 = (f32[16,2048]{1,0:T(8,128)S(1)}, f32[16,2048]{1,0:T(8,128)S(1)}, u32[]{:S(2)}, u32[]{:S(2)}) collective-permute-start(f32[16,2048]{1,0:T(8,128)S(1)} %get-tuple-element.85), channel_id=1, source_target_pairs={{0,24},{4,28},{8,0},{12,4},{16,8},{20,12},{24,16},{28,20},{1,25},{... | collective-permute-start | bytes 393224 | tf_op jit(solution)/shard_map/ppermute | solution.py:42
  346.6 7.8 %collective-permute-start.33 = (f32[16,2048]{1,0:T(8,128)S(1)}, f32[16,2048]{1,0:T(8,128)S(1)}, u32[]{:S(2)}, u32[]{:S(2)}) collective-permute-start(f32[16,2048]{1,0:T(8,128)S(1)} %get-tuple-element.86), channel_id=1, source_target_pairs={{0,16},{4,20},{8,24},{12,28},{16,0},{20,4},{24,8},{28,12},{1,17},{... | collective-permute-start | bytes 393224 | tf_op jit(solution)/shard_map/ppermute | solution.py:42
  468.9 11.9 %collective-permute-start.36 = (bf16[32,3696]{1,0:T(8,128)(2,1)S(1)}, bf16[32,3696]{1,0:T(8,128)(2,1)S(1)}, u32[]{:S(2)}, u32[]{:S(2)}) collective-permute-start(bf16[32,3696]{1,0:T(8,128)(2,1)S(1)} %fusion.163), channel_id=1, source_target_pairs={{0,2},{1,3},{2,0},{3,1},{4,6},{5,7},{6,4},{7,5},{8,10},{9,11},{10,... | collective-permute-start | bytes 709640 | tf_op jit(solution)/shard_map/ppermute | solution.py:52
  469.1 20.5 %collective-permute-start.35 = (bf16[32,3696]{1,0:T(8,128)(2,1)S(1)}, bf16[32,3696]{1,0:T(8,128)(2,1)S(1)}, u32[]{:S(2)}, u32[]{:S(2)}) collective-permute-start(bf16[32,3696]{1,0:T(8,128)(2,1)S(1)} %fusion.163), channel_id=1, source_target_pairs={{0,3},{1,0},{2,1},{3,2},{4,7},{5,4},{6,5},{7,6},{8,11},{9,8},{10,9... | collective-permute-start | bytes 709640 | tf_op jit(solution)/shard_map/ppermute | solution.py:52
  470.8 20.8 %collective-permute-start.37 = (bf16[32,3696]{1,0:T(8,128)(2,1)S(1)}, bf16[32,3696]{1,0:T(8,128)(2,1)S(1)}, u32[]{:S(2)}, u32[]{:S(2)}) collective-permute-start(bf16[32,3696]{1,0:T(8,128)(2,1)S(1)} %fusion.163), channel_id=1, source_target_pairs={{0,1},{1,2},{2,3},{3,0},{4,5},{5,6},{6,7},{7,4},{8,9},{9,10},{10,1... | collective-permute-start | bytes 709640 | tf_op jit(solution)/shard_map/ppermute | solution.py:52
  500.7 2.0 collective-permute-start.38
  502.8 6.4 %collective-permute-start.39 = (f32[16,2048]{1,0:T(8,128)S(1)}, f32[16,2048]{1,0:T(8,128)S(1)}, u32[]{:S(2)}, u32[]{:S(2)}) collective-permute-start(f32[16,2048]{1,0:T(8,128)S(1)} %get-tuple-element.81), channel_id=1, source_target_pairs={{0,8},{4,12},{8,16},{12,20},{16,24},{20,28},{24,0},{28,4},{1,9},{5... | collective-permute-start | bytes 393224 | tf_op jit(solution)/shard_map/ppermute | solution.py:42
  504.3 7.9 %collective-permute-start.41 = (f32[16,2048]{1,0:T(8,128)S(1)}, f32[16,2048]{1,0:T(8,128)S(1)}, u32[]{:S(2)}, u32[]{:S(2)}) collective-permute-start(f32[16,2048]{1,0:T(8,128)S(1)} %get-tuple-element.82), channel_id=1, source_target_pairs={{0,24},{4,28},{8,0},{12,4},{16,8},{20,12},{24,16},{28,20},{1,25},{... | collective-permute-start | bytes 393224 | tf_op jit(solution)/shard_map/ppermute | solution.py:42
  504.8 7.8 %collective-permute-start.40 = (f32[16,2048]{1,0:T(8,128)S(1)}, f32[16,2048]{1,0:T(8,128)S(1)}, u32[]{:S(2)}, u32[]{:S(2)}) collective-permute-start(f32[16,2048]{1,0:T(8,128)S(1)} %get-tuple-element.83), channel_id=1, source_target_pairs={{0,16},{4,20},{8,24},{12,28},{16,0},{20,4},{24,8},{28,12},{1,17},{... | collective-permute-start | bytes 393224 | tf_op jit(solution)/shard_map/ppermute | solution.py:42
  (11 other events, 90.0 us)
Sparse Core Ops, SparseCore 0:
  147.4 71.2 reduce-scatter.6
  396.2 71.2 reduce-scatter.8
